TPU v7x, 32 devices: a whole 2x2x4 slice. The times are simulated.
32 devices in a mesh: grp: 4 (over x, core), tp: 8 (over z, y).
Axes of the slice: x: 2, y: 2, z: 4, core: 2. Of those that a mesh axis runs over, the one named last changes fastest.
Arguments:
- hidden_in: bfloat16 [3072, 3584], P('grp'), may hold values from -6 to 6
- lengths: int32 [8, 8], P('grp'), may hold values from 1 to 96, 384 in all within a row
- dest: int32 [64, 1], P('grp'), may hold values from 0 to 3; in each aligned block of 16 rows (0 to 15, 16 to 31, ...) at most 4 rows name the same one
- attn_gain: float32 [3584], replicated, may hold values from 0.6 to 8
- q_weight: bfloat16 [3584, 2048], P('grp', 'tp'), may hold values from -0.09375 to 0.09375
- k_weight: bfloat16 [3584, 512], P('grp', 'tp'), may hold values from -0.09375 to 0.09375
- v_weight: bfloat16 [3584, 512], P('grp', 'tp'), may hold values from -0.09375 to 0.09375
- o_weight: bfloat16 [3584, 2048], P('grp', 'tp'), may hold values from -0.125 to 0.125
- ffn_gain: float32 [3584], replicated, may hold values from 0.1 to 1.9
- gate_weight: bfloat16 [3584, 10240], P('grp', 'tp'), may hold values from -0.09375 to 0.09375
- up_weight: bfloat16 [3584, 10240], P('grp', 'tp'), may hold values from -0.09375 to 0.09375
- down_weight: bfloat16 [3584, 10240], P('grp', 'tp'), may hold values from -0.0625 to 0.0625
Outputs:
- bank_in: bfloat16 [4, 4, 4, 3584], P('grp', None, None, 'tp')
Inputs may be any that keep to these rules, and one draw needn't show every extreme that they name: Each block's 8 lengths sum to 384. `dest`: among the programs of one index of grp, no bank shard is named by more than 4.
All inputs are finite; a program needn't handle non-finite values.
Results may differ from a plain program's by a relative error of at most 0.015.
The roundings to bfloat16 on the way count: a program that leaves them out, or rounds other values in their place, can miss the bound.
Values may be sent and summed in bfloat16 or wider, within the bound.
No kernel may reach another device: no remote copies, remote signals or barrier semaphores. Data moves between devices by JAX's collectives and lax.ppermute only.
A program may use at most 128 MiB of HBM per device.

v0:
```python
import jax
import jax.numpy as jnp
from jax import lax
from jax.sharding import PartitionSpec as P

HEAD_SIZE = 128
KVH = 4
HEADS = 16


EPSILON = 1e-06
HIGH = lax.Precision.HIGHEST


def rms_scale(rows, gain):
    rows = rows.astype(jnp.float32)
    factor = lax.rsqrt(jnp.mean(rows * rows, axis=1, keepdims=True) + EPSILON)
    return (rows * factor * gain[None, :]).astype(jnp.bfloat16)


def segment_ids(lengths, block_rows):
    bounds = jnp.cumsum(lengths, axis=1)
    position = lax.broadcasted_iota(jnp.int32, (lengths.shape[0], block_rows), 1)
    return jnp.sum((position[:, :, None] >= bounds[:, None, :]).astype(jnp.int32), axis=2)


def softmax_rows(attention_scores):
    top = jnp.max(attention_scores, axis=-1, keepdims=True)
    expo = jnp.exp(attention_scores - top)
    return (expo / jnp.sum(expo, axis=-1, keepdims=True)).astype(jnp.bfloat16)


def transposed_dot(left, right):
    return lax.dot_general(
        left, right, (((1,), (1,)), ((), ())), preferred_element_type=jnp.float32
    )


def on_device(
    hidden_in,
    lengths,
    dest,
    attn_gain,
    q_weight,
    k_weight,
    v_weight,
    o_weight,
    ffn_gain,
    gate_weight,
    up_weight,
    down_weight,
):
    row_count, width = hidden_in.shape
    blocks, per_block = lengths.shape
    block_rows = row_count // blocks
    programs = blocks * per_block
    tp_size = lax.axis_size("tp")
    grp_size = lax.axis_size("grp")
    local_heads = q_weight.shape[1] // HEAD_SIZE
    norm_in = rms_scale(hidden_in, attn_gain)
    q_full, k_full, v_full, o_full, gate_full, up_full, down_full = (
        lax.all_gather(q_weight, "grp", axis=0, tiled=True),
        lax.all_gather(k_weight, "grp", axis=0, tiled=True),
        lax.all_gather(v_weight, "grp", axis=0, tiled=True),
        lax.all_gather(o_weight, "grp", axis=0, tiled=True),
        lax.all_gather(gate_weight, "grp", axis=0, tiled=True),
        lax.all_gather(up_weight, "grp", axis=0, tiled=True),
        lax.all_gather(down_weight, "grp", axis=0, tiled=True),
    )
    queries = jnp.dot(norm_in, q_full, preferred_element_type=jnp.float32).astype(jnp.bfloat16)
    key_part = jnp.dot(norm_in, k_full, preferred_element_type=jnp.float32).astype(jnp.bfloat16)
    value_part = jnp.dot(norm_in, v_full, preferred_element_type=jnp.float32).astype(jnp.bfloat16)
    keys_all, vals_all = (
        lax.all_gather(key_part, "tp", axis=1, tiled=True),
        lax.all_gather(value_part, "tp", axis=1, tiled=True),
    )
    kv_count = keys_all.shape[1] // HEAD_SIZE
    kv_index = lax.axis_index("tp") * local_heads // (HEADS // KVH)
    key_head = lax.dynamic_slice_in_dim(
        keys_all.reshape(row_count, HEAD_SIZE, kv_count), kv_index, 1, 2
    )[:, :, 0]
    value_head = lax.dynamic_slice_in_dim(
        vals_all.reshape(row_count, HEAD_SIZE, kv_count), kv_index, 1, 2
    )[:, :, 0]
    segs = segment_ids(lengths, block_rows)
    same = segs[:, :, None] == segs[:, None, :]
    blocked_queries = queries.reshape(blocks, block_rows, local_heads, HEAD_SIZE)
    blocked_keys = key_head.reshape(blocks, block_rows, HEAD_SIZE)
    blocked_values = value_head.reshape(blocks, block_rows, HEAD_SIZE)
    attention_scores = jnp.einsum(
        "xwre,xpe->xrwp", blocked_queries, blocked_keys, preferred_element_type=jnp.float32
    ) * HEAD_SIZE ** (-0.5)
    attention_scores = jnp.where(same[:, None, :, :], attention_scores, -1e30)
    attention_probabilities = softmax_rows(attention_scores)
    attended_rows = jnp.einsum(
        "asfo,aon->afsn",
        attention_probabilities,
        blocked_values,
        preferred_element_type=jnp.float32,
    )
    attended_rows = attended_rows.astype(jnp.bfloat16).reshape(row_count, local_heads * HEAD_SIZE)
    attn_term = transposed_dot(attended_rows, o_full)
    attn_total = lax.psum(attn_term.astype(jnp.bfloat16), "tp").astype(jnp.float32)
    residual = hidden_in.astype(jnp.float32) + attn_total
    norm_mid = rms_scale(residual, ffn_gain)
    gate_pre = jnp.dot(norm_mid, gate_full, preferred_element_type=jnp.float32)
    up_pre = jnp.dot(norm_mid, up_full, preferred_element_type=jnp.float32)
    hidden_ffn = (jax.nn.silu(gate_pre) * up_pre).astype(jnp.bfloat16)
    ffn_term = transposed_dot(hidden_ffn, down_full)
    share = row_count // tp_size
    tp_index = lax.axis_index("tp")
    block_index = lax.broadcasted_iota(jnp.int32, (blocks, block_rows), 0)
    program_of_row = (block_index * per_block + segs).reshape(row_count)
    program_grid = lax.broadcasted_iota(jnp.int32, (programs, row_count), 0)
    selector = program_grid == program_of_row[None, :]
    selector_float = selector.astype(jnp.float32)
    residual_share = lax.dynamic_slice_in_dim(residual, tp_index * share, share, 0)
    selector_share = lax.dynamic_slice_in_dim(selector_float, tp_index * share, share, 1)
    ffn_share = lax.psum_scatter(
        ffn_term.astype(jnp.bfloat16), "tp", scatter_dimension=0, tiled=True
    ).astype(jnp.float32)
    pooled_part = jnp.dot(
        selector_share,
        residual_share + ffn_share,
        precision=HIGH,
        preferred_element_type=jnp.float32,
    )
    pooled_sums = lax.psum_scatter(
        pooled_part.astype(jnp.bfloat16), "tp", scatter_dimension=1, tiled=True
    ).astype(jnp.float32)
    counts = lengths.reshape(programs).astype(jnp.float32)
    embedded = (pooled_sums / counts[:, None]).astype(jnp.bfloat16)
    capacity = max(2, (programs + grp_size - 1) // grp_size)
    targets = dest[:, 0]
    grp_ids = lax.broadcasted_iota(jnp.int32, (programs, grp_size), 1)
    chosen = (targets[:, None] == grp_ids).astype(jnp.int32)
    earlier = jnp.cumsum(chosen, axis=0) - chosen
    slot_rank = jnp.sum(earlier * chosen, axis=1)
    slot_ids = targets * capacity + slot_rank
    slot_grid = lax.broadcasted_iota(jnp.int32, (grp_size * capacity, programs), 0)
    placer = (slot_grid == slot_ids[None, :]).astype(jnp.bfloat16)
    outgoing = jnp.dot(placer, embedded, preferred_element_type=jnp.float32).astype(jnp.bfloat16)
    outgoing = outgoing.reshape(grp_size, capacity, embedded.shape[1])
    incoming = lax.all_to_all(outgoing, "grp", split_axis=0, concat_axis=0, tiled=True)
    return incoming.reshape(1, grp_size, capacity, embedded.shape[1])


def solution(mesh):
    placed = (
        P("grp", None),
        P("grp", None),
        P("grp", None),
        P(),
        P("grp", "tp"),
        P("grp", "tp"),
        P("grp", "tp"),
        P("grp", "tp"),
        P(),
        P("grp", "tp"),
        P("grp", "tp"),
        P("grp", "tp"),
    )
    return jax.shard_map(
        on_device, mesh=mesh, in_specs=placed, out_specs=P("grp", None, None, "tp"), check_vma=False
    )
```

profile of v0, /device:TPU:0, one launch (start us, length us, event | category | flops | bytes accessed | tf_op | source)
XLA Modules:
  0.0 716.7 jit_solution(17084657934199434864)
XLA Ops:
  6.5 0.7 all-gather.6.cloned.1.call-update
  7.3 0.0 all-gather.8.cloned.1.call-start
  7.3 0.7 all-gather.8.cloned.1.call-update
  8.0 0.0 all-reduce.2.cloned.1.call-start
  8.1 0.0 copy-start
  8.1 3.9 fusion.1
  11.9 8.3 %all_gather.27 = bf16[3584,64]{0,1:T(8,128)(2,1)S(1)} all-gather(bf16[896,64]{0,1:T(8,128)(2,1)S(1)} %copy-done.2), channel_id=1, replica_groups=mesh['grp'=4,'tp'=8] {'grp'}, dimensions={0}, use_global_device_ids=true | all-gather | bytes 573440 | tf_op jit(solution)/shard_map/all_gather | solution.py:64
  20.2 2.2 fusion.3
  22.4 2.4 copy-done.1
  24.8 1.8 convolution_convert_fusion.6
  26.6 32.6 %all_gather.28 = bf16[768,512]{0,1:T(8,128)(2,1)S(1)} all-gather(bf16[768,64]{0,1:T(8,128)(2,1)S(1)} %convolution_convert_fusion.6), channel_id=1, replica_groups=mesh['grp'=4,'tp'=8] {'tp'}, dimensions={1}, use_global_device_ids=true | all-gather | bytes 884736 | tf_op jit(solution)/shard_map/all_gather | solution.py:75
  59.2 0.2 reshape.71
  59.3 0.0 copy-start.5
  59.4 6.5 all_gather.29
  65.9 4.3 convolution_convert_fusion.5
  70.2 32.1 %all_gather.30 = bf16[768,512]{0,1:T(8,128)(2,1)S(1)} all-gather(bf16[768,64]{0,1:T(8,128)(2,1)S(1)} %convolution_convert_fusion.5), channel_id=1, replica_groups=mesh['grp'=4,'tp'=8] {'tp'}, dimensions={1}, use_global_device_ids=true | all-gather | bytes 884736 | tf_op jit(solution)/shard_map/all_gather | solution.py:74
  102.3 0.2 reshape.72
  102.4 0.8 constant_dynamic-slice_fusion
  103.3 0.4 copy.29
  103.7 0.2 reduce_window_sum.23
  103.9 0.4 copy.41
  104.3 0.1 convert_reduce_fusion
  104.4 0.2 broadcast_compare_fusion
  104.6 0.0 all-gather.6.cloned.1.call-done
  104.6 4.7 convolution_convert_fusion.4
  109.3 0.1 reshape.73
  109.5 2.4 fusion.32
  111.8 2.1 fusion.9
  113.9 0.4 copy.33
  114.3 0.0 all-gather.8.cloned.1.call-done
  114.4 5.5 convolution_convert_fusion.1
  119.9 0.0 all-reduce.2.cloned.1.call-update
  119.9 0.0 all-gather.10.cloned.1.call-start
  119.9 0.5 all-gather.10.cloned.1.call-update
  120.5 0.0 all-gather.12.cloned.1.call-start
  120.5 0.5 all-gather.12.cloned.1.call-update
  121.1 0.2 all-gather.14.cloned.1.call-start
  121.3 0.3 all-gather.14.cloned.1.call-update
  121.6 0.0 copy-start.7
  121.7 0.0 reduce-scatter.5.cloned.1.call-start
  121.7 189.5 %all-reduce.2.cloned.1.call-done = bf16[768,3584]{1,0:T(8,128)(2,1)} async-done(((bf16[768,3584]{1,0:T(8,128)(2,1)}), bf16[768,3584]{1,0:T(8,128)(2,1)}) %all-reduce.2.cloned.1.call-update) | async-done | bytes 5505040 | tf_op jit(solution)/shard_map/psum | solution.py:103
  311.2 11.4 %convert_add_fusion = (f32[768,3584]{1,0:T(8,128)}, f32[768]{0:T(1024)S(1)}) fusion(bf16[768,3584]{1,0:T(8,128)(2,1)} %param.12, bf16[768,3584]{1,0:T(8,128)(2,1)} %all-reduce.2.cloned.1.call-done), kind=kLoop, calls=%fused_computation.1 | loop fusion | flops 13761792 | bytes 22023168 | tf_op jit(solution)/shard_map/add | solution.py:104
  322.6 51.9 %all-gather.10.cloned.1.call-done = bf16[3584,1280]{1,0:T(8,128)(2,1)} async-done(((bf16[896,1280]{1,0:T(8,128)(2,1)}), bf16[3584,1280]{1,0:T(8,128)(2,1)}) %all-gather.10.cloned.1.call-update) | async-done | bytes 9175056 | tf_op jit(solution)/shard_map/all_gather | solution.py:66
  374.5 14.7 %fusion.31 = f32[768,1280]{1,0:T(8,128)} fusion(bf16[3584,1280]{1,0:T(8,128)(2,1)} %all-gather.10.cloned.1.call-done, f32[3584]{0:T(1024)S(1)} %copy-done.7, f32[768]{0:T(1024)S(1)} %add_rsqrt_fusion, bf16[768,3584]{1,0:T(8,128)(2,1)} %param.12, bf16[768,3584]{1,0:T(8,128)(2,1)} %all-reduce.2.cloned.1.call-done), kind=kOutput, calls=%fused_computation.57 | convolution fusion | flops 7062945792 | bytes 24134656 | tf_op jit(solution)/shard_map/dot_general | solution.py:106
  389.1 49.6 %all-gather.12.cloned.1.call-done = bf16[3584,1280]{1,0:T(8,128)(2,1)} async-done(((bf16[896,1280]{1,0:T(8,128)(2,1)}), bf16[3584,1280]{1,0:T(8,128)(2,1)}) %all-gather.12.cloned.1.call-update) | async-done | bytes 9175056 | tf_op jit(solution)/shard_map/all_gather | solution.py:67
  438.7 64.3 %all-gather.14.cloned.1.call-done = bf16[3584,1280]{1,0:T(8,128)(2,1)} async-done(((bf16[896,1280]{1,0:T(8,128)(2,1)}), bf16[3584,1280]{1,0:T(8,128)(2,1)}) %all-gather.14.cloned.1.call-update) | async-done | bytes 9175056 | tf_op jit(solution)/shard_map/all_gather | solution.py:68
  503.0 25.9 %convolution_convert_fusion = bf16[768,3584]{1,0:T(8,128)(2,1)} fusion(bf16[3584,1280]{1,0:T(8,128)(2,1)} %all-gather.14.cloned.1.call-done, bf16[3584,1280]{1,0:T(8,128)(2,1)} %all-gather.12.cloned.1.call-done, f32[768,1280]{1,0:T(8,128)} %fusion.31, f32[3584]{0:T(1024)S(1)} %copy-done.7, f32[768]{0:T(1024)S(1)} %add_rsqrt_fusion, ...), kind=kOutput, calls=%fused_computation.9 | convolution fusion | flops 14118027264 | bytes 38814720 | tf_op jit(solution)/shard_map/dot_general | solution.py:34
  528.9 0.0 reduce-scatter.5.cloned.1.call-update
  529.0 0.0 reduce-scatter.7.cloned.1.call-start
  529.0 0.1 broadcast_add_fusion
  529.1 0.5 copy-done.6
  529.6 0.1 fusion.22
  529.7 0.1 dynamic-slice
  529.8 105.6 %reduce-scatter.5.cloned.1.call-done = bf16[96,3584]{1,0:T(8,128)(2,1)} async-done(((bf16[768,3584]{1,0:T(8,128)(2,1)}), bf16[96,3584]{1,0:T(8,128)(2,1)}) %reduce-scatter.5.cloned.1.call-update) | async-done | bytes 688144 | tf_op jit(solution)/shard_map/reduce_scatter | solution.py:119
  635.4 2.2 convolution_convert_fusion.2
  637.6 1.2 copy.39
  638.8 0.0 reduce-scatter.7.cloned.1.call-update
  638.8 0.2 select_reduce_fusion
  639.0 0.1 convert_element_type.92
  639.1 62.5 %reduce-scatter.7.cloned.1.call-done = bf16[448,16]{1,0:T(8,128)(2,1)} async-done(((bf16[3584,16]{1,0:T(8,128)(2,1)}), bf16[448,16]{1,0:T(8,128)(2,1)}) %reduce-scatter.7.cloned.1.call-update) | async-done | bytes 14352
  701.6 1.0 copy.40
  702.6 0.2 convolution_convert_fusion.7
  702.8 6.4 all_to_all.5
  709.2 0.6 copy.59
  (20 shorter events, 0.1 us)
Async XLA Ops:
  6.5 5.4 copy-start.2
  6.5 13.7 %copy-start.4 = (f32[3584]{0:T(1024)S(1)}, f32[3584]{0:T(1024)}, u32[]{:S(2)}) copy-start(f32[3584]{0:T(1024)} %param.15) | copy-start | bytes 43012
  6.5 98.1 %all-gather.6.cloned.1.call-start = ((), (), s32[]{:S(2)}) async-start(), calls=%async_computation.3 | async-start | bytes 2293760 | tf_op jit(solution)/shard_map/all_gather | solution.py:62
  7.3 107.1 %all-gather.8.cloned.1.call-start = ((), (), s32[]{:S(2)}) async-start(), calls=%async_computation.4 | async-start | bytes 2293760 | tf_op jit(solution)/shard_map/all_gather | solution.py:65
  8.0 303.2 %all-reduce.2.cloned.1.call-start = ((), (), s32[]{:S(2)}) async-start(), calls=%async_computation.5 | async-start | bytes 11010048 | tf_op jit(solution)/shard_map/psum | solution.py:103
  8.1 12.2 %copy-start = (bf16[768,3584]{1,0:T(8,128)(2,1)S(1)}, bf16[768,3584]{1,0:T(8,128)(2,1)}, u32[]{:S(2)}) copy-start(bf16[768,3584]{1,0:T(8,128)(2,1)} %param.12) | copy-start | bytes 16515076
  22.4 2.4 copy-start.1
  24.8 34.5 %copy-start.3 = (bf16[896,64]{0,1:T(8,128)(2,1)S(1)}, bf16[896,64]{0,1:T(8,128)(2,1)}, u32[]{:S(2)}) copy-start(bf16[896,64]{0,1:T(8,128)(2,1)} %param.17) | copy-start | bytes 344068
  59.3 44.3 %copy-start.5 = (s32[2,8]{1,0:T(2,128)S(1)}, s32[2,8]{1,0:T(2,128)}, u32[]{:S(2)}) copy-start(s32[2,8]{1,0:T(2,128)} %param.13) | copy-start | bytes 196
  119.9 254.6 %all-gather.10.cloned.1.call-start = ((), (), s32[]{:S(2)}) async-start(), calls=%async_computation.6 | async-start | bytes 11468800 | tf_op jit(solution)/shard_map/all_gather | solution.py:66
  120.5 318.2 %all-gather.12.cloned.1.call-start = ((), (), s32[]{:S(2)}) async-start(), calls=%async_computation.7 | async-start | bytes 11468800 | tf_op jit(solution)/shard_map/all_gather | solution.py:67
  121.1 381.9 %all-gather.14.cloned.1.call-start = ((), (), s32[]{:S(2)}) async-start(), calls=%async_computation.8 | async-start | bytes 11468800 | tf_op jit(solution)/shard_map/all_gather | solution.py:68
  121.6 252.8 %copy-start.7 = (f32[3584]{0:T(1024)S(1)}, f32[3584]{0:T(1024)}, u32[]{:S(2)}) copy-start(f32[3584]{0:T(1024)} %param.20) | copy-start | bytes 43012
  121.7 513.7 %reduce-scatter.5.cloned.1.call-start = ((), (), s32[]{:S(2)}) async-start(), calls=%async_computation.9 | async-start | bytes 6193152 | tf_op jit(solution)/shard_map/reduce_scatter | solution.py:119
  528.9 0.7 copy-start.6
  529.0 172.7 %reduce-scatter.7.cloned.1.call-start = ((), (), s32[]{:S(2)}) async-start(), calls=%async_computation.10 | async-start | bytes 1032192
Sparse Core Ops, SparseCore 0:
  8.9 23.8 all-gather.5
  34.3 21.1 all-gather.7
  120.0 191.1 all-reduce.1
  312.7 61.7 all-gather.9
  375.9 62.7 all-gather.11
  440.2 62.7 all-gather.13
  529.1 106.2 reduce-scatter.4
  639.0 62.6 reduce-scatter.6
where the time goes:
time: 717 us
  waiting for transfers between devices  526 us (73%)
  blocking collectives  85.8 us (12%)
  matrix products  63.7 us (9%)
  other arithmetic  18.3 us (3%)
  between operations  13.7 us (2%)
  local copies, waits for them, and re-layouts  8.39 us (1%)
    psum x1, waiting for transfers between devices, on_device(): lax.psum(attn_term.astype(jnp.bfloat16), 'tp').astype(jnp.float32)  189 us
    reduce_scatter x1, waiting for transfers between devices, on_device(): lax.psum_scatter(ffn_term.astype(jnp.bfloat16), 'tp', scatter_dimension=0...  106 us
    unnamed x9, waiting for transfers between devices  65.4 us
    all_gather x1, waiting for transfers between devices, on_device(): lax.all_gather(down_weight, 'grp', axis=0, tiled=True)  64.3 us
    all_gather x1, waiting for transfers between devices, on_device(): lax.all_gather(gate_weight, 'grp', axis=0, tiled=True)  51.9 us
    all_gather x1, waiting for transfers between devices, on_device(): lax.all_gather(up_weight, 'grp', axis=0, tiled=True)  49.6 us
    all_gather x1, blocking collectives, on_device(): lax.all_gather(value_part, 'tp', axis=1, tiled=True)  32.6 us
    all_gather x1, blocking collectives, on_device(): lax.all_gather(key_part, 'tp', axis=1, tiled=True)  32.1 us
  transfers between devices with their start and end apart: 8, of which 6 were waited for; matrix products, arithmetic and copies ran while one was open for 7% of the time, Pallas kernels for 0%

commit v1 on v0

v1 whole, which is shorter than its diff:
```python
import jax
import jax.numpy as jnp
from jax import lax
from jax.sharding import PartitionSpec as P

HEAD_SIZE = 128
KVH = 4
HEADS = 16


EPSILON = 1e-06
HIGH = lax.Precision.HIGHEST


def rms_scale(rows, gain):
    rows = rows.astype(jnp.float32)
    factor = lax.rsqrt(jnp.mean(rows * rows, axis=1, keepdims=True) + EPSILON)
    return (rows * factor * gain[None, :]).astype(jnp.bfloat16)


def segment_ids(lengths, block_rows):
    bounds = jnp.cumsum(lengths, axis=1)
    position = lax.broadcasted_iota(jnp.int32, (lengths.shape[0], block_rows), 1)
    return jnp.sum((position[:, :, None] >= bounds[:, None, :]).astype(jnp.int32), axis=2)


def softmax_rows(attention_scores):
    top = jnp.max(attention_scores, axis=-1, keepdims=True)
    expo = jnp.exp(attention_scores - top)
    return (expo / jnp.sum(expo, axis=-1, keepdims=True)).astype(jnp.bfloat16)


def transposed_dot(left, right):
    return lax.dot_general(
        left, right, (((1,), (1,)), ((), ())), preferred_element_type=jnp.float32
    )


def gather_grp(piece, chips):
    held = [piece]
    moving = piece
    if chips > 1:
        ring = [(2 * i + c, 2 * ((i + 1) % chips) + c) for i in range(chips) for c in range(2)]
        for _ in range(chips - 1):
            moving = lax.ppermute(moving, "grp", ring)
            held.append(moving)
    mine = jnp.stack(held)
    other = lax.ppermute(mine, "grp", [(g, g ^ 1) for g in range(2 * chips)])
    return jnp.concatenate([mine, other], 0)


def source_order(chips):
    g = lax.axis_index("grp")
    chip, core = g // 2, g % 2
    steps = jnp.arange(chips, dtype=jnp.int32)
    own = 2 * ((chip - steps) % chips) + core
    return jnp.concatenate([own, own - core + (1 - core)])


def take_blocks(x, order, size, axis):
    return jnp.concatenate(
        [lax.dynamic_slice_in_dim(x, order[k] * size, size, axis) for k in range(order.shape[0])],
        axis,
    )


def on_device(
    hidden_in,
    lengths,
    dest,
    attn_gain,
    q_weight,
    k_weight,
    v_weight,
    o_weight,
    ffn_gain,
    gate_weight,
    up_weight,
    down_weight,
):
    row_count, width = hidden_in.shape
    blocks, per_block = lengths.shape
    block_rows = row_count // blocks
    programs = blocks * per_block
    tp_size = lax.axis_size("tp")
    grp_size = lax.axis_size("grp")
    chips = grp_size // 2
    tp_index = lax.axis_index("tp")
    grp_index = lax.axis_index("grp")
    d_grp = width // grp_size
    d_tp = width // tp_size
    ratio = tp_size // grp_size
    capacity = max(2, (programs + grp_size - 1) // grp_size)
    local_heads = q_weight.shape[1] // HEAD_SIZE
    order = source_order(chips)

    q_cols, k_cols = q_weight.shape[1], k_weight.shape[1]
    qkv_full = gather_grp(jnp.concatenate([q_weight, k_weight, v_weight], 1), chips)
    qkv_full = qkv_full.reshape(width, -1)
    o_full = gather_grp(o_weight, chips).reshape(width, -1)
    gate_full = gather_grp(gate_weight, chips).reshape(width, -1)
    up_full = gather_grp(up_weight, chips).reshape(width, -1)

    hidden_perm = take_blocks(hidden_in, order, d_grp, 1)
    attn_gain_perm = take_blocks(attn_gain, order, d_grp, 0)
    ffn_gain_perm = take_blocks(ffn_gain, order, d_grp, 0)

    norm_in = rms_scale(hidden_perm, attn_gain_perm)
    qkv = jnp.dot(norm_in, qkv_full, preferred_element_type=jnp.float32).astype(jnp.bfloat16)
    queries = qkv[:, :q_cols]
    kv_part = qkv[:, q_cols:]
    kv_all = lax.all_to_all(
        jnp.broadcast_to(kv_part[None], (tp_size,) + kv_part.shape), "tp", 0, 0, tiled=True
    )
    per_dev = k_cols // KVH
    kv_index = tp_index * local_heads // (HEADS // KVH)

    def head_of(part):
        split = part.reshape(tp_size, row_count, per_dev, KVH)
        one = lax.dynamic_slice_in_dim(split, kv_index, 1, 3)[..., 0]
        return one.transpose(1, 0, 2).reshape(row_count, tp_size * per_dev)

    key_head = head_of(kv_all[:, :, :k_cols])
    value_head = head_of(kv_all[:, :, k_cols:])

    segs = segment_ids(lengths, block_rows)
    same = segs[:, :, None] == segs[:, None, :]
    blocked_queries = queries.reshape(blocks, block_rows, local_heads, HEAD_SIZE)
    blocked_keys = key_head.reshape(blocks, block_rows, HEAD_SIZE)
    blocked_values = value_head.reshape(blocks, block_rows, HEAD_SIZE)
    attention_scores = jnp.einsum(
        "xwre,xpe->xrwp", blocked_queries, blocked_keys, preferred_element_type=jnp.float32
    ) * HEAD_SIZE ** (-0.5)
    attention_scores = jnp.where(same[:, None, :, :], attention_scores, -1e30)
    attention_probabilities = softmax_rows(attention_scores)
    attended_rows = jnp.einsum(
        "asfo,aon->afsn",
        attention_probabilities,
        blocked_values,
        preferred_element_type=jnp.float32,
    )
    attended_rows = attended_rows.astype(jnp.bfloat16).reshape(row_count, local_heads * HEAD_SIZE)
    attn_term = transposed_dot(attended_rows, o_full)
    attn_total = lax.psum(attn_term.astype(jnp.bfloat16), "tp").astype(jnp.float32)
    residual = hidden_perm.astype(jnp.float32) + attn_total
    norm_mid = rms_scale(residual, ffn_gain_perm)
    gate_pre = jnp.dot(norm_mid, gate_full, preferred_element_type=jnp.float32)
    up_pre = jnp.dot(norm_mid, up_full, preferred_element_type=jnp.float32)
    hidden_ffn = (jax.nn.silu(gate_pre) * up_pre).astype(jnp.bfloat16)

    block_index = lax.broadcasted_iota(jnp.int32, (blocks, block_rows), 0)
    program_of_row = (block_index * per_block + segs).reshape(row_count)
    program_grid = lax.broadcasted_iota(jnp.int32, (programs, row_count), 0)
    selector = (program_grid == program_of_row[None, :]).astype(jnp.float32)
    hidden_sums = jnp.dot(
        selector.astype(jnp.bfloat16), hidden_ffn, preferred_element_type=jnp.float32
    )
    chunk_owner = tp_index // ratio
    owner_step = jnp.argmax(order == chunk_owner).astype(jnp.int32)
    chunk_start = owner_step * d_grp + (tp_index % ratio) * d_tp
    residual_chunk = lax.dynamic_slice_in_dim(residual, chunk_start, d_tp, 1)
    residual_sums = jnp.dot(selector, residual_chunk, precision=HIGH, preferred_element_type=jnp.float32)

    hidden_all = gather_grp(hidden_sums, chips).reshape(grp_size * programs, -1)
    down_part = lax.dot_general(
        hidden_all, down_weight.astype(jnp.float32), (((1,), (1,)), ((), ())),
        precision=HIGH, preferred_element_type=jnp.float32,
    )

    dest_all = gather_grp(dest[:, 0], chips)
    lengths_all = gather_grp(lengths.reshape(programs), chips).reshape(grp_size * programs)
    grp_ids = lax.broadcasted_iota(jnp.int32, (grp_size, programs, grp_size), 2)
    chosen = (dest_all[:, :, None] == grp_ids).astype(jnp.int32)
    earlier = jnp.cumsum(chosen, axis=1) - chosen
    slot_rank = jnp.sum(earlier * chosen, axis=2)
    slot_row = order[:, None] * capacity + slot_rank
    slots = grp_size * capacity
    target_grid = lax.broadcasted_iota(jnp.int32, (grp_size, slots, grp_size, programs), 0)
    row_grid = lax.broadcasted_iota(jnp.int32, (grp_size, slots, grp_size, programs), 1)
    placer = (
        (target_grid == dest_all[None, None]) & (row_grid == slot_row[None, None])
    ).astype(jnp.float32).reshape(grp_size, slots, grp_size * programs)
    down_slots = jnp.einsum("asq,qd->asd", placer, down_part, precision=HIGH)
    down_slots = down_slots.reshape(grp_size, slots, ratio, d_tp).transpose(0, 2, 1, 3)
    send = lax.dynamic_update_slice(
        jnp.zeros((grp_size, tp_size, slots, d_tp), jnp.float32),
        down_slots,
        (0, grp_index * ratio, 0, 0),
    )
    local_placer = placer[:, :, :programs]
    residual_slots = jnp.einsum("asq,qd->asd", local_placer, residual_sums, precision=HIGH)
    send = send + lax.dynamic_update_slice(
        jnp.zeros((grp_size, tp_size, slots, d_tp), jnp.float32),
        residual_slots[:, None],
        (0, tp_index, 0, 0),
    )
    received = lax.all_to_all(
        send.reshape(grp_size * tp_size, slots, d_tp), ("grp", "tp"), 0, 0, tiled=True
    )
    totals = jnp.sum(received, axis=0)
    mine = lax.dynamic_index_in_dim(placer, grp_index, 0, keepdims=False)
    counts = jnp.dot(mine, lengths_all.astype(jnp.float32), precision=HIGH)
    counts = jnp.where(counts > 0, counts, 1.0)
    embedded = (totals / counts[:, None]).astype(jnp.bfloat16)
    return embedded.reshape(1, grp_size, capacity, d_tp)


def solution(mesh):
    placed = (
        P("grp", None),
        P("grp", None),
        P("grp", None),
        P(),
        P("grp", "tp"),
        P("grp", "tp"),
        P("grp", "tp"),
        P("grp", "tp"),
        P(),
        P("grp", "tp"),
        P("grp", "tp"),
        P("grp", "tp"),
    )
    return jax.shard_map(
        on_device, mesh=mesh, in_specs=placed, out_specs=P("grp", None, None, "tp"), check_vma=False
    )
```

time: 717 us -> 452 us (0.63)
  waiting for transfers between devices: 526 us -> 295 us
  blocking collectives: 85.8 us -> 0 us
  other arithmetic: 18.3 us -> 55.5 us
  starting transfers between devices: 0.46 us -> 20 us
  matrix products: 63.7 us -> 46.4 us
  local copies, waits for them, and re-layouts: 8.39 us -> 16.4 us
    all_gather x5 -> x0, waiting for transfers between devices: 166 us -> none  [the longest x1 64.3 us: on_device(): lax.all_gather(down_weight, 'grp', axis=0, tiled=True)]
    reduce_scatter x1 -> x0, waiting for transfers between devices: 106 us -> none  [on_device(): lax.psum_scatter(ffn_term.astype(jnp.bfloat16), 'tp', scatter_dimension=0...]
    ppermute x0 -> x14, waiting for transfers between devices: none -> 102 us  [the longest x7 98.4 us: gather_grp(): moving = lax.ppermute(moving, 'grp', ring)]
    all_gather x4 -> x0, blocking collectives: 79.4 us -> none  [the longest x1 32.6 us: on_device(): lax.all_gather(value_part, 'tp', axis=1, tiled=True)]
    unnamed x9 -> x1, waiting for transfers between devices: 65.4 us -> 0.02 us
    all_to_all x0 -> x2, waiting for transfers between devices: none -> 26.1 us  [the longest x1 26.1 us: on_device(): lax.all_to_all(send.reshape(grp_size * tp_size, slots, d_tp), ('grp', 'tp...]
    dot_general x2 -> x1, matrix products: 31.5 us -> 5.57 us  [transposed_dot(): lax.dot_general(left, right, (((1,), (1,)), ((), ())), preferred_element_...]
    concatenate x0 -> x9, other arithmetic: none -> 25 us  [the longest x6 23 us: gather_grp(): return jnp.concatenate([mine, other], 0)]
  transfers between devices with their start and end apart: 8 -> 17, of which waited for: 6 -> 9; matrix products, arithmetic and copies ran while one was open for 7% -> 16% of each run, Pallas kernels for 0% -> 0%
where the time goes in v1:
time: 452 us; the launch traced here: 451 us
  waiting for transfers between devices  295 us (65%)
  other arithmetic  55.5 us (12%)
  matrix products  46.4 us (10%)
  starting transfers between devices  20 us (4%)
  between operations  17 us (4%)
  local copies, waits for them, and re-layouts  16.4 us (4%)
    psum x1, waiting for transfers between devices, on_device(): lax.psum(attn_term.astype(jnp.bfloat16), 'tp').astype(jnp.float32)  167 us
    ppermute x7, waiting for transfers between devices, gather_grp(): moving = lax.ppermute(moving, 'grp', ring)  98.4 us
    all_to_all x1, waiting for transfers between devices, on_device(): lax.all_to_all(send.reshape(grp_size * tp_size, slots, d_tp), ('grp', 'tp...  26.1 us
    concatenate x6, other arithmetic, gather_grp(): return jnp.concatenate([mine, other], 0)  23 us
    dot_general x1, matrix products, on_device(): jnp.dot(selector.astype(jnp.bfloat16), hidden_ffn, preferred_element_type...  14.4 us
    another operation x7, other arithmetic, gather_grp(): mine = jnp.stack(held)  13.7 us
    add x1, other arithmetic, on_device(): residual = hidden_perm.astype(jnp.float32) + attn_total  11.9 us
    dot_general x1, matrix products, on_device(): up_pre = jnp.dot(norm_mid, up_full, preferred_element_type=jnp.float32)  11.6 us
  transfers between devices with their start and end apart: 17, of which 9 were waited for; matrix products, arithmetic and copies ran while one was open for 16% of the time, Pallas kernels for 0%

profile of v1, /device:TPU:0, one launch (start us, length us, event | category | flops | bytes accessed | tf_op | source)
XLA Modules:
  0.0 450.6 jit_solution(4661509185440796981)
XLA Ops:
  6.5 1.2 copy.59
  7.8 1.1 copy.60
  8.8 2.0 pad_maximum_fusion.9
  10.9 2.9 collective-permute-start.2
  13.9 0.6 fusion.61
  15.7 1.2 fusion.76
  16.9 13.5 %collective-permute-done.2 = bf16[896,384]{1,0:T(8,128)(2,1)} collective-permute-done((bf16[896,384]{1,0:T(8,128)(2,1)}, bf16[896,384]{1,0:T(8,128)(2,1)}, u32[]{:S(2)}, u32[]{:S(2)}) %collective-permute-start.2) | collective-permute-done | bytes 688160 | tf_op jit(solution)/shard_map/ppermute | solution.py:45
  30.4 2.4 pad_maximum_fusion.7
  32.7 0.6 fusion.62
  34.7 3.1 constant_dynamic-slice_fusion.5
  37.8 1.4 fusion.1
  39.2 2.3 pad_maximum_fusion.5
  41.5 4.1 fusion.12
  45.6 0.8 copy-done.13
  46.4 0.1 copy.61
  46.6 1.2 broadcast_in_dim.19
  47.8 6.4 %all-to-all-start = ((bf16[8,768,128]{1,2,0:T(8,128)(2,1)}), bf16[8,768,128]{1,2,0:T(8,128)(2,1)}, u32[]{:S(2)}, u32[]{:S(2)}) async-start(bf16[8,768,128]{1,2,0:T(8,128)(2,1)} %broadcast_in_dim.19), calls=%async_computation | async-start | bytes 3145728 | tf_op jit(solution)/shard_map/all_to_all | solution.py:112
  54.3 1.5 collective-permute-start.8
  55.8 0.5 collective-permute-start.4
  56.4 81.2 %collective-permute-done.4 = bf16[896,256]{1,0:T(8,128)(2,1)S(1)} collective-permute-done((bf16[896,256]{1,0:T(8,128)(2,1)S(1)}, bf16[896,256]{1,0:T(8,128)(2,1)S(1)}, u32[]{:S(2)}, u32[]{:S(2)}) %collective-permute-start.4) | collective-permute-done | bytes 458784 | tf_op jit(solution)/shard_map/ppermute | solution.py:45
  137.6 1.0 pad_maximum_fusion.8
  138.6 0.2 reduce_window_sum.23
  138.9 0.9 broadcast_compare_fusion
  139.8 1.6 collective-permute-done.5
  141.4 2.6 pad_maximum_fusion.6
  144.0 1.0 slice.47
  145.0 0.9 reshape.188
  145.9 5.1 %pad_maximum_fusion.3 = bf16[2,896,1280]{2,1,0:T(8,128)(2,1)} fusion(bf16[1,896,1280]{2,1,0:T(8,128)(2,1)} %bitcast.25, bf16[1,896,1280]{2,1,0:T(8,128)(2,1)} %bitcast.96), kind=kLoop, calls=%fused_computation.16 | loop fusion | flops 2293760 | bytes 9175040 | tf_op jit(solution)/shard_map/stack | solution.py:47
  151.0 0.1 collective-permute-start.7
  151.1 4.1 pad_maximum_fusion.4
  155.2 0.4 collective-permute-start.9
  155.6 1.5 fusion.58
  157.1 0.4 copy.82
  157.7 0.4 copy.83
  158.3 3.5 fusion.63
  161.8 2.0 fusion.15
  163.8 0.6 copy.70
  164.4 5.6 %convolution_convert_fusion = bf16[768,3584]{1,0:T(8,128)(2,1)} fusion(bf16[3584,256]{1,0:T(8,128)(2,1)} %bitcast.102, bf16[96,8,2,128]{3,2,1,0:T(2,128)(2,1)S(1)} %bitcast.105), kind=kOutput, calls=%fused_computation.11 | convolution fusion | flops 1412038656 | bytes 7733248 | tf_op jit(solution)/shard_map/dot_general | solution.py:34
  170.1 1.7 collective-permute-start.12
  171.9 0.5 collective-permute-start
  172.5 0.8 compare_reduce_fusion
  174.4 1.0 collective-permute-done
  175.5 1.1 collective-permute-done.1
  176.7 0.2 select_reduce_fusion
  177.0 9.9 %pad_maximum_fusion = bf16[4,896,1280]{2,1,0:T(8,128)(2,1)} fusion(bf16[2,896,1280]{2,1,0:T(8,128)(2,1)} %collective-permute-done.7, bf16[1,896,1280]{2,1,0:T(8,128)(2,1)} %bitcast.25, bf16[1,896,1280]{2,1,0:T(8,128)(2,1)} %bitcast.97), kind=kLoop, calls=%fused_computation.9 | loop fusion | flops 9175040 | bytes 18350080 | tf_op jit(solution)/shard_map/concatenate | solution.py:49
  186.9 8.2 %pad_maximum_fusion.1 = bf16[4,896,1280]{2,1,0:T(8,128)(2,1)} fusion(bf16[2,896,1280]{2,1,0:T(8,128)(2,1)} %collective-permute-done.9, bf16[1,896,1280]{2,1,0:T(8,128)(2,1)} %bitcast.28, bf16[1,896,1280]{2,1,0:T(8,128)(2,1)S(1)} %bitcast.99), kind=kLoop, calls=%fused_computation.10 | loop fusion | flops 9175040 | bytes 18350080 | tf_op jit(solution)/shard_map/concatenate | solution.py:49
  195.1 167.2 %all-reduce.2.cloned.1.call-done = bf16[768,3584]{1,0:T(8,128)(2,1)} async-done(((bf16[768,3584]{1,0:T(8,128)(2,1)}), bf16[768,3584]{1,0:T(8,128)(2,1)}) %all-reduce.2.cloned.1.call-update) | async-done | bytes 5505040 | tf_op jit(solution)/shard_map/psum | solution.py:144
  362.4 11.9 %convert_add_fusion = (f32[768,3584]{1,0:T(8,128)}, f32[768]{0:T(1024)S(1)}) fusion(bf16[768,3584]{1,0:T(8,128)(2,1)} %all-reduce.2.cloned.1.call-done, bf16[768,896]{1,0:T(8,128)(2,1)} %copy-done.5, bf16[768,896]{1,0:T(8,128)(2,1)} %copy-done.7, bf16[768,896]{1,0:T(8,128)(2,1)} %copy-done.3, bf16[768,896]{1,0:T(8,128)(2,1)} %copy-done.1), kind=kLoop, calls=%fused_computation.1 | loop fusion | flops 33029376 | bytes 22023168 | tf_op jit(solution)/shard_map/add | solution.py:145
  374.3 11.6 %fusion.56 = f32[768,1280]{1,0:T(8,128)} fusion(bf16[3584,1280]{1,0:T(8,128)(2,1)S(1)} %bitcast.101, f32[3584]{0:T(1024)S(1)} %pad_maximum_fusion.13, f32[768]{0:T(1024)S(1)} %add_rsqrt_fusion, bf16[768,3584]{1,0:T(8,128)(2,1)} %all-reduce.2.cloned.1.call-done, bf16[768,896]{1,0:T(8,128)(2,1)S(1)} %copy-done.6, bf16[768,896]{1,0:T(8,128)(2,1)S(1)} %copy-done.8, ...), kind=kOutput, calls=%fused_computation.111 | convolution fusion | flops 7082213376 | bytes 24134656 | tf_op jit(solution)/shard_map/dot_general | solution.py:148
  386.0 14.4 %fusion.9 = f32[16,1280]{1,0:T(8,128)S(1)} fusion(f32[768,1280]{1,0:T(8,128)} %fusion.56, s32[768]{0:T(1024)S(1)} %add.143, bf16[3584,1280]{1,0:T(8,128)(2,1)} %bitcast.100, f32[3584]{0:T(1024)S(1)} %pad_maximum_fusion.13, f32[768]{0:T(1024)S(1)} %add_rsqrt_fusion, bf16[768,3584]{1,0:T(8,128)(2,1)} %all-reduce.2.cloned.1.call-done, ...), kind=kOutput, calls=%fused_computation.24 | convolution fusion | flops 7119605760 | bytes 24219648 | tf_op jit(solution)/shard_map/dot_general | solution.py:155
  400.4 1.5 collective-permute-start.10
  402.2 2.8 collective-permute-done.10
  405.2 2.3 fusion.21
  407.6 2.1 convolution_bitcast_fusion.1
  409.7 0.3 dot_general.49
  410.0 0.3 convolution_bitcast_fusion
  410.4 0.2 fusion.20
  410.6 1.1 copy.73
  411.7 3.7 all-to-all-start.1
  415.4 0.3 collective-permute-start.13
  415.7 0.9 collective-permute-done.13
  416.7 0.1 compare_select_fusion
  416.9 26.1 %all-to-all-done.1 = f32[32,16,448]{2,1,0:T(8,128)S(1)} async-done(((f32[32,16,448]{2,1,0:T(8,128)}), f32[32,16,448]{2,1,0:T(8,128)S(1)}, u32[]{:S(2)}, u32[]{:S(2)}) %all-to-all-start.1) | async-done | bytes 917536 | tf_op jit(solution)/shard_map/all_to_all | solution.py:197
  443.1 0.7 divide_convert_fusion.2
  (93 shorter events, 2.4 us)
Async XLA Ops:
  6.5 401.0 %copy-start = (bf16[896,1280]{1,0:T(8,128)(2,1)S(1)}, bf16[896,1280]{1,0:T(8,128)(2,1)}, u32[]{:S(2)}) copy-start(bf16[896,1280]{1,0:T(8,128)(2,1)} %param.23) | copy-start | bytes 6881284
  6.5 28.0 %copy-start.14 = (f32[3584]{0:T(1024)S(1)}, f32[3584]{0:T(1024)}, u32[]{:S(2)}) copy-start(f32[3584]{0:T(1024)} %param.15) | copy-start | bytes 43012
  10.9 19.5 %collective-permute-start.2 = (bf16[896,384]{1,0:T(8,128)(2,1)}, bf16[896,384]{1,0:T(8,128)(2,1)}, u32[]{:S(2)}, u32[]{:S(2)}) collective-permute-start(bf16[896,384]{1,0:T(8,128)(2,1)} %pad_maximum_fusion.9), channel_id=1, source_target_pairs={{0,16},{8,24},{16,0},{24,8},{1,17},{9,25},{17,1},{25,9},{2,18},{10... | collective-permute-start | bytes 2064392 | tf_op jit(solution)/shard_map/ppermute | solution.py:45
  13.8 132.1 %collective-permute-start.6 = (bf16[896,1280]{1,0:T(8,128)(2,1)}, bf16[896,1280]{1,0:T(8,128)(2,1)}, u32[]{:S(2)}, u32[]{:S(2)}) collective-permute-start(bf16[896,1280]{1,0:T(8,128)(2,1)} %param.21), channel_id=1, source_target_pairs={{0,16},{8,24},{16,0},{24,8},{1,17},{9,25},{17,1},{25,9},{2,18},{10... | collective-permute-start | bytes 6881288 | tf_op jit(solution)/shard_map/ppermute | solution.py:45
  32.7 6.4 %collective-permute-start.3 = (bf16[2,896,384]{2,1,0:T(8,128)(2,1)}, bf16[2,896,384]{2,1,0:T(8,128)(2,1)}, u32[]{:S(2)}, u32[]{:S(2)}) collective-permute-start(bf16[2,896,384]{2,1,0:T(8,128)(2,1)} %pad_maximum_fusion.7), channel_id=1, source_target_pairs={{0,8},{8,0},{16,24},{24,16},{1,9},{9,1},{17,25},{25,17},{2,10},{10... | collective-permute-start | bytes 4128776 | tf_op jit(solution)/shard_map/ppermute | solution.py:48
  37.7 3.7 copy-start.1
  37.7 3.7 copy-start.3
  37.7 3.7 copy-start.5
  37.8 3.7 copy-start.7
  45.6 0.8 copy-start.13
  46.4 9.4 %copy-start.12 = (bf16[896,256]{1,0:T(8,128)(2,1)S(1)}, bf16[896,256]{1,0:T(8,128)(2,1)}, u32[]{:S(2)}) copy-start(bf16[896,256]{1,0:T(8,128)(2,1)} %param.19) | copy-start | bytes 1376260
  46.4 92.2 %copy-start.17 = (s32[2,8]{1,0:T(2,128)S(1)}, s32[2,8]{1,0:T(2,128)}, u32[]{:S(2)}) copy-start(s32[2,8]{1,0:T(2,128)} %param.13) | copy-start | bytes 196
  47.8 107.8 %all-to-all-start = ((bf16[8,768,128]{1,2,0:T(8,128)(2,1)}), bf16[8,768,128]{1,2,0:T(8,128)(2,1)}, u32[]{:S(2)}, u32[]{:S(2)}) async-start(bf16[8,768,128]{1,2,0:T(8,128)(2,1)} %broadcast_in_dim.19), calls=%async_computation | async-start | bytes 3145728 | tf_op jit(solution)/shard_map/all_to_all | solution.py:112
  54.3 308.1 %all-reduce.2.cloned.1.call-start = ((), (), s32[]{:S(2)}) async-start(), calls=%async_computation.2 | async-start | bytes 11010048 | tf_op jit(solution)/shard_map/psum | solution.py:144
  54.3 96.8 %collective-permute-start.8 = (bf16[896,1280]{1,0:T(8,128)(2,1)}, bf16[896,1280]{1,0:T(8,128)(2,1)}, u32[]{:S(2)}, u32[]{:S(2)}) collective-permute-start(bf16[896,1280]{1,0:T(8,128)(2,1)} %param.22), channel_id=1, source_target_pairs={{0,16},{8,24},{16,0},{24,8},{1,17},{9,25},{17,1},{25,9},{2,18},{10... | collective-permute-start | bytes 6881288 | tf_op jit(solution)/shard_map/ppermute | solution.py:45
  55.8 81.7 %collective-permute-start.4 = (bf16[896,256]{1,0:T(8,128)(2,1)S(1)}, bf16[896,256]{1,0:T(8,128)(2,1)S(1)}, u32[]{:S(2)}, u32[]{:S(2)}) collective-permute-start(bf16[896,256]{1,0:T(8,128)(2,1)S(1)} %copy-done.12), channel_id=1, source_target_pairs={{0,16},{8,24},{16,0},{24,8},{1,17},{9,25},{17,1},{25,9},{2,18},{10... | collective-permute-start | bytes 1376264 | tf_op jit(solution)/shard_map/ppermute | solution.py:45
  138.6 2.8 collective-permute-start.5
  145.9 5.2 %copy-start.9 = (bf16[896,1280]{1,0:T(8,128)(2,1)S(1)}, bf16[896,1280]{1,0:T(8,128)(2,1)}, u32[]{:S(2)}) copy-start(bf16[896,1280]{1,0:T(8,128)(2,1)} %param.22) | copy-start | bytes 6881284
  151.0 26.0 %collective-permute-start.7 = (bf16[2,896,1280]{2,1,0:T(8,128)(2,1)}, bf16[2,896,1280]{2,1,0:T(8,128)(2,1)}, u32[]{:S(2)}, u32[]{:S(2)}) collective-permute-start(bf16[2,896,1280]{2,1,0:T(8,128)(2,1)} %pad_maximum_fusion.3), channel_id=1, source_target_pairs={{0,8},{8,0},{16,24},{24,16},{1,9},{9,1},{17,25},{25,17},{2,10},{10... | collective-permute-start | bytes 13762568 | tf_op jit(solution)/shard_map/ppermute | solution.py:48
  155.2 31.7 %collective-permute-start.9 = (bf16[2,896,1280]{2,1,0:T(8,128)(2,1)}, bf16[2,896,1280]{2,1,0:T(8,128)(2,1)}, u32[]{:S(2)}, u32[]{:S(2)}) collective-permute-start(bf16[2,896,1280]{2,1,0:T(8,128)(2,1)} %pad_maximum_fusion.4), channel_id=1, source_target_pairs={{0,8},{8,0},{16,24},{24,16},{1,9},{9,1},{17,25},{25,17},{2,10},{10... | collective-permute-start | bytes 13762568 | tf_op jit(solution)/shard_map/ppermute | solution.py:48
  170.0 1.8 copy-start.16
  170.0 4.2 copy-start.15
  170.1 4.3 collective-permute-start.12
  171.9 3.5 collective-permute-start
  175.4 1.2 collective-permute-start.1
  177.0 9.9 %copy-start.10 = (bf16[896,1280]{1,0:T(8,128)(2,1)S(1)}, bf16[896,1280]{1,0:T(8,128)(2,1)}, u32[]{:S(2)}) copy-start(bf16[896,1280]{1,0:T(8,128)(2,1)} %param.22) | copy-start | bytes 6881284
  362.4 11.9 %copy-start.2 = (bf16[768,896]{1,0:T(8,128)(2,1)S(1)}, bf16[768,896]{1,0:T(8,128)(2,1)}, u32[]{:S(2)}) copy-start(bf16[768,896]{1,0:T(8,128)(2,1)} %copy-done.1) | copy-start | bytes 4128772
  362.4 11.9 %copy-start.4 = (bf16[768,896]{1,0:T(8,128)(2,1)S(1)}, bf16[768,896]{1,0:T(8,128)(2,1)}, u32[]{:S(2)}) copy-start(bf16[768,896]{1,0:T(8,128)(2,1)} %copy-done.3) | copy-start | bytes 4128772
  362.4 11.9 %copy-start.6 = (bf16[768,896]{1,0:T(8,128)(2,1)S(1)}, bf16[768,896]{1,0:T(8,128)(2,1)}, u32[]{:S(2)}) copy-start(bf16[768,896]{1,0:T(8,128)(2,1)} %copy-done.5) | copy-start | bytes 4128772
  362.4 11.9 %copy-start.8 = (bf16[768,896]{1,0:T(8,128)(2,1)S(1)}, bf16[768,896]{1,0:T(8,128)(2,1)}, u32[]{:S(2)}) copy-start(bf16[768,896]{1,0:T(8,128)(2,1)} %copy-done.7) | copy-start | bytes 4128772
  362.4 11.9 %copy-start.11 = (bf16[4,896,1280]{2,1,0:T(8,128)(2,1)S(1)}, bf16[4,896,1280]{2,1,0:T(8,128)(2,1)}, u32[]{:S(2)}) copy-start(bf16[4,896,1280]{2,1,0:T(8,128)(2,1)} %pad_maximum_fusion.1) | copy-start | bytes 27525124
  400.4 4.5 %collective-permute-start.10 = (f32[16,1280]{1,0:T(8,128)S(1)}, f32[16,1280]{1,0:T(8,128)S(1)}, u32[]{:S(2)}, u32[]{:S(2)}) collective-permute-start(f32[16,1280]{1,0:T(8,128)S(1)} %fusion.9), channel_id=1, source_target_pairs={{0,16},{8,24},{16,0},{24,8},{1,17},{9,25},{17,1},{25,9},{2,18},{10... | collective-permute-start | bytes 245768 | tf_op jit(solution)/shard_map/ppermute | solution.py:45
  404.9 2.6 collective-permute-start.11
  411.7 31.3 %all-to-all-start.1 = ((f32[32,16,448]{2,1,0:T(8,128)}), f32[32,16,448]{2,1,0:T(8,128)S(1)}, u32[]{:S(2)}, u32[]{:S(2)}) async-start(f32[32,16,448]{2,1,0:T(8,128)} %bitcast.103), calls=%async_computation.1 | async-start | bytes 2097152 | tf_op jit(solution)/shard_map/all_to_all | solution.py:197
  415.4 1.2 collective-permute-start.13
Sparse Core Ops, SparseCore 0:
  170.2 192.1 all-reduce.1

commit v2 on v1

--- a/solution.py
+++ b/solution.py
@@ -97,9 +97,11 @@
     q_cols, k_cols = q_weight.shape[1], k_weight.shape[1]
     qkv_full = gather_grp(jnp.concatenate([q_weight, k_weight, v_weight], 1), chips)
     qkv_full = qkv_full.reshape(width, -1)
-    o_full = gather_grp(o_weight, chips).reshape(width, -1)
-    gate_full = gather_grp(gate_weight, chips).reshape(width, -1)
-    up_full = gather_grp(up_weight, chips).reshape(width, -1)
+    o_after, qkv_full = lax.optimization_barrier((o_weight, qkv_full))
+    o_full = gather_grp(o_after, chips).reshape(width, -1)
+    gate_after, up_after, o_full = lax.optimization_barrier((gate_weight, up_weight, o_full))
+    gate_full = gather_grp(gate_after, chips).reshape(width, -1)
+    up_full = gather_grp(up_after, chips).reshape(width, -1)
 
     hidden_perm = take_blocks(hidden_in, order, d_grp, 1)
     attn_gain_perm = take_blocks(attn_gain, order, d_grp, 0)
@@ -128,25 +130,33 @@
     blocked_queries = queries.reshape(blocks, block_rows, local_heads, HEAD_SIZE)
     blocked_keys = key_head.reshape(blocks, block_rows, HEAD_SIZE)
     blocked_values = value_head.reshape(blocks, block_rows, HEAD_SIZE)
-    attention_scores = jnp.einsum(
-        "xwre,xpe->xrwp", blocked_queries, blocked_keys, preferred_element_type=jnp.float32
-    ) * HEAD_SIZE ** (-0.5)
-    attention_scores = jnp.where(same[:, None, :, :], attention_scores, -1e30)
-    attention_probabilities = softmax_rows(attention_scores)
-    attended_rows = jnp.einsum(
-        "asfo,aon->afsn",
-        attention_probabilities,
-        blocked_values,
-        preferred_element_type=jnp.float32,
-    )
-    attended_rows = attended_rows.astype(jnp.bfloat16).reshape(row_count, local_heads * HEAD_SIZE)
-    attn_term = transposed_dot(attended_rows, o_full)
-    attn_total = lax.psum(attn_term.astype(jnp.bfloat16), "tp").astype(jnp.float32)
-    residual = hidden_perm.astype(jnp.float32) + attn_total
-    norm_mid = rms_scale(residual, ffn_gain_perm)
-    gate_pre = jnp.dot(norm_mid, gate_full, preferred_element_type=jnp.float32)
-    up_pre = jnp.dot(norm_mid, up_full, preferred_element_type=jnp.float32)
-    hidden_ffn = (jax.nn.silu(gate_pre) * up_pre).astype(jnp.bfloat16)
+    hidden_blocks = hidden_perm.reshape(blocks, block_rows, width)
+    residual_parts, hidden_parts = [], []
+    for b in range(blocks):
+        attention_scores = jnp.einsum(
+            "wre,pe->rwp", blocked_queries[b], blocked_keys[b], preferred_element_type=jnp.float32
+        ) * HEAD_SIZE ** (-0.5)
+        attention_scores = jnp.where(same[b][None, :, :], attention_scores, -1e30)
+        attention_probabilities = softmax_rows(attention_scores)
+        attended_rows = jnp.einsum(
+            "sfo,on->fsn",
+            attention_probabilities,
+            blocked_values[b],
+            preferred_element_type=jnp.float32,
+        )
+        attended_rows = attended_rows.astype(jnp.bfloat16).reshape(block_rows, local_heads * HEAD_SIZE)
+        attn_term = transposed_dot(attended_rows, o_full).astype(jnp.bfloat16)
+        if residual_parts:
+            attn_term, _ = lax.optimization_barrier((attn_term, residual_parts[-1]))
+        attn_total = lax.psum(attn_term, "tp").astype(jnp.float32)
+        residual_b = hidden_blocks[b].astype(jnp.float32) + attn_total
+        norm_mid = rms_scale(residual_b, ffn_gain_perm)
+        gate_pre = jnp.dot(norm_mid, gate_full, preferred_element_type=jnp.float32)
+        up_pre = jnp.dot(norm_mid, up_full, preferred_element_type=jnp.float32)
+        hidden_parts.append((jax.nn.silu(gate_pre) * up_pre).astype(jnp.bfloat16))
+        residual_parts.append(residual_b)
+    residual = jnp.concatenate(residual_parts, 0)
+    hidden_ffn = jnp.concatenate(hidden_parts, 0)
 
     block_index = lax.broadcasted_iota(jnp.int32, (blocks, block_rows), 0)
     program_of_row = (block_index * per_block + segs).reshape(row_count)

time: 452 us -> 436 us (0.965)
  waiting for transfers between devices: 295 us -> 282 us
  other arithmetic: 55.5 us -> 49.6 us
    ppermute x7, waiting for transfers between devices: 98.4 us -> 70.5 us  [gather_grp(): moving = lax.ppermute(moving, 'grp', ring)]
    all_to_all x1, waiting for transfers between devices: 0.01 us -> 18.3 us  [on_device(): lax.all_to_all(jnp.broadcast_to(kv_part[None], (tp_size,) + kv_part.shape...]
    dot_general x1 -> x6, matrix products: 2.04 us -> 17.8 us  [the longest x2 10.7 us: on_device(): gate_pre = jnp.dot(norm_mid, gate_full, preferred_element_type=jnp.float32)]
    dot_general x1, matrix products: 14.4 us -> 0.38 us  [on_device(): jnp.dot(selector.astype(jnp.bfloat16), hidden_ffn, preferred_element_type...]
    reduce_sum x1 -> x2, other arithmetic: 1.37 us -> 8.22 us  [rms_scale(): factor = lax.rsqrt(jnp.mean(rows * rows, axis=1, keepdims=True) + EPSILON)]
    concatenate x6, other arithmetic: 23 us -> 16.4 us  [gather_grp(): return jnp.concatenate([mine, other], 0)]
    add x1, other arithmetic: 11.9 us -> 5.88 us  [on_device(): residual_b = hidden_blocks[b].astype(jnp.float32) + attn_total]
    psum x1 -> x2, waiting for transfers between devices: 167 us -> 164 us  [on_device(): attn_total = lax.psum(attn_term, 'tp').astype(jnp.float32)]
  transfers between devices with their start and end apart: 17 -> 18, of which waited for: 9 -> 11; matrix products, arithmetic and copies ran while one was open for 16% -> 13% of each run, Pallas kernels for 0% -> 0%
where the time goes in v2:
time: 436 us
  waiting for transfers between devices  282 us (65%)
  other arithmetic  49.6 us (11%)
  matrix products  47.3 us (11%)
  starting transfers between devices  20.8 us (5%)
  local copies, waits for them, and re-layouts  18.2 us (4%)
  between operations  17.2 us (4%)
    psum x2, waiting for transfers between devices, on_device(): attn_total = lax.psum(attn_term, 'tp').astype(jnp.float32)  164 us
    ppermute x7, waiting for transfers between devices, gather_grp(): moving = lax.ppermute(moving, 'grp', ring)  70.5 us
    all_to_all x1, waiting for transfers between devices, on_device(): lax.all_to_all(send.reshape(grp_size * tp_size, slots, d_tp), ('grp', 'tp...  26.1 us
    all_to_all x1, waiting for transfers between devices, on_device(): lax.all_to_all(jnp.broadcast_to(kv_part[None], (tp_size,) + kv_part.shape...  18.3 us
    concatenate x6, other arithmetic, gather_grp(): return jnp.concatenate([mine, other], 0)  16.4 us
    another operation x7, other arithmetic, gather_grp(): mine = jnp.stack(held)  14.4 us
    dot_general x2, matrix products, on_device(): gate_pre = jnp.dot(norm_mid, gate_full, preferred_element_type=jnp.float32)  10.7 us
    dot_general x2, matrix products, on_device(): up_pre = jnp.dot(norm_mid, up_full, preferred_element_type=jnp.float32)  10.4 us
  transfers between devices with their start and end apart: 18, of which 11 were waited for; matrix products, arithmetic and copies ran while one was open for 13% of the time, Pallas kernels for 0%

profile of v2, /device:TPU:0, one launch (start us, length us, event | category | flops | bytes accessed | tf_op | source)
XLA Modules:
  0.0 435.5 jit_solution(6589989745433262680)
XLA Ops:
  6.5 1.2 copy.61
  7.8 1.1 copy.62
  8.8 2.0 pad_maximum_fusion.9
  10.9 2.9 collective-permute-start.2
  13.8 0.6 copy-done.20
  14.4 0.6 fusion.63
  15.0 1.2 fusion.92
  16.2 13.4 %collective-permute-done.2 = bf16[896,384]{1,0:T(8,128)(2,1)} collective-permute-done((bf16[896,384]{1,0:T(8,128)(2,1)}, bf16[896,384]{1,0:T(8,128)(2,1)}, u32[]{:S(2)}, u32[]{:S(2)}) %collective-permute-start.2) | collective-permute-done | bytes 688160 | tf_op jit(solution)/shard_map/ppermute | solution.py:45
  29.5 2.3 pad_maximum_fusion.7
  31.9 0.6 fusion.64
  35.2 3.1 constant_dynamic-slice_fusion.5
  38.2 1.5 fusion.2
  39.7 3.4 pad_maximum_fusion.5
  43.2 2.8 fusion.24
  45.9 0.8 copy-done.11
  46.8 1.3 broadcast_in_dim.29
  48.1 6.2 %all-to-all-start = ((bf16[8,768,128]{1,2,0:T(8,128)(2,1)}), bf16[8,768,128]{1,2,0:T(8,128)(2,1)}, u32[]{:S(2)}, u32[]{:S(2)}) async-start(bf16[8,768,128]{1,2,0:T(8,128)(2,1)} %broadcast_in_dim.29), calls=%async_computation | async-start | bytes 3145728 | tf_op jit(solution)/shard_map/all_to_all | solution.py:114
  54.4 1.6 collective-permute-start.4
  55.9 11.2 %collective-permute-done.4 = bf16[896,256]{1,0:T(8,128)(2,1)S(1)} collective-permute-done((bf16[896,256]{1,0:T(8,128)(2,1)S(1)}, bf16[896,256]{1,0:T(8,128)(2,1)S(1)}, u32[]{:S(2)}, u32[]{:S(2)}) %collective-permute-start.4) | collective-permute-done | bytes 458784 | tf_op jit(solution)/shard_map/ppermute | solution.py:45
  67.1 1.0 pad_maximum_fusion.8
  68.6 0.7 slice_bitcast_fusion
  69.4 1.8 fusion.58
  71.1 2.6 pad_maximum_fusion.6
  73.8 18.3 %all-to-all-done = bf16[8,768,128]{1,2,0:T(8,128)(2,1)} async-done(((bf16[8,768,128]{1,2,0:T(8,128)(2,1)}), bf16[8,768,128]{1,2,0:T(8,128)(2,1)}, u32[]{:S(2)}, u32[]{:S(2)}) %all-to-all-start) | async-done | bytes 1572896 | tf_op jit(solution)/shard_map/all_to_all | solution.py:114
  92.1 1.5 fusion.57
  94.2 0.6 copy-done.13
  94.8 1.4 fusion.21
  96.3 1.6 fusion.65
  98.4 0.7 fusion.60
  99.1 2.1 convolution_convert_fusion.3
  101.2 4.0 convolution_convert_fusion.1
  105.4 1.6 collective-permute-start.6
  107.0 0.5 collective-permute-start.8
  107.5 1.2 fusion.66
  108.7 1.5 fusion.19
  110.1 2.0 convolution_convert_fusion.2
  112.1 4.2 convolution_convert_fusion
  116.3 42.2 %collective-permute-done.6 = bf16[896,1280]{1,0:T(8,128)(2,1)} collective-permute-done((bf16[896,1280]{1,0:T(8,128)(2,1)}, bf16[896,1280]{1,0:T(8,128)(2,1)}, u32[]{:S(2)}, u32[]{:S(2)}) %collective-permute-start.6) | collective-permute-done | bytes 2293792 | tf_op jit(solution)/shard_map/ppermute | solution.py:45
  158.6 5.0 %pad_maximum_fusion.3 = bf16[2,896,1280]{2,1,0:T(8,128)(2,1)} fusion(bf16[1,896,1280]{2,1,0:T(8,128)(2,1)} %bitcast.30, bf16[1,896,1280]{2,1,0:T(8,128)(2,1)} %bitcast.137), kind=kLoop, calls=%fused_computation.23 | loop fusion | flops 2293760 | bytes 9175040 | tf_op jit(solution)/shard_map/stack | solution.py:47
  163.5 59.4 %all-reduce.3.cloned.1.call-done = bf16[384,3584]{1,0:T(8,128)(2,1)} async-done(((bf16[384,3584]{1,0:T(8,128)(2,1)}), bf16[384,3584]{1,0:T(8,128)(2,1)}) %all-reduce.3.cloned.1.call-update) | async-done | bytes 2752528 | tf_op jit(solution)/shard_map/psum | solution.py:151
  222.9 5.9 %convert_add_fusion.1 = f32[384,3584]{1,0:T(8,128)} fusion(bf16[384,3584]{1,0:T(8,128)(2,1)} %all-reduce.3.cloned.1.call-done, bf16[768,3584]{1,0:T(8,128)(2,1)} %copy-done.1), kind=kLoop, calls=%fused_computation.20 | loop fusion | flops 4128768 | bytes 11010048 | tf_op jit(solution)/shard_map/add | solution.py:152
  228.9 4.9 %pad_maximum_fusion.4 = bf16[2,896,1280]{2,1,0:T(8,128)(2,1)} fusion(bf16[1,896,1280]{2,1,0:T(8,128)(2,1)} %bitcast.33, bf16[1,896,1280]{2,1,0:T(8,128)(2,1)} %bitcast.139), kind=kLoop, calls=%fused_computation.24 | loop fusion | flops 2293760 | bytes 9175040 | tf_op jit(solution)/shard_map/stack | solution.py:47
  233.9 1.4 collective-permute-start.12
  235.3 0.6 collective-permute-start
  235.9 0.8 compare_reduce_fusion
  237.9 1.0 collective-permute-done
  238.9 2.6 collective-permute-done.1
  241.9 104.6 %all-reduce.5.cloned.1.call-done = bf16[384,3584]{1,0:T(8,128)(2,1)} async-done(((bf16[384,3584]{1,0:T(8,128)(2,1)}), bf16[384,3584]{1,0:T(8,128)(2,1)}) %all-reduce.5.cloned.1.call-update) | async-done | bytes 2752528 | tf_op jit(solution)/shard_map/psum | solution.py:151
  346.6 6.7 %multiply_reduce_fusion.1 = (f32[384]{0:T(512)S(1)}, f32[384]{0:T(512)S(1)}, f32[384,3584]{1,0:T(8,128)}) fusion(bf16[384,3584]{1,0:T(8,128)(2,1)} %all-reduce.3.cloned.1.call-done, bf16[768,3584]{1,0:T(8,128)(2,1)} %copy-done.1, bf16[384,3584]{1,0:T(8,128)(2,1)} %all-reduce.5.cloned.1.call-done), kind=kLoop, calls=%fused_computation.19 | loop fusion | flops 13761792 | bytes 16518144 | tf_op jit(solution)/shard_map/reduce_sum | solution.py:17
  353.4 5.2 %pad_maximum_fusion = bf16[4,896,1280]{2,1,0:T(8,128)(2,1)S(1)} fusion(bf16[2,896,1280]{2,1,0:T(8,128)(2,1)} %collective-permute-done.7, bf16[1,896,1280]{2,1,0:T(8,128)(2,1)} %bitcast.30, bf16[1,896,1280]{2,1,0:T(8,128)(2,1)S(1)} %bitcast.138), kind=kLoop, calls=%fused_computation.9 | loop fusion | flops 9175040 | bytes 18350080 | tf_op jit(solution)/shard_map/concatenate | solution.py:49
  358.6 5.1 %pad_maximum_fusion.1 = bf16[4,896,1280]{2,1,0:T(8,128)(2,1)S(1)} fusion(bf16[2,896,1280]{2,1,0:T(8,128)(2,1)} %collective-permute-done.9, bf16[1,896,1280]{2,1,0:T(8,128)(2,1)} %bitcast.33, bf16[1,896,1280]{2,1,0:T(8,128)(2,1)S(1)} %bitcast.140), kind=kLoop, calls=%fused_computation.10 | loop fusion | flops 9175040 | bytes 18350080 | tf_op jit(solution)/shard_map/concatenate | solution.py:49
  363.8 5.4 %fusion.54 = f32[384,1280]{1,0:T(8,128)} fusion(bf16[3584,1280]{1,0:T(8,128)(2,1)S(1)} %bitcast.143, f32[3584]{0:T(1024)S(1)} %pad_maximum_fusion.13, f32[384]{0:T(512)S(1)} %add_rsqrt_fusion.2, bf16[384,3584]{1,0:T(8,128)(2,1)S(1)} %copy-done.2, bf16[768,3584]{1,0:T(8,128)(2,1)S(1)} %bitcast.134), kind=kOutput, calls=%fused_computation.129 | convolution fusion | flops 3531472896 | bytes 16664576 | tf_op jit(solution)/shard_map/dot_general | solution.py:154
  369.2 5.4 %fusion.56 = f32[384,1280]{1,0:T(8,128)} fusion(bf16[3584,1280]{1,0:T(8,128)(2,1)S(1)} %bitcast.144, f32[384]{0:T(512)S(1)} %add_rsqrt_fusion.1, f32[3584]{0:T(1024)S(1)} %pad_maximum_fusion.13, bf16[384,3584]{1,0:T(8,128)(2,1)S(1)} %copy-done.5, bf16[768,3584]{1,0:T(8,128)(2,1)S(1)} %bitcast.134), kind=kOutput, calls=%fused_computation.131 | convolution fusion | flops 3531472896 | bytes 16664576 | tf_op jit(solution)/shard_map/dot_general | solution.py:154
  374.6 5.9 %multiply_convert_fusion.3 = bf16[384,1280]{1,0:T(8,128)(2,1)S(1)} fusion(f32[384,1280]{1,0:T(8,128)} %fusion.54, bf16[3584,1280]{1,0:T(8,128)(2,1)S(1)} %bitcast.141, f32[3584]{0:T(1024)S(1)} %pad_maximum_fusion.13, f32[384]{0:T(512)S(1)} %add_rsqrt_fusion.2, bf16[384,3584]{1,0:T(8,128)(2,1)S(1)} %copy-done.2, bf16[768,3584]{1,0:T(8,128)(2,1)S(1)} %bitcast.134), kind=kOutput, calls=%fused_computation.31 | convolution fusion | flops 3534422016 | bytes 17647616 | tf_op jit(solution)/shard_map/dot_general | solution.py:155
  380.5 4.5 %multiply_convert_fusion.2 = bf16[384,1280]{1,0:T(8,128)(2,1)S(1)} fusion(f32[384,1280]{1,0:T(8,128)S(1)} %copy-done.25, bf16[3584,1280]{1,0:T(8,128)(2,1)S(1)} %bitcast.142, f32[384]{0:T(512)S(1)} %add_rsqrt_fusion.1, f32[3584]{0:T(1024)S(1)} %pad_maximum_fusion.13, bf16[384,3584]{1,0:T(8,128)(2,1)S(1)} %copy-done.5, bf16[768,3584]{1,0:T(8,128)(2,1)S(1)} %bitcast.134), kind=kOutput, calls=%fused_computation.30 | convolution fusion | flops 3534422016 | bytes 17647616 | tf_op jit(solution)/shard_map/dot_general | solution.py:155
  385.3 1.5 collective-permute-start.10
  387.0 2.8 collective-permute-done.10
  390.0 2.4 fusion.29
  392.4 2.1 convolution_bitcast_fusion.1
  395.5 1.1 copy.75
  396.6 3.7 all-to-all-start.1
  400.6 0.9 collective-permute-done.13
  401.8 26.1 %all-to-all-done.1 = f32[32,16,448]{2,1,0:T(8,128)S(1)} async-done(((f32[32,16,448]{2,1,0:T(8,128)}), f32[32,16,448]{2,1,0:T(8,128)S(1)}, u32[]{:S(2)}, u32[]{:S(2)}) %all-to-all-start.1) | async-done | bytes 917536 | tf_op jit(solution)/shard_map/all_to_all | solution.py:207
  428.0 0.7 divide_convert_fusion.4
  (125 shorter events, 5.6 us)
Async XLA Ops:
  6.5 385.9 %copy-start = (bf16[896,1280]{1,0:T(8,128)(2,1)S(1)}, bf16[896,1280]{1,0:T(8,128)(2,1)}, u32[]{:S(2)}) copy-start(bf16[896,1280]{1,0:T(8,128)(2,1)} %param.23) | copy-start | bytes 6881284
  8.8 26.2 %copy-start.16 = (f32[3584]{0:T(1024)S(1)}, f32[3584]{0:T(1024)}, u32[]{:S(2)}) copy-start(f32[3584]{0:T(1024)} %param.15) | copy-start | bytes 43012
  10.9 18.7 %collective-permute-start.2 = (bf16[896,384]{1,0:T(8,128)(2,1)}, bf16[896,384]{1,0:T(8,128)(2,1)}, u32[]{:S(2)}, u32[]{:S(2)}) collective-permute-start(bf16[896,384]{1,0:T(8,128)(2,1)} %pad_maximum_fusion.9), channel_id=1, source_target_pairs={{0,16},{8,24},{16,0},{24,8},{1,17},{9,25},{17,1},{25,9},{2,18},{10... | collective-permute-start | bytes 2064392 | tf_op jit(solution)/shard_map/ppermute | solution.py:45
  13.8 0.6 copy-start.20
  13.8 18.1 %copy-start.18 = (s32[2]{0:T(128)}, s32[2]{0:T(128)S(1)}, u32[]{:S(2)}) copy-start(s32[2]{0:T(128)S(1)} %get-tuple-element.52) | copy-start | bytes 28
  31.9 7.9 %collective-permute-start.3 = (bf16[2,896,384]{2,1,0:T(8,128)(2,1)}, bf16[2,896,384]{2,1,0:T(8,128)(2,1)}, u32[]{:S(2)}, u32[]{:S(2)}) collective-permute-start(bf16[2,896,384]{2,1,0:T(8,128)(2,1)} %pad_maximum_fusion.7), channel_id=1, source_target_pairs={{0,8},{8,0},{16,24},{24,16},{1,9},{9,1},{17,25},{25,17},{2,10},{10... | collective-permute-start | bytes 4128776 | tf_op jit(solution)/shard_map/ppermute | solution.py:48
  39.7 3.4 copy-start.1
  45.9 0.8 copy-start.11
  46.8 7.6 %copy-start.6 = (bf16[896,256]{1,0:T(8,128)(2,1)S(1)}, bf16[896,256]{1,0:T(8,128)(2,1)}, u32[]{:S(2)}) copy-start(bf16[896,256]{1,0:T(8,128)(2,1)} %param.19) | copy-start | bytes 1376260
  48.1 20.0 %copy-start.23 = (s32[2,8]{1,0:T(2,128)S(1)}, s32[2,8]{1,0:T(2,128)}, u32[]{:S(2)}) copy-start(s32[2,8]{1,0:T(2,128)} %param.13) | copy-start | bytes 196
  48.1 44.0 %all-to-all-start = ((bf16[8,768,128]{1,2,0:T(8,128)(2,1)}), bf16[8,768,128]{1,2,0:T(8,128)(2,1)}, u32[]{:S(2)}, u32[]{:S(2)}) async-start(bf16[8,768,128]{1,2,0:T(8,128)(2,1)} %broadcast_in_dim.29), calls=%async_computation | async-start | bytes 3145728 | tf_op jit(solution)/shard_map/all_to_all | solution.py:114
  54.3 168.6 %all-reduce.3.cloned.1.call-start = ((), (), s32[]{:S(2)}) async-start(), calls=%async_computation.2 | async-start | bytes 5505024 | tf_op jit(solution)/shard_map/psum | solution.py:151
  54.4 12.7 %collective-permute-start.4 = (bf16[896,256]{1,0:T(8,128)(2,1)S(1)}, bf16[896,256]{1,0:T(8,128)(2,1)S(1)}, u32[]{:S(2)}, u32[]{:S(2)}) collective-permute-start(bf16[896,256]{1,0:T(8,128)(2,1)S(1)} %copy-done.6), channel_id=1, source_target_pairs={{0,16},{8,24},{16,0},{24,8},{1,17},{9,25},{17,1},{25,9},{2,18},{10... | collective-permute-start | bytes 1376264 | tf_op jit(solution)/shard_map/ppermute | solution.py:45
  68.1 3.0 collective-permute-start.5
  68.4 1.0 copy-start.14
  69.4 38.1 %copy-start.9 = (pred[384,384]{0,1:T(8,128)(4,1)}, pred[384,384]{0,1:T(8,128)(4,1)S(1)}, u32[]{:S(2)}) copy-start(pred[384,384]{0,1:T(8,128)(4,1)S(1)} %get-tuple-element.32) | copy-start | bytes 442372
  71.1 36.4 %copy-start.7 = (bf16[384,256]{0,1:T(8,128)(2,1)}, bf16[384,256]{0,1:T(8,128)(2,1)S(1)}, u32[]{:S(2)}) copy-start(bf16[384,256]{0,1:T(8,128)(2,1)S(1)} %get-tuple-element.30) | copy-start | bytes 589828
  92.1 2.7 copy-start.8
  92.1 2.7 copy-start.10
  94.2 0.6 copy-start.13
  94.2 13.3 %copy-start.12 = (bf16[384,8,16]{0,2,1:T(8,128)(2,1)}, bf16[384,8,16]{0,2,1:T(8,128)(2,1)S(1)}, u32[]{:S(2)}) copy-start(bf16[384,8,16]{0,2,1:T(8,128)(2,1)S(1)} %get-tuple-element.34) | copy-start | bytes 294916
  105.2 241.4 %all-reduce.5.cloned.1.call-start = ((), (), s32[]{:S(2)}) async-start(), calls=%async_computation.3 | async-start | bytes 5505024 | tf_op jit(solution)/shard_map/psum | solution.py:151
  105.4 53.2 %collective-permute-start.6 = (bf16[896,1280]{1,0:T(8,128)(2,1)}, bf16[896,1280]{1,0:T(8,128)(2,1)}, u32[]{:S(2)}, u32[]{:S(2)}) collective-permute-start(bf16[896,1280]{1,0:T(8,128)(2,1)} %param.21), channel_id=1, source_target_pairs={{0,16},{8,24},{16,0},{24,8},{1,17},{9,25},{17,1},{25,9},{2,18},{10... | collective-permute-start | bytes 6881288 | tf_op jit(solution)/shard_map/ppermute | solution.py:45
  107.0 121.9 %collective-permute-start.8 = (bf16[896,1280]{1,0:T(8,128)(2,1)}, bf16[896,1280]{1,0:T(8,128)(2,1)}, u32[]{:S(2)}, u32[]{:S(2)}) collective-permute-start(bf16[896,1280]{1,0:T(8,128)(2,1)} %param.22), channel_id=1, source_target_pairs={{0,16},{8,24},{16,0},{24,8},{1,17},{9,25},{17,1},{25,9},{2,18},{10... | collective-permute-start | bytes 6881288 | tf_op jit(solution)/shard_map/ppermute | solution.py:45
  163.5 189.8 %collective-permute-start.7 = (bf16[2,896,1280]{2,1,0:T(8,128)(2,1)}, bf16[2,896,1280]{2,1,0:T(8,128)(2,1)}, u32[]{:S(2)}, u32[]{:S(2)}) collective-permute-start(bf16[2,896,1280]{2,1,0:T(8,128)(2,1)} %pad_maximum_fusion.3), channel_id=1, source_target_pairs={{0,8},{8,0},{16,24},{24,16},{1,9},{9,1},{17,25},{25,17},{2,10},{10... | collective-permute-start | bytes 13762568 | tf_op jit(solution)/shard_map/ppermute | solution.py:48
  228.8 5.0 %copy-start.24 = (s32[2,8]{1,0:T(2,128)S(1)}, s32[2,8]{1,0:T(2,128)}, u32[]{:S(2)}) copy-start(s32[2,8]{1,0:T(2,128)} %param.13) | copy-start | bytes 196
  228.8 6.4 %copy-start.22 = (s32[16,1]{0,1:T(1,128)S(1)}, s32[16,1]{0,1:T(1,128)}, u32[]{:S(2)}) copy-start(s32[16,1]{0,1:T(1,128)} %param.14) | copy-start | bytes 196
  228.9 7.1 %copy-start.19 = (s32[2]{0:T(128)S(1)}, s32[2]{0:T(128)}, u32[]{:S(2)}) copy-start(s32[2]{0:T(128)} %copy-done.18) | copy-start | bytes 28
  228.9 7.1 %copy-start.21 = (s32[2]{0:T(128)S(1)}, s32[2]{0:T(128)}, u32[]{:S(2)}) copy-start(s32[2]{0:T(128)} %copy-done.20) | copy-start | bytes 28
  228.9 8.6 %copy-start.15 = (s32[2,384]{1,0:T(2,128)S(1)}, s32[2,384]{1,0:T(2,128)}, u32[]{:S(2)}) copy-start(s32[2,384]{1,0:T(2,128)} %copy-done.14) | copy-start | bytes 9220
  228.9 8.9 %copy-start.17 = (f32[3584]{0:T(1024)S(1)}, f32[3584]{0:T(1024)}, u32[]{:S(2)}) copy-start(f32[3584]{0:T(1024)} %param.20) | copy-start | bytes 43012
  233.8 124.8 %collective-permute-start.9 = (bf16[2,896,1280]{2,1,0:T(8,128)(2,1)}, bf16[2,896,1280]{2,1,0:T(8,128)(2,1)}, u32[]{:S(2)}, u32[]{:S(2)}) collective-permute-start(bf16[2,896,1280]{2,1,0:T(8,128)(2,1)} %pad_maximum_fusion.4), channel_id=1, source_target_pairs={{0,8},{8,0},{16,24},{24,16},{1,9},{9,1},{17,25},{25,17},{2,10},{10... | collective-permute-start | bytes 13762568 | tf_op jit(solution)/shard_map/ppermute | solution.py:48
  233.9 4.0 collective-permute-start.12
  235.3 3.5 collective-permute-start
  238.8 2.7 collective-permute-start.1
  346.6 6.8 %copy-start.3 = (bf16[896,1280]{1,0:T(8,128)(2,1)S(1)}, bf16[896,1280]{1,0:T(8,128)(2,1)}, u32[]{:S(2)}) copy-start(bf16[896,1280]{1,0:T(8,128)(2,1)} %param.21) | copy-start | bytes 6881284
  353.4 5.3 %copy-start.4 = (bf16[896,1280]{1,0:T(8,128)(2,1)S(1)}, bf16[896,1280]{1,0:T(8,128)(2,1)}, u32[]{:S(2)}) copy-start(bf16[896,1280]{1,0:T(8,128)(2,1)} %param.22) | copy-start | bytes 6881284
  353.4 10.4 %slice-start = ((s8[5505024]{0:T(1024)(128)(4,1)}), s8[4194304]{0:T(1024)(128)(4,1)S(1)}, s32[]{:S(2)}) async-start(s8[5505024]{0:T(1024)(128)(4,1)} %bitcast.133), calls=%async_computation.4 | async-start | bytes 8388608
  358.6 5.2 %slice-start.1 = ((s8[5505024]{0:T(1024)(128)(4,1)}), s8[1310720]{0:T(1024)(128)(4,1)S(1)}, s32[]{:S(2)}) async-start(s8[5505024]{0:T(1024)(128)(4,1)} %bitcast.133), calls=%async_computation.5 | async-start | bytes 2621440
  358.6 5.2 %copy-start.2 = (bf16[384,3584]{1,0:T(8,128)(2,1)S(1)}, bf16[384,3584]{1,0:T(8,128)(2,1)}, u32[]{:S(2)}) copy-start(bf16[384,3584]{1,0:T(8,128)(2,1)} %all-reduce.3.cloned.1.call-done) | copy-start | bytes 8257540
  363.8 5.4 %copy-start.5 = (bf16[384,3584]{1,0:T(8,128)(2,1)S(1)}, bf16[384,3584]{1,0:T(8,128)(2,1)}, u32[]{:S(2)}) copy-start(bf16[384,3584]{1,0:T(8,128)(2,1)} %all-reduce.5.cloned.1.call-done) | copy-start | bytes 8257540
  374.6 5.9 %copy-start.25 = (f32[384,1280]{1,0:T(8,128)S(1)}, f32[384,1280]{1,0:T(8,128)}, u32[]{:S(2)}) copy-start(f32[384,1280]{1,0:T(8,128)} %fusion.56) | copy-start | bytes 5898244
  385.3 4.5 %collective-permute-start.10 = (f32[16,1280]{1,0:T(8,128)S(1)}, f32[16,1280]{1,0:T(8,128)S(1)}, u32[]{:S(2)}, u32[]{:S(2)}) collective-permute-start(f32[16,1280]{1,0:T(8,128)S(1)} %fusion.9), channel_id=1, source_target_pairs={{0,16},{8,24},{16,0},{24,8},{1,17},{9,25},{17,1},{25,9},{2,18},{10... | collective-permute-start | bytes 245768 | tf_op jit(solution)/shard_map/ppermute | solution.py:45
  389.8 2.6 collective-permute-start.11
  396.6 31.3 %all-to-all-start.1 = ((f32[32,16,448]{2,1,0:T(8,128)}), f32[32,16,448]{2,1,0:T(8,128)S(1)}, u32[]{:S(2)}, u32[]{:S(2)}) async-start(f32[32,16,448]{2,1,0:T(8,128)} %bitcast.145), calls=%async_computation.1 | async-start | bytes 2097152 | tf_op jit(solution)/shard_map/all_to_all | solution.py:207
  400.3 1.2 collective-permute-start.13
Sparse Core Ops, SparseCore 0:
  105.3 117.5 all-reduce.2
  228.9 117.5 all-reduce.4

commit v3 on v1

--- a/solution.py
+++ b/solution.py
@@ -62,6 +62,42 @@
         [lax.dynamic_slice_in_dim(x, order[k] * size, size, axis) for k in range(order.shape[0])],
         axis,
     )
+
+
+def ring_walk(n):
+    if n % 2:
+        return list(range(n))
+    return list(range(0, n, 2)) + list(range(n - 1, 0, -2))
+
+
+def ring_psum(x, axis, n):
+    walk = ring_walk(n)
+    place = [0] * n
+    for p, t in enumerate(walk):
+        place[t] = p
+    pos = jnp.asarray(place, jnp.int32)[lax.axis_index(axis)]
+    rows, half = x.shape[0], x.shape[1] // 2
+    size = rows // n
+    parts = []
+    for sign, local in ((1, x[:, :half]), (-1, x[:, half:])):
+        pairs = [(walk[p], walk[(p + sign) % n]) for p in range(n)]
+
+        def chunk(k):
+            return lax.dynamic_slice_in_dim(local, ((pos - sign * k) % n) * size, size, 0)
+
+        acc = chunk(0)
+        for step in range(n - 1):
+            got = lax.ppermute(acc, axis, pairs)
+            acc = (got.astype(jnp.float32) + chunk(step + 1).astype(jnp.float32)).astype(x.dtype)
+        out = jnp.zeros_like(local)
+        moving = acc
+        for step in range(n):
+            if step:
+                moving = lax.ppermute(moving, axis, pairs)
+            where = ((pos + sign - sign * step) % n) * size
+            out = lax.dynamic_update_slice_in_dim(out, moving, where, 0)
+        parts.append(out)
+    return jnp.concatenate(parts, 1)
 
 
 def on_device(
@@ -97,9 +133,11 @@
     q_cols, k_cols = q_weight.shape[1], k_weight.shape[1]
     qkv_full = gather_grp(jnp.concatenate([q_weight, k_weight, v_weight], 1), chips)
     qkv_full = qkv_full.reshape(width, -1)
-    o_full = gather_grp(o_weight, chips).reshape(width, -1)
-    gate_full = gather_grp(gate_weight, chips).reshape(width, -1)
-    up_full = gather_grp(up_weight, chips).reshape(width, -1)
+    o_after, qkv_full = lax.optimization_barrier((o_weight, qkv_full))
+    o_full = gather_grp(o_after, chips).reshape(width, -1)
+    gate_after, up_after, o_full = lax.optimization_barrier((gate_weight, up_weight, o_full))
+    gate_full = gather_grp(gate_after, chips).reshape(width, -1)
+    up_full = gather_grp(up_after, chips).reshape(width, -1)
 
     hidden_perm = take_blocks(hidden_in, order, d_grp, 1)
     attn_gain_perm = take_blocks(attn_gain, order, d_grp, 0)
@@ -140,8 +178,8 @@
         preferred_element_type=jnp.float32,
     )
     attended_rows = attended_rows.astype(jnp.bfloat16).reshape(row_count, local_heads * HEAD_SIZE)
-    attn_term = transposed_dot(attended_rows, o_full)
-    attn_total = lax.psum(attn_term.astype(jnp.bfloat16), "tp").astype(jnp.float32)
+    attn_term = transposed_dot(attended_rows, o_full).astype(jnp.bfloat16)
+    attn_total = ring_psum(attn_term, "tp", tp_size).astype(jnp.float32)
     residual = hidden_perm.astype(jnp.float32) + attn_total
     norm_mid = rms_scale(residual, ffn_gain_perm)
     gate_pre = jnp.dot(norm_mid, gate_full, preferred_element_type=jnp.float32)

time: 452 us -> 331 us (0.73)
  waiting for transfers between devices: 295 us -> 150 us
  starting transfers between devices: 20 us -> 51.4 us
  other arithmetic: 55.5 us -> 45.5 us
  local copies, waits for them, and re-layouts: 16.4 us -> 21.9 us
    psum x1 -> x0, waiting for transfers between devices: 167 us -> none  [on_device(): lax.psum(attn_term.astype(jnp.bfloat16), 'tp').astype(jnp.float32)]
    ppermute x0 -> x28, waiting for transfers between devices: none -> 83.5 us  [the longest x14 42.1 us: ring_psum(): moving = lax.ppermute(moving, axis, pairs)]
    ppermute x7, waiting for transfers between devices: 98.4 us -> 33.8 us  [gather_grp(): moving = lax.ppermute(moving, 'grp', ring)]
    ppermute x0 -> x28, starting transfers between devices: none -> 28.8 us  [the longest x14 14.6 us: ring_psum(): moving = lax.ppermute(moving, axis, pairs)]
    add x1 -> x0, other arithmetic: 11.9 us -> none  [on_device(): residual = hidden_perm.astype(jnp.float32) + attn_total]
    all_to_all x1, waiting for transfers between devices: 0.01 us -> 4.94 us  [on_device(): lax.all_to_all(jnp.broadcast_to(kv_part[None], (tp_size,) + kv_part.shape...]
  transfers between devices with their start and end apart: 17 -> 44, of which waited for: 9 -> 24; matrix products, arithmetic and copies ran while one was open for 16% -> 21% of each run, Pallas kernels for 0% -> 0%
where the time goes in v3:
time: 331 us; the launch traced here: 329 us
  waiting for transfers between devices  150 us (45%)
  starting transfers between devices  51.4 us (16%)
  other arithmetic  45.5 us (14%)
  matrix products  45.2 us (14%)
  local copies, waits for them, and re-layouts  21.9 us (7%)
  between operations  15.3 us (5%)
    ppermute x14, waiting for transfers between devices, ring_psum(): moving = lax.ppermute(moving, axis, pairs)  42.1 us
    ppermute x14, waiting for transfers between devices, ring_psum(): got = lax.ppermute(acc, axis, pairs)  41.4 us
    ppermute x7, waiting for transfers between devices, gather_grp(): moving = lax.ppermute(moving, 'grp', ring)  33.8 us
    all_to_all x1, waiting for transfers between devices, on_device(): lax.all_to_all(send.reshape(grp_size * tp_size, slots, d_tp), ('grp', 'tp...  26.1 us
    concatenate x6, other arithmetic, gather_grp(): return jnp.concatenate([mine, other], 0)  23 us
    dot_general x1, matrix products, on_device(): jnp.dot(selector.astype(jnp.bfloat16), hidden_ffn, preferred_element_type...  15.6 us
    ppermute x14, starting transfers between devices, ring_psum(): moving = lax.ppermute(moving, axis, pairs)  14.6 us
    ppermute x14, starting transfers between devices, ring_psum(): got = lax.ppermute(acc, axis, pairs)  14.3 us
  transfers between devices with their start and end apart: 44, of which 24 were waited for; matrix products, arithmetic and copies ran while one was open for 21% of the time, Pallas kernels for 0%

profile of v3, /device:TPU:0, one launch (start us, length us, event | category | flops | bytes accessed | tf_op | source)
XLA Modules:
  0.0 329.5 jit_solution(2309665275457145710)
XLA Ops:
  2.3 2.0 pad_maximum_fusion.9
  4.3 2.9 collective-permute-start.2
  10.3 12.7 %collective-permute-done.2 = bf16[896,384]{1,0:T(8,128)(2,1)} collective-permute-done((bf16[896,384]{1,0:T(8,128)(2,1)}, bf16[896,384]{1,0:T(8,128)(2,1)}, u32[]{:S(2)}, u32[]{:S(2)}) %collective-permute-start.2) | collective-permute-done | bytes 688160 | tf_op jit(solution)/shard_map/ppermute | solution.py:45
  23.0 2.3 pad_maximum_fusion.7
  27.5 3.1 constant_dynamic-slice_fusion.8
  32.0 2.3 pad_maximum_fusion.5
  34.3 4.1 %fusion.12 = bf16[768,384]{1,0:T(8,128)(2,1)S(1)} fusion(bf16[3584,384]{1,0:T(8,128)(2,1)S(1)} %bitcast.105, f32[3584]{0:T(1024)S(1)} %pad_maximum_fusion.12, f32[768]{0:T(1024)S(1)} %add_rsqrt_fusion.1, bf16[768,896]{1,0:T(8,128)(2,1)S(1)} %get-tuple-element.27, bf16[768,896]{1,0:T(8,128)(2,1)S(1)} %get-tuple-element.28, ...), kind=kOutput, calls=%fused_computation.29 | convolution fusion | flops 2144501760 | bytes 8864768 | tf_op jit(solution)/shard_map/dot_general | solution.py:147
  40.7 6.1 %all-to-all-start = ((bf16[8,768,128]{1,2,0:T(8,128)(2,1)}), bf16[8,768,128]{1,2,0:T(8,128)(2,1)}, u32[]{:S(2)}, u32[]{:S(2)}) async-start(bf16[8,768,128]{1,2,0:T(8,128)(2,1)} %broadcast_in_dim.19), calls=%async_computation | async-start | bytes 3145728 | tf_op jit(solution)/shard_map/all_to_all | solution.py:150
  46.9 1.5 collective-permute-start.40
  49.7 1.5 collective-permute-start.4
  58.3 3.6 %collective-permute-done.4 = bf16[896,256]{1,0:T(8,128)(2,1)S(1)} collective-permute-done((bf16[896,256]{1,0:T(8,128)(2,1)S(1)}, bf16[896,256]{1,0:T(8,128)(2,1)S(1)}, u32[]{:S(2)}, u32[]{:S(2)}) %collective-permute-start.4) | collective-permute-done | bytes 458784 | tf_op jit(solution)/shard_map/ppermute | solution.py:45
  71.9 1.8 slice.55
  73.7 1.9 reshape.188
  75.6 2.6 pad_maximum_fusion.6
  78.2 1.5 collective-permute-start.36
  79.7 4.9 %all-to-all-done = bf16[8,768,128]{1,2,0:T(8,128)(2,1)} async-done(((bf16[8,768,128]{1,2,0:T(8,128)(2,1)}), bf16[8,768,128]{1,2,0:T(8,128)(2,1)}, u32[]{:S(2)}, u32[]{:S(2)}) %all-to-all-start) | async-done | bytes 1572896 | tf_op jit(solution)/shard_map/all_to_all | solution.py:150
  84.6 1.5 fusion.62
  88.3 3.5 %fusion.67 = (f32[2,2,384]{2,1,0:T(2,128)S(1)}, f32[2,2,384,384]{2,3,1,0:T(8,128)}) fusion(pred[2,384,384]{1,2,0:T(8,128)(4,1)} %broadcast_compare_fusion, bf16[2,384,2,128]{3,2,1,0:T(2,128)(2,1)S(1)} %copy-done.13, bf16[2,384,128,1]{1,0,2,3:T(2,128)(2,1)} %bitcast.120), kind=kOutput, calls=%fused_computation.151 | convolution fusion | flops 153354624 | bytes 3250176 | tf_op jit(solution)/shard_map/sub | solution.py:29
  91.8 2.0 fusion.15
  94.3 3.1 convolution_convert_fusion
  99.1 1.5 collective-permute-start.34
  100.6 1.5 collective-permute-start.20
  102.1 5.2 %collective-permute-done.6 = bf16[96,1792]{1,0:T(8,128)(2,1)S(1)} collective-permute-done((bf16[96,1792]{1,0:T(8,128)(2,1)S(1)}, bf16[96,1792]{1,0:T(8,128)(2,1)S(1)}, u32[]{:S(2)}, u32[]{:S(2)}) %collective-permute-start.6) | collective-permute-done | bytes 344096 | tf_op jit(solution)/shard_map/ppermute | solution.py:90
  107.7 2.0 collective-permute-done.20
  109.8 1.5 collective-permute-start.21
  111.3 4.7 %collective-permute-done.7 = bf16[96,1792]{1,0:T(8,128)(2,1)S(1)} collective-permute-done((bf16[96,1792]{1,0:T(8,128)(2,1)S(1)}, bf16[96,1792]{1,0:T(8,128)(2,1)S(1)}, u32[]{:S(2)}, u32[]{:S(2)}) %collective-permute-start.7) | collective-permute-done | bytes 344096 | tf_op jit(solution)/shard_map/ppermute | solution.py:90
  118.2 1.7 collective-permute-start.22
  119.9 11.3 %collective-permute-done.36 = bf16[896,1280]{1,0:T(8,128)(2,1)} collective-permute-done((bf16[896,1280]{1,0:T(8,128)(2,1)}, bf16[896,1280]{1,0:T(8,128)(2,1)}, u32[]{:S(2)}, u32[]{:S(2)}) %collective-permute-start.36) | collective-permute-done | bytes 2293792 | tf_op jit(solution)/shard_map/ppermute | solution.py:45
  131.2 4.9 %pad_maximum_fusion.4 = bf16[2,896,1280]{2,1,0:T(8,128)(2,1)} fusion(bf16[1,896,1280]{2,1,0:T(8,128)(2,1)} %bitcast.29, bf16[1,896,1280]{2,1,0:T(8,128)(2,1)} %bitcast.28), kind=kLoop, calls=%fused_computation.17 | loop fusion | flops 2293760 | bytes 9175040 | tf_op jit(solution)/shard_map/stack | solution.py:47
  136.2 1.8 collective-permute-start.9
  138.4 8.3 %collective-permute-done.9 = bf16[96,1792]{1,0:T(8,128)(2,1)S(1)} collective-permute-done((bf16[96,1792]{1,0:T(8,128)(2,1)S(1)}, bf16[96,1792]{1,0:T(8,128)(2,1)S(1)}, u32[]{:S(2)}, u32[]{:S(2)}) %collective-permute-start.9) | collective-permute-done | bytes 344096 | tf_op jit(solution)/shard_map/ppermute | solution.py:90
  146.8 1.8 collective-permute-start.10
  149.0 7.5 %collective-permute-done.10 = bf16[96,1792]{1,0:T(8,128)(2,1)S(1)} collective-permute-done((bf16[96,1792]{1,0:T(8,128)(2,1)S(1)}, bf16[96,1792]{1,0:T(8,128)(2,1)S(1)}, u32[]{:S(2)}, u32[]{:S(2)}) %collective-permute-start.10) | collective-permute-done | bytes 344096 | tf_op jit(solution)/shard_map/ppermute | solution.py:90
  156.6 1.8 collective-permute-start.11
  158.8 6.6 %collective-permute-done.11 = bf16[96,1792]{1,0:T(8,128)(2,1)S(1)} collective-permute-done((bf16[96,1792]{1,0:T(8,128)(2,1)S(1)}, bf16[96,1792]{1,0:T(8,128)(2,1)S(1)}, u32[]{:S(2)}, u32[]{:S(2)}) %collective-permute-start.11) | collective-permute-done | bytes 344096 | tf_op jit(solution)/shard_map/ppermute | solution.py:90
  165.6 1.8 collective-permute-start.12
  167.8 5.7 %collective-permute-done.12 = bf16[96,1792]{1,0:T(8,128)(2,1)S(1)} collective-permute-done((bf16[96,1792]{1,0:T(8,128)(2,1)S(1)}, bf16[96,1792]{1,0:T(8,128)(2,1)S(1)}, u32[]{:S(2)}, u32[]{:S(2)}) %collective-permute-start.12) | collective-permute-done | bytes 344096 | tf_op jit(solution)/shard_map/ppermute | solution.py:90
  173.8 1.8 collective-permute-start.13
  176.2 3.4 %collective-permute-done.34 = bf16[896,1280]{1,0:T(8,128)(2,1)S(1)} collective-permute-done((bf16[896,1280]{1,0:T(8,128)(2,1)S(1)}, bf16[896,1280]{1,0:T(8,128)(2,1)S(1)}, u32[]{:S(2)}, u32[]{:S(2)}) %collective-permute-start.34) | collective-permute-done | bytes 2293792 | tf_op jit(solution)/shard_map/ppermute | solution.py:45
  179.6 2.5 pad_maximum_fusion.3
  182.2 1.7 collective-permute-start.14
  184.3 8.3 %collective-permute-done.14 = bf16[96,1792]{1,0:T(8,128)(2,1)S(1)} collective-permute-done((bf16[96,1792]{1,0:T(8,128)(2,1)S(1)}, bf16[96,1792]{1,0:T(8,128)(2,1)S(1)}, u32[]{:S(2)}, u32[]{:S(2)}) %collective-permute-start.14) | collective-permute-done | bytes 344096 | tf_op jit(solution)/shard_map/ppermute | solution.py:96
  192.6 1.7 collective-permute-start.15
  194.8 7.5 %collective-permute-done.15 = bf16[96,1792]{1,0:T(8,128)(2,1)S(1)} collective-permute-done((bf16[96,1792]{1,0:T(8,128)(2,1)S(1)}, bf16[96,1792]{1,0:T(8,128)(2,1)S(1)}, u32[]{:S(2)}, u32[]{:S(2)}) %collective-permute-start.15) | collective-permute-done | bytes 344096 | tf_op jit(solution)/shard_map/ppermute | solution.py:96
  202.3 1.7 collective-permute-start.16
  204.5 6.6 %collective-permute-done.16 = bf16[96,1792]{1,0:T(8,128)(2,1)S(1)} collective-permute-done((bf16[96,1792]{1,0:T(8,128)(2,1)S(1)}, bf16[96,1792]{1,0:T(8,128)(2,1)S(1)}, u32[]{:S(2)}, u32[]{:S(2)}) %collective-permute-start.16) | collective-permute-done | bytes 344096 | tf_op jit(solution)/shard_map/ppermute | solution.py:96
  211.1 1.7 collective-permute-start.17
  213.3 6.1 %collective-permute-done.17 = bf16[96,1792]{1,0:T(8,128)(2,1)S(1)} collective-permute-done((bf16[96,1792]{1,0:T(8,128)(2,1)S(1)}, bf16[96,1792]{1,0:T(8,128)(2,1)S(1)}, u32[]{:S(2)}, u32[]{:S(2)}) %collective-permute-start.17) | collective-permute-done | bytes 344096 | tf_op jit(solution)/shard_map/ppermute | solution.py:96
  219.4 1.7 collective-permute-start.18
  221.5 6.5 %collective-permute-done.18 = bf16[96,1792]{1,0:T(8,128)(2,1)S(1)} collective-permute-done((bf16[96,1792]{1,0:T(8,128)(2,1)S(1)}, bf16[96,1792]{1,0:T(8,128)(2,1)S(1)}, u32[]{:S(2)}, u32[]{:S(2)}) %collective-permute-start.18) | collective-permute-done | bytes 344096 | tf_op jit(solution)/shard_map/ppermute | solution.py:96
  228.1 1.7 collective-permute-start.19
  230.2 5.1 %collective-permute-done.19 = bf16[96,1792]{1,0:T(8,128)(2,1)S(1)} collective-permute-done((bf16[96,1792]{1,0:T(8,128)(2,1)S(1)}, bf16[96,1792]{1,0:T(8,128)(2,1)S(1)}, u32[]{:S(2)}, u32[]{:S(2)}) %collective-permute-start.19) | collective-permute-done | bytes 344096 | tf_op jit(solution)/shard_map/ppermute | solution.py:96
  235.3 1.8 collective-permute-done.33
  237.2 2.4 multiply_reduce_fusion
  239.7 11.2 %pad_maximum_fusion.1 = bf16[4,896,1280]{2,1,0:T(8,128)(2,1)} fusion(bf16[2,896,1280]{2,1,0:T(8,128)(2,1)} %collective-permute-done.37, bf16[1,896,1280]{2,1,0:T(8,128)(2,1)} %bitcast.29, bf16[1,896,1280]{2,1,0:T(8,128)(2,1)} %bitcast.28), kind=kLoop, calls=%fused_computation.10 | loop fusion | flops 9175040 | bytes 18350080 | tf_op jit(solution)/shard_map/concatenate | solution.py:49
  250.9 11.8 %fusion.59 = f32[768,1280]{1,0:T(8,128)} fusion(bf16[3584,1280]{1,0:T(8,128)(2,1)} %bitcast.102, f32[768,3584]{1,0:T(8,128)S(1)} %get-tuple-element.18, f32[3584]{0:T(1024)S(1)} %pad_maximum_fusion.13, f32[768]{0:T(1024)S(1)} %add_rsqrt_fusion), kind=kOutput, calls=%fused_computation.143 | convolution fusion | flops 7054688256 | bytes 24134656 | tf_op jit(solution)/shard_map/dot_general | solution.py:186
  262.7 6.9 %pad_maximum_fusion = bf16[4,896,1280]{2,1,0:T(8,128)(2,1)} fusion(bf16[2,896,1280]{2,1,0:T(8,128)(2,1)} %collective-permute-done.35, bf16[1,896,1280]{2,1,0:T(8,128)(2,1)S(1)} %bitcast.100, bf16[1,896,1280]{2,1,0:T(8,128)(2,1)S(1)} %bitcast.98), kind=kLoop, calls=%fused_computation.9 | loop fusion | flops 9175040 | bytes 18350080 | tf_op jit(solution)/shard_map/concatenate | solution.py:49
  269.7 15.6 %fusion.9 = f32[16,1280]{1,0:T(8,128)S(1)} fusion(f32[768,1280]{1,0:T(8,128)} %fusion.59, s32[768]{0:T(1024)S(1)} %add.382, bf16[3584,1280]{1,0:T(8,128)(2,1)} %bitcast.101, f32[768,3584]{1,0:T(8,128)} %copy-done.1, f32[3584]{0:T(1024)S(1)} %pad_maximum_fusion.13, f32[768]{0:T(1024)S(1)} %add_rsqrt_fusion), kind=kOutput, calls=%fused_computation.24 | convolution fusion | flops 7092080640 | bytes 24219648 | tf_op jit(solution)/shard_map/dot_general | solution.py:193
  285.2 1.5 collective-permute-start.38
  286.9 2.8 collective-permute-done.38
  289.9 2.3 fusion.21
  292.3 2.1 convolution_bitcast_fusion.1
  296.4 4.6 %all-to-all-start.1 = ((f32[32,16,448]{2,1,0:T(8,128)}), f32[32,16,448]{2,1,0:T(8,128)S(1)}, u32[]{:S(2)}, u32[]{:S(2)}) async-start(f32[32,16,448]{2,1,0:T(8,128)} %bitcast.104), calls=%async_computation.1 | async-start | bytes 2097152 | tf_op jit(solution)/shard_map/all_to_all | solution.py:235
  302.6 26.1 %all-to-all-done.1 = f32[32,16,448]{2,1,0:T(8,128)S(1)} async-done(((f32[32,16,448]{2,1,0:T(8,128)}), f32[32,16,448]{2,1,0:T(8,128)S(1)}, u32[]{:S(2)}, u32[]{:S(2)}) %all-to-all-start.1) | async-done | bytes 917536 | tf_op jit(solution)/shard_map/all_to_all | solution.py:235
  (182 shorter events, 32.0 us)
Async XLA Ops:
  0.0 292.3 %copy-start = (bf16[896,1280]{1,0:T(8,128)(2,1)S(1)}, bf16[896,1280]{1,0:T(8,128)(2,1)}, u32[]{:S(2)}) copy-start(bf16[896,1280]{1,0:T(8,128)(2,1)} %param.24) | copy-start | bytes 6881284
  2.3 25.1 %copy-start.14 = (f32[3584]{0:T(1024)S(1)}, f32[3584]{0:T(1024)}, u32[]{:S(2)}) copy-start(f32[3584]{0:T(1024)} %param.16) | copy-start | bytes 43012
  4.3 18.7 %collective-permute-start.2 = (bf16[896,384]{1,0:T(8,128)(2,1)}, bf16[896,384]{1,0:T(8,128)(2,1)}, u32[]{:S(2)}, u32[]{:S(2)}) collective-permute-start(bf16[896,384]{1,0:T(8,128)(2,1)} %pad_maximum_fusion.9), channel_id=1, source_target_pairs={{0,16},{8,24},{16,0},{24,8},{1,17},{9,25},{17,1},{25,9},{2,18},{10... | collective-permute-start | bytes 2064392 | tf_op jit(solution)/shard_map/ppermute | solution.py:45
  25.4 6.6 %collective-permute-start.3 = (bf16[2,896,384]{2,1,0:T(8,128)(2,1)}, bf16[2,896,384]{2,1,0:T(8,128)(2,1)}, u32[]{:S(2)}, u32[]{:S(2)}) collective-permute-start(bf16[2,896,384]{2,1,0:T(8,128)(2,1)} %pad_maximum_fusion.7), channel_id=1, source_target_pairs={{0,8},{8,0},{16,24},{24,16},{1,9},{9,1},{17,25},{25,17},{2,10},{10... | collective-permute-start | bytes 4128776 | tf_op jit(solution)/shard_map/ppermute | solution.py:48
  30.6 3.7 %copy-start.2 = (bf16[768,896]{1,0:T(8,128)(2,1)}, bf16[768,896]{1,0:T(8,128)(2,1)S(1)}, u32[]{:S(2)}) copy-start(bf16[768,896]{1,0:T(8,128)(2,1)S(1)} %get-tuple-element.25) | copy-start | bytes 4128772
  30.6 3.7 %copy-start.4 = (bf16[768,896]{1,0:T(8,128)(2,1)}, bf16[768,896]{1,0:T(8,128)(2,1)S(1)}, u32[]{:S(2)}) copy-start(bf16[768,896]{1,0:T(8,128)(2,1)S(1)} %get-tuple-element.26) | copy-start | bytes 4128772
  30.6 3.7 %copy-start.6 = (bf16[768,896]{1,0:T(8,128)(2,1)}, bf16[768,896]{1,0:T(8,128)(2,1)S(1)}, u32[]{:S(2)}) copy-start(bf16[768,896]{1,0:T(8,128)(2,1)S(1)} %get-tuple-element.27) | copy-start | bytes 4128772
  30.6 3.7 %copy-start.8 = (bf16[768,896]{1,0:T(8,128)(2,1)}, bf16[768,896]{1,0:T(8,128)(2,1)S(1)}, u32[]{:S(2)}) copy-start(bf16[768,896]{1,0:T(8,128)(2,1)S(1)} %get-tuple-element.28) | copy-start | bytes 4128772
  38.4 0.8 copy-start.12
  39.2 7.6 %copy-start.17 = (s32[2,8]{1,0:T(2,128)S(1)}, s32[2,8]{1,0:T(2,128)}, u32[]{:S(2)}) copy-start(s32[2,8]{1,0:T(2,128)} %param.14) | copy-start | bytes 196
  39.2 9.2 %copy-start.16 = (s32[16,1]{0,1:T(1,128)S(1)}, s32[16,1]{0,1:T(1,128)}, u32[]{:S(2)}) copy-start(s32[16,1]{0,1:T(1,128)} %param.15) | copy-start | bytes 196
  39.2 10.5 %copy-start.11 = (bf16[896,256]{1,0:T(8,128)(2,1)S(1)}, bf16[896,256]{1,0:T(8,128)(2,1)}, u32[]{:S(2)}) copy-start(bf16[896,256]{1,0:T(8,128)(2,1)} %param.20) | copy-start | bytes 1376260
  39.3 12.2 %copy-start.18 = (s32[8]{0:T(128)S(1)}, s32[8]{0:T(128)}, u32[]{:S(2)}) copy-start(s32[8]{0:T(128)} %constant.311.clone) | copy-start | bytes 100
  39.3 18.8 %copy-start.15 = (f32[3584]{0:T(1024)S(1)}, f32[3584]{0:T(1024)}, u32[]{:S(2)}) copy-start(f32[3584]{0:T(1024)} %param.21) | copy-start | bytes 43012
  40.7 43.9 %all-to-all-start = ((bf16[8,768,128]{1,2,0:T(8,128)(2,1)}), bf16[8,768,128]{1,2,0:T(8,128)(2,1)}, u32[]{:S(2)}, u32[]{:S(2)}) async-start(bf16[8,768,128]{1,2,0:T(8,128)(2,1)} %broadcast_in_dim.19), calls=%async_computation | async-start | bytes 3145728 | tf_op jit(solution)/shard_map/all_to_all | solution.py:150
  46.9 23.3 %collective-permute-start.40 = (s32[16]{0:T(128)S(1)}, s32[16]{0:T(128)S(1)}, u32[]{:S(2)}, u32[]{:S(2)}) collective-permute-start(s32[16]{0:T(128)S(1)} %reshape.195), channel_id=1, source_target_pairs={{0,16},{8,24},{16,0},{24,8},{1,17},{9,25},{17,1},{25,9},{2,18},{10... | collective-permute-start | bytes 200 | tf_op jit(solution)/shard_map/ppermute | solution.py:45
  48.4 21.7 %collective-permute-start = (s32[16]{0:T(128)S(1)}, s32[16]{0:T(128)S(1)}, u32[]{:S(2)}, u32[]{:S(2)}) collective-permute-start(s32[16]{0:T(128)S(1)} %bitcast.122), channel_id=1, source_target_pairs={{0,16},{8,24},{16,0},{24,8},{1,17},{9,25},{17,1},{25,9},{2,18},{10... | collective-permute-start | bytes 200 | tf_op jit(solution)/shard_map/ppermute | solution.py:45
  49.7 12.1 %collective-permute-start.4 = (bf16[896,256]{1,0:T(8,128)(2,1)S(1)}, bf16[896,256]{1,0:T(8,128)(2,1)S(1)}, u32[]{:S(2)}, u32[]{:S(2)}) collective-permute-start(bf16[896,256]{1,0:T(8,128)(2,1)S(1)} %copy-done.11), channel_id=1, source_target_pairs={{0,16},{8,24},{16,0},{24,8},{1,17},{9,25},{17,1},{25,9},{2,18},{10... | collective-permute-start | bytes 1376264 | tf_op jit(solution)/shard_map/ppermute | solution.py:45
  62.9 12.7 %collective-permute-start.5 = (bf16[2,896,256]{2,1,0:T(8,128)(2,1)}, bf16[2,896,256]{2,1,0:T(8,128)(2,1)}, u32[]{:S(2)}, u32[]{:S(2)}) collective-permute-start(bf16[2,896,256]{2,1,0:T(8,128)(2,1)} %pad_maximum_fusion.8), channel_id=1, source_target_pairs={{0,8},{8,0},{16,24},{24,16},{1,9},{9,1},{17,25},{25,17},{2,10},{10... | collective-permute-start | bytes 2752520 | tf_op jit(solution)/shard_map/ppermute | solution.py:48
  70.2 1.4 collective-permute-start.1
  78.2 53.0 %collective-permute-start.36 = (bf16[896,1280]{1,0:T(8,128)(2,1)}, bf16[896,1280]{1,0:T(8,128)(2,1)}, u32[]{:S(2)}, u32[]{:S(2)}) collective-permute-start(bf16[896,1280]{1,0:T(8,128)(2,1)} %param.23), channel_id=1, source_target_pairs={{0,16},{8,24},{16,0},{24,8},{1,17},{9,25},{17,1},{25,9},{2,18},{10... | collective-permute-start | bytes 6881288 | tf_op jit(solution)/shard_map/ppermute | solution.py:45
  87.3 1.0 copy-start.13
  97.4 1.6 copy-start.10
  97.9 9.4 %collective-permute-start.6 = (bf16[96,1792]{1,0:T(8,128)(2,1)S(1)}, bf16[96,1792]{1,0:T(8,128)(2,1)S(1)}, u32[]{:S(2)}, u32[]{:S(2)}) collective-permute-start(bf16[96,1792]{1,0:T(8,128)(2,1)S(1)} %constant_dynamic-slice_fusion.2), channel_id=1, source_target_pairs={{0,2},{2,4},{4,6},{6,7},{7,5},{5,3},{3,1},{1,0},{8,10},{10,12},{12... | collective-permute-start | bytes 1032200 | tf_op jit(solution)/shard_map/ppermute | solution.py:90
  99.1 80.5 %collective-permute-start.34 = (bf16[896,1280]{1,0:T(8,128)(2,1)S(1)}, bf16[896,1280]{1,0:T(8,128)(2,1)S(1)}, u32[]{:S(2)}, u32[]{:S(2)}) collective-permute-start(bf16[896,1280]{1,0:T(8,128)(2,1)S(1)} %copy-done.10), channel_id=1, source_target_pairs={{0,16},{8,24},{16,0},{24,8},{1,17},{9,25},{17,1},{25,9},{2,18},{10... | collective-permute-start | bytes 6881288 | tf_op jit(solution)/shard_map/ppermute | solution.py:45
  100.6 9.1 %collective-permute-start.20 = (bf16[96,1792]{1,0:T(8,128)(2,1)S(1)}, bf16[96,1792]{1,0:T(8,128)(2,1)S(1)}, u32[]{:S(2)}, u32[]{:S(2)}) collective-permute-start(bf16[96,1792]{1,0:T(8,128)(2,1)S(1)} %constant_dynamic-slice_fusion.1), channel_id=1, source_target_pairs={{0,1},{2,0},{4,2},{6,4},{7,6},{5,7},{3,5},{1,3},{8,9},{10,8},{12,1... | collective-permute-start | bytes 1032200 | tf_op jit(solution)/shard_map/ppermute | solution.py:90
  107.4 8.6 %collective-permute-start.7 = (bf16[96,1792]{1,0:T(8,128)(2,1)S(1)}, bf16[96,1792]{1,0:T(8,128)(2,1)S(1)}, u32[]{:S(2)}, u32[]{:S(2)}) collective-permute-start(bf16[96,1792]{1,0:T(8,128)(2,1)S(1)} %add_convert_fusion.13), channel_id=1, source_target_pairs={{0,2},{2,4},{4,6},{6,7},{7,5},{5,3},{3,1},{1,0},{8,10},{10,12},{12... | collective-permute-start | bytes 1032200 | tf_op jit(solution)/shard_map/ppermute | solution.py:90
  109.8 8.3 %collective-permute-start.21 = (bf16[96,1792]{1,0:T(8,128)(2,1)S(1)}, bf16[96,1792]{1,0:T(8,128)(2,1)S(1)}, u32[]{:S(2)}, u32[]{:S(2)}) collective-permute-start(bf16[96,1792]{1,0:T(8,128)(2,1)S(1)} %add_convert_fusion.6), channel_id=1, source_target_pairs={{0,1},{2,0},{4,2},{6,4},{7,6},{5,7},{3,5},{1,3},{8,9},{10,8},{12,1... | collective-permute-start | bytes 1032200 | tf_op jit(solution)/shard_map/ppermute | solution.py:90
  116.1 19.9 %collective-permute-start.8 = (bf16[96,1792]{1,0:T(8,128)(2,1)S(1)}, bf16[96,1792]{1,0:T(8,128)(2,1)S(1)}, u32[]{:S(2)}, u32[]{:S(2)}) collective-permute-start(bf16[96,1792]{1,0:T(8,128)(2,1)S(1)} %add_convert_fusion.12), channel_id=1, source_target_pairs={{0,2},{2,4},{4,6},{6,7},{7,5},{5,3},{3,1},{1,0},{8,10},{10,12},{12... | collective-permute-start | bytes 1032200 | tf_op jit(solution)/shard_map/ppermute | solution.py:90
  118.2 19.8 %collective-permute-start.22 = (bf16[96,1792]{1,0:T(8,128)(2,1)S(1)}, bf16[96,1792]{1,0:T(8,128)(2,1)S(1)}, u32[]{:S(2)}, u32[]{:S(2)}) collective-permute-start(bf16[96,1792]{1,0:T(8,128)(2,1)S(1)} %add_convert_fusion.5), channel_id=1, source_target_pairs={{0,1},{2,0},{4,2},{6,4},{7,6},{5,7},{3,5},{1,3},{8,9},{10,8},{12,1... | collective-permute-start | bytes 1032200 | tf_op jit(solution)/shard_map/ppermute | solution.py:90
  136.1 103.6 %collective-permute-start.37 = (bf16[2,896,1280]{2,1,0:T(8,128)(2,1)}, bf16[2,896,1280]{2,1,0:T(8,128)(2,1)}, u32[]{:S(2)}, u32[]{:S(2)}) collective-permute-start(bf16[2,896,1280]{2,1,0:T(8,128)(2,1)} %pad_maximum_fusion.4), channel_id=1, source_target_pairs={{0,8},{8,0},{16,24},{24,16},{1,9},{9,1},{17,25},{25,17},{2,10},{10... | collective-permute-start | bytes 13762568 | tf_op jit(solution)/shard_map/ppermute | solution.py:48
  136.2 10.5 %collective-permute-start.9 = (bf16[96,1792]{1,0:T(8,128)(2,1)S(1)}, bf16[96,1792]{1,0:T(8,128)(2,1)S(1)}, u32[]{:S(2)}, u32[]{:S(2)}) collective-permute-start(bf16[96,1792]{1,0:T(8,128)(2,1)S(1)} %add_convert_fusion.11), channel_id=1, source_target_pairs={{0,2},{2,4},{4,6},{6,7},{7,5},{5,3},{3,1},{1,0},{8,10},{10,12},{12... | collective-permute-start | bytes 1032200 | tf_op jit(solution)/shard_map/ppermute | solution.py:90
  138.0 10.5 %collective-permute-start.23 = (bf16[96,1792]{1,0:T(8,128)(2,1)S(1)}, bf16[96,1792]{1,0:T(8,128)(2,1)S(1)}, u32[]{:S(2)}, u32[]{:S(2)}) collective-permute-start(bf16[96,1792]{1,0:T(8,128)(2,1)S(1)} %add_convert_fusion.4), channel_id=1, source_target_pairs={{0,1},{2,0},{4,2},{6,4},{7,6},{5,7},{3,5},{1,3},{8,9},{10,8},{12,1... | collective-permute-start | bytes 1032200 | tf_op jit(solution)/shard_map/ppermute | solution.py:90
  146.8 9.8 %collective-permute-start.10 = (bf16[96,1792]{1,0:T(8,128)(2,1)S(1)}, bf16[96,1792]{1,0:T(8,128)(2,1)S(1)}, u32[]{:S(2)}, u32[]{:S(2)}) collective-permute-start(bf16[96,1792]{1,0:T(8,128)(2,1)S(1)} %add_convert_fusion.10), channel_id=1, source_target_pairs={{0,2},{2,4},{4,6},{6,7},{7,5},{5,3},{3,1},{1,0},{8,10},{10,12},{12... | collective-permute-start | bytes 1032200 | tf_op jit(solution)/shard_map/ppermute | solution.py:90
  148.7 9.7 %collective-permute-start.24 = (bf16[96,1792]{1,0:T(8,128)(2,1)S(1)}, bf16[96,1792]{1,0:T(8,128)(2,1)S(1)}, u32[]{:S(2)}, u32[]{:S(2)}) collective-permute-start(bf16[96,1792]{1,0:T(8,128)(2,1)S(1)} %add_convert_fusion.3), channel_id=1, source_target_pairs={{0,1},{2,0},{4,2},{6,4},{7,6},{5,7},{3,5},{1,3},{8,9},{10,8},{12,1... | collective-permute-start | bytes 1032200 | tf_op jit(solution)/shard_map/ppermute | solution.py:90
  156.6 8.9 %collective-permute-start.11 = (bf16[96,1792]{1,0:T(8,128)(2,1)S(1)}, bf16[96,1792]{1,0:T(8,128)(2,1)S(1)}, u32[]{:S(2)}, u32[]{:S(2)}) collective-permute-start(bf16[96,1792]{1,0:T(8,128)(2,1)S(1)} %add_convert_fusion.9), channel_id=1, source_target_pairs={{0,2},{2,4},{4,6},{6,7},{7,5},{5,3},{3,1},{1,0},{8,10},{10,12},{12... | collective-permute-start | bytes 1032200 | tf_op jit(solution)/shard_map/ppermute | solution.py:90
  158.5 8.9 %collective-permute-start.25 = (bf16[96,1792]{1,0:T(8,128)(2,1)S(1)}, bf16[96,1792]{1,0:T(8,128)(2,1)S(1)}, u32[]{:S(2)}, u32[]{:S(2)}) collective-permute-start(bf16[96,1792]{1,0:T(8,128)(2,1)S(1)} %add_convert_fusion.2), channel_id=1, source_target_pairs={{0,1},{2,0},{4,2},{6,4},{7,6},{5,7},{3,5},{1,3},{8,9},{10,8},{12,1... | collective-permute-start | bytes 1032200 | tf_op jit(solution)/shard_map/ppermute | solution.py:90
  165.6 7.9 %collective-permute-start.12 = (bf16[96,1792]{1,0:T(8,128)(2,1)S(1)}, bf16[96,1792]{1,0:T(8,128)(2,1)S(1)}, u32[]{:S(2)}, u32[]{:S(2)}) collective-permute-start(bf16[96,1792]{1,0:T(8,128)(2,1)S(1)} %add_convert_fusion.8), channel_id=1, source_target_pairs={{0,2},{2,4},{4,6},{6,7},{7,5},{5,3},{3,1},{1,0},{8,10},{10,12},{12... | collective-permute-start | bytes 1032200 | tf_op jit(solution)/shard_map/ppermute | solution.py:90
  167.4 8.1 %collective-permute-start.26 = (bf16[96,1792]{1,0:T(8,128)(2,1)S(1)}, bf16[96,1792]{1,0:T(8,128)(2,1)S(1)}, u32[]{:S(2)}, u32[]{:S(2)}) collective-permute-start(bf16[96,1792]{1,0:T(8,128)(2,1)S(1)} %add_convert_fusion.1), channel_id=1, source_target_pairs={{0,1},{2,0},{4,2},{6,4},{7,6},{5,7},{3,5},{1,3},{8,9},{10,8},{12,1... | collective-permute-start | bytes 1032200 | tf_op jit(solution)/shard_map/ppermute | solution.py:90
  173.8 8.4 %collective-permute-start.13 = (bf16[96,1792]{1,0:T(8,128)(2,1)S(1)}, bf16[96,1792]{1,0:T(8,128)(2,1)S(1)}, u32[]{:S(2)}, u32[]{:S(2)}) collective-permute-start(bf16[96,1792]{1,0:T(8,128)(2,1)S(1)} %get-tuple-element.20), channel_id=1, source_target_pairs={{0,2},{2,4},{4,6},{6,7},{7,5},{5,3},{3,1},{1,0},{8,10},{10,12},{12... | collective-permute-start | bytes 1032200 | tf_op jit(solution)/shard_map/ppermute | solution.py:96
  175.9 8.1 %collective-permute-start.27 = (bf16[96,1792]{1,0:T(8,128)(2,1)S(1)}, bf16[96,1792]{1,0:T(8,128)(2,1)S(1)}, u32[]{:S(2)}, u32[]{:S(2)}) collective-permute-start(bf16[96,1792]{1,0:T(8,128)(2,1)S(1)} %get-tuple-element.22), channel_id=1, source_target_pairs={{0,1},{2,0},{4,2},{6,4},{7,6},{5,7},{3,5},{1,3},{8,9},{10,8},{12,1... | collective-permute-start | bytes 1032200 | tf_op jit(solution)/shard_map/ppermute | solution.py:96
  182.2 80.6 %collective-permute-start.35 = (bf16[2,896,1280]{2,1,0:T(8,128)(2,1)}, bf16[2,896,1280]{2,1,0:T(8,128)(2,1)}, u32[]{:S(2)}, u32[]{:S(2)}) collective-permute-start(bf16[2,896,1280]{2,1,0:T(8,128)(2,1)} %pad_maximum_fusion.3), channel_id=1, source_target_pairs={{0,8},{8,0},{16,24},{24,16},{1,9},{9,1},{17,25},{25,17},{2,10},{10... | collective-permute-start | bytes 13762568 | tf_op jit(solution)/shard_map/ppermute | solution.py:48
  182.2 10.5 %collective-permute-start.14 = (bf16[96,1792]{1,0:T(8,128)(2,1)S(1)}, bf16[96,1792]{1,0:T(8,128)(2,1)S(1)}, u32[]{:S(2)}, u32[]{:S(2)}) collective-permute-start(bf16[96,1792]{1,0:T(8,128)(2,1)S(1)} %collective-permute-done.13), channel_id=1, source_target_pairs={{0,2},{2,4},{4,6},{6,7},{7,5},{5,3},{3,1},{1,0},{8,10},{10,12},{12... | collective-permute-start | bytes 1032200 | tf_op jit(solution)/shard_map/ppermute | solution.py:96
  184.0 10.5 %collective-permute-start.28 = (bf16[96,1792]{1,0:T(8,128)(2,1)S(1)}, bf16[96,1792]{1,0:T(8,128)(2,1)S(1)}, u32[]{:S(2)}, u32[]{:S(2)}) collective-permute-start(bf16[96,1792]{1,0:T(8,128)(2,1)S(1)} %collective-permute-done.27), channel_id=1, source_target_pairs={{0,1},{2,0},{4,2},{6,4},{7,6},{5,7},{3,5},{1,3},{8,9},{10,8},{12,1... | collective-permute-start | bytes 1032200 | tf_op jit(solution)/shard_map/ppermute | solution.py:96
  192.6 9.7 %collective-permute-start.15 = (bf16[96,1792]{1,0:T(8,128)(2,1)S(1)}, bf16[96,1792]{1,0:T(8,128)(2,1)S(1)}, u32[]{:S(2)}, u32[]{:S(2)}) collective-permute-start(bf16[96,1792]{1,0:T(8,128)(2,1)S(1)} %collective-permute-done.14), channel_id=1, source_target_pairs={{0,2},{2,4},{4,6},{6,7},{7,5},{5,3},{3,1},{1,0},{8,10},{10,12},{12... | collective-permute-start | bytes 1032200 | tf_op jit(solution)/shard_map/ppermute | solution.py:96
  194.4 9.7 %collective-permute-start.29 = (bf16[96,1792]{1,0:T(8,128)(2,1)S(1)}, bf16[96,1792]{1,0:T(8,128)(2,1)S(1)}, u32[]{:S(2)}, u32[]{:S(2)}) collective-permute-start(bf16[96,1792]{1,0:T(8,128)(2,1)S(1)} %collective-permute-done.28), channel_id=1, source_target_pairs={{0,1},{2,0},{4,2},{6,4},{7,6},{5,7},{3,5},{1,3},{8,9},{10,8},{12,1... | collective-permute-start | bytes 1032200 | tf_op jit(solution)/shard_map/ppermute | solution.py:96
  202.3 8.8 %collective-permute-start.16 = (bf16[96,1792]{1,0:T(8,128)(2,1)S(1)}, bf16[96,1792]{1,0:T(8,128)(2,1)S(1)}, u32[]{:S(2)}, u32[]{:S(2)}) collective-permute-start(bf16[96,1792]{1,0:T(8,128)(2,1)S(1)} %collective-permute-done.15), channel_id=1, source_target_pairs={{0,2},{2,4},{4,6},{6,7},{7,5},{5,3},{3,1},{1,0},{8,10},{10,12},{12... | collective-permute-start | bytes 1032200 | tf_op jit(solution)/shard_map/ppermute | solution.py:96
  204.1 8.8 %collective-permute-start.30 = (bf16[96,1792]{1,0:T(8,128)(2,1)S(1)}, bf16[96,1792]{1,0:T(8,128)(2,1)S(1)}, u32[]{:S(2)}, u32[]{:S(2)}) collective-permute-start(bf16[96,1792]{1,0:T(8,128)(2,1)S(1)} %collective-permute-done.29), channel_id=1, source_target_pairs={{0,1},{2,0},{4,2},{6,4},{7,6},{5,7},{3,5},{1,3},{8,9},{10,8},{12,1... | collective-permute-start | bytes 1032200 | tf_op jit(solution)/shard_map/ppermute | solution.py:96
  204.5 32.7 %copy-start.3 = (bf16[768,896]{1,0:T(8,128)(2,1)S(1)}, bf16[768,896]{1,0:T(8,128)(2,1)}, u32[]{:S(2)}) copy-start(bf16[768,896]{1,0:T(8,128)(2,1)} %copy-done.2) | copy-start | bytes 4128772
  204.5 32.7 %copy-start.5 = (bf16[768,896]{1,0:T(8,128)(2,1)S(1)}, bf16[768,896]{1,0:T(8,128)(2,1)}, u32[]{:S(2)}) copy-start(bf16[768,896]{1,0:T(8,128)(2,1)} %copy-done.4) | copy-start | bytes 4128772
  204.5 32.7 %copy-start.7 = (bf16[768,896]{1,0:T(8,128)(2,1)S(1)}, bf16[768,896]{1,0:T(8,128)(2,1)}, u32[]{:S(2)}) copy-start(bf16[768,896]{1,0:T(8,128)(2,1)} %copy-done.6) | copy-start | bytes 4128772
  204.5 32.7 %copy-start.9 = (bf16[768,896]{1,0:T(8,128)(2,1)S(1)}, bf16[768,896]{1,0:T(8,128)(2,1)}, u32[]{:S(2)}) copy-start(bf16[768,896]{1,0:T(8,128)(2,1)} %copy-done.8) | copy-start | bytes 4128772
  211.1 8.2 %collective-permute-start.17 = (bf16[96,1792]{1,0:T(8,128)(2,1)S(1)}, bf16[96,1792]{1,0:T(8,128)(2,1)S(1)}, u32[]{:S(2)}, u32[]{:S(2)}) collective-permute-start(bf16[96,1792]{1,0:T(8,128)(2,1)S(1)} %collective-permute-done.16), channel_id=1, source_target_pairs={{0,2},{2,4},{4,6},{6,7},{7,5},{5,3},{3,1},{1,0},{8,10},{10,12},{12... | collective-permute-start | bytes 1032200 | tf_op jit(solution)/shard_map/ppermute | solution.py:96
  212.9 8.2 %collective-permute-start.31 = (bf16[96,1792]{1,0:T(8,128)(2,1)S(1)}, bf16[96,1792]{1,0:T(8,128)(2,1)S(1)}, u32[]{:S(2)}, u32[]{:S(2)}) collective-permute-start(bf16[96,1792]{1,0:T(8,128)(2,1)S(1)} %collective-permute-done.30), channel_id=1, source_target_pairs={{0,1},{2,0},{4,2},{6,4},{7,6},{5,7},{3,5},{1,3},{8,9},{10,8},{12,1... | collective-permute-start | bytes 1032200 | tf_op jit(solution)/shard_map/ppermute | solution.py:96
  219.4 8.7 %collective-permute-start.18 = (bf16[96,1792]{1,0:T(8,128)(2,1)S(1)}, bf16[96,1792]{1,0:T(8,128)(2,1)S(1)}, u32[]{:S(2)}, u32[]{:S(2)}) collective-permute-start(bf16[96,1792]{1,0:T(8,128)(2,1)S(1)} %collective-permute-done.17), channel_id=1, source_target_pairs={{0,2},{2,4},{4,6},{6,7},{7,5},{5,3},{3,1},{1,0},{8,10},{10,12},{12... | collective-permute-start | bytes 1032200 | tf_op jit(solution)/shard_map/ppermute | solution.py:96
  221.2 8.7 %collective-permute-start.32 = (bf16[96,1792]{1,0:T(8,128)(2,1)S(1)}, bf16[96,1792]{1,0:T(8,128)(2,1)S(1)}, u32[]{:S(2)}, u32[]{:S(2)}) collective-permute-start(bf16[96,1792]{1,0:T(8,128)(2,1)S(1)} %collective-permute-done.31), channel_id=1, source_target_pairs={{0,1},{2,0},{4,2},{6,4},{7,6},{5,7},{3,5},{1,3},{8,9},{10,8},{12,1... | collective-permute-start | bytes 1032200 | tf_op jit(solution)/shard_map/ppermute | solution.py:96
  228.1 7.2 %collective-permute-start.19 = (bf16[96,1792]{1,0:T(8,128)(2,1)S(1)}, bf16[96,1792]{1,0:T(8,128)(2,1)S(1)}, u32[]{:S(2)}, u32[]{:S(2)}) collective-permute-start(bf16[96,1792]{1,0:T(8,128)(2,1)S(1)} %collective-permute-done.18), channel_id=1, source_target_pairs={{0,2},{2,4},{4,6},{6,7},{7,5},{5,3},{3,1},{1,0},{8,10},{10,12},{12... | collective-permute-start | bytes 1032200 | tf_op jit(solution)/shard_map/ppermute | solution.py:96
  229.9 7.3 %collective-permute-start.33 = (bf16[96,1792]{1,0:T(8,128)(2,1)S(1)}, bf16[96,1792]{1,0:T(8,128)(2,1)S(1)}, u32[]{:S(2)}, u32[]{:S(2)}) collective-permute-start(bf16[96,1792]{1,0:T(8,128)(2,1)S(1)} %collective-permute-done.32), channel_id=1, source_target_pairs={{0,1},{2,0},{4,2},{6,4},{7,6},{5,7},{3,5},{1,3},{8,9},{10,8},{12,1... | collective-permute-start | bytes 1032200 | tf_op jit(solution)/shard_map/ppermute | solution.py:96
  239.7 11.2 %copy-start.1 = (f32[768,3584]{1,0:T(8,128)}, f32[768,3584]{1,0:T(8,128)S(1)}, u32[]{:S(2)}) copy-start(f32[768,3584]{1,0:T(8,128)S(1)} %get-tuple-element.18) | copy-start | bytes 33030148
  285.2 4.4 %collective-permute-start.38 = (f32[16,1280]{1,0:T(8,128)S(1)}, f32[16,1280]{1,0:T(8,128)S(1)}, u32[]{:S(2)}, u32[]{:S(2)}) collective-permute-start(f32[16,1280]{1,0:T(8,128)S(1)} %fusion.9), channel_id=1, source_target_pairs={{0,16},{8,24},{16,0},{24,8},{1,17},{9,25},{17,1},{25,9},{2,18},{10... | collective-permute-start | bytes 245768 | tf_op jit(solution)/shard_map/ppermute | solution.py:45
  289.7 2.6 collective-permute-start.39
  296.4 32.2 %all-to-all-start.1 = ((f32[32,16,448]{2,1,0:T(8,128)}), f32[32,16,448]{2,1,0:T(8,128)S(1)}, u32[]{:S(2)}, u32[]{:S(2)}) async-start(f32[32,16,448]{2,1,0:T(8,128)} %bitcast.104), calls=%async_computation.1 | async-start | bytes 2097152 | tf_op jit(solution)/shard_map/all_to_all | solution.py:235
  301.1 1.2 collective-permute-start.41

commit v4 on v3

--- a/solution.py
+++ b/solution.py
@@ -76,10 +76,15 @@
     for p, t in enumerate(walk):
         place[t] = p
     pos = jnp.asarray(place, jnp.int32)[lax.axis_index(axis)]
-    rows, half = x.shape[0], x.shape[1] // 2
+    rows, quarter = x.shape[0], x.shape[1] // 4
     size = rows // n
     parts = []
-    for sign, local in ((1, x[:, :half]), (-1, x[:, half:])):
+    for sign, local in (
+        (1, x[:, :quarter]),
+        (-1, x[:, quarter : 2 * quarter]),
+        (1, x[:, 2 * quarter : 3 * quarter]),
+        (-1, x[:, 3 * quarter :]),
+    ):
         pairs = [(walk[p], walk[(p + sign) % n]) for p in range(n)]
 
         def chunk(k):

time: 331 us -> 356 us (1.076)
  starting transfers between devices: 51.4 us -> 110 us
  waiting for transfers between devices: 150 us -> 120 us
    ppermute x14 -> x28, starting transfers between devices: 14.6 us -> 44.9 us  [ring_psum(): moving = lax.ppermute(moving, axis, pairs)]
    ppermute x14 -> x28, starting transfers between devices: 14.3 us -> 41.5 us  [ring_psum(): got = lax.ppermute(acc, axis, pairs)]
    ppermute x14 -> x28, waiting for transfers between devices: 42.1 us -> 16 us  [ring_psum(): moving = lax.ppermute(moving, axis, pairs)]
    ppermute x7, waiting for transfers between devices: 33.8 us -> 57.5 us  [gather_grp(): moving = lax.ppermute(moving, 'grp', ring)]
    ppermute x14 -> x28, waiting for transfers between devices: 41.4 us -> 19 us  [ring_psum(): got = lax.ppermute(acc, axis, pairs)]
    all_to_all x1, waiting for transfers between devices: 4.94 us -> 0.01 us  [on_device(): lax.all_to_all(jnp.broadcast_to(kv_part[None], (tp_size,) + kv_part.shape...]
  transfers between devices with their start and end apart: 44 -> 72, of which waited for: 24 -> 48; matrix products, arithmetic and copies ran while one was open for 21% -> 18% of each run, Pallas kernels for 0% -> 0%
where the time goes in v4:
time: 356 us; the launch traced here: 355 us
  waiting for transfers between devices  120 us (34%)
  starting transfers between devices  110 us (31%)
  other arithmetic  45.3 us (13%)
  matrix products  42.7 us (12%)
  local copies, waits for them, and re-layouts  21.2 us (6%)
  between operations  15.3 us (4%)
    ppermute x7, waiting for transfers between devices, gather_grp(): moving = lax.ppermute(moving, 'grp', ring)  57.5 us
    ppermute x28, starting transfers between devices, ring_psum(): moving = lax.ppermute(moving, axis, pairs)  44.9 us
    ppermute x28, starting transfers between devices, ring_psum(): got = lax.ppermute(acc, axis, pairs)  41.5 us
    all_to_all x1, waiting for transfers between devices, on_device(): lax.all_to_all(send.reshape(grp_size * tp_size, slots, d_tp), ('grp', 'tp...  26.1 us
    concatenate x6, other arithmetic, gather_grp(): return jnp.concatenate([mine, other], 0)  22.5 us
    ppermute x28, waiting for transfers between devices, ring_psum(): got = lax.ppermute(acc, axis, pairs)  19 us
    ppermute x28, waiting for transfers between devices, ring_psum(): moving = lax.ppermute(moving, axis, pairs)  16 us
    dot_general x1, matrix products, on_device(): jnp.dot(selector.astype(jnp.bfloat16), hidden_ffn, preferred_element_type...  15.6 us
  transfers between devices with their start and end apart: 72, of which 48 were waited for; matrix products, arithmetic and copies ran while one was open for 18% of the time, Pallas kernels for 0%

profile of v4, /device:TPU:0, one launch (start us, length us, event | category | flops | bytes accessed | tf_op | source)
XLA Modules:
  0.0 354.8 jit_solution(12113190262066271751)
XLA Ops:
  2.3 2.1 pad_maximum_fusion.9
  4.3 2.9 collective-permute-start.2
  10.3 12.7 %collective-permute-done.2 = bf16[896,384]{1,0:T(8,128)(2,1)} collective-permute-done((bf16[896,384]{1,0:T(8,128)(2,1)}, bf16[896,384]{1,0:T(8,128)(2,1)}, u32[]{:S(2)}, u32[]{:S(2)}) %collective-permute-start.2) | collective-permute-done | bytes 688160 | tf_op jit(solution)/shard_map/ppermute | solution.py:45
  23.0 2.4 pad_maximum_fusion.7
  27.4 3.1 constant_dynamic-slice_fusion.10
  31.9 2.3 pad_maximum_fusion.5
  34.2 4.1 %fusion.12 = bf16[768,384]{1,0:T(8,128)(2,1)S(1)} fusion(bf16[3584,384]{1,0:T(8,128)(2,1)S(1)} %bitcast.101, f32[3584]{0:T(1024)S(1)} %pad_maximum_fusion.12, f32[768]{0:T(1024)S(1)} %add_rsqrt_fusion.1, bf16[768,896]{1,0:T(8,128)(2,1)S(1)} %get-tuple-element.33, bf16[768,896]{1,0:T(8,128)(2,1)S(1)} %get-tuple-element.34, ...), kind=kOutput, calls=%fused_computation.29 | convolution fusion | flops 2144501760 | bytes 8864768 | tf_op jit(solution)/shard_map/dot_general | solution.py:152
  40.6 6.2 %all-to-all-start = ((bf16[8,768,128]{1,2,0:T(8,128)(2,1)}), bf16[8,768,128]{1,2,0:T(8,128)(2,1)}, u32[]{:S(2)}, u32[]{:S(2)}) async-start(bf16[8,768,128]{1,2,0:T(8,128)(2,1)} %broadcast_in_dim.19), calls=%async_computation | async-start | bytes 3145728 | tf_op jit(solution)/shard_map/all_to_all | solution.py:155
  52.7 9.6 %collective-permute-done.4 = bf16[896,256]{1,0:T(8,128)(2,1)S(1)} collective-permute-done((bf16[896,256]{1,0:T(8,128)(2,1)S(1)}, bf16[896,256]{1,0:T(8,128)(2,1)S(1)}, u32[]{:S(2)}, u32[]{:S(2)}) %collective-permute-start.4) | collective-permute-done | bytes 458784 | tf_op jit(solution)/shard_map/ppermute | solution.py:45
  78.0 1.8 slice.63
  79.8 1.8 reshape.188
  81.6 2.6 pad_maximum_fusion.6
  90.0 3.5 fusion.67
  93.5 2.0 fusion.15
  95.9 3.1 convolution_convert_fusion
  99.6 1.8 collective-permute-start.6
  101.7 1.8 collective-permute-start.34
  103.5 3.4 collective-permute-done.6
  106.9 1.7 collective-permute-start.48
  109.8 2.0 collective-permute-start.21
  111.9 1.9 collective-permute-done.48
  113.7 1.7 collective-permute-start.35
  117.4 2.0 collective-permute-start.8
  121.0 1.7 collective-permute-start.22
  124.7 1.7 collective-permute-start.50
  133.3 1.7 collective-permute-start.51
  137.5 1.9 collective-permute-start.24
  141.9 1.9 collective-permute-start.52
  144.2 2.6 collective-permute-start.11
  148.5 1.8 collective-permute-start.39
  150.6 2.8 pad_maximum_fusion.4
  153.4 32.4 %collective-permute-done.62 = bf16[896,1280]{1,0:T(8,128)(2,1)} collective-permute-done((bf16[896,1280]{1,0:T(8,128)(2,1)}, bf16[896,1280]{1,0:T(8,128)(2,1)}, u32[]{:S(2)}, u32[]{:S(2)}) %collective-permute-start.62) | collective-permute-done | bytes 2293792 | tf_op jit(solution)/shard_map/ppermute | solution.py:45
  185.7 4.8 %pad_maximum_fusion.3 = bf16[2,896,1280]{2,1,0:T(8,128)(2,1)} fusion(bf16[1,896,1280]{2,1,0:T(8,128)(2,1)} %bitcast.26, bf16[1,896,1280]{2,1,0:T(8,128)(2,1)} %bitcast.25), kind=kLoop, calls=%fused_computation.16 | loop fusion | flops 2293760 | bytes 9175040 | tf_op jit(solution)/shard_map/stack | solution.py:47
  191.2 1.8 collective-permute-start.12
  193.4 1.8 collective-permute-start.40
  195.2 3.2 collective-permute-done.12
  198.5 1.7 collective-permute-start.54
  201.4 2.0 collective-permute-start.27
  204.8 1.7 collective-permute-start.41
  209.0 1.7 collective-permute-start.14
  215.8 1.7 collective-permute-start.56
  218.7 1.7 collective-permute-start.15
  222.3 2.0 collective-permute-start.43
  224.9 1.7 collective-permute-start.57
  229.1 1.9 collective-permute-start.30
  238.6 1.7 collective-permute-start.31
  242.8 1.9 collective-permute-start.59
  244.7 1.8 collective-permute-start.18
  246.6 2.1 collective-permute-start.32
  250.8 1.8 collective-permute-start.60
  253.2 2.1 collective-permute-start.19
  256.4 2.0 collective-permute-start.47
  258.8 2.0 collective-permute-start.61
  261.8 2.4 collective-permute-done.61
  264.3 2.4 multiply_reduce_fusion
  266.7 8.6 %pad_maximum_fusion.1 = bf16[4,896,1280]{2,1,0:T(8,128)(2,1)S(1)} fusion(bf16[2,896,1280]{2,1,0:T(8,128)(2,1)} %collective-permute-done.65, bf16[1,896,1280]{2,1,0:T(8,128)(2,1)} %bitcast.29, bf16[1,896,1280]{2,1,0:T(8,128)(2,1)} %bitcast.28), kind=kLoop, calls=%fused_computation.10 | loop fusion | flops 9175040 | bytes 18350080 | tf_op jit(solution)/shard_map/concatenate | solution.py:49
  275.3 9.3 %fusion.59 = f32[768,1280]{1,0:T(8,128)} fusion(bf16[3584,1280]{1,0:T(8,128)(2,1)S(1)} %bitcast.98, f32[768,3584]{1,0:T(8,128)S(1)} %get-tuple-element.18, f32[3584]{0:T(1024)S(1)} %pad_maximum_fusion.13, f32[768]{0:T(1024)S(1)} %add_rsqrt_fusion), kind=kOutput, calls=%fused_computation.175 | convolution fusion | flops 7054688256 | bytes 24134656 | tf_op jit(solution)/shard_map/dot_general | solution.py:191
  284.6 9.1 %pad_maximum_fusion = bf16[4,896,1280]{2,1,0:T(8,128)(2,1)} fusion(bf16[2,896,1280]{2,1,0:T(8,128)(2,1)} %collective-permute-done.63, bf16[1,896,1280]{2,1,0:T(8,128)(2,1)} %bitcast.26, bf16[1,896,1280]{2,1,0:T(8,128)(2,1)} %bitcast.25), kind=kLoop, calls=%fused_computation.9 | loop fusion | flops 9175040 | bytes 18350080 | tf_op jit(solution)/shard_map/concatenate | solution.py:49
  293.7 15.6 %fusion.9 = f32[16,1280]{1,0:T(8,128)S(1)} fusion(f32[768,1280]{1,0:T(8,128)} %fusion.59, s32[768]{0:T(1024)S(1)} %add.504, bf16[3584,1280]{1,0:T(8,128)(2,1)} %bitcast.97, f32[768,3584]{1,0:T(8,128)} %copy-done.1, f32[3584]{0:T(1024)S(1)} %pad_maximum_fusion.13, f32[768]{0:T(1024)S(1)} %add_rsqrt_fusion), kind=kOutput, calls=%fused_computation.24 | convolution fusion | flops 7092080640 | bytes 24219648 | tf_op jit(solution)/shard_map/dot_general | solution.py:198
  310.9 2.8 collective-permute-done.66
  313.9 2.3 fusion.21
  316.3 2.1 convolution_bitcast_fusion.1
  320.5 5.9 %all-to-all-start.1 = ((f32[32,16,448]{2,1,0:T(8,128)}), f32[32,16,448]{2,1,0:T(8,128)S(1)}, u32[]{:S(2)}, u32[]{:S(2)}) async-start(f32[32,16,448]{2,1,0:T(8,128)} %bitcast.100), calls=%async_computation.1 | async-start | bytes 2097152 | tf_op jit(solution)/shard_map/all_to_all | solution.py:240
  327.9 26.1 %all-to-all-done.1 = f32[32,16,448]{2,1,0:T(8,128)S(1)} async-done(((f32[32,16,448]{2,1,0:T(8,128)}), f32[32,16,448]{2,1,0:T(8,128)S(1)}, u32[]{:S(2)}, u32[]{:S(2)}) %all-to-all-start.1) | async-done | bytes 917536 | tf_op jit(solution)/shard_map/all_to_all | solution.py:240
  (268 shorter events, 84.7 us)
Async XLA Ops:
  4.3 18.7 %collective-permute-start.2 = (bf16[896,384]{1,0:T(8,128)(2,1)}, bf16[896,384]{1,0:T(8,128)(2,1)}, u32[]{:S(2)}, u32[]{:S(2)}) collective-permute-start(bf16[896,384]{1,0:T(8,128)(2,1)} %pad_maximum_fusion.9), channel_id=1, source_target_pairs={{0,16},{8,24},{16,0},{24,8},{1,17},{9,25},{17,1},{25,9},{2,18},{10... | collective-permute-start | bytes 2064392 | tf_op jit(solution)/shard_map/ppermute | solution.py:45
  25.4 6.5 %collective-permute-start.3 = (bf16[2,896,384]{2,1,0:T(8,128)(2,1)}, bf16[2,896,384]{2,1,0:T(8,128)(2,1)}, u32[]{:S(2)}, u32[]{:S(2)}) collective-permute-start(bf16[2,896,384]{2,1,0:T(8,128)(2,1)} %pad_maximum_fusion.7), channel_id=1, source_target_pairs={{0,8},{8,0},{16,24},{24,16},{1,9},{9,1},{17,25},{25,17},{2,10},{10... | collective-permute-start | bytes 4128776 | tf_op jit(solution)/shard_map/ppermute | solution.py:48
  40.6 45.6 %all-to-all-start = ((bf16[8,768,128]{1,2,0:T(8,128)(2,1)}), bf16[8,768,128]{1,2,0:T(8,128)(2,1)}, u32[]{:S(2)}, u32[]{:S(2)}) async-start(bf16[8,768,128]{1,2,0:T(8,128)(2,1)} %broadcast_in_dim.19), calls=%async_computation | async-start | bytes 3145728 | tf_op jit(solution)/shard_map/all_to_all | solution.py:155
  46.9 29.2 %collective-permute-start.68 = (s32[16]{0:T(128)S(1)}, s32[16]{0:T(128)S(1)}, u32[]{:S(2)}, u32[]{:S(2)}) collective-permute-start(s32[16]{0:T(128)S(1)} %reshape.195), channel_id=1, source_target_pairs={{0,16},{8,24},{16,0},{24,8},{1,17},{9,25},{17,1},{25,9},{2,18},{10... | collective-permute-start | bytes 200 | tf_op jit(solution)/shard_map/ppermute | solution.py:45
  48.5 27.7 %collective-permute-start = (s32[16]{0:T(128)S(1)}, s32[16]{0:T(128)S(1)}, u32[]{:S(2)}, u32[]{:S(2)}) collective-permute-start(s32[16]{0:T(128)S(1)} %bitcast.118), channel_id=1, source_target_pairs={{0,16},{8,24},{16,0},{24,8},{1,17},{9,25},{17,1},{25,9},{2,18},{10... | collective-permute-start | bytes 200 | tf_op jit(solution)/shard_map/ppermute | solution.py:45
  50.1 12.1 %collective-permute-start.4 = (bf16[896,256]{1,0:T(8,128)(2,1)S(1)}, bf16[896,256]{1,0:T(8,128)(2,1)S(1)}, u32[]{:S(2)}, u32[]{:S(2)}) collective-permute-start(bf16[896,256]{1,0:T(8,128)(2,1)S(1)} %copy-done.10), channel_id=1, source_target_pairs={{0,16},{8,24},{16,0},{24,8},{1,17},{9,25},{17,1},{25,9},{2,18},{10... | collective-permute-start | bytes 1376264 | tf_op jit(solution)/shard_map/ppermute | solution.py:45
  63.3 18.3 %collective-permute-start.5 = (bf16[2,896,256]{2,1,0:T(8,128)(2,1)}, bf16[2,896,256]{2,1,0:T(8,128)(2,1)}, u32[]{:S(2)}, u32[]{:S(2)}) collective-permute-start(bf16[2,896,256]{2,1,0:T(8,128)(2,1)} %pad_maximum_fusion.8), channel_id=1, source_target_pairs={{0,8},{8,0},{16,24},{24,16},{1,9},{9,1},{17,25},{25,17},{2,10},{10... | collective-permute-start | bytes 2752520 | tf_op jit(solution)/shard_map/ppermute | solution.py:48
  84.2 66.1 %collective-permute-start.64 = (bf16[896,1280]{1,0:T(8,128)(2,1)}, bf16[896,1280]{1,0:T(8,128)(2,1)}, u32[]{:S(2)}, u32[]{:S(2)}) collective-permute-start(bf16[896,1280]{1,0:T(8,128)(2,1)} %param.23), channel_id=1, source_target_pairs={{0,16},{8,24},{16,0},{24,8},{1,17},{9,25},{17,1},{25,9},{2,18},{10... | collective-permute-start | bytes 6881288 | tf_op jit(solution)/shard_map/ppermute | solution.py:45
  85.7 100.0 %collective-permute-start.62 = (bf16[896,1280]{1,0:T(8,128)(2,1)}, bf16[896,1280]{1,0:T(8,128)(2,1)}, u32[]{:S(2)}, u32[]{:S(2)}) collective-permute-start(bf16[896,1280]{1,0:T(8,128)(2,1)} %param.22), channel_id=1, source_target_pairs={{0,16},{8,24},{16,0},{24,8},{1,17},{9,25},{17,1},{25,9},{2,18},{10... | collective-permute-start | bytes 6881288 | tf_op jit(solution)/shard_map/ppermute | solution.py:45
  99.6 7.3 %collective-permute-start.6 = (bf16[96,896]{1,0:T(8,128)(2,1)S(1)}, bf16[96,896]{1,0:T(8,128)(2,1)S(1)}, u32[]{:S(2)}, u32[]{:S(2)}) collective-permute-start(bf16[96,896]{1,0:T(8,128)(2,1)S(1)} %constant_dynamic-slice_fusion.4), channel_id=1, source_target_pairs={{0,2},{2,4},{4,6},{6,7},{7,5},{5,3},{3,1},{1,0},{8,10},{10,12},{12... | collective-permute-start | bytes 516104 | tf_op jit(solution)/shard_map/ppermute | solution.py:95
  101.4 7.3 %collective-permute-start.20 = (bf16[96,896]{1,0:T(8,128)(2,1)S(1)}, bf16[96,896]{1,0:T(8,128)(2,1)S(1)}, u32[]{:S(2)}, u32[]{:S(2)}) collective-permute-start(bf16[96,896]{1,0:T(8,128)(2,1)S(1)} %constant_dynamic-slice_fusion.3), channel_id=1, source_target_pairs={{0,1},{2,0},{4,2},{6,4},{7,6},{5,7},{3,5},{1,3},{8,9},{10,8},{12,1... | collective-permute-start | bytes 516104 | tf_op jit(solution)/shard_map/ppermute | solution.py:95
  101.7 8.1 %collective-permute-start.34 = (bf16[96,896]{1,0:T(8,128)(2,1)S(1)}, bf16[96,896]{1,0:T(8,128)(2,1)S(1)}, u32[]{:S(2)}, u32[]{:S(2)}) collective-permute-start(bf16[96,896]{1,0:T(8,128)(2,1)S(1)} %constant_dynamic-slice_fusion.2), channel_id=1, source_target_pairs={{0,2},{2,4},{4,6},{6,7},{7,5},{5,3},{3,1},{1,0},{8,10},{10,12},{12... | collective-permute-start | bytes 516104 | tf_op jit(solution)/shard_map/ppermute | solution.py:95
  106.9 6.9 %collective-permute-start.48 = (bf16[96,896]{1,0:T(8,128)(2,1)S(1)}, bf16[96,896]{1,0:T(8,128)(2,1)S(1)}, u32[]{:S(2)}, u32[]{:S(2)}) collective-permute-start(bf16[96,896]{1,0:T(8,128)(2,1)S(1)} %constant_dynamic-slice_fusion.1), channel_id=1, source_target_pairs={{0,1},{2,0},{4,2},{6,4},{7,6},{5,7},{3,5},{1,3},{8,9},{10,8},{12,1... | collective-permute-start | bytes 516104 | tf_op jit(solution)/shard_map/ppermute | solution.py:95
  108.7 7.1 %collective-permute-start.7 = (bf16[96,896]{1,0:T(8,128)(2,1)S(1)}, bf16[96,896]{1,0:T(8,128)(2,1)S(1)}, u32[]{:S(2)}, u32[]{:S(2)}) collective-permute-start(bf16[96,896]{1,0:T(8,128)(2,1)S(1)} %add_convert_fusion.27), channel_id=1, source_target_pairs={{0,2},{2,4},{4,6},{6,7},{7,5},{5,3},{3,1},{1,0},{8,10},{10,12},{12... | collective-permute-start | bytes 516104 | tf_op jit(solution)/shard_map/ppermute | solution.py:95
  109.8 7.6 %collective-permute-start.21 = (bf16[96,896]{1,0:T(8,128)(2,1)S(1)}, bf16[96,896]{1,0:T(8,128)(2,1)S(1)}, u32[]{:S(2)}, u32[]{:S(2)}) collective-permute-start(bf16[96,896]{1,0:T(8,128)(2,1)S(1)} %add_convert_fusion.20), channel_id=1, source_target_pairs={{0,1},{2,0},{4,2},{6,4},{7,6},{5,7},{3,5},{1,3},{8,9},{10,8},{12,1... | collective-permute-start | bytes 516104 | tf_op jit(solution)/shard_map/ppermute | solution.py:95
  113.7 7.2 %collective-permute-start.35 = (bf16[96,896]{1,0:T(8,128)(2,1)S(1)}, bf16[96,896]{1,0:T(8,128)(2,1)S(1)}, u32[]{:S(2)}, u32[]{:S(2)}) collective-permute-start(bf16[96,896]{1,0:T(8,128)(2,1)S(1)} %add_convert_fusion.13), channel_id=1, source_target_pairs={{0,2},{2,4},{4,6},{6,7},{7,5},{5,3},{3,1},{1,0},{8,10},{10,12},{12... | collective-permute-start | bytes 516104 | tf_op jit(solution)/shard_map/ppermute | solution.py:95
  115.8 7.0 %collective-permute-start.49 = (bf16[96,896]{1,0:T(8,128)(2,1)S(1)}, bf16[96,896]{1,0:T(8,128)(2,1)S(1)}, u32[]{:S(2)}, u32[]{:S(2)}) collective-permute-start(bf16[96,896]{1,0:T(8,128)(2,1)S(1)} %add_convert_fusion.6), channel_id=1, source_target_pairs={{0,1},{2,0},{4,2},{6,4},{7,6},{5,7},{3,5},{1,3},{8,9},{10,8},{12,1... | collective-permute-start | bytes 516104 | tf_op jit(solution)/shard_map/ppermute | solution.py:95
  117.4 7.2 %collective-permute-start.8 = (bf16[96,896]{1,0:T(8,128)(2,1)S(1)}, bf16[96,896]{1,0:T(8,128)(2,1)S(1)}, u32[]{:S(2)}, u32[]{:S(2)}) collective-permute-start(bf16[96,896]{1,0:T(8,128)(2,1)S(1)} %add_convert_fusion.26), channel_id=1, source_target_pairs={{0,2},{2,4},{4,6},{6,7},{7,5},{5,3},{3,1},{1,0},{8,10},{10,12},{12... | collective-permute-start | bytes 516104 | tf_op jit(solution)/shard_map/ppermute | solution.py:95
  121.0 6.6 %collective-permute-start.22 = (bf16[96,896]{1,0:T(8,128)(2,1)S(1)}, bf16[96,896]{1,0:T(8,128)(2,1)S(1)}, u32[]{:S(2)}, u32[]{:S(2)}) collective-permute-start(bf16[96,896]{1,0:T(8,128)(2,1)S(1)} %add_convert_fusion.19), channel_id=1, source_target_pairs={{0,1},{2,0},{4,2},{6,4},{7,6},{5,7},{3,5},{1,3},{8,9},{10,8},{12,1... | collective-permute-start | bytes 516104 | tf_op jit(solution)/shard_map/ppermute | solution.py:95
  122.8 6.3 %collective-permute-start.36 = (bf16[96,896]{1,0:T(8,128)(2,1)S(1)}, bf16[96,896]{1,0:T(8,128)(2,1)S(1)}, u32[]{:S(2)}, u32[]{:S(2)}) collective-permute-start(bf16[96,896]{1,0:T(8,128)(2,1)S(1)} %add_convert_fusion.12), channel_id=1, source_target_pairs={{0,2},{2,4},{4,6},{6,7},{7,5},{5,3},{3,1},{1,0},{8,10},{10,12},{12... | collective-permute-start | bytes 516104 | tf_op jit(solution)/shard_map/ppermute | solution.py:95
  124.7 6.7 %collective-permute-start.50 = (bf16[96,896]{1,0:T(8,128)(2,1)S(1)}, bf16[96,896]{1,0:T(8,128)(2,1)S(1)}, u32[]{:S(2)}, u32[]{:S(2)}) collective-permute-start(bf16[96,896]{1,0:T(8,128)(2,1)S(1)} %add_convert_fusion.5), channel_id=1, source_target_pairs={{0,1},{2,0},{4,2},{6,4},{7,6},{5,7},{3,5},{1,3},{8,9},{10,8},{12,1... | collective-permute-start | bytes 516104 | tf_op jit(solution)/shard_map/ppermute | solution.py:95
  127.6 5.7 %collective-permute-start.9 = (bf16[96,896]{1,0:T(8,128)(2,1)S(1)}, bf16[96,896]{1,0:T(8,128)(2,1)S(1)}, u32[]{:S(2)}, u32[]{:S(2)}) collective-permute-start(bf16[96,896]{1,0:T(8,128)(2,1)S(1)} %add_convert_fusion.25), channel_id=1, source_target_pairs={{0,2},{2,4},{4,6},{6,7},{7,5},{5,3},{3,1},{1,0},{8,10},{10,12},{12... | collective-permute-start | bytes 516104 | tf_op jit(solution)/shard_map/ppermute | solution.py:95
  129.1 6.1 %collective-permute-start.23 = (bf16[96,896]{1,0:T(8,128)(2,1)S(1)}, bf16[96,896]{1,0:T(8,128)(2,1)S(1)}, u32[]{:S(2)}, u32[]{:S(2)}) collective-permute-start(bf16[96,896]{1,0:T(8,128)(2,1)S(1)} %add_convert_fusion.18), channel_id=1, source_target_pairs={{0,1},{2,0},{4,2},{6,4},{7,6},{5,7},{3,5},{1,3},{8,9},{10,8},{12,1... | collective-permute-start | bytes 516104 | tf_op jit(solution)/shard_map/ppermute | solution.py:95
  131.4 6.1 %collective-permute-start.37 = (bf16[96,896]{1,0:T(8,128)(2,1)S(1)}, bf16[96,896]{1,0:T(8,128)(2,1)S(1)}, u32[]{:S(2)}, u32[]{:S(2)}) collective-permute-start(bf16[96,896]{1,0:T(8,128)(2,1)S(1)} %add_convert_fusion.11), channel_id=1, source_target_pairs={{0,2},{2,4},{4,6},{6,7},{7,5},{5,3},{3,1},{1,0},{8,10},{10,12},{12... | collective-permute-start | bytes 516104 | tf_op jit(solution)/shard_map/ppermute | solution.py:95
  133.3 6.2 %collective-permute-start.51 = (bf16[96,896]{1,0:T(8,128)(2,1)S(1)}, bf16[96,896]{1,0:T(8,128)(2,1)S(1)}, u32[]{:S(2)}, u32[]{:S(2)}) collective-permute-start(bf16[96,896]{1,0:T(8,128)(2,1)S(1)} %add_convert_fusion.4), channel_id=1, source_target_pairs={{0,1},{2,0},{4,2},{6,4},{7,6},{5,7},{3,5},{1,3},{8,9},{10,8},{12,1... | collective-permute-start | bytes 516104 | tf_op jit(solution)/shard_map/ppermute | solution.py:95
  135.2 6.7 %collective-permute-start.10 = (bf16[96,896]{1,0:T(8,128)(2,1)S(1)}, bf16[96,896]{1,0:T(8,128)(2,1)S(1)}, u32[]{:S(2)}, u32[]{:S(2)}) collective-permute-start(bf16[96,896]{1,0:T(8,128)(2,1)S(1)} %add_convert_fusion.24), channel_id=1, source_target_pairs={{0,2},{2,4},{4,6},{6,7},{7,5},{5,3},{3,1},{1,0},{8,10},{10,12},{12... | collective-permute-start | bytes 516104 | tf_op jit(solution)/shard_map/ppermute | solution.py:95
  137.5 6.7 %collective-permute-start.24 = (bf16[96,896]{1,0:T(8,128)(2,1)S(1)}, bf16[96,896]{1,0:T(8,128)(2,1)S(1)}, u32[]{:S(2)}, u32[]{:S(2)}) collective-permute-start(bf16[96,896]{1,0:T(8,128)(2,1)S(1)} %add_convert_fusion.17), channel_id=1, source_target_pairs={{0,1},{2,0},{4,2},{6,4},{7,6},{5,7},{3,5},{1,3},{8,9},{10,8},{12,1... | collective-permute-start | bytes 516104 | tf_op jit(solution)/shard_map/ppermute | solution.py:95
  139.5 7.3 %collective-permute-start.38 = (bf16[96,896]{1,0:T(8,128)(2,1)S(1)}, bf16[96,896]{1,0:T(8,128)(2,1)S(1)}, u32[]{:S(2)}, u32[]{:S(2)}) collective-permute-start(bf16[96,896]{1,0:T(8,128)(2,1)S(1)} %add_convert_fusion.10), channel_id=1, source_target_pairs={{0,2},{2,4},{4,6},{6,7},{7,5},{5,3},{3,1},{1,0},{8,10},{10,12},{12... | collective-permute-start | bytes 516104 | tf_op jit(solution)/shard_map/ppermute | solution.py:95
  141.9 6.6 %collective-permute-start.52 = (bf16[96,896]{1,0:T(8,128)(2,1)S(1)}, bf16[96,896]{1,0:T(8,128)(2,1)S(1)}, u32[]{:S(2)}, u32[]{:S(2)}) collective-permute-start(bf16[96,896]{1,0:T(8,128)(2,1)S(1)} %add_convert_fusion.3), channel_id=1, source_target_pairs={{0,1},{2,0},{4,2},{6,4},{7,6},{5,7},{3,5},{1,3},{8,9},{10,8},{12,1... | collective-permute-start | bytes 516104 | tf_op jit(solution)/shard_map/ppermute | solution.py:95
  144.2 46.4 %collective-permute-start.11 = (bf16[96,896]{1,0:T(8,128)(2,1)S(1)}, bf16[96,896]{1,0:T(8,128)(2,1)S(1)}, u32[]{:S(2)}, u32[]{:S(2)}) collective-permute-start(bf16[96,896]{1,0:T(8,128)(2,1)S(1)} %add_convert_fusion.23), channel_id=1, source_target_pairs={{0,2},{2,4},{4,6},{6,7},{7,5},{5,3},{3,1},{1,0},{8,10},{10,12},{12... | collective-permute-start | bytes 516104 | tf_op jit(solution)/shard_map/ppermute | solution.py:95
  146.8 44.3 %collective-permute-start.25 = (bf16[96,896]{1,0:T(8,128)(2,1)S(1)}, bf16[96,896]{1,0:T(8,128)(2,1)S(1)}, u32[]{:S(2)}, u32[]{:S(2)}) collective-permute-start(bf16[96,896]{1,0:T(8,128)(2,1)S(1)} %add_convert_fusion.16), channel_id=1, source_target_pairs={{0,1},{2,0},{4,2},{6,4},{7,6},{5,7},{3,5},{1,3},{8,9},{10,8},{12,1... | collective-permute-start | bytes 516104 | tf_op jit(solution)/shard_map/ppermute | solution.py:95
  148.5 44.5 %collective-permute-start.39 = (bf16[96,896]{1,0:T(8,128)(2,1)S(1)}, bf16[96,896]{1,0:T(8,128)(2,1)S(1)}, u32[]{:S(2)}, u32[]{:S(2)}) collective-permute-start(bf16[96,896]{1,0:T(8,128)(2,1)S(1)} %add_convert_fusion.9), channel_id=1, source_target_pairs={{0,2},{2,4},{4,6},{6,7},{7,5},{5,3},{3,1},{1,0},{8,10},{10,12},{12... | collective-permute-start | bytes 516104 | tf_op jit(solution)/shard_map/ppermute | solution.py:95
  150.4 43.0 %collective-permute-start.53 = (bf16[96,896]{1,0:T(8,128)(2,1)S(1)}, bf16[96,896]{1,0:T(8,128)(2,1)S(1)}, u32[]{:S(2)}, u32[]{:S(2)}) collective-permute-start(bf16[96,896]{1,0:T(8,128)(2,1)S(1)} %add_convert_fusion.2), channel_id=1, source_target_pairs={{0,1},{2,0},{4,2},{6,4},{7,6},{5,7},{3,5},{1,3},{8,9},{10,8},{12,1... | collective-permute-start | bytes 516104 | tf_op jit(solution)/shard_map/ppermute | solution.py:95
  185.7 81.0 %collective-permute-start.65 = (bf16[2,896,1280]{2,1,0:T(8,128)(2,1)S(1)}, bf16[2,896,1280]{2,1,0:T(8,128)(2,1)}, u32[]{:S(2)}, u32[]{:S(2)}) collective-permute-start(bf16[2,896,1280]{2,1,0:T(8,128)(2,1)S(1)} %pad_maximum_fusion.4), channel_id=1, source_target_pairs={{0,8},{8,0},{16,24},{24,16},{1,9},{9,1},{17,25},{25,17},{2,10},{10... | collective-permute-start | bytes 13762568 | tf_op jit(solution)/shard_map/ppermute | solution.py:48
  190.6 94.0 %collective-permute-start.63 = (bf16[2,896,1280]{2,1,0:T(8,128)(2,1)}, bf16[2,896,1280]{2,1,0:T(8,128)(2,1)}, u32[]{:S(2)}, u32[]{:S(2)}) collective-permute-start(bf16[2,896,1280]{2,1,0:T(8,128)(2,1)} %pad_maximum_fusion.3), channel_id=1, source_target_pairs={{0,8},{8,0},{16,24},{24,16},{1,9},{9,1},{17,25},{25,17},{2,10},{10... | collective-permute-start | bytes 13762568 | tf_op jit(solution)/shard_map/ppermute | solution.py:48
  191.2 7.3 %collective-permute-start.12 = (bf16[96,896]{1,0:T(8,128)(2,1)S(1)}, bf16[96,896]{1,0:T(8,128)(2,1)S(1)}, u32[]{:S(2)}, u32[]{:S(2)}) collective-permute-start(bf16[96,896]{1,0:T(8,128)(2,1)S(1)} %add_convert_fusion.22), channel_id=1, source_target_pairs={{0,2},{2,4},{4,6},{6,7},{7,5},{5,3},{3,1},{1,0},{8,10},{10,12},{12... | collective-permute-start | bytes 516104 | tf_op jit(solution)/shard_map/ppermute | solution.py:95
  193.0 7.4 %collective-permute-start.26 = (bf16[96,896]{1,0:T(8,128)(2,1)S(1)}, bf16[96,896]{1,0:T(8,128)(2,1)S(1)}, u32[]{:S(2)}, u32[]{:S(2)}) collective-permute-start(bf16[96,896]{1,0:T(8,128)(2,1)S(1)} %add_convert_fusion.15), channel_id=1, source_target_pairs={{0,1},{2,0},{4,2},{6,4},{7,6},{5,7},{3,5},{1,3},{8,9},{10,8},{12,1... | collective-permute-start | bytes 516104 | tf_op jit(solution)/shard_map/ppermute | solution.py:95
  193.4 8.0 %collective-permute-start.40 = (bf16[96,896]{1,0:T(8,128)(2,1)S(1)}, bf16[96,896]{1,0:T(8,128)(2,1)S(1)}, u32[]{:S(2)}, u32[]{:S(2)}) collective-permute-start(bf16[96,896]{1,0:T(8,128)(2,1)S(1)} %add_convert_fusion.8), channel_id=1, source_target_pairs={{0,2},{2,4},{4,6},{6,7},{7,5},{5,3},{3,1},{1,0},{8,10},{10,12},{12... | collective-permute-start | bytes 516104 | tf_op jit(solution)/shard_map/ppermute | solution.py:95
  198.5 6.4 %collective-permute-start.54 = (bf16[96,896]{1,0:T(8,128)(2,1)S(1)}, bf16[96,896]{1,0:T(8,128)(2,1)S(1)}, u32[]{:S(2)}, u32[]{:S(2)}) collective-permute-start(bf16[96,896]{1,0:T(8,128)(2,1)S(1)} %add_convert_fusion.1), channel_id=1, source_target_pairs={{0,1},{2,0},{4,2},{6,4},{7,6},{5,7},{3,5},{1,3},{8,9},{10,8},{12,1... | collective-permute-start | bytes 516104 | tf_op jit(solution)/shard_map/ppermute | solution.py:95
  200.4 6.7 %collective-permute-start.13 = (bf16[96,896]{1,0:T(8,128)(2,1)S(1)}, bf16[96,896]{1,0:T(8,128)(2,1)S(1)}, u32[]{:S(2)}, u32[]{:S(2)}) collective-permute-start(bf16[96,896]{1,0:T(8,128)(2,1)S(1)} %get-tuple-element.20), channel_id=1, source_target_pairs={{0,2},{2,4},{4,6},{6,7},{7,5},{5,3},{3,1},{1,0},{8,10},{10,12},{12... | collective-permute-start | bytes 516104 | tf_op jit(solution)/shard_map/ppermute | solution.py:101
  201.4 7.6 %collective-permute-start.27 = (bf16[96,896]{1,0:T(8,128)(2,1)S(1)}, bf16[96,896]{1,0:T(8,128)(2,1)S(1)}, u32[]{:S(2)}, u32[]{:S(2)}) collective-permute-start(bf16[96,896]{1,0:T(8,128)(2,1)S(1)} %get-tuple-element.22), channel_id=1, source_target_pairs={{0,1},{2,0},{4,2},{6,4},{7,6},{5,7},{3,5},{1,3},{8,9},{10,8},{12,1... | collective-permute-start | bytes 516104 | tf_op jit(solution)/shard_map/ppermute | solution.py:101
  204.8 6.9 %collective-permute-start.41 = (bf16[96,896]{1,0:T(8,128)(2,1)S(1)}, bf16[96,896]{1,0:T(8,128)(2,1)S(1)}, u32[]{:S(2)}, u32[]{:S(2)}) collective-permute-start(bf16[96,896]{1,0:T(8,128)(2,1)S(1)} %get-tuple-element.24), channel_id=1, source_target_pairs={{0,2},{2,4},{4,6},{6,7},{7,5},{5,3},{3,1},{1,0},{8,10},{10,12},{12... | collective-permute-start | bytes 516104 | tf_op jit(solution)/shard_map/ppermute | solution.py:101
  207.1 7.0 %collective-permute-start.55 = (bf16[96,896]{1,0:T(8,128)(2,1)S(1)}, bf16[96,896]{1,0:T(8,128)(2,1)S(1)}, u32[]{:S(2)}, u32[]{:S(2)}) collective-permute-start(bf16[96,896]{1,0:T(8,128)(2,1)S(1)} %get-tuple-element.26), channel_id=1, source_target_pairs={{0,1},{2,0},{4,2},{6,4},{7,6},{5,7},{3,5},{1,3},{8,9},{10,8},{12,1... | collective-permute-start | bytes 516104 | tf_op jit(solution)/shard_map/ppermute | solution.py:101
  209.0 6.8 %collective-permute-start.14 = (bf16[96,896]{1,0:T(8,128)(2,1)S(1)}, bf16[96,896]{1,0:T(8,128)(2,1)S(1)}, u32[]{:S(2)}, u32[]{:S(2)}) collective-permute-start(bf16[96,896]{1,0:T(8,128)(2,1)S(1)} %collective-permute-done.13), channel_id=1, source_target_pairs={{0,2},{2,4},{4,6},{6,7},{7,5},{5,3},{3,1},{1,0},{8,10},{10,12},{12... | collective-permute-start | bytes 516104 | tf_op jit(solution)/shard_map/ppermute | solution.py:101
  211.7 7.1 %collective-permute-start.28 = (bf16[96,896]{1,0:T(8,128)(2,1)S(1)}, bf16[96,896]{1,0:T(8,128)(2,1)S(1)}, u32[]{:S(2)}, u32[]{:S(2)}) collective-permute-start(bf16[96,896]{1,0:T(8,128)(2,1)S(1)} %collective-permute-done.27), channel_id=1, source_target_pairs={{0,1},{2,0},{4,2},{6,4},{7,6},{5,7},{3,5},{1,3},{8,9},{10,8},{12,1... | collective-permute-start | bytes 516104 | tf_op jit(solution)/shard_map/ppermute | solution.py:101
  214.1 6.5 %collective-permute-start.42 = (bf16[96,896]{1,0:T(8,128)(2,1)S(1)}, bf16[96,896]{1,0:T(8,128)(2,1)S(1)}, u32[]{:S(2)}, u32[]{:S(2)}) collective-permute-start(bf16[96,896]{1,0:T(8,128)(2,1)S(1)} %collective-permute-done.41), channel_id=1, source_target_pairs={{0,2},{2,4},{4,6},{6,7},{7,5},{5,3},{3,1},{1,0},{8,10},{10,12},{12... | collective-permute-start | bytes 516104 | tf_op jit(solution)/shard_map/ppermute | solution.py:101
  215.8 6.5 %collective-permute-start.56 = (bf16[96,896]{1,0:T(8,128)(2,1)S(1)}, bf16[96,896]{1,0:T(8,128)(2,1)S(1)}, u32[]{:S(2)}, u32[]{:S(2)}) collective-permute-start(bf16[96,896]{1,0:T(8,128)(2,1)S(1)} %collective-permute-done.55), channel_id=1, source_target_pairs={{0,1},{2,0},{4,2},{6,4},{7,6},{5,7},{3,5},{1,3},{8,9},{10,8},{12,1... | collective-permute-start | bytes 516104 | tf_op jit(solution)/shard_map/ppermute | solution.py:101
  218.7 6.2 %collective-permute-start.15 = (bf16[96,896]{1,0:T(8,128)(2,1)S(1)}, bf16[96,896]{1,0:T(8,128)(2,1)S(1)}, u32[]{:S(2)}, u32[]{:S(2)}) collective-permute-start(bf16[96,896]{1,0:T(8,128)(2,1)S(1)} %collective-permute-done.14), channel_id=1, source_target_pairs={{0,2},{2,4},{4,6},{6,7},{7,5},{5,3},{3,1},{1,0},{8,10},{10,12},{12... | collective-permute-start | bytes 516104 | tf_op jit(solution)/shard_map/ppermute | solution.py:101
  220.5 6.2 %collective-permute-start.29 = (bf16[96,896]{1,0:T(8,128)(2,1)S(1)}, bf16[96,896]{1,0:T(8,128)(2,1)S(1)}, u32[]{:S(2)}, u32[]{:S(2)}) collective-permute-start(bf16[96,896]{1,0:T(8,128)(2,1)S(1)} %collective-permute-done.28), channel_id=1, source_target_pairs={{0,1},{2,0},{4,2},{6,4},{7,6},{5,7},{3,5},{1,3},{8,9},{10,8},{12,1... | collective-permute-start | bytes 516104 | tf_op jit(solution)/shard_map/ppermute | solution.py:101
  222.3 6.8 %collective-permute-start.43 = (bf16[96,896]{1,0:T(8,128)(2,1)S(1)}, bf16[96,896]{1,0:T(8,128)(2,1)S(1)}, u32[]{:S(2)}, u32[]{:S(2)}) collective-permute-start(bf16[96,896]{1,0:T(8,128)(2,1)S(1)} %collective-permute-done.42), channel_id=1, source_target_pairs={{0,2},{2,4},{4,6},{6,7},{7,5},{5,3},{3,1},{1,0},{8,10},{10,12},{12... | collective-permute-start | bytes 516104 | tf_op jit(solution)/shard_map/ppermute | solution.py:101
  224.9 6.5 %collective-permute-start.57 = (bf16[96,896]{1,0:T(8,128)(2,1)S(1)}, bf16[96,896]{1,0:T(8,128)(2,1)S(1)}, u32[]{:S(2)}, u32[]{:S(2)}) collective-permute-start(bf16[96,896]{1,0:T(8,128)(2,1)S(1)} %collective-permute-done.56), channel_id=1, source_target_pairs={{0,1},{2,0},{4,2},{6,4},{7,6},{5,7},{3,5},{1,3},{8,9},{10,8},{12,1... | collective-permute-start | bytes 516104 | tf_op jit(solution)/shard_map/ppermute | solution.py:101
  226.7 7.1 %collective-permute-start.16 = (bf16[96,896]{1,0:T(8,128)(2,1)S(1)}, bf16[96,896]{1,0:T(8,128)(2,1)S(1)}, u32[]{:S(2)}, u32[]{:S(2)}) collective-permute-start(bf16[96,896]{1,0:T(8,128)(2,1)S(1)} %collective-permute-done.15), channel_id=1, source_target_pairs={{0,2},{2,4},{4,6},{6,7},{7,5},{5,3},{3,1},{1,0},{8,10},{10,12},{12... | collective-permute-start | bytes 516104 | tf_op jit(solution)/shard_map/ppermute | solution.py:101
  229.1 7.2 %collective-permute-start.30 = (bf16[96,896]{1,0:T(8,128)(2,1)S(1)}, bf16[96,896]{1,0:T(8,128)(2,1)S(1)}, u32[]{:S(2)}, u32[]{:S(2)}) collective-permute-start(bf16[96,896]{1,0:T(8,128)(2,1)S(1)} %collective-permute-done.29), channel_id=1, source_target_pairs={{0,1},{2,0},{4,2},{6,4},{7,6},{5,7},{3,5},{1,3},{8,9},{10,8},{12,1... | collective-permute-start | bytes 516104 | tf_op jit(solution)/shard_map/ppermute | solution.py:101
  231.5 7.1 %collective-permute-start.44 = (bf16[96,896]{1,0:T(8,128)(2,1)S(1)}, bf16[96,896]{1,0:T(8,128)(2,1)S(1)}, u32[]{:S(2)}, u32[]{:S(2)}) collective-permute-start(bf16[96,896]{1,0:T(8,128)(2,1)S(1)} %collective-permute-done.43), channel_id=1, source_target_pairs={{0,2},{2,4},{4,6},{6,7},{7,5},{5,3},{3,1},{1,0},{8,10},{10,12},{12... | collective-permute-start | bytes 516104 | tf_op jit(solution)/shard_map/ppermute | solution.py:101
  233.8 6.6 %collective-permute-start.58 = (bf16[96,896]{1,0:T(8,128)(2,1)S(1)}, bf16[96,896]{1,0:T(8,128)(2,1)S(1)}, u32[]{:S(2)}, u32[]{:S(2)}) collective-permute-start(bf16[96,896]{1,0:T(8,128)(2,1)S(1)} %collective-permute-done.57), channel_id=1, source_target_pairs={{0,1},{2,0},{4,2},{6,4},{7,6},{5,7},{3,5},{1,3},{8,9},{10,8},{12,1... | collective-permute-start | bytes 516104 | tf_op jit(solution)/shard_map/ppermute | solution.py:101
  236.2 6.6 %collective-permute-start.17 = (bf16[96,896]{1,0:T(8,128)(2,1)S(1)}, bf16[96,896]{1,0:T(8,128)(2,1)S(1)}, u32[]{:S(2)}, u32[]{:S(2)}) collective-permute-start(bf16[96,896]{1,0:T(8,128)(2,1)S(1)} %collective-permute-done.16), channel_id=1, source_target_pairs={{0,2},{2,4},{4,6},{6,7},{7,5},{5,3},{3,1},{1,0},{8,10},{10,12},{12... | collective-permute-start | bytes 516104 | tf_op jit(solution)/shard_map/ppermute | solution.py:101
  238.6 6.2 %collective-permute-start.31 = (bf16[96,896]{1,0:T(8,128)(2,1)S(1)}, bf16[96,896]{1,0:T(8,128)(2,1)S(1)}, u32[]{:S(2)}, u32[]{:S(2)}) collective-permute-start(bf16[96,896]{1,0:T(8,128)(2,1)S(1)} %collective-permute-done.30), channel_id=1, source_target_pairs={{0,1},{2,0},{4,2},{6,4},{7,6},{5,7},{3,5},{1,3},{8,9},{10,8},{12,1... | collective-permute-start | bytes 516104 | tf_op jit(solution)/shard_map/ppermute | solution.py:101
  240.4 6.1 %collective-permute-start.45 = (bf16[96,896]{1,0:T(8,128)(2,1)S(1)}, bf16[96,896]{1,0:T(8,128)(2,1)S(1)}, u32[]{:S(2)}, u32[]{:S(2)}) collective-permute-start(bf16[96,896]{1,0:T(8,128)(2,1)S(1)} %collective-permute-done.44), channel_id=1, source_target_pairs={{0,2},{2,4},{4,6},{6,7},{7,5},{5,3},{3,1},{1,0},{8,10},{10,12},{12... | collective-permute-start | bytes 516104 | tf_op jit(solution)/shard_map/ppermute | solution.py:101
  242.8 6.1 %collective-permute-start.59 = (bf16[96,896]{1,0:T(8,128)(2,1)S(1)}, bf16[96,896]{1,0:T(8,128)(2,1)S(1)}, u32[]{:S(2)}, u32[]{:S(2)}) collective-permute-start(bf16[96,896]{1,0:T(8,128)(2,1)S(1)} %collective-permute-done.58), channel_id=1, source_target_pairs={{0,1},{2,0},{4,2},{6,4},{7,6},{5,7},{3,5},{1,3},{8,9},{10,8},{12,1... | collective-permute-start | bytes 516104 | tf_op jit(solution)/shard_map/ppermute | solution.py:101
  244.7 6.0 %collective-permute-start.18 = (bf16[96,896]{1,0:T(8,128)(2,1)S(1)}, bf16[96,896]{1,0:T(8,128)(2,1)S(1)}, u32[]{:S(2)}, u32[]{:S(2)}) collective-permute-start(bf16[96,896]{1,0:T(8,128)(2,1)S(1)} %collective-permute-done.17), channel_id=1, source_target_pairs={{0,2},{2,4},{4,6},{6,7},{7,5},{5,3},{3,1},{1,0},{8,10},{10,12},{12... | collective-permute-start | bytes 516104 | tf_op jit(solution)/shard_map/ppermute | solution.py:101
  246.6 6.7 %collective-permute-start.32 = (bf16[96,896]{1,0:T(8,128)(2,1)S(1)}, bf16[96,896]{1,0:T(8,128)(2,1)S(1)}, u32[]{:S(2)}, u32[]{:S(2)}) collective-permute-start(bf16[96,896]{1,0:T(8,128)(2,1)S(1)} %collective-permute-done.31), channel_id=1, source_target_pairs={{0,1},{2,0},{4,2},{6,4},{7,6},{5,7},{3,5},{1,3},{8,9},{10,8},{12,1... | collective-permute-start | bytes 516104 | tf_op jit(solution)/shard_map/ppermute | solution.py:101
  248.9 6.4 %collective-permute-start.46 = (bf16[96,896]{1,0:T(8,128)(2,1)S(1)}, bf16[96,896]{1,0:T(8,128)(2,1)S(1)}, u32[]{:S(2)}, u32[]{:S(2)}) collective-permute-start(bf16[96,896]{1,0:T(8,128)(2,1)S(1)} %collective-permute-done.45), channel_id=1, source_target_pairs={{0,2},{2,4},{4,6},{6,7},{7,5},{5,3},{3,1},{1,0},{8,10},{10,12},{12... | collective-permute-start | bytes 516104 | tf_op jit(solution)/shard_map/ppermute | solution.py:101
  250.8 5.7 %collective-permute-start.60 = (bf16[96,896]{1,0:T(8,128)(2,1)S(1)}, bf16[96,896]{1,0:T(8,128)(2,1)S(1)}, u32[]{:S(2)}, u32[]{:S(2)}) collective-permute-start(bf16[96,896]{1,0:T(8,128)(2,1)S(1)} %collective-permute-done.59), channel_id=1, source_target_pairs={{0,1},{2,0},{4,2},{6,4},{7,6},{5,7},{3,5},{1,3},{8,9},{10,8},{12,1... | collective-permute-start | bytes 516104 | tf_op jit(solution)/shard_map/ppermute | solution.py:101
  320.5 33.5 %all-to-all-start.1 = ((f32[32,16,448]{2,1,0:T(8,128)}), f32[32,16,448]{2,1,0:T(8,128)S(1)}, u32[]{:S(2)}, u32[]{:S(2)}) async-start(f32[32,16,448]{2,1,0:T(8,128)} %bitcast.100), calls=%async_computation.1 | async-start | bytes 2097152 | tf_op jit(solution)/shard_map/all_to_all | solution.py:240
  (26 other events, 506.2 us)

commit v5 on v3

--- a/solution.py
+++ b/solution.py
@@ -146,20 +146,22 @@
     norm_in = rms_scale(hidden_perm, attn_gain_perm)
     qkv = jnp.dot(norm_in, qkv_full, preferred_element_type=jnp.float32).astype(jnp.bfloat16)
     queries = qkv[:, :q_cols]
-    kv_part = qkv[:, q_cols:]
-    kv_all = lax.all_to_all(
-        jnp.broadcast_to(kv_part[None], (tp_size,) + kv_part.shape), "tp", 0, 0, tiled=True
-    )
     per_dev = k_cols // KVH
-    kv_index = tp_index * local_heads // (HEADS // KVH)
-
-    def head_of(part):
-        split = part.reshape(tp_size, row_count, per_dev, KVH)
-        one = lax.dynamic_slice_in_dim(split, kv_index, 1, 3)[..., 0]
-        return one.transpose(1, 0, 2).reshape(row_count, tp_size * per_dev)
-
-    key_head = head_of(kv_all[:, :, :k_cols])
-    value_head = head_of(kv_all[:, :, k_cols:])
+    group_heads = HEADS // KVH
+    key_split = qkv[:, q_cols : q_cols + k_cols].reshape(row_count, per_dev, KVH)
+    value_split = qkv[:, q_cols + k_cols :].reshape(row_count, per_dev, KVH)
+    outgoing_kv = jnp.stack(
+        [
+            jnp.concatenate(
+                [key_split[:, :, u * local_heads // group_heads], value_split[:, :, u * local_heads // group_heads]],
+                1,
+            )
+            for u in range(tp_size)
+        ]
+    )
+    kv_in = lax.all_to_all(outgoing_kv, "tp", 0, 0, tiled=True)
+    key_head = kv_in[:, :, :per_dev].transpose(1, 0, 2).reshape(row_count, tp_size * per_dev)
+    value_head = kv_in[:, :, per_dev:].transpose(1, 0, 2).reshape(row_count, tp_size * per_dev)
 
     segs = segment_ids(lengths, block_rows)
     same = segs[:, :, None] == segs[:, None, :]
@@ -219,23 +221,22 @@
         (target_grid == dest_all[None, None]) & (row_grid == slot_row[None, None])
     ).astype(jnp.float32).reshape(grp_size, slots, grp_size * programs)
     down_slots = jnp.einsum("asq,qd->asd", placer, down_part, precision=HIGH)
-    down_slots = down_slots.reshape(grp_size, slots, ratio, d_tp).transpose(0, 2, 1, 3)
-    send = lax.dynamic_update_slice(
-        jnp.zeros((grp_size, tp_size, slots, d_tp), jnp.float32),
-        down_slots,
-        (0, grp_index * ratio, 0, 0),
-    )
+    totals = jnp.zeros((slots, d_tp), jnp.float32)
+    for k in range(tp_size):
+        pairs = []
+        for g in range(grp_size):
+            for t in range(tp_size):
+                u = (t - k) % tp_size
+                pairs.append((g * tp_size + t, (u // ratio) * tp_size + g * ratio + u % ratio))
+        u = (tp_index - k) % tp_size
+        piece = lax.dynamic_index_in_dim(down_slots, u // ratio, 0, keepdims=False)
+        piece = lax.dynamic_slice_in_dim(piece, (u % ratio) * d_tp, d_tp, 1)
+        totals = totals + lax.ppermute(piece, ("grp", "tp"), pairs)
     local_placer = placer[:, :, :programs]
-    residual_slots = jnp.einsum("asq,qd->asd", local_placer, residual_sums, precision=HIGH)
-    send = send + lax.dynamic_update_slice(
-        jnp.zeros((grp_size, tp_size, slots, d_tp), jnp.float32),
-        residual_slots[:, None],
-        (0, tp_index, 0, 0),
-    )
-    received = lax.all_to_all(
-        send.reshape(grp_size * tp_size, slots, d_tp), ("grp", "tp"), 0, 0, tiled=True
-    )
-    totals = jnp.sum(received, axis=0)
+    own_rows = lax.dynamic_slice_in_dim(local_placer, grp_index * capacity, capacity, 1)
+    residual_slots = jnp.einsum("asq,qd->asd", own_rows, residual_sums, precision=HIGH)
+    residual_in = lax.all_to_all(residual_slots, "grp", 0, 0, tiled=True)
+    totals = totals + residual_in.reshape(slots, d_tp)
     mine = lax.dynamic_index_in_dim(placer, grp_index, 0, keepdims=False)
     counts = jnp.dot(mine, lengths_all.astype(jnp.float32), precision=HIGH)
     counts = jnp.where(counts > 0, counts, 1.0)

time: 331 us -> 328 us (level)
  waiting for transfers between devices: 150 us -> 131 us
  starting transfers between devices: 51.4 us -> 61.6 us
  other arithmetic: 45.5 us -> 51 us
    all_to_all x2, waiting for transfers between devices: 31 us -> 0.01 us  [the longest x1 0.01 us: on_device(): kv_in = lax.all_to_all(outgoing_kv, 'tp', 0, 0, tiled=True)]
    ppermute x0 -> x8, starting transfers between devices: none -> 13.9 us  [on_device(): totals = totals + lax.ppermute(piece, ('grp', 'tp'), pairs)]
    ppermute x7, waiting for transfers between devices: 33.8 us -> 43.9 us  [gather_grp(): moving = lax.ppermute(moving, 'grp', ring)]
    ppermute x0 -> x8, waiting for transfers between devices: none -> 5.49 us  [on_device(): totals = totals + lax.ppermute(piece, ('grp', 'tp'), pairs)]
    concatenate x6, other arithmetic: 23 us -> 18 us  [gather_grp(): return jnp.concatenate([mine, other], 0)]
    unnamed x0 -> x7, other arithmetic: none -> 4.33 us
    convert_element_type x12, other arithmetic: 1.01 us -> 4.95 us  [ring_psum(): (got.astype(jnp.float32) + chunk(step + 1).astype(jnp.float32)).astype(x....]
  transfers between devices with their start and end apart: 44 -> 52, of which waited for: 24 -> 25; matrix products, arithmetic and copies ran while one was open for 21% -> 33% of each run, Pallas kernels for 0% -> 0%
where the time goes in v5:
time: 328 us; the launch traced here: 326 us
  waiting for transfers between devices  131 us (40%)
  starting transfers between devices  61.6 us (19%)
  other arithmetic  51 us (16%)
  matrix products  45.1 us (14%)
  local copies, waits for them, and re-layouts  21.1 us (6%)
  between operations  15.3 us (5%)
    ppermute x7, waiting for transfers between devices, gather_grp(): moving = lax.ppermute(moving, 'grp', ring)  43.9 us
    ppermute x14, waiting for transfers between devices, ring_psum(): moving = lax.ppermute(moving, axis, pairs)  41.9 us
    ppermute x14, waiting for transfers between devices, ring_psum(): got = lax.ppermute(acc, axis, pairs)  39.5 us
    concatenate x6, other arithmetic, gather_grp(): return jnp.concatenate([mine, other], 0)  18 us
    dot_general x1, matrix products, on_device(): jnp.dot(selector.astype(jnp.bfloat16), hidden_ffn, preferred_element_type...  15.6 us
    ppermute x14, starting transfers between devices, ring_psum(): got = lax.ppermute(acc, axis, pairs)  15.2 us
    ppermute x14, starting transfers between devices, ring_psum(): moving = lax.ppermute(moving, axis, pairs)  14.6 us
    ppermute x8, starting transfers between devices, on_device(): totals = totals + lax.ppermute(piece, ('grp', 'tp'), pairs)  13.9 us
  transfers between devices with their start and end apart: 52, of which 25 were waited for; matrix products, arithmetic and copies ran while one was open for 33% of the time, Pallas kernels for 0%

profile of v5, /device:TPU:0, one launch (start us, length us, event | category | flops | bytes accessed | tf_op | source)
XLA Modules:
  0.0 325.7 jit_solution(15337650483359108645)
XLA Ops:
  2.3 2.0 pad_maximum_fusion.9
  4.3 2.9 collective-permute-start.2
  7.3 1.3 reshape.147
  8.6 2.0 collective-permute-start
  31.5 3.0 constant_dynamic-slice_fusion.7
  34.6 1.4 fusion.1
  37.4 4.3 %fusion.12 = bf16[768,384]{0,1:T(8,128)(2,1)S(1)} fusion(bf16[3584,384]{1,0:T(8,128)(2,1)S(1)} %bitcast.155, f32[3584]{0:T(1024)S(1)} %pad_maximum_fusion.12, f32[768]{0:T(1024)S(1)} %add_rsqrt_fusion.1, bf16[768,896]{1,0:T(8,128)(2,1)S(1)} %get-tuple-element.27, bf16[768,896]{1,0:T(8,128)(2,1)S(1)} %get-tuple-element.28, ...), kind=kOutput, calls=%fused_computation.29 | convolution fusion | flops 2144501760 | bytes 8864768 | tf_op jit(solution)/shard_map/dot_general | solution.py:147
  48.0 5.8 %all-to-all-start = ((bf16[8,768,32]{1,2,0:T(8,128)(2,1)}), bf16[8,768,32]{1,2,0:T(8,128)(2,1)S(1)}, u32[]{:S(2)}, u32[]{:S(2)}) async-start(bf16[8,768,32]{1,2,0:T(8,128)(2,1)} %fusion.41), calls=%async_computation | async-start | bytes 786432 | tf_op jit(solution)/shard_map/all_to_all | solution.py:162
  60.9 1.4 reduce_window_sum.22
  63.1 4.1 %collective-permute-done.4 = bf16[896,256]{1,0:T(8,128)(2,1)} collective-permute-done((bf16[896,256]{1,0:T(8,128)(2,1)S(1)}, bf16[896,256]{1,0:T(8,128)(2,1)}, u32[]{:S(2)}, u32[]{:S(2)}) %collective-permute-start.4) | collective-permute-done | bytes 458784 | tf_op jit(solution)/shard_map/ppermute | solution.py:45
  67.2 2.0 pad_maximum_fusion.8
  69.4 4.1 %fusion.73 = (f32[2,2,384]{2,1,0:T(2,128)}, f32[2,2,384,384]{2,3,1,0:T(8,128)}) fusion(pred[2,384,384]{1,2,0:T(8,128)(4,1)} %broadcast_compare_fusion, bf16[2,384,2,128]{1,0,3,2:T(2,128)(2,1)} %reshape.140, bf16[2,384,128,1]{1,0,2,3:T(2,128)(2,1)S(1)} %bitcast.182), kind=kOutput, calls=%fused_computation.169 | convolution fusion | flops 153354624 | bytes 3250176 | tf_op jit(solution)/shard_map/sub | solution.py:29
  73.5 2.0 fusion.15
  76.0 1.5 pad_maximum_fusion.6
  77.5 1.6 convolution_convert_fusion
  79.1 1.9 fusion.65
  81.0 1.5 copy-done.11
  83.3 1.7 collective-permute-start.6
  87.4 1.5 collective-permute-start.34
  88.9 5.1 %collective-permute-done.6 = bf16[96,1792]{1,0:T(8,128)(2,1)S(1)} collective-permute-done((bf16[96,1792]{1,0:T(8,128)(2,1)}, bf16[96,1792]{1,0:T(8,128)(2,1)S(1)}, u32[]{:S(2)}, u32[]{:S(2)}) %collective-permute-start.6) | collective-permute-done | bytes 344096 | tf_op jit(solution)/shard_map/ppermute | solution.py:90
  95.1 1.8 collective-permute-start.7
  98.5 6.4 %collective-permute-done.7 = bf16[96,1792]{1,0:T(8,128)(2,1)S(1)} collective-permute-done((bf16[96,1792]{1,0:T(8,128)(2,1)S(1)}, bf16[96,1792]{1,0:T(8,128)(2,1)S(1)}, u32[]{:S(2)}, u32[]{:S(2)}) %collective-permute-start.7) | collective-permute-done | bytes 344096 | tf_op jit(solution)/shard_map/ppermute | solution.py:90
  105.9 1.8 collective-permute-start.8
  108.1 6.6 %collective-permute-done.8 = bf16[96,1792]{1,0:T(8,128)(2,1)S(1)} collective-permute-done((bf16[96,1792]{1,0:T(8,128)(2,1)S(1)}, bf16[96,1792]{1,0:T(8,128)(2,1)S(1)}, u32[]{:S(2)}, u32[]{:S(2)}) %collective-permute-start.8) | collective-permute-done | bytes 344096 | tf_op jit(solution)/shard_map/ppermute | solution.py:90
  115.8 2.0 collective-permute-start.9
  118.2 5.9 %collective-permute-done.9 = bf16[96,1792]{1,0:T(8,128)(2,1)S(1)} collective-permute-done((bf16[96,1792]{1,0:T(8,128)(2,1)S(1)}, bf16[96,1792]{1,0:T(8,128)(2,1)S(1)}, u32[]{:S(2)}, u32[]{:S(2)}) %collective-permute-start.9) | collective-permute-done | bytes 344096 | tf_op jit(solution)/shard_map/ppermute | solution.py:90
  124.2 1.8 collective-permute-start.10
  126.5 6.1 %collective-permute-done.10 = bf16[96,1792]{1,0:T(8,128)(2,1)S(1)} collective-permute-done((bf16[96,1792]{1,0:T(8,128)(2,1)S(1)}, bf16[96,1792]{1,0:T(8,128)(2,1)S(1)}, u32[]{:S(2)}, u32[]{:S(2)}) %collective-permute-start.10) | collective-permute-done | bytes 344096 | tf_op jit(solution)/shard_map/ppermute | solution.py:90
  132.6 1.8 collective-permute-start.11
  135.1 6.6 %collective-permute-done.11 = bf16[96,1792]{1,0:T(8,128)(2,1)S(1)} collective-permute-done((bf16[96,1792]{1,0:T(8,128)(2,1)S(1)}, bf16[96,1792]{1,0:T(8,128)(2,1)S(1)}, u32[]{:S(2)}, u32[]{:S(2)}) %collective-permute-start.11) | collective-permute-done | bytes 344096 | tf_op jit(solution)/shard_map/ppermute | solution.py:90
  141.8 1.8 collective-permute-start.12
  144.6 2.8 pad_maximum_fusion.4
  147.4 1.7 collective-permute-done.12
  149.4 1.8 collective-permute-start.13
  152.2 35.8 %collective-permute-done.34 = bf16[896,1280]{1,0:T(8,128)(2,1)S(1)} collective-permute-done((bf16[896,1280]{1,0:T(8,128)(2,1)}, bf16[896,1280]{1,0:T(8,128)(2,1)S(1)}, u32[]{:S(2)}, u32[]{:S(2)}) %collective-permute-start.34) | collective-permute-done | bytes 2293792 | tf_op jit(solution)/shard_map/ppermute | solution.py:45
  188.0 2.6 pad_maximum_fusion.3
  190.6 1.7 collective-permute-start.14
  192.7 8.3 %collective-permute-done.14 = bf16[96,1792]{1,0:T(8,128)(2,1)S(1)} collective-permute-done((bf16[96,1792]{1,0:T(8,128)(2,1)S(1)}, bf16[96,1792]{1,0:T(8,128)(2,1)S(1)}, u32[]{:S(2)}, u32[]{:S(2)}) %collective-permute-start.14) | collective-permute-done | bytes 344096 | tf_op jit(solution)/shard_map/ppermute | solution.py:96
  201.1 1.7 collective-permute-start.15
  203.2 7.5 %collective-permute-done.15 = bf16[96,1792]{1,0:T(8,128)(2,1)S(1)} collective-permute-done((bf16[96,1792]{1,0:T(8,128)(2,1)S(1)}, bf16[96,1792]{1,0:T(8,128)(2,1)S(1)}, u32[]{:S(2)}, u32[]{:S(2)}) %collective-permute-start.15) | collective-permute-done | bytes 344096 | tf_op jit(solution)/shard_map/ppermute | solution.py:96
  210.8 1.7 collective-permute-start.16
  212.9 6.6 %collective-permute-done.16 = bf16[96,1792]{1,0:T(8,128)(2,1)S(1)} collective-permute-done((bf16[96,1792]{1,0:T(8,128)(2,1)S(1)}, bf16[96,1792]{1,0:T(8,128)(2,1)S(1)}, u32[]{:S(2)}, u32[]{:S(2)}) %collective-permute-start.16) | collective-permute-done | bytes 344096 | tf_op jit(solution)/shard_map/ppermute | solution.py:96
  219.6 1.7 collective-permute-start.17
  221.7 6.1 %collective-permute-done.17 = bf16[96,1792]{1,0:T(8,128)(2,1)S(1)} collective-permute-done((bf16[96,1792]{1,0:T(8,128)(2,1)S(1)}, bf16[96,1792]{1,0:T(8,128)(2,1)S(1)}, u32[]{:S(2)}, u32[]{:S(2)}) %collective-permute-start.17) | collective-permute-done | bytes 344096 | tf_op jit(solution)/shard_map/ppermute | solution.py:96
  227.8 1.7 collective-permute-start.18
  229.9 6.5 %collective-permute-done.18 = bf16[96,1792]{1,0:T(8,128)(2,1)S(1)} collective-permute-done((bf16[96,1792]{1,0:T(8,128)(2,1)S(1)}, bf16[96,1792]{1,0:T(8,128)(2,1)S(1)}, u32[]{:S(2)}, u32[]{:S(2)}) %collective-permute-start.18) | collective-permute-done | bytes 344096 | tf_op jit(solution)/shard_map/ppermute | solution.py:96
  236.5 1.7 collective-permute-start.19
  238.7 5.0 %collective-permute-done.19 = bf16[96,1792]{1,0:T(8,128)(2,1)S(1)} collective-permute-done((bf16[96,1792]{1,0:T(8,128)(2,1)S(1)}, bf16[96,1792]{1,0:T(8,128)(2,1)S(1)}, u32[]{:S(2)}, u32[]{:S(2)}) %collective-permute-start.19) | collective-permute-done | bytes 344096 | tf_op jit(solution)/shard_map/ppermute | solution.py:96
  243.7 1.7 collective-permute-done.33
  245.6 2.4 multiply_reduce_fusion
  248.1 8.6 %pad_maximum_fusion.1 = bf16[4,896,1280]{2,1,0:T(8,128)(2,1)} fusion(bf16[2,896,1280]{2,1,0:T(8,128)(2,1)} %collective-permute-done.37, bf16[1,896,1280]{2,1,0:T(8,128)(2,1)S(1)} %bitcast.151, bf16[1,896,1280]{2,1,0:T(8,128)(2,1)S(1)} %bitcast.145), kind=kLoop, calls=%fused_computation.10 | loop fusion | flops 9175040 | bytes 18350080 | tf_op jit(solution)/shard_map/concatenate | solution.py:49
  256.6 11.9 %fusion.63 = f32[768,1280]{1,0:T(8,128)} fusion(bf16[3584,1280]{1,0:T(8,128)(2,1)} %bitcast.153, f32[768,3584]{1,0:T(8,128)S(1)} %get-tuple-element.18, f32[3584]{0:T(1024)S(1)} %copy-done.22, f32[768]{0:T(1024)S(1)} %add_rsqrt_fusion), kind=kOutput, calls=%fused_computation.159 | convolution fusion | flops 7054688256 | bytes 24134656 | tf_op jit(solution)/shard_map/dot_general | solution.py:188
  268.5 6.9 %pad_maximum_fusion = bf16[4,896,1280]{2,1,0:T(8,128)(2,1)} fusion(bf16[2,896,1280]{2,1,0:T(8,128)(2,1)} %collective-permute-done.35, bf16[1,896,1280]{2,1,0:T(8,128)(2,1)S(1)} %bitcast.149, bf16[1,896,1280]{2,1,0:T(8,128)(2,1)S(1)} %bitcast.147), kind=kLoop, calls=%fused_computation.9 | loop fusion | flops 9175040 | bytes 18350080 | tf_op jit(solution)/shard_map/concatenate | solution.py:49
  275.5 15.6 %fusion.9 = f32[16,1280]{1,0:T(8,128)S(1)} fusion(f32[768,1280]{1,0:T(8,128)} %fusion.63, s32[768]{0:T(1024)S(1)} %add.528, bf16[3584,1280]{1,0:T(8,128)(2,1)} %bitcast.152, f32[768,3584]{1,0:T(8,128)} %copy-done.1, f32[3584]{0:T(1024)S(1)} %copy-done.22, f32[768]{0:T(1024)S(1)} %add_rsqrt_fusion), kind=kOutput, calls=%fused_computation.24 | convolution fusion | flops 7092080640 | bytes 24219648 | tf_op jit(solution)/shard_map/dot_general | solution.py:195
  291.6 3.9 %collective-permute-done.38 = f32[16,1280]{1,0:T(8,128)S(1)} collective-permute-done((f32[16,1280]{1,0:T(8,128)S(1)}, f32[16,1280]{1,0:T(8,128)S(1)}, u32[]{:S(2)}, u32[]{:S(2)}) %collective-permute-start.38) | collective-permute-done | bytes 81952 | tf_op jit(solution)/shard_map/ppermute | solution.py:45
  296.3 2.3 fusion.19
  298.7 2.1 convolution_bitcast_fusion
  302.0 5.6 %collective-permute-start.41 = (f32[16,448]{1,0:T(8,128)S(1)}, f32[16,448]{1,0:T(8,128)S(1)}, u32[]{:S(2)}, u32[]{:S(2)}) collective-permute-start(f32[16,448]{1,0:T(8,128)S(1)} %get-tuple-element.33), channel_id=1, source_target_pairs={{0,25},{1,0},{2,1},{3,8},{4,9},{5,16},{6,17},{7,24},{8,27},{9,2},{... | collective-permute-start | bytes 86024 | tf_op jit(solution)/shard_map/ppermute | solution.py:234
  308.6 3.3 %all-to-all-start.1 = ((f32[4,4,448]{2,1,0:T(4,128)}), f32[4,4,448]{2,1,0:T(4,128)S(1)}, u32[]{:S(2)}, u32[]{:S(2)}) async-start(f32[4,4,448]{2,1,0:T(4,128)} %fusion.51), calls=%async_computation.1 | async-start | bytes 65536 | tf_op jit(solution)/shard_map/all_to_all | solution.py:238
  311.8 3.4 %collective-permute-start.43 = (f32[16,448]{1,0:T(8,128)S(1)}, f32[16,448]{1,0:T(8,128)S(1)}, u32[]{:S(2)}, u32[]{:S(2)}) collective-permute-start(f32[16,448]{1,0:T(8,128)S(1)} %get-tuple-element.38), channel_id=1, source_target_pairs={{0,17},{1,24},{2,25},{3,0},{4,1},{5,8},{6,9},{7,16},{8,19},{9,26},... | collective-permute-start | bytes 86024 | tf_op jit(solution)/shard_map/ppermute | solution.py:234
  315.3 1.3 collective-permute-start.44
  317.6 1.7 collective-permute-start.47
  320.3 2.7 collective-permute-done.45
  323.7 1.3 collective-permute-done.47
  (220 shorter events, 47.1 us)
Async XLA Ops:
  0.0 298.7 %copy-start = (bf16[896,1280]{1,0:T(8,128)(2,1)S(1)}, bf16[896,1280]{1,0:T(8,128)(2,1)}, u32[]{:S(2)}) copy-start(bf16[896,1280]{1,0:T(8,128)(2,1)} %param.24) | copy-start | bytes 6881284
  0.0 27.8 %copy-start.25 = (s32[2,8]{1,0:T(2,128)S(1)}, s32[2,8]{1,0:T(2,128)}, u32[]{:S(2)}) copy-start(s32[2,8]{1,0:T(2,128)} %param.14) | copy-start | bytes 196
  0.0 28.4 %copy-start.20 = (f32[3584]{0:T(1024)S(1)}, f32[3584]{0:T(1024)}, u32[]{:S(2)}) copy-start(f32[3584]{0:T(1024)} %param.16) | copy-start | bytes 43012
  0.0 28.5 %copy-start.21 = (f32[3584]{0:T(1024)S(1)}, f32[3584]{0:T(1024)}, u32[]{:S(2)}) copy-start(f32[3584]{0:T(1024)} %param.21) | copy-start | bytes 43012
  4.3 26.2 %collective-permute-start.2 = (bf16[896,384]{1,0:T(8,128)(2,1)}, bf16[896,384]{1,0:T(8,128)(2,1)S(1)}, u32[]{:S(2)}, u32[]{:S(2)}) collective-permute-start(bf16[896,384]{1,0:T(8,128)(2,1)} %pad_maximum_fusion.9), channel_id=1, source_target_pairs={{0,16},{8,24},{16,0},{24,8},{1,17},{9,25},{17,1},{25,9},{2,18},{10... | collective-permute-start | bytes 2064392 | tf_op jit(solution)/shard_map/ppermute | solution.py:45
  8.5 48.5 %collective-permute-start.48 = (s32[16]{0:T(128)}, s32[16]{0:T(128)}, u32[]{:S(2)}, u32[]{:S(2)}) collective-permute-start(s32[16]{0:T(128)} %reshape.147), channel_id=1, source_target_pairs={{0,16},{8,24},{16,0},{24,8},{1,17},{9,25},{17,1},{25,9},{2,18},{10... | collective-permute-start | bytes 200 | tf_op jit(solution)/shard_map/ppermute | solution.py:45
  8.6 48.5 %collective-permute-start = (s32[16]{0:T(128)}, s32[16]{0:T(128)}, u32[]{:S(2)}, u32[]{:S(2)}) collective-permute-start(s32[16]{0:T(128)} %bitcast.185), channel_id=1, source_target_pairs={{0,16},{8,24},{16,0},{24,8},{1,17},{9,25},{17,1},{25,9},{2,18},{10... | collective-permute-start | bytes 200 | tf_op jit(solution)/shard_map/ppermute | solution.py:45
  30.7 6.3 %collective-permute-start.3 = (bf16[2,896,384]{2,1,0:T(8,128)(2,1)S(1)}, bf16[2,896,384]{2,1,0:T(8,128)(2,1)S(1)}, u32[]{:S(2)}, u32[]{:S(2)}) collective-permute-start(bf16[2,896,384]{2,1,0:T(8,128)(2,1)S(1)} %pad_maximum_fusion.7), channel_id=1, source_target_pairs={{0,8},{8,0},{16,24},{24,16},{1,9},{9,1},{17,25},{25,17},{2,10},{10... | collective-permute-start | bytes 4128776 | tf_op jit(solution)/shard_map/ppermute | solution.py:48
  48.0 21.3 %all-to-all-start = ((bf16[8,768,32]{1,2,0:T(8,128)(2,1)}), bf16[8,768,32]{1,2,0:T(8,128)(2,1)S(1)}, u32[]{:S(2)}, u32[]{:S(2)}) async-start(bf16[8,768,32]{1,2,0:T(8,128)(2,1)} %fusion.41), calls=%async_computation | async-start | bytes 786432 | tf_op jit(solution)/shard_map/all_to_all | solution.py:162
  54.5 12.7 %collective-permute-start.4 = (bf16[896,256]{1,0:T(8,128)(2,1)S(1)}, bf16[896,256]{1,0:T(8,128)(2,1)}, u32[]{:S(2)}, u32[]{:S(2)}) collective-permute-start(bf16[896,256]{1,0:T(8,128)(2,1)S(1)} %copy-done.17), channel_id=1, source_target_pairs={{0,16},{8,24},{16,0},{24,8},{1,17},{9,25},{17,1},{25,9},{2,18},{10... | collective-permute-start | bytes 1376264 | tf_op jit(solution)/shard_map/ppermute | solution.py:45
  58.3 1.1 collective-permute-start.1
  58.3 237.3 %collective-permute-start.49 = (s32[2,16]{1,0:T(2,128)}, s32[2,16]{1,0:T(2,128)}, u32[]{:S(2)}, u32[]{:S(2)}) collective-permute-start(s32[2,16]{1,0:T(2,128)} %get-tuple-element.64), channel_id=1, source_target_pairs={{0,8},{8,0},{16,24},{24,16},{1,9},{9,1},{17,25},{25,17},{2,10},{10... | collective-permute-start | bytes 392 | tf_op jit(solution)/shard_map/ppermute | solution.py:48
  69.3 6.7 %collective-permute-start.5 = (bf16[2,896,256]{2,1,0:T(8,128)(2,1)}, bf16[2,896,256]{2,1,0:T(8,128)(2,1)}, u32[]{:S(2)}, u32[]{:S(2)}) collective-permute-start(bf16[2,896,256]{2,1,0:T(8,128)(2,1)} %pad_maximum_fusion.8), channel_id=1, source_target_pairs={{0,8},{8,0},{16,24},{24,16},{1,9},{9,1},{17,25},{25,17},{2,10},{10... | collective-permute-start | bytes 2752520 | tf_op jit(solution)/shard_map/ppermute | solution.py:48
  83.3 10.7 %collective-permute-start.6 = (bf16[96,1792]{1,0:T(8,128)(2,1)}, bf16[96,1792]{1,0:T(8,128)(2,1)S(1)}, u32[]{:S(2)}, u32[]{:S(2)}) collective-permute-start(bf16[96,1792]{1,0:T(8,128)(2,1)} %constant_dynamic-slice_fusion.3), channel_id=1, source_target_pairs={{0,2},{2,4},{4,6},{6,7},{7,5},{5,3},{3,1},{1,0},{8,10},{10,12},{12... | collective-permute-start | bytes 1032200 | tf_op jit(solution)/shard_map/ppermute | solution.py:90
  85.4 22.3 %copy-start.10 = (bf16[768,1792]{1,0:T(8,128)(2,1)S(1)}, bf16[768,1792]{1,0:T(8,128)(2,1)}, u32[]{:S(2)}) copy-start(bf16[768,1792]{1,0:T(8,128)(2,1)} %get-tuple-element.24) | copy-start | bytes 8257540
  86.5 10.3 %collective-permute-start.20 = (bf16[96,1792]{1,0:T(8,128)(2,1)S(1)}, bf16[96,1792]{1,0:T(8,128)(2,1)S(1)}, u32[]{:S(2)}, u32[]{:S(2)}) collective-permute-start(bf16[96,1792]{1,0:T(8,128)(2,1)S(1)} %constant_dynamic-slice_fusion.2), channel_id=1, source_target_pairs={{0,1},{2,0},{4,2},{6,4},{7,6},{5,7},{3,5},{1,3},{8,9},{10,8},{12,1... | collective-permute-start | bytes 1032200 | tf_op jit(solution)/shard_map/ppermute | solution.py:90
  86.9 57.7 %collective-permute-start.36 = (bf16[896,1280]{1,0:T(8,128)(2,1)}, bf16[896,1280]{1,0:T(8,128)(2,1)S(1)}, u32[]{:S(2)}, u32[]{:S(2)}) collective-permute-start(bf16[896,1280]{1,0:T(8,128)(2,1)} %param.23), channel_id=1, source_target_pairs={{0,16},{8,24},{16,0},{24,8},{1,17},{9,25},{17,1},{25,9},{2,18},{10... | collective-permute-start | bytes 6881288 | tf_op jit(solution)/shard_map/ppermute | solution.py:45
  87.4 100.6 %collective-permute-start.34 = (bf16[896,1280]{1,0:T(8,128)(2,1)}, bf16[896,1280]{1,0:T(8,128)(2,1)S(1)}, u32[]{:S(2)}, u32[]{:S(2)}) collective-permute-start(bf16[896,1280]{1,0:T(8,128)(2,1)} %param.22), channel_id=1, source_target_pairs={{0,16},{8,24},{16,0},{24,8},{1,17},{9,25},{17,1},{25,9},{2,18},{10... | collective-permute-start | bytes 6881288 | tf_op jit(solution)/shard_map/ppermute | solution.py:45
  95.1 29.1 %copy-start.12 = (bf16[768,1792]{1,0:T(8,128)(2,1)S(1)}, bf16[768,1792]{1,0:T(8,128)(2,1)}, u32[]{:S(2)}) copy-start(bf16[768,1792]{1,0:T(8,128)(2,1)} %copy-done.11) | copy-start | bytes 8257540
  95.1 9.7 %collective-permute-start.7 = (bf16[96,1792]{1,0:T(8,128)(2,1)S(1)}, bf16[96,1792]{1,0:T(8,128)(2,1)S(1)}, u32[]{:S(2)}, u32[]{:S(2)}) collective-permute-start(bf16[96,1792]{1,0:T(8,128)(2,1)S(1)} %add_convert_fusion.13), channel_id=1, source_target_pairs={{0,2},{2,4},{4,6},{6,7},{7,5},{5,3},{3,1},{1,0},{8,10},{10,12},{12... | collective-permute-start | bytes 1032200 | tf_op jit(solution)/shard_map/ppermute | solution.py:90
  98.0 9.7 %collective-permute-start.21 = (bf16[96,1792]{1,0:T(8,128)(2,1)S(1)}, bf16[96,1792]{1,0:T(8,128)(2,1)S(1)}, u32[]{:S(2)}, u32[]{:S(2)}) collective-permute-start(bf16[96,1792]{1,0:T(8,128)(2,1)S(1)} %add_convert_fusion.6), channel_id=1, source_target_pairs={{0,1},{2,0},{4,2},{6,4},{7,6},{5,7},{3,5},{1,3},{8,9},{10,8},{12,1... | collective-permute-start | bytes 1032200 | tf_op jit(solution)/shard_map/ppermute | solution.py:90
  105.9 8.9 %collective-permute-start.8 = (bf16[96,1792]{1,0:T(8,128)(2,1)S(1)}, bf16[96,1792]{1,0:T(8,128)(2,1)S(1)}, u32[]{:S(2)}, u32[]{:S(2)}) collective-permute-start(bf16[96,1792]{1,0:T(8,128)(2,1)S(1)} %add_convert_fusion.12), channel_id=1, source_target_pairs={{0,2},{2,4},{4,6},{6,7},{7,5},{5,3},{3,1},{1,0},{8,10},{10,12},{12... | collective-permute-start | bytes 1032200 | tf_op jit(solution)/shard_map/ppermute | solution.py:90
  107.8 10.0 %collective-permute-start.22 = (bf16[96,1792]{1,0:T(8,128)(2,1)S(1)}, bf16[96,1792]{1,0:T(8,128)(2,1)S(1)}, u32[]{:S(2)}, u32[]{:S(2)}) collective-permute-start(bf16[96,1792]{1,0:T(8,128)(2,1)S(1)} %add_convert_fusion.5), channel_id=1, source_target_pairs={{0,1},{2,0},{4,2},{6,4},{7,6},{5,7},{3,5},{1,3},{8,9},{10,8},{12,1... | collective-permute-start | bytes 1032200 | tf_op jit(solution)/shard_map/ppermute | solution.py:90
  115.8 8.3 %collective-permute-start.9 = (bf16[96,1792]{1,0:T(8,128)(2,1)S(1)}, bf16[96,1792]{1,0:T(8,128)(2,1)S(1)}, u32[]{:S(2)}, u32[]{:S(2)}) collective-permute-start(bf16[96,1792]{1,0:T(8,128)(2,1)S(1)} %add_convert_fusion.11), channel_id=1, source_target_pairs={{0,2},{2,4},{4,6},{6,7},{7,5},{5,3},{3,1},{1,0},{8,10},{10,12},{12... | collective-permute-start | bytes 1032200 | tf_op jit(solution)/shard_map/ppermute | solution.py:90
  117.9 8.1 %collective-permute-start.23 = (bf16[96,1792]{1,0:T(8,128)(2,1)S(1)}, bf16[96,1792]{1,0:T(8,128)(2,1)S(1)}, u32[]{:S(2)}, u32[]{:S(2)}) collective-permute-start(bf16[96,1792]{1,0:T(8,128)(2,1)S(1)} %add_convert_fusion.4), channel_id=1, source_target_pairs={{0,1},{2,0},{4,2},{6,4},{7,6},{5,7},{3,5},{1,3},{8,9},{10,8},{12,1... | collective-permute-start | bytes 1032200 | tf_op jit(solution)/shard_map/ppermute | solution.py:90
  124.2 20.4 %copy-start.13 = (bf16[896,1280]{1,0:T(8,128)(2,1)S(1)}, bf16[896,1280]{1,0:T(8,128)(2,1)}, u32[]{:S(2)}) copy-start(bf16[896,1280]{1,0:T(8,128)(2,1)} %param.23) | copy-start | bytes 6881284
  124.2 8.3 %collective-permute-start.10 = (bf16[96,1792]{1,0:T(8,128)(2,1)S(1)}, bf16[96,1792]{1,0:T(8,128)(2,1)S(1)}, u32[]{:S(2)}, u32[]{:S(2)}) collective-permute-start(bf16[96,1792]{1,0:T(8,128)(2,1)S(1)} %add_convert_fusion.10), channel_id=1, source_target_pairs={{0,2},{2,4},{4,6},{6,7},{7,5},{5,3},{3,1},{1,0},{8,10},{10,12},{12... | collective-permute-start | bytes 1032200 | tf_op jit(solution)/shard_map/ppermute | solution.py:90
  126.1 8.6 %collective-permute-start.24 = (bf16[96,1792]{1,0:T(8,128)(2,1)S(1)}, bf16[96,1792]{1,0:T(8,128)(2,1)S(1)}, u32[]{:S(2)}, u32[]{:S(2)}) collective-permute-start(bf16[96,1792]{1,0:T(8,128)(2,1)S(1)} %add_convert_fusion.3), channel_id=1, source_target_pairs={{0,1},{2,0},{4,2},{6,4},{7,6},{5,7},{3,5},{1,3},{8,9},{10,8},{12,1... | collective-permute-start | bytes 1032200 | tf_op jit(solution)/shard_map/ppermute | solution.py:90
  132.6 9.1 %collective-permute-start.11 = (bf16[96,1792]{1,0:T(8,128)(2,1)S(1)}, bf16[96,1792]{1,0:T(8,128)(2,1)S(1)}, u32[]{:S(2)}, u32[]{:S(2)}) collective-permute-start(bf16[96,1792]{1,0:T(8,128)(2,1)S(1)} %add_convert_fusion.9), channel_id=1, source_target_pairs={{0,2},{2,4},{4,6},{6,7},{7,5},{5,3},{3,1},{1,0},{8,10},{10,12},{12... | collective-permute-start | bytes 1032200 | tf_op jit(solution)/shard_map/ppermute | solution.py:90
  134.8 9.4 %collective-permute-start.25 = (bf16[96,1792]{1,0:T(8,128)(2,1)S(1)}, bf16[96,1792]{1,0:T(8,128)(2,1)S(1)}, u32[]{:S(2)}, u32[]{:S(2)}) collective-permute-start(bf16[96,1792]{1,0:T(8,128)(2,1)S(1)} %add_convert_fusion.2), channel_id=1, source_target_pairs={{0,1},{2,0},{4,2},{6,4},{7,6},{5,7},{3,5},{1,3},{8,9},{10,8},{12,1... | collective-permute-start | bytes 1032200 | tf_op jit(solution)/shard_map/ppermute | solution.py:90
  141.8 7.3 %collective-permute-start.12 = (bf16[96,1792]{1,0:T(8,128)(2,1)S(1)}, bf16[96,1792]{1,0:T(8,128)(2,1)S(1)}, u32[]{:S(2)}, u32[]{:S(2)}) collective-permute-start(bf16[96,1792]{1,0:T(8,128)(2,1)S(1)} %add_convert_fusion.8), channel_id=1, source_target_pairs={{0,2},{2,4},{4,6},{6,7},{7,5},{5,3},{3,1},{1,0},{8,10},{10,12},{12... | collective-permute-start | bytes 1032200 | tf_op jit(solution)/shard_map/ppermute | solution.py:90
  144.2 7.3 %collective-permute-start.26 = (bf16[96,1792]{1,0:T(8,128)(2,1)S(1)}, bf16[96,1792]{1,0:T(8,128)(2,1)S(1)}, u32[]{:S(2)}, u32[]{:S(2)}) collective-permute-start(bf16[96,1792]{1,0:T(8,128)(2,1)S(1)} %add_convert_fusion.1), channel_id=1, source_target_pairs={{0,1},{2,0},{4,2},{6,4},{7,6},{5,7},{3,5},{1,3},{8,9},{10,8},{12,1... | collective-permute-start | bytes 1032200 | tf_op jit(solution)/shard_map/ppermute | solution.py:90
  147.4 100.6 %collective-permute-start.37 = (bf16[2,896,1280]{2,1,0:T(8,128)(2,1)}, bf16[2,896,1280]{2,1,0:T(8,128)(2,1)}, u32[]{:S(2)}, u32[]{:S(2)}) collective-permute-start(bf16[2,896,1280]{2,1,0:T(8,128)(2,1)} %pad_maximum_fusion.4), channel_id=1, source_target_pairs={{0,8},{8,0},{16,24},{24,16},{1,9},{9,1},{17,25},{25,17},{2,10},{10... | collective-permute-start | bytes 13762568 | tf_op jit(solution)/shard_map/ppermute | solution.py:48
  149.3 38.7 %copy-start.14 = (bf16[896,1280]{1,0:T(8,128)(2,1)S(1)}, bf16[896,1280]{1,0:T(8,128)(2,1)}, u32[]{:S(2)}) copy-start(bf16[896,1280]{1,0:T(8,128)(2,1)} %param.22) | copy-start | bytes 6881284
  149.4 41.2 %collective-permute-start.13 = (bf16[96,1792]{1,0:T(8,128)(2,1)S(1)}, bf16[96,1792]{1,0:T(8,128)(2,1)S(1)}, u32[]{:S(2)}, u32[]{:S(2)}) collective-permute-start(bf16[96,1792]{1,0:T(8,128)(2,1)S(1)} %get-tuple-element.20), channel_id=1, source_target_pairs={{0,2},{2,4},{4,6},{6,7},{7,5},{5,3},{3,1},{1,0},{8,10},{10,12},{12... | collective-permute-start | bytes 1032200 | tf_op jit(solution)/shard_map/ppermute | solution.py:96
  151.8 40.5 %collective-permute-start.27 = (bf16[96,1792]{1,0:T(8,128)(2,1)S(1)}, bf16[96,1792]{1,0:T(8,128)(2,1)S(1)}, u32[]{:S(2)}, u32[]{:S(2)}) collective-permute-start(bf16[96,1792]{1,0:T(8,128)(2,1)S(1)} %get-tuple-element.22), channel_id=1, source_target_pairs={{0,1},{2,0},{4,2},{6,4},{7,6},{5,7},{3,5},{1,3},{8,9},{10,8},{12,1... | collective-permute-start | bytes 1032200 | tf_op jit(solution)/shard_map/ppermute | solution.py:96
  190.6 77.9 %collective-permute-start.35 = (bf16[2,896,1280]{2,1,0:T(8,128)(2,1)}, bf16[2,896,1280]{2,1,0:T(8,128)(2,1)}, u32[]{:S(2)}, u32[]{:S(2)}) collective-permute-start(bf16[2,896,1280]{2,1,0:T(8,128)(2,1)} %pad_maximum_fusion.3), channel_id=1, source_target_pairs={{0,8},{8,0},{16,24},{24,16},{1,9},{9,1},{17,25},{25,17},{2,10},{10... | collective-permute-start | bytes 13762568 | tf_op jit(solution)/shard_map/ppermute | solution.py:48
  190.6 10.5 %collective-permute-start.14 = (bf16[96,1792]{1,0:T(8,128)(2,1)S(1)}, bf16[96,1792]{1,0:T(8,128)(2,1)S(1)}, u32[]{:S(2)}, u32[]{:S(2)}) collective-permute-start(bf16[96,1792]{1,0:T(8,128)(2,1)S(1)} %collective-permute-done.13), channel_id=1, source_target_pairs={{0,2},{2,4},{4,6},{6,7},{7,5},{5,3},{3,1},{1,0},{8,10},{10,12},{12... | collective-permute-start | bytes 1032200 | tf_op jit(solution)/shard_map/ppermute | solution.py:96
  192.3 10.5 %collective-permute-start.28 = (bf16[96,1792]{1,0:T(8,128)(2,1)S(1)}, bf16[96,1792]{1,0:T(8,128)(2,1)S(1)}, u32[]{:S(2)}, u32[]{:S(2)}) collective-permute-start(bf16[96,1792]{1,0:T(8,128)(2,1)S(1)} %collective-permute-done.27), channel_id=1, source_target_pairs={{0,1},{2,0},{4,2},{6,4},{7,6},{5,7},{3,5},{1,3},{8,9},{10,8},{12,1... | collective-permute-start | bytes 1032200 | tf_op jit(solution)/shard_map/ppermute | solution.py:96
  201.1 9.7 %collective-permute-start.15 = (bf16[96,1792]{1,0:T(8,128)(2,1)S(1)}, bf16[96,1792]{1,0:T(8,128)(2,1)S(1)}, u32[]{:S(2)}, u32[]{:S(2)}) collective-permute-start(bf16[96,1792]{1,0:T(8,128)(2,1)S(1)} %collective-permute-done.14), channel_id=1, source_target_pairs={{0,2},{2,4},{4,6},{6,7},{7,5},{5,3},{3,1},{1,0},{8,10},{10,12},{12... | collective-permute-start | bytes 1032200 | tf_op jit(solution)/shard_map/ppermute | solution.py:96
  202.8 9.7 %collective-permute-start.29 = (bf16[96,1792]{1,0:T(8,128)(2,1)S(1)}, bf16[96,1792]{1,0:T(8,128)(2,1)S(1)}, u32[]{:S(2)}, u32[]{:S(2)}) collective-permute-start(bf16[96,1792]{1,0:T(8,128)(2,1)S(1)} %collective-permute-done.28), channel_id=1, source_target_pairs={{0,1},{2,0},{4,2},{6,4},{7,6},{5,7},{3,5},{1,3},{8,9},{10,8},{12,1... | collective-permute-start | bytes 1032200 | tf_op jit(solution)/shard_map/ppermute | solution.py:96
  210.8 8.8 %collective-permute-start.16 = (bf16[96,1792]{1,0:T(8,128)(2,1)S(1)}, bf16[96,1792]{1,0:T(8,128)(2,1)S(1)}, u32[]{:S(2)}, u32[]{:S(2)}) collective-permute-start(bf16[96,1792]{1,0:T(8,128)(2,1)S(1)} %collective-permute-done.15), channel_id=1, source_target_pairs={{0,2},{2,4},{4,6},{6,7},{7,5},{5,3},{3,1},{1,0},{8,10},{10,12},{12... | collective-permute-start | bytes 1032200 | tf_op jit(solution)/shard_map/ppermute | solution.py:96
  212.5 8.8 %collective-permute-start.30 = (bf16[96,1792]{1,0:T(8,128)(2,1)S(1)}, bf16[96,1792]{1,0:T(8,128)(2,1)S(1)}, u32[]{:S(2)}, u32[]{:S(2)}) collective-permute-start(bf16[96,1792]{1,0:T(8,128)(2,1)S(1)} %collective-permute-done.29), channel_id=1, source_target_pairs={{0,1},{2,0},{4,2},{6,4},{7,6},{5,7},{3,5},{1,3},{8,9},{10,8},{12,1... | collective-permute-start | bytes 1032200 | tf_op jit(solution)/shard_map/ppermute | solution.py:96
  212.9 32.6 %copy-start.3 = (bf16[768,896]{1,0:T(8,128)(2,1)S(1)}, bf16[768,896]{1,0:T(8,128)(2,1)}, u32[]{:S(2)}) copy-start(bf16[768,896]{1,0:T(8,128)(2,1)} %copy-done.2) | copy-start | bytes 4128772
  212.9 32.6 %copy-start.5 = (bf16[768,896]{1,0:T(8,128)(2,1)S(1)}, bf16[768,896]{1,0:T(8,128)(2,1)}, u32[]{:S(2)}) copy-start(bf16[768,896]{1,0:T(8,128)(2,1)} %copy-done.4) | copy-start | bytes 4128772
  212.9 32.6 %copy-start.7 = (bf16[768,896]{1,0:T(8,128)(2,1)S(1)}, bf16[768,896]{1,0:T(8,128)(2,1)}, u32[]{:S(2)}) copy-start(bf16[768,896]{1,0:T(8,128)(2,1)} %copy-done.6) | copy-start | bytes 4128772
  212.9 32.6 %copy-start.9 = (bf16[768,896]{1,0:T(8,128)(2,1)S(1)}, bf16[768,896]{1,0:T(8,128)(2,1)}, u32[]{:S(2)}) copy-start(bf16[768,896]{1,0:T(8,128)(2,1)} %copy-done.8) | copy-start | bytes 4128772
  219.6 8.2 %collective-permute-start.17 = (bf16[96,1792]{1,0:T(8,128)(2,1)S(1)}, bf16[96,1792]{1,0:T(8,128)(2,1)S(1)}, u32[]{:S(2)}, u32[]{:S(2)}) collective-permute-start(bf16[96,1792]{1,0:T(8,128)(2,1)S(1)} %collective-permute-done.16), channel_id=1, source_target_pairs={{0,2},{2,4},{4,6},{6,7},{7,5},{5,3},{3,1},{1,0},{8,10},{10,12},{12... | collective-permute-start | bytes 1032200 | tf_op jit(solution)/shard_map/ppermute | solution.py:96
  221.3 8.2 %collective-permute-start.31 = (bf16[96,1792]{1,0:T(8,128)(2,1)S(1)}, bf16[96,1792]{1,0:T(8,128)(2,1)S(1)}, u32[]{:S(2)}, u32[]{:S(2)}) collective-permute-start(bf16[96,1792]{1,0:T(8,128)(2,1)S(1)} %collective-permute-done.30), channel_id=1, source_target_pairs={{0,1},{2,0},{4,2},{6,4},{7,6},{5,7},{3,5},{1,3},{8,9},{10,8},{12,1... | collective-permute-start | bytes 1032200 | tf_op jit(solution)/shard_map/ppermute | solution.py:96
  227.8 8.7 %collective-permute-start.18 = (bf16[96,1792]{1,0:T(8,128)(2,1)S(1)}, bf16[96,1792]{1,0:T(8,128)(2,1)S(1)}, u32[]{:S(2)}, u32[]{:S(2)}) collective-permute-start(bf16[96,1792]{1,0:T(8,128)(2,1)S(1)} %collective-permute-done.17), channel_id=1, source_target_pairs={{0,2},{2,4},{4,6},{6,7},{7,5},{5,3},{3,1},{1,0},{8,10},{10,12},{12... | collective-permute-start | bytes 1032200 | tf_op jit(solution)/shard_map/ppermute | solution.py:96
  229.5 8.7 %collective-permute-start.32 = (bf16[96,1792]{1,0:T(8,128)(2,1)S(1)}, bf16[96,1792]{1,0:T(8,128)(2,1)S(1)}, u32[]{:S(2)}, u32[]{:S(2)}) collective-permute-start(bf16[96,1792]{1,0:T(8,128)(2,1)S(1)} %collective-permute-done.31), channel_id=1, source_target_pairs={{0,1},{2,0},{4,2},{6,4},{7,6},{5,7},{3,5},{1,3},{8,9},{10,8},{12,1... | collective-permute-start | bytes 1032200 | tf_op jit(solution)/shard_map/ppermute | solution.py:96
  236.5 7.2 %collective-permute-start.19 = (bf16[96,1792]{1,0:T(8,128)(2,1)S(1)}, bf16[96,1792]{1,0:T(8,128)(2,1)S(1)}, u32[]{:S(2)}, u32[]{:S(2)}) collective-permute-start(bf16[96,1792]{1,0:T(8,128)(2,1)S(1)} %collective-permute-done.18), channel_id=1, source_target_pairs={{0,2},{2,4},{4,6},{6,7},{7,5},{5,3},{3,1},{1,0},{8,10},{10,12},{12... | collective-permute-start | bytes 1032200 | tf_op jit(solution)/shard_map/ppermute | solution.py:96
  238.2 7.3 %collective-permute-start.33 = (bf16[96,1792]{1,0:T(8,128)(2,1)S(1)}, bf16[96,1792]{1,0:T(8,128)(2,1)S(1)}, u32[]{:S(2)}, u32[]{:S(2)}) collective-permute-start(bf16[96,1792]{1,0:T(8,128)(2,1)S(1)} %collective-permute-done.32), channel_id=1, source_target_pairs={{0,1},{2,0},{4,2},{6,4},{7,6},{5,7},{3,5},{1,3},{8,9},{10,8},{12,1... | collective-permute-start | bytes 1032200 | tf_op jit(solution)/shard_map/ppermute | solution.py:96
  291.0 4.4 %collective-permute-start.38 = (f32[16,1280]{1,0:T(8,128)S(1)}, f32[16,1280]{1,0:T(8,128)S(1)}, u32[]{:S(2)}, u32[]{:S(2)}) collective-permute-start(f32[16,1280]{1,0:T(8,128)S(1)} %fusion.9), channel_id=1, source_target_pairs={{0,16},{8,24},{16,0},{24,8},{1,17},{9,25},{17,1},{25,9},{2,18},{10... | collective-permute-start | bytes 245768 | tf_op jit(solution)/shard_map/ppermute | solution.py:45
  295.5 3.2 collective-permute-start.39
  301.3 15.3 %collective-permute-start.40 = (f32[16,448]{1,0:T(8,128)S(1)}, f32[16,448]{1,0:T(8,128)S(1)}, u32[]{:S(2)}, u32[]{:S(2)}) collective-permute-start(f32[16,448]{1,0:T(8,128)S(1)} %get-tuple-element.40), channel_id=1, source_target_pairs={{0,0},{1,1},{2,8},{3,9},{4,16},{5,17},{6,24},{7,25},{8,2},{9,3},{1... | collective-permute-start | bytes 86024 | tf_op jit(solution)/shard_map/ppermute | solution.py:234
  302.0 15.4 %collective-permute-start.41 = (f32[16,448]{1,0:T(8,128)S(1)}, f32[16,448]{1,0:T(8,128)S(1)}, u32[]{:S(2)}, u32[]{:S(2)}) collective-permute-start(f32[16,448]{1,0:T(8,128)S(1)} %get-tuple-element.33), channel_id=1, source_target_pairs={{0,25},{1,0},{2,1},{3,8},{4,9},{5,16},{6,17},{7,24},{8,27},{9,2},{... | collective-permute-start | bytes 86024 | tf_op jit(solution)/shard_map/ppermute | solution.py:234
  307.6 10.0 %collective-permute-start.42 = (f32[16,448]{1,0:T(8,128)S(1)}, f32[16,448]{1,0:T(8,128)S(1)}, u32[]{:S(2)}, u32[]{:S(2)}) collective-permute-start(f32[16,448]{1,0:T(8,128)S(1)} %get-tuple-element.39), channel_id=1, source_target_pairs={{0,24},{1,25},{2,0},{3,1},{4,8},{5,9},{6,16},{7,17},{8,26},{9,27},... | collective-permute-start | bytes 86024 | tf_op jit(solution)/shard_map/ppermute | solution.py:234
  308.6 10.9 %all-to-all-start.1 = ((f32[4,4,448]{2,1,0:T(4,128)}), f32[4,4,448]{2,1,0:T(4,128)S(1)}, u32[]{:S(2)}, u32[]{:S(2)}) async-start(f32[4,4,448]{2,1,0:T(4,128)} %fusion.51), calls=%async_computation.1 | async-start | bytes 65536 | tf_op jit(solution)/shard_map/all_to_all | solution.py:238
  311.8 7.6 %collective-permute-start.43 = (f32[16,448]{1,0:T(8,128)S(1)}, f32[16,448]{1,0:T(8,128)S(1)}, u32[]{:S(2)}, u32[]{:S(2)}) collective-permute-start(f32[16,448]{1,0:T(8,128)S(1)} %get-tuple-element.38), channel_id=1, source_target_pairs={{0,17},{1,24},{2,25},{3,0},{4,1},{5,8},{6,9},{7,16},{8,19},{9,26},... | collective-permute-start | bytes 86024 | tf_op jit(solution)/shard_map/ppermute | solution.py:234
  315.3 5.0 %collective-permute-start.44 = (f32[16,448]{1,0:T(8,128)S(1)}, f32[16,448]{1,0:T(8,128)S(1)}, u32[]{:S(2)}, u32[]{:S(2)}) collective-permute-start(f32[16,448]{1,0:T(8,128)S(1)} %get-tuple-element.37), channel_id=1, source_target_pairs={{0,16},{1,17},{2,24},{3,25},{4,0},{5,1},{6,8},{7,9},{8,18},{9,19},... | collective-permute-start | bytes 86024 | tf_op jit(solution)/shard_map/ppermute | solution.py:234
  316.6 6.3 %collective-permute-start.45 = (f32[16,448]{1,0:T(8,128)S(1)}, f32[16,448]{1,0:T(8,128)S(1)}, u32[]{:S(2)}, u32[]{:S(2)}) collective-permute-start(f32[16,448]{1,0:T(8,128)S(1)} %get-tuple-element.36), channel_id=1, source_target_pairs={{0,9},{1,16},{2,17},{3,24},{4,25},{5,0},{6,1},{7,8},{8,11},{9,18},... | collective-permute-start | bytes 86024 | tf_op jit(solution)/shard_map/ppermute | solution.py:234
  317.4 6.3 %collective-permute-start.46 = (f32[16,448]{1,0:T(8,128)S(1)}, f32[16,448]{1,0:T(8,128)S(1)}, u32[]{:S(2)}, u32[]{:S(2)}) collective-permute-start(f32[16,448]{1,0:T(8,128)S(1)} %get-tuple-element.35), channel_id=1, source_target_pairs={{0,8},{1,9},{2,16},{3,17},{4,24},{5,25},{6,0},{7,1},{8,10},{9,11},... | collective-permute-start | bytes 86024 | tf_op jit(solution)/shard_map/ppermute | solution.py:234
  317.6 7.3 %collective-permute-start.47 = (f32[16,448]{1,0:T(8,128)S(1)}, f32[16,448]{1,0:T(8,128)S(1)}, u32[]{:S(2)}, u32[]{:S(2)}) collective-permute-start(f32[16,448]{1,0:T(8,128)S(1)} %get-tuple-element.34), channel_id=1, source_target_pairs={{0,1},{1,8},{2,9},{3,16},{4,17},{5,24},{6,25},{7,0},{8,3},{9,10},{... | collective-permute-start | bytes 86024 | tf_op jit(solution)/shard_map/ppermute | solution.py:234
  (16 other events, 114.6 us)

commit v6 on v5

--- a/solution.py
+++ b/solution.py
@@ -36,7 +36,7 @@
     )
 
 
-def gather_grp(piece, chips):
+def gather_chips(piece, chips):
     held = [piece]
     moving = piece
     if chips > 1:
@@ -44,9 +44,16 @@
         for _ in range(chips - 1):
             moving = lax.ppermute(moving, "grp", ring)
             held.append(moving)
-    mine = jnp.stack(held)
+    return jnp.stack(held)
+
+
+def gather_cores(mine, chips):
     other = lax.ppermute(mine, "grp", [(g, g ^ 1) for g in range(2 * chips)])
     return jnp.concatenate([mine, other], 0)
+
+
+def gather_grp(piece, chips):
+    return gather_cores(gather_chips(piece, chips), chips)
 
 
 def source_order(chips):
@@ -70,7 +77,7 @@
     return list(range(0, n, 2)) + list(range(n - 1, 0, -2))
 
 
-def ring_psum(x, axis, n):
+def ring_psum(x, axis, n, ride):
     walk = ring_walk(n)
     place = [0] * n
     for p, t in enumerate(walk):
@@ -94,10 +101,12 @@
         for step in range(n):
             if step:
                 moving = lax.ppermute(moving, axis, pairs)
+            if step == min(2, n - 1) and sign == 1:
+                moving, ride = lax.optimization_barrier((moving, ride))
             where = ((pos + sign - sign * step) % n) * size
             out = lax.dynamic_update_slice_in_dim(out, moving, where, 0)
         parts.append(out)
-    return jnp.concatenate(parts, 1)
+    return jnp.concatenate(parts, 1), ride
 
 
 def on_device(
@@ -136,8 +145,8 @@
     o_after, qkv_full = lax.optimization_barrier((o_weight, qkv_full))
     o_full = gather_grp(o_after, chips).reshape(width, -1)
     gate_after, up_after, o_full = lax.optimization_barrier((gate_weight, up_weight, o_full))
-    gate_full = gather_grp(gate_after, chips).reshape(width, -1)
-    up_full = gather_grp(up_after, chips).reshape(width, -1)
+    gate_chips = gather_chips(gate_after, chips)
+    up_chips = gather_chips(up_after, chips)
 
     hidden_perm = take_blocks(hidden_in, order, d_grp, 1)
     attn_gain_perm = take_blocks(attn_gain, order, d_grp, 0)
@@ -181,7 +190,10 @@
     )
     attended_rows = attended_rows.astype(jnp.bfloat16).reshape(row_count, local_heads * HEAD_SIZE)
     attn_term = transposed_dot(attended_rows, o_full).astype(jnp.bfloat16)
-    attn_total = ring_psum(attn_term, "tp", tp_size).astype(jnp.float32)
+    attn_total, (gate_chips, up_chips) = ring_psum(attn_term, "tp", tp_size, (gate_chips, up_chips))
+    attn_total = attn_total.astype(jnp.float32)
+    gate_full = gather_cores(gate_chips, chips).reshape(width, -1)
+    up_full = gather_cores(up_chips, chips).reshape(width, -1)
     residual = hidden_perm.astype(jnp.float32) + attn_total
     norm_mid = rms_scale(residual, ffn_gain_perm)
     gate_pre = jnp.dot(norm_mid, gate_full, preferred_element_type=jnp.float32)

time: 328 us -> 334 us (1.018)
  local copies, waits for them, and re-layouts: 21.1 us -> 34.6 us
  waiting for transfers between devices: 131 us -> 118 us
  other arithmetic: 51 us -> 55.5 us
    dynamic_update_slice x14, local copies, waits for them, and re-layouts: 0.38 us -> 10.7 us  [ring_psum(): out = lax.dynamic_update_slice_in_dim(out, moving, where, 0)]
    ppermute x14, waiting for transfers between devices: 44.5 us -> 34.3 us  [the longest x7 34.3 us: gather_chips(): moving = lax.ppermute(moving, 'grp', ring)]
    ppermute x8, waiting for transfers between devices: 5.49 us -> 1.42 us  [on_device(): totals = totals + lax.ppermute(piece, ('grp', 'tp'), pairs)]
  transfers between devices with their start and end apart: 52 -> 52, of which waited for: 25 -> 25; matrix products, arithmetic and copies ran while one was open for 33% -> 37% of each run, Pallas kernels for 0% -> 0%
where the time goes in v6:
time: 334 us; the launch traced here: 330 us
  waiting for transfers between devices  118 us (35%)
  starting transfers between devices  64.1 us (19%)
  other arithmetic  55.5 us (17%)
  matrix products  42.4 us (13%)
  local copies, waits for them, and re-layouts  34.6 us (10%)
  between operations  15.1 us (5%)
    ppermute x14, waiting for transfers between devices, ring_psum(): got = lax.ppermute(acc, axis, pairs)  42.8 us
    ppermute x14, waiting for transfers between devices, ring_psum(): moving = lax.ppermute(moving, axis, pairs)  39.9 us
    ppermute x7, waiting for transfers between devices, gather_chips(): moving = lax.ppermute(moving, 'grp', ring)  34.3 us
    concatenate x6, other arithmetic, gather_cores(): return jnp.concatenate([mine, other], 0)  19.4 us
    ppermute x8, starting transfers between devices, on_device(): totals = totals + lax.ppermute(piece, ('grp', 'tp'), pairs)  15.6 us
    dot_general x1, matrix products, on_device(): jnp.dot(selector.astype(jnp.bfloat16), hidden_ffn, preferred_element_type...  15.5 us
    ppermute x14, starting transfers between devices, ring_psum(): got = lax.ppermute(acc, axis, pairs)  15.3 us
    ppermute x14, starting transfers between devices, ring_psum(): moving = lax.ppermute(moving, axis, pairs)  14.1 us
  transfers between devices with their start and end apart: 52, of which 25 were waited for; matrix products, arithmetic and copies ran while one was open for 37% of the time, Pallas kernels for 0%

profile of v6, /device:TPU:0, one launch (start us, length us, event | category | flops | bytes accessed | tf_op | source)
XLA Modules:
  0.0 330.1 jit_solution(11976581162028839876)
XLA Ops:
  2.3 2.0 pad_maximum_fusion.9
  4.3 2.9 collective-permute-start.2
  8.7 2.0 collective-permute-start.48
  31.1 2.4 pad_maximum_fusion.7
  34.4 3.1 constant_dynamic-slice_fusion.7
  38.9 2.3 pad_maximum_fusion.5
  41.2 4.3 %fusion.12 = bf16[768,384]{0,1:T(8,128)(2,1)S(1)} fusion(bf16[3584,384]{1,0:T(8,128)(2,1)S(1)} %bitcast.149, f32[3584]{0:T(1024)S(1)} %pad_maximum_fusion.12, f32[768]{0:T(1024)S(1)} %add_rsqrt_fusion.1, bf16[768,896]{1,0:T(8,128)(2,1)S(1)} %get-tuple-element.33, bf16[768,896]{1,0:T(8,128)(2,1)S(1)} %get-tuple-element.34, ...), kind=kOutput, calls=%fused_computation.29 | convolution fusion | flops 2144501760 | bytes 8864768 | tf_op jit(solution)/shard_map/dot_general | solution.py:156
  51.8 5.8 %all-to-all-start = ((bf16[8,768,32]{1,2,0:T(8,128)(2,1)}), bf16[8,768,32]{1,2,0:T(8,128)(2,1)S(1)}, u32[]{:S(2)}, u32[]{:S(2)}) async-start(bf16[8,768,32]{1,2,0:T(8,128)(2,1)} %fusion.41), calls=%async_computation | async-start | bytes 786432 | tf_op jit(solution)/shard_map/all_to_all | solution.py:171
  64.5 7.4 %collective-permute-done.4 = bf16[896,256]{1,0:T(8,128)(2,1)} collective-permute-done((bf16[896,256]{1,0:T(8,128)(2,1)S(1)}, bf16[896,256]{1,0:T(8,128)(2,1)}, u32[]{:S(2)}, u32[]{:S(2)}) %collective-permute-start.4) | collective-permute-done | bytes 458784 | tf_op jit(solution)/shard_map/ppermute | solution.py:45
  71.9 2.0 pad_maximum_fusion.8
  74.1 4.1 %fusion.73 = (f32[2,2,384]{2,1,0:T(2,128)}, f32[2,2,384,384]{2,3,1,0:T(8,128)}) fusion(pred[2,384,384]{1,2,0:T(8,128)(4,1)} %broadcast_compare_fusion, bf16[2,384,2,128]{1,0,3,2:T(2,128)(2,1)} %reshape.140, bf16[2,384,128,1]{1,0,2,3:T(2,128)(2,1)S(1)} %bitcast.178), kind=kOutput, calls=%fused_computation.169 | convolution fusion | flops 153354624 | bytes 3250176 | tf_op jit(solution)/shard_map/sub | solution.py:29
  78.2 2.0 fusion.15
  82.1 1.6 convolution_convert_fusion
  83.8 1.9 fusion.65
  87.2 1.8 collective-permute-start.22
  93.2 4.5 %collective-permute-done.22 = bf16[96,1792]{1,0:T(8,128)(2,1)S(1)} collective-permute-done((bf16[96,1792]{1,0:T(8,128)(2,1)S(1)}, bf16[96,1792]{1,0:T(8,128)(2,1)S(1)}, u32[]{:S(2)}, u32[]{:S(2)}) %collective-permute-start.22) | collective-permute-done | bytes 344096 | tf_op jit(solution)/shard_map/ppermute | solution.py:97
  98.8 1.8 collective-permute-start.23
  102.6 6.0 %collective-permute-done.23 = bf16[96,1792]{1,0:T(8,128)(2,1)S(1)} collective-permute-done((bf16[96,1792]{1,0:T(8,128)(2,1)S(1)}, bf16[96,1792]{1,0:T(8,128)(2,1)S(1)}, u32[]{:S(2)}, u32[]{:S(2)}) %collective-permute-start.23) | collective-permute-done | bytes 344096 | tf_op jit(solution)/shard_map/ppermute | solution.py:97
  108.7 1.8 collective-permute-start.24
  113.1 4.4 %collective-permute-done.24 = bf16[96,1792]{1,0:T(8,128)(2,1)S(1)} collective-permute-done((bf16[96,1792]{1,0:T(8,128)(2,1)S(1)}, bf16[96,1792]{1,0:T(8,128)(2,1)S(1)}, u32[]{:S(2)}, u32[]{:S(2)}) %collective-permute-start.24) | collective-permute-done | bytes 344096 | tf_op jit(solution)/shard_map/ppermute | solution.py:97
  117.6 1.8 collective-permute-start.25
  119.4 1.8 collective-permute-done.8
  121.9 3.9 %collective-permute-done.25 = bf16[96,1792]{1,0:T(8,128)(2,1)S(1)} collective-permute-done((bf16[96,1792]{1,0:T(8,128)(2,1)S(1)}, bf16[96,1792]{1,0:T(8,128)(2,1)S(1)}, u32[]{:S(2)}, u32[]{:S(2)}) %collective-permute-start.25) | collective-permute-done | bytes 344096 | tf_op jit(solution)/shard_map/ppermute | solution.py:97
  125.8 1.8 collective-permute-start.26
  127.6 2.0 collective-permute-done.9
  130.1 4.0 %collective-permute-done.26 = bf16[96,1792]{1,0:T(8,128)(2,1)S(1)} collective-permute-done((bf16[96,1792]{1,0:T(8,128)(2,1)S(1)}, bf16[96,1792]{1,0:T(8,128)(2,1)S(1)}, u32[]{:S(2)}, u32[]{:S(2)}) %collective-permute-start.26) | collective-permute-done | bytes 344096 | tf_op jit(solution)/shard_map/ppermute | solution.py:97
  134.2 1.8 collective-permute-start.27
  136.0 2.3 collective-permute-done.10
  138.8 4.5 %collective-permute-done.27 = bf16[96,1792]{1,0:T(8,128)(2,1)S(1)} collective-permute-done((bf16[96,1792]{1,0:T(8,128)(2,1)S(1)}, bf16[96,1792]{1,0:T(8,128)(2,1)S(1)}, u32[]{:S(2)}, u32[]{:S(2)}) %collective-permute-start.27) | collective-permute-done | bytes 344096 | tf_op jit(solution)/shard_map/ppermute | solution.py:97
  143.4 1.8 collective-permute-start.28
  145.2 2.7 collective-permute-done.11
  148.3 2.5 pad_maximum_fusion.3
  150.8 5.0 %collective-permute-done.12 = bf16[96,1792]{1,0:T(8,128)(2,1)S(1)} collective-permute-done((bf16[96,1792]{1,0:T(8,128)(2,1)S(1)}, bf16[96,1792]{1,0:T(8,128)(2,1)S(1)}, u32[]{:S(2)}, u32[]{:S(2)}) %collective-permute-start.12) | collective-permute-done | bytes 344096 | tf_op jit(solution)/shard_map/ppermute | solution.py:97
  155.7 1.7 broadcast.177.clone.1
  158.6 1.7 broadcast.177.clone
  161.3 1.7 collective-permute-start.29
  163.0 6.0 %collective-permute-done.13 = bf16[96,1792]{1,0:T(8,128)(2,1)S(1)} collective-permute-done((bf16[96,1792]{1,0:T(8,128)(2,1)S(1)}, bf16[96,1792]{1,0:T(8,128)(2,1)S(1)}, u32[]{:S(2)}, u32[]{:S(2)}) %collective-permute-start.13) | collective-permute-done | bytes 344096 | tf_op jit(solution)/shard_map/ppermute | solution.py:103
  169.3 23.0 %collective-permute-done.16 = bf16[896,1280]{1,0:T(8,128)(2,1)S(1)} collective-permute-done((bf16[896,1280]{1,0:T(8,128)(2,1)}, bf16[896,1280]{1,0:T(8,128)(2,1)S(1)}, u32[]{:S(2)}, u32[]{:S(2)}) %collective-permute-start.16) | collective-permute-done | bytes 2293792 | tf_op jit(solution)/shard_map/ppermute | solution.py:45
  192.4 2.5 pad_maximum_fusion.4
  195.3 1.7 collective-permute-start.30
  198.9 6.9 %collective-permute-done.30 = bf16[96,1792]{1,0:T(8,128)(2,1)S(1)} collective-permute-done((bf16[96,1792]{1,0:T(8,128)(2,1)S(1)}, bf16[96,1792]{1,0:T(8,128)(2,1)S(1)}, u32[]{:S(2)}, u32[]{:S(2)}) %collective-permute-start.30) | collective-permute-done | bytes 344096 | tf_op jit(solution)/shard_map/ppermute | solution.py:103
  205.8 1.7 collective-permute-start.31
  209.0 6.5 %collective-permute-done.31 = bf16[96,1792]{1,0:T(8,128)(2,1)S(1)} collective-permute-done((bf16[96,1792]{1,0:T(8,128)(2,1)S(1)}, bf16[96,1792]{1,0:T(8,128)(2,1)S(1)}, u32[]{:S(2)}, u32[]{:S(2)}) %collective-permute-start.31) | collective-permute-done | bytes 344096 | tf_op jit(solution)/shard_map/ppermute | solution.py:103
  215.5 1.7 collective-permute-start.32
  219.1 5.2 %collective-permute-done.32 = bf16[96,1792]{1,0:T(8,128)(2,1)S(1)} collective-permute-done((bf16[96,1792]{1,0:T(8,128)(2,1)S(1)}, bf16[96,1792]{1,0:T(8,128)(2,1)S(1)}, u32[]{:S(2)}, u32[]{:S(2)}) %collective-permute-start.32) | collective-permute-done | bytes 344096 | tf_op jit(solution)/shard_map/ppermute | solution.py:103
  224.3 1.7 collective-permute-start.33
  227.9 4.7 %collective-permute-done.33 = bf16[96,1792]{1,0:T(8,128)(2,1)S(1)} collective-permute-done((bf16[96,1792]{1,0:T(8,128)(2,1)S(1)}, bf16[96,1792]{1,0:T(8,128)(2,1)S(1)}, u32[]{:S(2)}, u32[]{:S(2)}) %collective-permute-start.33) | collective-permute-done | bytes 344096 | tf_op jit(solution)/shard_map/ppermute | solution.py:103
  232.5 1.7 collective-permute-start.34
  236.1 5.1 %collective-permute-done.34 = bf16[96,1792]{1,0:T(8,128)(2,1)S(1)} collective-permute-done((bf16[96,1792]{1,0:T(8,128)(2,1)S(1)}, bf16[96,1792]{1,0:T(8,128)(2,1)S(1)}, u32[]{:S(2)}, u32[]{:S(2)}) %collective-permute-start.34) | collective-permute-done | bytes 344096 | tf_op jit(solution)/shard_map/ppermute | solution.py:103
  241.2 1.7 collective-permute-start.35
  244.8 3.7 %collective-permute-done.35 = bf16[96,1792]{1,0:T(8,128)(2,1)S(1)} collective-permute-done((bf16[96,1792]{1,0:T(8,128)(2,1)S(1)}, bf16[96,1792]{1,0:T(8,128)(2,1)S(1)}, u32[]{:S(2)}, u32[]{:S(2)}) %collective-permute-start.35) | collective-permute-done | bytes 344096 | tf_op jit(solution)/shard_map/ppermute | solution.py:103
  249.2 1.7 collective-permute-done.21
  251.7 5.1 %multiply_reduce_fusion = (f32[768]{0:T(1024)S(1)}, f32[768,3584]{1,0:T(8,128)S(1)}) fusion(bf16[768,1792]{1,0:T(8,128)(2,1)} %constant_dynamic-update-slice_fusion, bf16[768,1792]{1,0:T(8,128)(2,1)} %constant_dynamic-update-slice_fusion.8, bf16[768,896]{1,0:T(8,128)(2,1)S(1)} %copy-done.7, bf16[768,896]{1,0:T(8,128)(2,1)S(1)} %copy-done.9, ...), kind=kLoop, calls=%fused_computation.8 | loop fusion | flops 41286912 | bytes 22023168 | tf_op jit(solution)/shard_map/reduce_sum | solution.py:17
  256.8 8.1 %pad_maximum_fusion.1 = bf16[4,896,1280]{2,1,0:T(8,128)(2,1)S(1)} fusion(bf16[2,896,1280]{2,1,0:T(8,128)(2,1)} %collective-permute-done.37, bf16[2,896,1280]{2,1,0:T(8,128)(2,1)} %pad_maximum_fusion.4), kind=kLoop, calls=%fused_computation.10 | loop fusion | flops 4587520 | bytes 18350080 | tf_op jit(solution)/shard_map/concatenate | solution.py:52
  265.0 9.2 %fusion.63 = f32[768,1280]{1,0:T(8,128)} fusion(bf16[3584,1280]{1,0:T(8,128)(2,1)S(1)} %bitcast.147, f32[768,3584]{1,0:T(8,128)S(1)} %get-tuple-element.24, f32[3584]{0:T(1024)S(1)} %copy-done.18, f32[768]{0:T(1024)S(1)} %add_rsqrt_fusion), kind=kOutput, calls=%fused_computation.159 | convolution fusion | flops 7054688256 | bytes 24134656 | tf_op jit(solution)/shard_map/dot_general | solution.py:200
  274.2 6.9 %pad_maximum_fusion = bf16[4,896,1280]{2,1,0:T(8,128)(2,1)} fusion(bf16[2,896,1280]{2,1,0:T(8,128)(2,1)} %collective-permute-done.36, bf16[2,896,1280]{2,1,0:T(8,128)(2,1)S(1)} %bitcast.145), kind=kLoop, calls=%fused_computation.9 | loop fusion | flops 4587520 | bytes 18350080 | tf_op jit(solution)/shard_map/concatenate | solution.py:52
  281.0 15.5 %fusion.9 = f32[16,1280]{1,0:T(8,128)S(1)} fusion(f32[768,1280]{1,0:T(8,128)} %fusion.63, s32[768]{0:T(1024)S(1)} %add.528, bf16[3584,1280]{1,0:T(8,128)(2,1)} %bitcast.146, f32[768,3584]{1,0:T(8,128)} %copy-done.1, f32[3584]{0:T(1024)S(1)} %copy-done.18, f32[768]{0:T(1024)S(1)} %add_rsqrt_fusion), kind=kOutput, calls=%fused_computation.24 | convolution fusion | flops 7092080640 | bytes 24219648 | tf_op jit(solution)/shard_map/dot_general | solution.py:207
  297.1 3.9 %collective-permute-done.38 = f32[16,1280]{1,0:T(8,128)S(1)} collective-permute-done((f32[16,1280]{1,0:T(8,128)S(1)}, f32[16,1280]{1,0:T(8,128)S(1)}, u32[]{:S(2)}, u32[]{:S(2)}) %collective-permute-start.38) | collective-permute-done | bytes 81952 | tf_op jit(solution)/shard_map/ppermute | solution.py:45
  301.9 2.3 fusion.19
  304.3 2.1 convolution_bitcast_fusion
  310.5 4.6 %all-to-all-start.1 = ((f32[4,4,448]{2,1,0:T(4,128)}), f32[4,4,448]{2,1,0:T(4,128)S(1)}, u32[]{:S(2)}, u32[]{:S(2)}) async-start(f32[4,4,448]{2,1,0:T(4,128)} %fusion.51), calls=%async_computation.1 | async-start | bytes 65536 | tf_op jit(solution)/shard_map/all_to_all | solution.py:250
  315.1 2.0 collective-permute-start.44
  317.2 3.4 %collective-permute-start.43 = (f32[16,448]{1,0:T(8,128)S(1)}, f32[16,448]{1,0:T(8,128)S(1)}, u32[]{:S(2)}, u32[]{:S(2)}) collective-permute-start(f32[16,448]{1,0:T(8,128)S(1)} %get-tuple-element.44), channel_id=1, source_target_pairs={{0,17},{1,24},{2,25},{3,0},{4,1},{5,8},{6,9},{7,16},{8,19},{9,26},... | collective-permute-start | bytes 86024 | tf_op jit(solution)/shard_map/ppermute | solution.py:246
  322.6 5.3 %collective-permute-start.41 = (f32[16,448]{1,0:T(8,128)S(1)}, f32[16,448]{1,0:T(8,128)S(1)}, u32[]{:S(2)}, u32[]{:S(2)}) collective-permute-start(f32[16,448]{1,0:T(8,128)S(1)} %get-tuple-element.39), channel_id=1, source_target_pairs={{0,25},{1,0},{2,1},{3,8},{4,9},{5,16},{6,17},{7,24},{8,27},{9,2},{... | collective-permute-start | bytes 86024 | tf_op jit(solution)/shard_map/ppermute | solution.py:246
  (217 shorter events, 66.1 us)
Async XLA Ops:
  0.0 304.3 %copy-start = (bf16[896,1280]{1,0:T(8,128)(2,1)S(1)}, bf16[896,1280]{1,0:T(8,128)(2,1)}, u32[]{:S(2)}) copy-start(bf16[896,1280]{1,0:T(8,128)(2,1)} %param.24) | copy-start | bytes 6881284
  0.0 29.2 %copy-start.21 = (s32[2,8]{1,0:T(2,128)S(1)}, s32[2,8]{1,0:T(2,128)}, u32[]{:S(2)}) copy-start(s32[2,8]{1,0:T(2,128)} %param.14) | copy-start | bytes 196
  4.3 26.8 %collective-permute-start.2 = (bf16[896,384]{1,0:T(8,128)(2,1)}, bf16[896,384]{1,0:T(8,128)(2,1)}, u32[]{:S(2)}, u32[]{:S(2)}) collective-permute-start(bf16[896,384]{1,0:T(8,128)(2,1)} %pad_maximum_fusion.9), channel_id=1, source_target_pairs={{0,16},{8,24},{16,0},{24,8},{1,17},{9,25},{17,1},{25,9},{2,18},{10... | collective-permute-start | bytes 2064392 | tf_op jit(solution)/shard_map/ppermute | solution.py:45
  7.3 54.6 %collective-permute-start = (s32[16]{0:T(128)}, s32[16]{0:T(128)}, u32[]{:S(2)}, u32[]{:S(2)}) collective-permute-start(s32[16]{0:T(128)} %bitcast.181), channel_id=1, source_target_pairs={{0,16},{8,24},{16,0},{24,8},{1,17},{9,25},{17,1},{25,9},{2,18},{10... | collective-permute-start | bytes 200 | tf_op jit(solution)/shard_map/ppermute | solution.py:45
  8.7 53.3 %collective-permute-start.48 = (s32[16]{0:T(128)}, s32[16]{0:T(128)}, u32[]{:S(2)}, u32[]{:S(2)}) collective-permute-start(s32[16]{0:T(128)} %reshape.147), channel_id=1, source_target_pairs={{0,16},{8,24},{16,0},{24,8},{1,17},{9,25},{17,1},{25,9},{2,18},{10... | collective-permute-start | bytes 200 | tf_op jit(solution)/shard_map/ppermute | solution.py:45
  13.4 20.9 %copy-start.17 = (f32[3584]{0:T(1024)S(1)}, f32[3584]{0:T(1024)}, u32[]{:S(2)}) copy-start(f32[3584]{0:T(1024)} %param.16) | copy-start | bytes 43012
  33.5 5.4 %collective-permute-start.3 = (bf16[2,896,384]{2,1,0:T(8,128)(2,1)}, bf16[2,896,384]{2,1,0:T(8,128)(2,1)}, u32[]{:S(2)}, u32[]{:S(2)}) collective-permute-start(bf16[2,896,384]{2,1,0:T(8,128)(2,1)} %pad_maximum_fusion.7), channel_id=1, source_target_pairs={{0,8},{8,0},{16,24},{24,16},{1,9},{9,1},{17,25},{25,17},{2,10},{10... | collective-permute-start | bytes 4128776 | tf_op jit(solution)/shard_map/ppermute | solution.py:51
  51.8 22.1 %all-to-all-start = ((bf16[8,768,32]{1,2,0:T(8,128)(2,1)}), bf16[8,768,32]{1,2,0:T(8,128)(2,1)S(1)}, u32[]{:S(2)}, u32[]{:S(2)}) async-start(bf16[8,768,32]{1,2,0:T(8,128)(2,1)} %fusion.41), calls=%async_computation | async-start | bytes 786432 | tf_op jit(solution)/shard_map/all_to_all | solution.py:171
  59.2 12.8 %collective-permute-start.4 = (bf16[896,256]{1,0:T(8,128)(2,1)S(1)}, bf16[896,256]{1,0:T(8,128)(2,1)}, u32[]{:S(2)}, u32[]{:S(2)}) collective-permute-start(bf16[896,256]{1,0:T(8,128)(2,1)S(1)} %copy-done.15), channel_id=1, source_target_pairs={{0,16},{8,24},{16,0},{24,8},{1,17},{9,25},{17,1},{25,9},{2,18},{10... | collective-permute-start | bytes 1376264 | tf_op jit(solution)/shard_map/ppermute | solution.py:45
  63.2 25.9 %collective-permute-start.1 = (s32[2,16]{1,0:T(2,128)}, s32[2,16]{1,0:T(2,128)S(1)}, u32[]{:S(2)}, u32[]{:S(2)}) collective-permute-start(s32[2,16]{1,0:T(2,128)} %get-tuple-element.69), channel_id=1, source_target_pairs={{0,8},{8,0},{16,24},{24,16},{1,9},{9,1},{17,25},{25,17},{2,10},{10... | collective-permute-start | bytes 392 | tf_op jit(solution)/shard_map/ppermute | solution.py:51
  63.2 238.0 %collective-permute-start.49 = (s32[2,16]{1,0:T(2,128)S(1)}, s32[2,16]{1,0:T(2,128)S(1)}, u32[]{:S(2)}, u32[]{:S(2)}) collective-permute-start(s32[2,16]{1,0:T(2,128)S(1)} %get-tuple-element.70), channel_id=1, source_target_pairs={{0,8},{8,0},{16,24},{24,16},{1,9},{9,1},{17,25},{25,17},{2,10},{10... | collective-permute-start | bytes 392 | tf_op jit(solution)/shard_map/ppermute | solution.py:51
  73.9 6.7 %collective-permute-start.5 = (bf16[2,896,256]{2,1,0:T(8,128)(2,1)}, bf16[2,896,256]{2,1,0:T(8,128)(2,1)}, u32[]{:S(2)}, u32[]{:S(2)}) collective-permute-start(bf16[2,896,256]{2,1,0:T(8,128)(2,1)} %pad_maximum_fusion.8), channel_id=1, source_target_pairs={{0,8},{8,0},{16,24},{24,16},{1,9},{9,1},{17,25},{25,17},{2,10},{10... | collective-permute-start | bytes 2752520 | tf_op jit(solution)/shard_map/ppermute | solution.py:51
  87.2 10.5 %collective-permute-start.22 = (bf16[96,1792]{1,0:T(8,128)(2,1)S(1)}, bf16[96,1792]{1,0:T(8,128)(2,1)S(1)}, u32[]{:S(2)}, u32[]{:S(2)}) collective-permute-start(bf16[96,1792]{1,0:T(8,128)(2,1)S(1)} %constant_dynamic-slice_fusion.2), channel_id=1, source_target_pairs={{0,1},{2,0},{4,2},{6,4},{7,6},{5,7},{3,5},{1,3},{8,9},{10,8},{12,1... | collective-permute-start | bytes 1032200 | tf_op jit(solution)/shard_map/ppermute | solution.py:97
  89.7 18.9 %copy-start.11 = (bf16[768,1792]{1,0:T(8,128)(2,1)S(1)}, bf16[768,1792]{1,0:T(8,128)(2,1)}, u32[]{:S(2)}) copy-start(bf16[768,1792]{1,0:T(8,128)(2,1)} %copy-done.10) | copy-start | bytes 8257540
  90.9 30.4 %copy-start.12 = (bf16[768,1792]{1,0:T(8,128)(2,1)S(1)}, bf16[768,1792]{1,0:T(8,128)(2,1)}, u32[]{:S(2)}) copy-start(bf16[768,1792]{1,0:T(8,128)(2,1)} %get-tuple-element.29) | copy-start | bytes 8257540
  90.9 10.2 %collective-permute-start.6 = (bf16[96,1792]{1,0:T(8,128)(2,1)S(1)}, bf16[96,1792]{1,0:T(8,128)(2,1)S(1)}, u32[]{:S(2)}, u32[]{:S(2)}) collective-permute-start(bf16[96,1792]{1,0:T(8,128)(2,1)S(1)} %constant_dynamic-slice_fusion.3), channel_id=1, source_target_pairs={{0,2},{2,4},{4,6},{6,7},{7,5},{5,3},{3,1},{1,0},{8,10},{10,12},{12... | collective-permute-start | bytes 1032200 | tf_op jit(solution)/shard_map/ppermute | solution.py:97
  91.2 57.1 %collective-permute-start.15 = (bf16[896,1280]{1,0:T(8,128)(2,1)}, bf16[896,1280]{1,0:T(8,128)(2,1)S(1)}, u32[]{:S(2)}, u32[]{:S(2)}) collective-permute-start(bf16[896,1280]{1,0:T(8,128)(2,1)} %param.22), channel_id=1, source_target_pairs={{0,16},{8,24},{16,0},{24,8},{1,17},{9,25},{17,1},{25,9},{2,18},{10... | collective-permute-start | bytes 6881288 | tf_op jit(solution)/shard_map/ppermute | solution.py:45
  91.8 100.6 %collective-permute-start.16 = (bf16[896,1280]{1,0:T(8,128)(2,1)}, bf16[896,1280]{1,0:T(8,128)(2,1)S(1)}, u32[]{:S(2)}, u32[]{:S(2)}) collective-permute-start(bf16[896,1280]{1,0:T(8,128)(2,1)} %param.23), channel_id=1, source_target_pairs={{0,16},{8,24},{16,0},{24,8},{1,17},{9,25},{17,1},{25,9},{2,18},{10... | collective-permute-start | bytes 6881288 | tf_op jit(solution)/shard_map/ppermute | solution.py:45
  98.8 9.8 %collective-permute-start.23 = (bf16[96,1792]{1,0:T(8,128)(2,1)S(1)}, bf16[96,1792]{1,0:T(8,128)(2,1)S(1)}, u32[]{:S(2)}, u32[]{:S(2)}) collective-permute-start(bf16[96,1792]{1,0:T(8,128)(2,1)S(1)} %add_convert_fusion.6), channel_id=1, source_target_pairs={{0,1},{2,0},{4,2},{6,4},{7,6},{5,7},{3,5},{1,3},{8,9},{10,8},{12,1... | collective-permute-start | bytes 1032200 | tf_op jit(solution)/shard_map/ppermute | solution.py:97
  102.2 9.4 %collective-permute-start.7 = (bf16[96,1792]{1,0:T(8,128)(2,1)S(1)}, bf16[96,1792]{1,0:T(8,128)(2,1)S(1)}, u32[]{:S(2)}, u32[]{:S(2)}) collective-permute-start(bf16[96,1792]{1,0:T(8,128)(2,1)S(1)} %add_convert_fusion.13), channel_id=1, source_target_pairs={{0,2},{2,4},{4,6},{6,7},{7,5},{5,3},{3,1},{1,0},{8,10},{10,12},{12... | collective-permute-start | bytes 1032200 | tf_op jit(solution)/shard_map/ppermute | solution.py:97
  108.7 8.9 %collective-permute-start.24 = (bf16[96,1792]{1,0:T(8,128)(2,1)S(1)}, bf16[96,1792]{1,0:T(8,128)(2,1)S(1)}, u32[]{:S(2)}, u32[]{:S(2)}) collective-permute-start(bf16[96,1792]{1,0:T(8,128)(2,1)S(1)} %add_convert_fusion.5), channel_id=1, source_target_pairs={{0,1},{2,0},{4,2},{6,4},{7,6},{5,7},{3,5},{1,3},{8,9},{10,8},{12,1... | collective-permute-start | bytes 1032200 | tf_op jit(solution)/shard_map/ppermute | solution.py:97
  112.7 8.5 %collective-permute-start.8 = (bf16[96,1792]{1,0:T(8,128)(2,1)S(1)}, bf16[96,1792]{1,0:T(8,128)(2,1)S(1)}, u32[]{:S(2)}, u32[]{:S(2)}) collective-permute-start(bf16[96,1792]{1,0:T(8,128)(2,1)S(1)} %add_convert_fusion.12), channel_id=1, source_target_pairs={{0,2},{2,4},{4,6},{6,7},{7,5},{5,3},{3,1},{1,0},{8,10},{10,12},{12... | collective-permute-start | bytes 1032200 | tf_op jit(solution)/shard_map/ppermute | solution.py:97
  117.6 8.1 %collective-permute-start.25 = (bf16[96,1792]{1,0:T(8,128)(2,1)S(1)}, bf16[96,1792]{1,0:T(8,128)(2,1)S(1)}, u32[]{:S(2)}, u32[]{:S(2)}) collective-permute-start(bf16[96,1792]{1,0:T(8,128)(2,1)S(1)} %add_convert_fusion.4), channel_id=1, source_target_pairs={{0,1},{2,0},{4,2},{6,4},{7,6},{5,7},{3,5},{1,3},{8,9},{10,8},{12,1... | collective-permute-start | bytes 1032200 | tf_op jit(solution)/shard_map/ppermute | solution.py:97
  121.3 8.3 %collective-permute-start.9 = (bf16[96,1792]{1,0:T(8,128)(2,1)S(1)}, bf16[96,1792]{1,0:T(8,128)(2,1)S(1)}, u32[]{:S(2)}, u32[]{:S(2)}) collective-permute-start(bf16[96,1792]{1,0:T(8,128)(2,1)S(1)} %add_convert_fusion.11), channel_id=1, source_target_pairs={{0,2},{2,4},{4,6},{6,7},{7,5},{5,3},{3,1},{1,0},{8,10},{10,12},{12... | collective-permute-start | bytes 1032200 | tf_op jit(solution)/shard_map/ppermute | solution.py:97
  125.8 22.5 %copy-start.13 = (bf16[896,1280]{1,0:T(8,128)(2,1)S(1)}, bf16[896,1280]{1,0:T(8,128)(2,1)}, u32[]{:S(2)}) copy-start(bf16[896,1280]{1,0:T(8,128)(2,1)} %param.22) | copy-start | bytes 6881284
  125.8 8.3 %collective-permute-start.26 = (bf16[96,1792]{1,0:T(8,128)(2,1)S(1)}, bf16[96,1792]{1,0:T(8,128)(2,1)S(1)}, u32[]{:S(2)}, u32[]{:S(2)}) collective-permute-start(bf16[96,1792]{1,0:T(8,128)(2,1)S(1)} %add_convert_fusion.3), channel_id=1, source_target_pairs={{0,1},{2,0},{4,2},{6,4},{7,6},{5,7},{3,5},{1,3},{8,9},{10,8},{12,1... | collective-permute-start | bytes 1032200 | tf_op jit(solution)/shard_map/ppermute | solution.py:97
  129.7 8.6 %collective-permute-start.10 = (bf16[96,1792]{1,0:T(8,128)(2,1)S(1)}, bf16[96,1792]{1,0:T(8,128)(2,1)S(1)}, u32[]{:S(2)}, u32[]{:S(2)}) collective-permute-start(bf16[96,1792]{1,0:T(8,128)(2,1)S(1)} %add_convert_fusion.10), channel_id=1, source_target_pairs={{0,2},{2,4},{4,6},{6,7},{7,5},{5,3},{3,1},{1,0},{8,10},{10,12},{12... | collective-permute-start | bytes 1032200 | tf_op jit(solution)/shard_map/ppermute | solution.py:97
  134.2 9.1 %collective-permute-start.27 = (bf16[96,1792]{1,0:T(8,128)(2,1)S(1)}, bf16[96,1792]{1,0:T(8,128)(2,1)S(1)}, u32[]{:S(2)}, u32[]{:S(2)}) collective-permute-start(bf16[96,1792]{1,0:T(8,128)(2,1)S(1)} %add_convert_fusion.2), channel_id=1, source_target_pairs={{0,1},{2,0},{4,2},{6,4},{7,6},{5,7},{3,5},{1,3},{8,9},{10,8},{12,1... | collective-permute-start | bytes 1032200 | tf_op jit(solution)/shard_map/ppermute | solution.py:97
  138.4 9.4 %collective-permute-start.11 = (bf16[96,1792]{1,0:T(8,128)(2,1)S(1)}, bf16[96,1792]{1,0:T(8,128)(2,1)S(1)}, u32[]{:S(2)}, u32[]{:S(2)}) collective-permute-start(bf16[96,1792]{1,0:T(8,128)(2,1)S(1)} %add_convert_fusion.9), channel_id=1, source_target_pairs={{0,2},{2,4},{4,6},{6,7},{7,5},{5,3},{3,1},{1,0},{8,10},{10,12},{12... | collective-permute-start | bytes 1032200 | tf_op jit(solution)/shard_map/ppermute | solution.py:97
  143.4 15.2 %collective-permute-start.28 = (bf16[96,1792]{1,0:T(8,128)(2,1)S(1)}, bf16[96,1792]{1,0:T(8,128)(2,1)S(1)}, u32[]{:S(2)}, u32[]{:S(2)}) collective-permute-start(bf16[96,1792]{1,0:T(8,128)(2,1)S(1)} %add_convert_fusion.1), channel_id=1, source_target_pairs={{0,1},{2,0},{4,2},{6,4},{7,6},{5,7},{3,5},{1,3},{8,9},{10,8},{12,1... | collective-permute-start | bytes 1032200 | tf_op jit(solution)/shard_map/ppermute | solution.py:97
  147.9 7.8 %collective-permute-start.12 = (bf16[96,1792]{1,0:T(8,128)(2,1)S(1)}, bf16[96,1792]{1,0:T(8,128)(2,1)S(1)}, u32[]{:S(2)}, u32[]{:S(2)}) collective-permute-start(bf16[96,1792]{1,0:T(8,128)(2,1)S(1)} %add_convert_fusion.8), channel_id=1, source_target_pairs={{0,2},{2,4},{4,6},{6,7},{7,5},{5,3},{3,1},{1,0},{8,10},{10,12},{12... | collective-permute-start | bytes 1032200 | tf_op jit(solution)/shard_map/ppermute | solution.py:97
  157.5 34.9 %copy-start.14 = (bf16[896,1280]{1,0:T(8,128)(2,1)S(1)}, bf16[896,1280]{1,0:T(8,128)(2,1)}, u32[]{:S(2)}) copy-start(bf16[896,1280]{1,0:T(8,128)(2,1)} %param.23) | copy-start | bytes 6881284
  158.3 10.7 %collective-permute-start.13 = (bf16[96,1792]{1,0:T(8,128)(2,1)S(1)}, bf16[96,1792]{1,0:T(8,128)(2,1)S(1)}, u32[]{:S(2)}, u32[]{:S(2)}) collective-permute-start(bf16[96,1792]{1,0:T(8,128)(2,1)S(1)} %get-tuple-element.26), channel_id=1, source_target_pairs={{0,2},{2,4},{4,6},{6,7},{7,5},{5,3},{3,1},{1,0},{8,10},{10,12},{12... | collective-permute-start | bytes 1032200 | tf_op jit(solution)/shard_map/ppermute | solution.py:103
  161.3 34.0 %collective-permute-start.29 = (bf16[96,1792]{1,0:T(8,128)(2,1)}, bf16[96,1792]{1,0:T(8,128)(2,1)S(1)}, u32[]{:S(2)}, u32[]{:S(2)}) collective-permute-start(bf16[96,1792]{1,0:T(8,128)(2,1)} %get-tuple-element.28), channel_id=1, source_target_pairs={{0,1},{2,0},{4,2},{6,4},{7,6},{5,7},{3,5},{1,3},{8,9},{10,8},{12,1... | collective-permute-start | bytes 1032200 | tf_op jit(solution)/shard_map/ppermute | solution.py:103
  169.0 25.8 %collective-permute-start.14 = (bf16[96,1792]{1,0:T(8,128)(2,1)S(1)}, bf16[96,1792]{1,0:T(8,128)(2,1)S(1)}, u32[]{:S(2)}, u32[]{:S(2)}) collective-permute-start(bf16[96,1792]{1,0:T(8,128)(2,1)S(1)} %collective-permute-done.13), channel_id=1, source_target_pairs={{0,2},{2,4},{4,6},{6,7},{7,5},{5,3},{3,1},{1,0},{8,10},{10,12},{12... | collective-permute-start | bytes 1032200 | tf_op jit(solution)/shard_map/ppermute | solution.py:103
  194.8 62.0 %collective-permute-start.37 = (bf16[2,896,1280]{2,1,0:T(8,128)(2,1)}, bf16[2,896,1280]{2,1,0:T(8,128)(2,1)}, u32[]{:S(2)}, u32[]{:S(2)}) collective-permute-start(bf16[2,896,1280]{2,1,0:T(8,128)(2,1)} %pad_maximum_fusion.4), channel_id=1, source_target_pairs={{0,8},{8,0},{16,24},{24,16},{1,9},{9,1},{17,25},{25,17},{2,10},{10... | collective-permute-start | bytes 13762568 | tf_op jit(solution)/shard_map/ppermute | solution.py:51
  195.3 10.5 %collective-permute-start.30 = (bf16[96,1792]{1,0:T(8,128)(2,1)S(1)}, bf16[96,1792]{1,0:T(8,128)(2,1)S(1)}, u32[]{:S(2)}, u32[]{:S(2)}) collective-permute-start(bf16[96,1792]{1,0:T(8,128)(2,1)S(1)} %collective-permute-done.29), channel_id=1, source_target_pairs={{0,1},{2,0},{4,2},{6,4},{7,6},{5,7},{3,5},{1,3},{8,9},{10,8},{12,1... | collective-permute-start | bytes 1032200 | tf_op jit(solution)/shard_map/ppermute | solution.py:103
  198.5 19.4 %collective-permute-start.17 = (bf16[96,1792]{1,0:T(8,128)(2,1)S(1)}, bf16[96,1792]{1,0:T(8,128)(2,1)S(1)}, u32[]{:S(2)}, u32[]{:S(2)}) collective-permute-start(bf16[96,1792]{1,0:T(8,128)(2,1)S(1)} %collective-permute-done.14), channel_id=1, source_target_pairs={{0,2},{2,4},{4,6},{6,7},{7,5},{5,3},{3,1},{1,0},{8,10},{10,12},{12... | collective-permute-start | bytes 1032200 | tf_op jit(solution)/shard_map/ppermute | solution.py:103
  205.8 9.7 %collective-permute-start.31 = (bf16[96,1792]{1,0:T(8,128)(2,1)S(1)}, bf16[96,1792]{1,0:T(8,128)(2,1)S(1)}, u32[]{:S(2)}, u32[]{:S(2)}) collective-permute-start(bf16[96,1792]{1,0:T(8,128)(2,1)S(1)} %collective-permute-done.30), channel_id=1, source_target_pairs={{0,1},{2,0},{4,2},{6,4},{7,6},{5,7},{3,5},{1,3},{8,9},{10,8},{12,1... | collective-permute-start | bytes 1032200 | tf_op jit(solution)/shard_map/ppermute | solution.py:103
  208.2 65.9 %collective-permute-start.36 = (bf16[2,896,1280]{2,1,0:T(8,128)(2,1)}, bf16[2,896,1280]{2,1,0:T(8,128)(2,1)}, u32[]{:S(2)}, u32[]{:S(2)}) collective-permute-start(bf16[2,896,1280]{2,1,0:T(8,128)(2,1)} %pad_maximum_fusion.3), channel_id=1, source_target_pairs={{0,8},{8,0},{16,24},{24,16},{1,9},{9,1},{17,25},{25,17},{2,10},{10... | collective-permute-start | bytes 13762568 | tf_op jit(solution)/shard_map/ppermute | solution.py:51
  215.5 8.8 %collective-permute-start.32 = (bf16[96,1792]{1,0:T(8,128)(2,1)S(1)}, bf16[96,1792]{1,0:T(8,128)(2,1)S(1)}, u32[]{:S(2)}, u32[]{:S(2)}) collective-permute-start(bf16[96,1792]{1,0:T(8,128)(2,1)S(1)} %collective-permute-done.31), channel_id=1, source_target_pairs={{0,1},{2,0},{4,2},{6,4},{7,6},{5,7},{3,5},{1,3},{8,9},{10,8},{12,1... | collective-permute-start | bytes 1032200 | tf_op jit(solution)/shard_map/ppermute | solution.py:103
  217.9 8.8 %collective-permute-start.18 = (bf16[96,1792]{1,0:T(8,128)(2,1)S(1)}, bf16[96,1792]{1,0:T(8,128)(2,1)S(1)}, u32[]{:S(2)}, u32[]{:S(2)}) collective-permute-start(bf16[96,1792]{1,0:T(8,128)(2,1)S(1)} %collective-permute-done.17), channel_id=1, source_target_pairs={{0,2},{2,4},{4,6},{6,7},{7,5},{5,3},{3,1},{1,0},{8,10},{10,12},{12... | collective-permute-start | bytes 1032200 | tf_op jit(solution)/shard_map/ppermute | solution.py:103
  219.1 32.6 %copy-start.3 = (bf16[768,896]{1,0:T(8,128)(2,1)S(1)}, bf16[768,896]{1,0:T(8,128)(2,1)}, u32[]{:S(2)}) copy-start(bf16[768,896]{1,0:T(8,128)(2,1)} %copy-done.2) | copy-start | bytes 4128772
  219.1 32.6 %copy-start.5 = (bf16[768,896]{1,0:T(8,128)(2,1)S(1)}, bf16[768,896]{1,0:T(8,128)(2,1)}, u32[]{:S(2)}) copy-start(bf16[768,896]{1,0:T(8,128)(2,1)} %copy-done.4) | copy-start | bytes 4128772
  219.1 32.6 %copy-start.7 = (bf16[768,896]{1,0:T(8,128)(2,1)S(1)}, bf16[768,896]{1,0:T(8,128)(2,1)}, u32[]{:S(2)}) copy-start(bf16[768,896]{1,0:T(8,128)(2,1)} %copy-done.6) | copy-start | bytes 4128772
  219.1 32.6 %copy-start.9 = (bf16[768,896]{1,0:T(8,128)(2,1)S(1)}, bf16[768,896]{1,0:T(8,128)(2,1)}, u32[]{:S(2)}) copy-start(bf16[768,896]{1,0:T(8,128)(2,1)} %copy-done.8) | copy-start | bytes 4128772
  224.3 8.2 %collective-permute-start.33 = (bf16[96,1792]{1,0:T(8,128)(2,1)S(1)}, bf16[96,1792]{1,0:T(8,128)(2,1)S(1)}, u32[]{:S(2)}, u32[]{:S(2)}) collective-permute-start(bf16[96,1792]{1,0:T(8,128)(2,1)S(1)} %collective-permute-done.32), channel_id=1, source_target_pairs={{0,1},{2,0},{4,2},{6,4},{7,6},{5,7},{3,5},{1,3},{8,9},{10,8},{12,1... | collective-permute-start | bytes 1032200 | tf_op jit(solution)/shard_map/ppermute | solution.py:103
  226.8 8.2 %collective-permute-start.19 = (bf16[96,1792]{1,0:T(8,128)(2,1)S(1)}, bf16[96,1792]{1,0:T(8,128)(2,1)S(1)}, u32[]{:S(2)}, u32[]{:S(2)}) collective-permute-start(bf16[96,1792]{1,0:T(8,128)(2,1)S(1)} %collective-permute-done.18), channel_id=1, source_target_pairs={{0,2},{2,4},{4,6},{6,7},{7,5},{5,3},{3,1},{1,0},{8,10},{10,12},{12... | collective-permute-start | bytes 1032200 | tf_op jit(solution)/shard_map/ppermute | solution.py:103
  232.5 8.7 %collective-permute-start.34 = (bf16[96,1792]{1,0:T(8,128)(2,1)S(1)}, bf16[96,1792]{1,0:T(8,128)(2,1)S(1)}, u32[]{:S(2)}, u32[]{:S(2)}) collective-permute-start(bf16[96,1792]{1,0:T(8,128)(2,1)S(1)} %collective-permute-done.33), channel_id=1, source_target_pairs={{0,1},{2,0},{4,2},{6,4},{7,6},{5,7},{3,5},{1,3},{8,9},{10,8},{12,1... | collective-permute-start | bytes 1032200 | tf_op jit(solution)/shard_map/ppermute | solution.py:103
  235.0 8.7 %collective-permute-start.20 = (bf16[96,1792]{1,0:T(8,128)(2,1)S(1)}, bf16[96,1792]{1,0:T(8,128)(2,1)S(1)}, u32[]{:S(2)}, u32[]{:S(2)}) collective-permute-start(bf16[96,1792]{1,0:T(8,128)(2,1)S(1)} %collective-permute-done.19), channel_id=1, source_target_pairs={{0,2},{2,4},{4,6},{6,7},{7,5},{5,3},{3,1},{1,0},{8,10},{10,12},{12... | collective-permute-start | bytes 1032200 | tf_op jit(solution)/shard_map/ppermute | solution.py:103
  241.2 7.2 %collective-permute-start.35 = (bf16[96,1792]{1,0:T(8,128)(2,1)S(1)}, bf16[96,1792]{1,0:T(8,128)(2,1)S(1)}, u32[]{:S(2)}, u32[]{:S(2)}) collective-permute-start(bf16[96,1792]{1,0:T(8,128)(2,1)S(1)} %collective-permute-done.34), channel_id=1, source_target_pairs={{0,1},{2,0},{4,2},{6,4},{7,6},{5,7},{3,5},{1,3},{8,9},{10,8},{12,1... | collective-permute-start | bytes 1032200 | tf_op jit(solution)/shard_map/ppermute | solution.py:103
  243.6 7.3 %collective-permute-start.21 = (bf16[96,1792]{1,0:T(8,128)(2,1)S(1)}, bf16[96,1792]{1,0:T(8,128)(2,1)S(1)}, u32[]{:S(2)}, u32[]{:S(2)}) collective-permute-start(bf16[96,1792]{1,0:T(8,128)(2,1)S(1)} %collective-permute-done.20), channel_id=1, source_target_pairs={{0,2},{2,4},{4,6},{6,7},{7,5},{5,3},{3,1},{1,0},{8,10},{10,12},{12... | collective-permute-start | bytes 1032200 | tf_op jit(solution)/shard_map/ppermute | solution.py:103
  281.0 20.1 %copy-start.20 = (s32[1,16]{1,0:T(1,128)S(1)}, s32[1,16]{1,0:T(1,128)}, u32[]{:S(2)}) copy-start(s32[1,16]{1,0:T(1,128)} %stack_reshape.3) | copy-start | bytes 196
  296.6 4.4 %collective-permute-start.38 = (f32[16,1280]{1,0:T(8,128)S(1)}, f32[16,1280]{1,0:T(8,128)S(1)}, u32[]{:S(2)}, u32[]{:S(2)}) collective-permute-start(f32[16,1280]{1,0:T(8,128)S(1)} %fusion.9), channel_id=1, source_target_pairs={{0,16},{8,24},{16,0},{24,8},{1,17},{9,25},{17,1},{25,9},{2,18},{10... | collective-permute-start | bytes 245768 | tf_op jit(solution)/shard_map/ppermute | solution.py:45
  301.1 3.2 collective-permute-start.39
  306.9 13.7 %collective-permute-start.47 = (f32[16,448]{1,0:T(8,128)S(1)}, f32[16,448]{1,0:T(8,128)S(1)}, u32[]{:S(2)}, u32[]{:S(2)}) collective-permute-start(f32[16,448]{1,0:T(8,128)S(1)} %get-tuple-element.40), channel_id=1, source_target_pairs={{0,1},{1,8},{2,9},{3,16},{4,17},{5,24},{6,25},{7,0},{8,3},{9,10},{... | collective-permute-start | bytes 86024 | tf_op jit(solution)/shard_map/ppermute | solution.py:246
  308.4 13.5 %collective-permute-start.46 = (f32[16,448]{1,0:T(8,128)S(1)}, f32[16,448]{1,0:T(8,128)S(1)}, u32[]{:S(2)}, u32[]{:S(2)}) collective-permute-start(f32[16,448]{1,0:T(8,128)S(1)} %get-tuple-element.41), channel_id=1, source_target_pairs={{0,8},{1,9},{2,16},{3,17},{4,24},{5,25},{6,0},{7,1},{8,10},{9,11},... | collective-permute-start | bytes 86024 | tf_op jit(solution)/shard_map/ppermute | solution.py:246
  309.4 13.2 %collective-permute-start.45 = (f32[16,448]{1,0:T(8,128)S(1)}, f32[16,448]{1,0:T(8,128)S(1)}, u32[]{:S(2)}, u32[]{:S(2)}) collective-permute-start(f32[16,448]{1,0:T(8,128)S(1)} %get-tuple-element.42), channel_id=1, source_target_pairs={{0,9},{1,16},{2,17},{3,24},{4,25},{5,0},{6,1},{7,8},{8,11},{9,18},... | collective-permute-start | bytes 86024 | tf_op jit(solution)/shard_map/ppermute | solution.py:246
  310.5 17.5 %all-to-all-start.1 = ((f32[4,4,448]{2,1,0:T(4,128)}), f32[4,4,448]{2,1,0:T(4,128)S(1)}, u32[]{:S(2)}, u32[]{:S(2)}) async-start(f32[4,4,448]{2,1,0:T(4,128)} %fusion.51), calls=%async_computation.1 | async-start | bytes 65536 | tf_op jit(solution)/shard_map/all_to_all | solution.py:250
  315.1 12.9 %collective-permute-start.44 = (f32[16,448]{1,0:T(8,128)S(1)}, f32[16,448]{1,0:T(8,128)S(1)}, u32[]{:S(2)}, u32[]{:S(2)}) collective-permute-start(f32[16,448]{1,0:T(8,128)S(1)} %get-tuple-element.43), channel_id=1, source_target_pairs={{0,16},{1,17},{2,24},{3,25},{4,0},{5,1},{6,8},{7,9},{8,18},{9,19},... | collective-permute-start | bytes 86024 | tf_op jit(solution)/shard_map/ppermute | solution.py:246
  317.2 10.9 %collective-permute-start.43 = (f32[16,448]{1,0:T(8,128)S(1)}, f32[16,448]{1,0:T(8,128)S(1)}, u32[]{:S(2)}, u32[]{:S(2)}) collective-permute-start(f32[16,448]{1,0:T(8,128)S(1)} %get-tuple-element.44), channel_id=1, source_target_pairs={{0,17},{1,24},{2,25},{3,0},{4,1},{5,8},{6,9},{7,16},{8,19},{9,26},... | collective-permute-start | bytes 86024 | tf_op jit(solution)/shard_map/ppermute | solution.py:246
  320.5 7.5 %collective-permute-start.42 = (f32[16,448]{1,0:T(8,128)S(1)}, f32[16,448]{1,0:T(8,128)S(1)}, u32[]{:S(2)}, u32[]{:S(2)}) collective-permute-start(f32[16,448]{1,0:T(8,128)S(1)} %get-tuple-element.45), channel_id=1, source_target_pairs={{0,24},{1,25},{2,0},{3,1},{4,8},{5,9},{6,16},{7,17},{8,26},{9,27},... | collective-permute-start | bytes 86024 | tf_op jit(solution)/shard_map/ppermute | solution.py:246
  321.9 6.1 %collective-permute-start.40 = (f32[16,448]{1,0:T(8,128)S(1)}, f32[16,448]{1,0:T(8,128)S(1)}, u32[]{:S(2)}, u32[]{:S(2)}) collective-permute-start(f32[16,448]{1,0:T(8,128)S(1)} %get-tuple-element.46), channel_id=1, source_target_pairs={{0,0},{1,1},{2,8},{3,9},{4,16},{5,17},{6,24},{7,25},{8,2},{9,3},{1... | collective-permute-start | bytes 86024 | tf_op jit(solution)/shard_map/ppermute | solution.py:246
  322.6 6.9 %collective-permute-start.41 = (f32[16,448]{1,0:T(8,128)S(1)}, f32[16,448]{1,0:T(8,128)S(1)}, u32[]{:S(2)}, u32[]{:S(2)}) collective-permute-start(f32[16,448]{1,0:T(8,128)S(1)} %get-tuple-element.39), channel_id=1, source_target_pairs={{0,25},{1,0},{2,1},{3,8},{4,9},{5,16},{6,17},{7,24},{8,27},{9,2},{... | collective-permute-start | bytes 86024 | tf_op jit(solution)/shard_map/ppermute | solution.py:246
  (14 other events, 98.3 us)

commit v7 on v6

--- a/solution.py
+++ b/solution.py
@@ -77,7 +77,7 @@
     return list(range(0, n, 2)) + list(range(n - 1, 0, -2))
 
 
-def ring_psum(x, axis, n, ride):
+def ring_psum(x, axis, n, ride, finish):
     walk = ring_walk(n)
     place = [0] * n
     for p, t in enumerate(walk):
@@ -102,6 +102,9 @@
             if step:
                 moving = lax.ppermute(moving, axis, pairs)
             if step == min(2, n - 1) and sign == 1:
+                moving, ride = lax.optimization_barrier((moving, ride))
+                ride = finish(ride)
+            if step == n - 1 and sign == 1:
                 moving, ride = lax.optimization_barrier((moving, ride))
             where = ((pos + sign - sign * step) % n) * size
             out = lax.dynamic_update_slice_in_dim(out, moving, where, 0)
@@ -190,10 +193,14 @@
     )
     attended_rows = attended_rows.astype(jnp.bfloat16).reshape(row_count, local_heads * HEAD_SIZE)
     attn_term = transposed_dot(attended_rows, o_full).astype(jnp.bfloat16)
-    attn_total, (gate_chips, up_chips) = ring_psum(attn_term, "tp", tp_size, (gate_chips, up_chips))
+    attn_total, (gate_full, up_full) = ring_psum(
+        attn_term,
+        "tp",
+        tp_size,
+        (gate_chips, up_chips),
+        lambda ride: tuple(gather_cores(w, chips).reshape(width, -1) for w in ride),
+    )
     attn_total = attn_total.astype(jnp.float32)
-    gate_full = gather_cores(gate_chips, chips).reshape(width, -1)
-    up_full = gather_cores(up_chips, chips).reshape(width, -1)
     residual = hidden_perm.astype(jnp.float32) + attn_total
     norm_mid = rms_scale(residual, ffn_gain_perm)
     gate_pre = jnp.dot(norm_mid, gate_full, preferred_element_type=jnp.float32)

time: 334 us -> 376 us (1.13)
  waiting for transfers between devices: 118 us -> 154 us
  starting transfers between devices: 64.1 us -> 72.9 us
    ppermute x14, waiting for transfers between devices: 42.8 us -> 77.1 us  [ring_psum(): got = lax.ppermute(acc, axis, pairs)]
    ppermute x14, starting transfers between devices: 15.3 us -> 24.4 us  [ring_psum(): got = lax.ppermute(acc, axis, pairs)]
    ppermute x7, waiting for transfers between devices: 34.3 us -> 26.6 us  [gather_chips(): moving = lax.ppermute(moving, 'grp', ring)]
    ppermute x14, waiting for transfers between devices: 39.9 us -> 45.6 us  [ring_psum(): moving = lax.ppermute(moving, axis, pairs)]
    unnamed x60 -> x58, local copies, waits for them, and re-layouts: 4.8 us -> 8.82 us
  transfers between devices with their start and end apart: 52 -> 52, of which waited for: 25 -> 31; matrix products, arithmetic and copies ran while one was open for 37% -> 28% of each run, Pallas kernels for 0% -> 0%
where the time goes in v7:
time: 376 us; the launch traced here: 374 us
  waiting for transfers between devices  154 us (41%)
  starting transfers between devices  72.9 us (19%)
  other arithmetic  53.1 us (14%)
  matrix products  42.5 us (11%)
  local copies, waits for them, and re-layouts  35.9 us (10%)
  between operations  15.1 us (4%)
    ppermute x14, waiting for transfers between devices, ring_psum(): got = lax.ppermute(acc, axis, pairs)  77.1 us
    ppermute x14, waiting for transfers between devices, ring_psum(): moving = lax.ppermute(moving, axis, pairs)  45.6 us
    ppermute x7, waiting for transfers between devices, gather_chips(): moving = lax.ppermute(moving, 'grp', ring)  26.6 us
    ppermute x14, starting transfers between devices, ring_psum(): got = lax.ppermute(acc, axis, pairs)  24.4 us
    concatenate x6, other arithmetic, gather_cores(): return jnp.concatenate([mine, other], 0)  17.6 us
    dot_general x1, matrix products, on_device(): jnp.dot(selector.astype(jnp.bfloat16), hidden_ffn, preferred_element_type...  15.6 us
    ppermute x8, starting transfers between devices, on_device(): totals = totals + lax.ppermute(piece, ('grp', 'tp'), pairs)  14 us
    ppermute x14, starting transfers between devices, ring_psum(): moving = lax.ppermute(moving, axis, pairs)  13.4 us
  transfers between devices with their start and end apart: 52, of which 31 were waited for; matrix products, arithmetic and copies ran while one was open for 28% of the time, Pallas kernels for 0%

profile of v7, /device:TPU:0, one launch (start us, length us, event | category | flops | bytes accessed | tf_op | source)
XLA Modules:
  0.0 373.5 jit_solution(4790026454091959250)
XLA Ops:
  2.3 2.0 pad_maximum_fusion.9
  4.3 2.9 collective-permute-start.2
  10.4 12.7 %collective-permute-done.2 = bf16[896,384]{1,0:T(8,128)(2,1)} collective-permute-done((bf16[896,384]{1,0:T(8,128)(2,1)}, bf16[896,384]{1,0:T(8,128)(2,1)}, u32[]{:S(2)}, u32[]{:S(2)}) %collective-permute-start.2) | collective-permute-done | bytes 688160 | tf_op jit(solution)/shard_map/ppermute | solution.py:45
  23.0 2.4 pad_maximum_fusion.7
  27.5 3.1 constant_dynamic-slice_fusion.7
  31.9 2.3 pad_maximum_fusion.5
  34.3 4.3 %fusion.12 = bf16[768,384]{0,1:T(8,128)(2,1)S(1)} fusion(bf16[3584,384]{1,0:T(8,128)(2,1)S(1)} %bitcast.149, f32[3584]{0:T(1024)S(1)} %pad_maximum_fusion.12, f32[768]{0:T(1024)S(1)} %add_rsqrt_fusion.1, bf16[768,896]{1,0:T(8,128)(2,1)S(1)} %get-tuple-element.39, bf16[768,896]{1,0:T(8,128)(2,1)S(1)} %get-tuple-element.40, ...), kind=kOutput, calls=%fused_computation.29 | convolution fusion | flops 2144501760 | bytes 8864768 | tf_op jit(solution)/shard_map/dot_general | solution.py:159
  44.9 6.1 %all-to-all-start = ((bf16[8,768,32]{1,2,0:T(8,128)(2,1)}), bf16[8,768,32]{1,2,0:T(8,128)(2,1)S(1)}, u32[]{:S(2)}, u32[]{:S(2)}) async-start(bf16[8,768,32]{1,2,0:T(8,128)(2,1)} %fusion.41), calls=%async_computation | async-start | bytes 786432 | tf_op jit(solution)/shard_map/all_to_all | solution.py:174
  70.9 8.2 %collective-permute-done.4 = bf16[896,256]{1,0:T(8,128)(2,1)} collective-permute-done((bf16[896,256]{1,0:T(8,128)(2,1)S(1)}, bf16[896,256]{1,0:T(8,128)(2,1)}, u32[]{:S(2)}, u32[]{:S(2)}) %collective-permute-start.4) | collective-permute-done | bytes 458784 | tf_op jit(solution)/shard_map/ppermute | solution.py:45
  79.1 2.0 pad_maximum_fusion.8
  81.3 4.1 %fusion.73 = (f32[2,2,384]{2,1,0:T(2,128)}, f32[2,2,384,384]{2,3,1,0:T(8,128)}) fusion(pred[2,384,384]{1,2,0:T(8,128)(4,1)} %broadcast_compare_fusion, bf16[2,384,2,128]{1,0,3,2:T(2,128)(2,1)} %reshape.140, bf16[2,384,128,1]{1,0,2,3:T(2,128)(2,1)S(1)} %bitcast.178), kind=kOutput, calls=%fused_computation.169 | convolution fusion | flops 153354624 | bytes 3250176 | tf_op jit(solution)/shard_map/sub | solution.py:29
  85.4 2.0 fusion.15
  91.0 1.9 fusion.65
  94.4 1.8 collective-permute-start.6
  97.1 7.9 %collective-permute-done.6 = bf16[96,1792]{1,0:T(8,128)(2,1)S(1)} collective-permute-done((bf16[96,1792]{1,0:T(8,128)(2,1)S(1)}, bf16[96,1792]{1,0:T(8,128)(2,1)S(1)}, u32[]{:S(2)}, u32[]{:S(2)}) %collective-permute-start.6) | collective-permute-done | bytes 344096 | tf_op jit(solution)/shard_map/ppermute | solution.py:97
  106.0 1.8 collective-permute-start.7
  110.9 4.8 %collective-permute-done.7 = bf16[96,1792]{1,0:T(8,128)(2,1)S(1)} collective-permute-done((bf16[96,1792]{1,0:T(8,128)(2,1)S(1)}, bf16[96,1792]{1,0:T(8,128)(2,1)S(1)}, u32[]{:S(2)}, u32[]{:S(2)}) %collective-permute-start.7) | collective-permute-done | bytes 344096 | tf_op jit(solution)/shard_map/ppermute | solution.py:97
  115.7 1.7 collective-permute-start.24
  118.6 6.0 %collective-permute-done.24 = bf16[96,1792]{1,0:T(8,128)(2,1)S(1)} collective-permute-done((bf16[96,1792]{1,0:T(8,128)(2,1)S(1)}, bf16[96,1792]{1,0:T(8,128)(2,1)S(1)}, u32[]{:S(2)}, u32[]{:S(2)}) %collective-permute-start.24) | collective-permute-done | bytes 344096 | tf_op jit(solution)/shard_map/ppermute | solution.py:97
  124.5 1.7 collective-permute-start.8
  126.4 6.0 %collective-permute-done.8 = bf16[96,1792]{1,0:T(8,128)(2,1)S(1)} collective-permute-done((bf16[96,1792]{1,0:T(8,128)(2,1)S(1)}, bf16[96,1792]{1,0:T(8,128)(2,1)S(1)}, u32[]{:S(2)}, u32[]{:S(2)}) %collective-permute-start.8) | collective-permute-done | bytes 344096 | tf_op jit(solution)/shard_map/ppermute | solution.py:97
  132.4 1.7 collective-permute-start.25
  135.2 4.4 %collective-permute-done.25 = bf16[96,1792]{1,0:T(8,128)(2,1)S(1)} collective-permute-done((bf16[96,1792]{1,0:T(8,128)(2,1)S(1)}, bf16[96,1792]{1,0:T(8,128)(2,1)S(1)}, u32[]{:S(2)}, u32[]{:S(2)}) %collective-permute-start.25) | collective-permute-done | bytes 344096 | tf_op jit(solution)/shard_map/ppermute | solution.py:97
  139.7 1.7 collective-permute-start.9
  141.5 5.4 %collective-permute-done.9 = bf16[96,1792]{1,0:T(8,128)(2,1)S(1)} collective-permute-done((bf16[96,1792]{1,0:T(8,128)(2,1)S(1)}, bf16[96,1792]{1,0:T(8,128)(2,1)S(1)}, u32[]{:S(2)}, u32[]{:S(2)}) %collective-permute-start.9) | collective-permute-done | bytes 344096 | tf_op jit(solution)/shard_map/ppermute | solution.py:97
  146.9 1.7 collective-permute-start.26
  148.7 5.4 %collective-permute-done.26 = bf16[96,1792]{1,0:T(8,128)(2,1)S(1)} collective-permute-done((bf16[96,1792]{1,0:T(8,128)(2,1)S(1)}, bf16[96,1792]{1,0:T(8,128)(2,1)S(1)}, u32[]{:S(2)}, u32[]{:S(2)}) %collective-permute-start.26) | collective-permute-done | bytes 344096 | tf_op jit(solution)/shard_map/ppermute | solution.py:97
  154.2 1.7 collective-permute-start.10
  156.0 5.4 %collective-permute-done.10 = bf16[96,1792]{1,0:T(8,128)(2,1)S(1)} collective-permute-done((bf16[96,1792]{1,0:T(8,128)(2,1)S(1)}, bf16[96,1792]{1,0:T(8,128)(2,1)S(1)}, u32[]{:S(2)}, u32[]{:S(2)}) %collective-permute-start.10) | collective-permute-done | bytes 344096 | tf_op jit(solution)/shard_map/ppermute | solution.py:97
  163.2 5.4 %collective-permute-done.27 = bf16[96,1792]{1,0:T(8,128)(2,1)S(1)} collective-permute-done((bf16[96,1792]{1,0:T(8,128)(2,1)S(1)}, bf16[96,1792]{1,0:T(8,128)(2,1)S(1)}, u32[]{:S(2)}, u32[]{:S(2)}) %collective-permute-start.27) | collective-permute-done | bytes 344096 | tf_op jit(solution)/shard_map/ppermute | solution.py:97
  168.7 1.7 collective-permute-start.11
  170.5 5.4 %collective-permute-done.11 = bf16[96,1792]{1,0:T(8,128)(2,1)S(1)} collective-permute-done((bf16[96,1792]{1,0:T(8,128)(2,1)S(1)}, bf16[96,1792]{1,0:T(8,128)(2,1)S(1)}, u32[]{:S(2)}, u32[]{:S(2)}) %collective-permute-start.11) | collective-permute-done | bytes 344096 | tf_op jit(solution)/shard_map/ppermute | solution.py:97
  177.8 5.4 %collective-permute-done.28 = bf16[96,1792]{1,0:T(8,128)(2,1)S(1)} collective-permute-done((bf16[96,1792]{1,0:T(8,128)(2,1)S(1)}, bf16[96,1792]{1,0:T(8,128)(2,1)S(1)}, u32[]{:S(2)}, u32[]{:S(2)}) %collective-permute-start.28) | collective-permute-done | bytes 344096 | tf_op jit(solution)/shard_map/ppermute | solution.py:97
  185.0 8.7 %collective-permute-done.12 = bf16[96,1792]{1,0:T(8,128)(2,1)S(1)} collective-permute-done((bf16[96,1792]{1,0:T(8,128)(2,1)S(1)}, bf16[96,1792]{1,0:T(8,128)(2,1)S(1)}, u32[]{:S(2)}, u32[]{:S(2)}) %collective-permute-start.12) | collective-permute-done | bytes 344096 | tf_op jit(solution)/shard_map/ppermute | solution.py:97
  193.7 1.9 collective-permute-start.29
  195.6 1.7 broadcast.177.clone.1
  198.3 2.5 pad_maximum_fusion.3
  200.8 4.7 %collective-permute-done.13 = bf16[96,1792]{1,0:T(8,128)(2,1)S(1)} collective-permute-done((bf16[96,1792]{1,0:T(8,128)(2,1)S(1)}, bf16[96,1792]{1,0:T(8,128)(2,1)S(1)}, u32[]{:S(2)}, u32[]{:S(2)}) %collective-permute-start.13) | collective-permute-done | bytes 344096 | tf_op jit(solution)/shard_map/ppermute | solution.py:103
  205.6 2.9 collective-permute-done.16
  208.4 2.5 pad_maximum_fusion.4
  210.9 1.8 collective-permute-done.14
  216.8 6.6 %collective-permute-done.30 = bf16[96,1792]{1,0:T(8,128)(2,1)} collective-permute-done((bf16[96,1792]{1,0:T(8,128)(2,1)S(1)}, bf16[96,1792]{1,0:T(8,128)(2,1)}, u32[]{:S(2)}, u32[]{:S(2)}) %collective-permute-start.30) | collective-permute-done | bytes 344096 | tf_op jit(solution)/shard_map/ppermute | solution.py:97
  225.1 2.0 constant_dynamic-update-slice_fusion.7
  229.9 7.2 %collective-permute-done.31 = bf16[96,1792]{1,0:T(8,128)(2,1)S(1)} collective-permute-done((bf16[96,1792]{1,0:T(8,128)(2,1)}, bf16[96,1792]{1,0:T(8,128)(2,1)S(1)}, u32[]{:S(2)}, u32[]{:S(2)}) %collective-permute-start.31) | collective-permute-done | bytes 344096 | tf_op jit(solution)/shard_map/ppermute | solution.py:103
  240.6 5.3 %collective-permute-done.32 = bf16[96,1792]{1,0:T(8,128)(2,1)S(1)} collective-permute-done((bf16[96,1792]{1,0:T(8,128)(2,1)S(1)}, bf16[96,1792]{1,0:T(8,128)(2,1)S(1)}, u32[]{:S(2)}, u32[]{:S(2)}) %collective-permute-start.32) | collective-permute-done | bytes 344096 | tf_op jit(solution)/shard_map/ppermute | solution.py:103
  249.4 4.7 %collective-permute-done.33 = bf16[96,1792]{1,0:T(8,128)(2,1)S(1)} collective-permute-done((bf16[96,1792]{1,0:T(8,128)(2,1)S(1)}, bf16[96,1792]{1,0:T(8,128)(2,1)S(1)}, u32[]{:S(2)}, u32[]{:S(2)}) %collective-permute-start.33) | collective-permute-done | bytes 344096 | tf_op jit(solution)/shard_map/ppermute | solution.py:103
  257.7 5.1 %collective-permute-done.34 = bf16[96,1792]{1,0:T(8,128)(2,1)S(1)} collective-permute-done((bf16[96,1792]{1,0:T(8,128)(2,1)S(1)}, bf16[96,1792]{1,0:T(8,128)(2,1)S(1)}, u32[]{:S(2)}, u32[]{:S(2)}) %collective-permute-start.34) | collective-permute-done | bytes 344096 | tf_op jit(solution)/shard_map/ppermute | solution.py:103
  266.4 5.9 %collective-permute-done.35 = bf16[96,1792]{1,0:T(8,128)(2,1)S(1)} collective-permute-done((bf16[96,1792]{1,0:T(8,128)(2,1)S(1)}, bf16[96,1792]{1,0:T(8,128)(2,1)S(1)}, u32[]{:S(2)}, u32[]{:S(2)}) %collective-permute-start.35) | collective-permute-done | bytes 344096 | tf_op jit(solution)/shard_map/ppermute | solution.py:103
  275.8 6.8 %collective-permute-done.36 = bf16[96,1792]{1,0:T(8,128)(2,1)S(1)} collective-permute-done((bf16[96,1792]{1,0:T(8,128)(2,1)S(1)}, bf16[96,1792]{1,0:T(8,128)(2,1)S(1)}, u32[]{:S(2)}, u32[]{:S(2)}) %collective-permute-start.36) | collective-permute-done | bytes 344096 | tf_op jit(solution)/shard_map/ppermute | solution.py:103
  285.7 4.2 %collective-permute-done.37 = bf16[96,1792]{1,0:T(8,128)(2,1)S(1)} collective-permute-done((bf16[96,1792]{1,0:T(8,128)(2,1)S(1)}, bf16[96,1792]{1,0:T(8,128)(2,1)S(1)}, u32[]{:S(2)}, u32[]{:S(2)}) %collective-permute-start.37) | collective-permute-done | bytes 344096 | tf_op jit(solution)/shard_map/ppermute | solution.py:103
  290.6 5.0 %pad_maximum_fusion.1 = bf16[4,896,1280]{2,1,0:T(8,128)(2,1)S(1)} fusion(bf16[2,896,1280]{2,1,0:T(8,128)(2,1)} %collective-permute-done.23, bf16[2,896,1280]{2,1,0:T(8,128)(2,1)} %pad_maximum_fusion.4), kind=kLoop, calls=%fused_computation.10 | loop fusion | flops 4587520 | bytes 18350080 | tf_op jit(solution)/shard_map/concatenate | solution.py:52
  295.7 8.2 %pad_maximum_fusion = bf16[4,896,1280]{2,1,0:T(8,128)(2,1)} fusion(bf16[2,896,1280]{2,1,0:T(8,128)(2,1)} %collective-permute-done.22, bf16[2,896,1280]{2,1,0:T(8,128)(2,1)S(1)} %bitcast.145), kind=kLoop, calls=%fused_computation.9 | loop fusion | flops 4587520 | bytes 18350080 | tf_op jit(solution)/shard_map/concatenate | solution.py:52
  304.7 5.1 %multiply_reduce_fusion = (f32[768]{0:T(1024)S(1)}, f32[768,3584]{1,0:T(8,128)S(1)}) fusion(bf16[768,1792]{1,0:T(8,128)(2,1)} %constant_dynamic-update-slice_fusion, bf16[768,1792]{1,0:T(8,128)(2,1)} %constant_dynamic-update-slice_fusion.8, bf16[768,896]{1,0:T(8,128)(2,1)S(1)} %copy-done.7, bf16[768,896]{1,0:T(8,128)(2,1)S(1)} %copy-done.9, ...), kind=kLoop, calls=%fused_computation.8 | loop fusion | flops 41286912 | bytes 22023168 | tf_op jit(solution)/shard_map/reduce_sum | solution.py:17
  309.8 4.1 %copy-done.1 = f32[768,3584]{1,0:T(8,128)} copy-done((f32[768,3584]{1,0:T(8,128)}, f32[768,3584]{1,0:T(8,128)S(1)}, u32[]{:S(2)}) %copy-start.1) | copy-done | bytes 11010072
  313.9 9.2 %fusion.63 = f32[768,1280]{1,0:T(8,128)} fusion(bf16[3584,1280]{1,0:T(8,128)(2,1)S(1)} %bitcast.146, f32[768,3584]{1,0:T(8,128)S(1)} %get-tuple-element.30, f32[3584]{0:T(1024)S(1)} %pad_maximum_fusion.13, f32[768]{0:T(1024)S(1)} %add_rsqrt_fusion), kind=kOutput, calls=%fused_computation.159 | convolution fusion | flops 7054688256 | bytes 24134656 | tf_op jit(solution)/shard_map/dot_general | solution.py:207
  323.1 15.6 %fusion.9 = f32[16,1280]{1,0:T(8,128)S(1)} fusion(f32[768,1280]{1,0:T(8,128)} %fusion.63, s32[768]{0:T(1024)S(1)} %add.528, bf16[3584,1280]{1,0:T(8,128)(2,1)} %bitcast.147, f32[768,3584]{1,0:T(8,128)} %copy-done.1, f32[3584]{0:T(1024)S(1)} %pad_maximum_fusion.13, f32[768]{0:T(1024)S(1)} %add_rsqrt_fusion), kind=kOutput, calls=%fused_computation.24 | convolution fusion | flops 7092080640 | bytes 24219648 | tf_op jit(solution)/shard_map/dot_general | solution.py:214
  340.2 2.9 collective-permute-done.38
  343.9 2.3 fusion.19
  346.3 2.1 convolution_bitcast_fusion
  349.6 5.7 %collective-permute-start.41 = (f32[16,448]{1,0:T(8,128)S(1)}, f32[16,448]{1,0:T(8,128)S(1)}, u32[]{:S(2)}, u32[]{:S(2)}) collective-permute-start(f32[16,448]{1,0:T(8,128)S(1)} %get-tuple-element.45), channel_id=1, source_target_pairs={{0,25},{1,0},{2,1},{3,8},{4,9},{5,16},{6,17},{7,24},{8,27},{9,2},{... | collective-permute-start | bytes 86024 | tf_op jit(solution)/shard_map/ppermute | solution.py:253
  356.1 4.1 %all-to-all-start.1 = ((f32[4,4,448]{2,1,0:T(4,128)}), f32[4,4,448]{2,1,0:T(4,128)S(1)}, u32[]{:S(2)}, u32[]{:S(2)}) async-start(f32[4,4,448]{2,1,0:T(4,128)} %fusion.51), calls=%async_computation.1 | async-start | bytes 65536 | tf_op jit(solution)/shard_map/all_to_all | solution.py:257
  360.3 3.6 collective-permute-start.43
  365.9 1.9 collective-permute-start.47
  369.6 2.1 collective-permute-done.46
  (215 shorter events, 80.7 us)
Async XLA Ops:
  0.0 346.3 %copy-start = (bf16[896,1280]{1,0:T(8,128)(2,1)S(1)}, bf16[896,1280]{1,0:T(8,128)(2,1)}, u32[]{:S(2)}) copy-start(bf16[896,1280]{1,0:T(8,128)(2,1)} %param.24) | copy-start | bytes 6881284
  2.3 25.0 %copy-start.17 = (f32[3584]{0:T(1024)S(1)}, f32[3584]{0:T(1024)}, u32[]{:S(2)}) copy-start(f32[3584]{0:T(1024)} %param.16) | copy-start | bytes 43012
  4.3 18.7 %collective-permute-start.2 = (bf16[896,384]{1,0:T(8,128)(2,1)}, bf16[896,384]{1,0:T(8,128)(2,1)}, u32[]{:S(2)}, u32[]{:S(2)}) collective-permute-start(bf16[896,384]{1,0:T(8,128)(2,1)} %pad_maximum_fusion.9), channel_id=1, source_target_pairs={{0,16},{8,24},{16,0},{24,8},{1,17},{9,25},{17,1},{25,9},{2,18},{10... | collective-permute-start | bytes 2064392 | tf_op jit(solution)/shard_map/ppermute | solution.py:45
  25.5 6.5 %collective-permute-start.3 = (bf16[2,896,384]{2,1,0:T(8,128)(2,1)}, bf16[2,896,384]{2,1,0:T(8,128)(2,1)}, u32[]{:S(2)}, u32[]{:S(2)}) collective-permute-start(bf16[2,896,384]{2,1,0:T(8,128)(2,1)} %pad_maximum_fusion.7), channel_id=1, source_target_pairs={{0,8},{8,0},{16,24},{24,16},{1,9},{9,1},{17,25},{25,17},{2,10},{10... | collective-permute-start | bytes 4128776 | tf_op jit(solution)/shard_map/ppermute | solution.py:51
  39.4 11.5 %copy-start.20 = (s32[2,8]{1,0:T(2,128)S(1)}, s32[2,8]{1,0:T(2,128)}, u32[]{:S(2)}) copy-start(s32[2,8]{1,0:T(2,128)} %param.14) | copy-start | bytes 196
  39.4 27.5 %copy-start.15 = (bf16[896,256]{1,0:T(8,128)(2,1)S(1)}, bf16[896,256]{1,0:T(8,128)(2,1)}, u32[]{:S(2)}) copy-start(bf16[896,256]{1,0:T(8,128)(2,1)} %param.20) | copy-start | bytes 1376260
  39.4 30.6 %slice-start.2 = ((bf16[768,384]{0,1:T(8,128)(2,1)}), bf16[768,256]{0,1:T(8,128)(2,1)S(1)}, s32[]{:S(2)}) async-start(bf16[768,384]{0,1:T(8,128)(2,1)} %copy-done.16), calls=%async_computation.4 | async-start | bytes 786432 | tf_op jit(solution)/shard_map/slice | solution.py:160
  44.9 36.3 %all-to-all-start = ((bf16[8,768,32]{1,2,0:T(8,128)(2,1)}), bf16[8,768,32]{1,2,0:T(8,128)(2,1)S(1)}, u32[]{:S(2)}, u32[]{:S(2)}) async-start(bf16[8,768,32]{1,2,0:T(8,128)(2,1)} %fusion.41), calls=%async_computation | async-start | bytes 786432 | tf_op jit(solution)/shard_map/all_to_all | solution.py:174
  51.5 163.8 %collective-permute-start.48 = (s32[16]{0:T(128)}, s32[16]{0:T(128)}, u32[]{:S(2)}, u32[]{:S(2)}) collective-permute-start(s32[16]{0:T(128)} %reshape.147), channel_id=1, source_target_pairs={{0,16},{8,24},{16,0},{24,8},{1,17},{9,25},{17,1},{25,9},{2,18},{10... | collective-permute-start | bytes 200 | tf_op jit(solution)/shard_map/ppermute | solution.py:45
  53.0 162.3 %collective-permute-start = (s32[16]{0:T(128)}, s32[16]{0:T(128)}, u32[]{:S(2)}, u32[]{:S(2)}) collective-permute-start(s32[16]{0:T(128)} %bitcast.1), channel_id=1, source_target_pairs={{0,16},{8,24},{16,0},{24,8},{1,17},{9,25},{17,1},{25,9},{2,18},{10... | collective-permute-start | bytes 200 | tf_op jit(solution)/shard_map/ppermute | solution.py:45
  66.9 12.2 %collective-permute-start.4 = (bf16[896,256]{1,0:T(8,128)(2,1)S(1)}, bf16[896,256]{1,0:T(8,128)(2,1)}, u32[]{:S(2)}, u32[]{:S(2)}) collective-permute-start(bf16[896,256]{1,0:T(8,128)(2,1)S(1)} %copy-done.15), channel_id=1, source_target_pairs={{0,16},{8,24},{16,0},{24,8},{1,17},{9,25},{17,1},{25,9},{2,18},{10... | collective-permute-start | bytes 1376264 | tf_op jit(solution)/shard_map/ppermute | solution.py:45
  81.2 6.7 %collective-permute-start.5 = (bf16[2,896,256]{2,1,0:T(8,128)(2,1)}, bf16[2,896,256]{2,1,0:T(8,128)(2,1)}, u32[]{:S(2)}, u32[]{:S(2)}) collective-permute-start(bf16[2,896,256]{2,1,0:T(8,128)(2,1)} %pad_maximum_fusion.8), channel_id=1, source_target_pairs={{0,8},{8,0},{16,24},{24,16},{1,9},{9,1},{17,25},{25,17},{2,10},{10... | collective-permute-start | bytes 2752520 | tf_op jit(solution)/shard_map/ppermute | solution.py:51
  94.4 10.5 %collective-permute-start.6 = (bf16[96,1792]{1,0:T(8,128)(2,1)S(1)}, bf16[96,1792]{1,0:T(8,128)(2,1)S(1)}, u32[]{:S(2)}, u32[]{:S(2)}) collective-permute-start(bf16[96,1792]{1,0:T(8,128)(2,1)S(1)} %constant_dynamic-slice_fusion.3), channel_id=1, source_target_pairs={{0,2},{2,4},{4,6},{6,7},{7,5},{5,3},{3,1},{1,0},{8,10},{10,12},{12... | collective-permute-start | bytes 1032200 | tf_op jit(solution)/shard_map/ppermute | solution.py:97
  96.2 30.1 %copy-start.10 = (bf16[768,1792]{1,0:T(8,128)(2,1)S(1)}, bf16[768,1792]{1,0:T(8,128)(2,1)}, u32[]{:S(2)}) copy-start(bf16[768,1792]{1,0:T(8,128)(2,1)} %get-tuple-element.36) | copy-start | bytes 8257540
  97.1 51.6 %copy-start.12 = (bf16[768,1792]{1,0:T(8,128)(2,1)S(1)}, bf16[768,1792]{1,0:T(8,128)(2,1)}, u32[]{:S(2)}) copy-start(bf16[768,1792]{1,0:T(8,128)(2,1)} %copy-done.11) | copy-start | bytes 8257540
  106.0 9.7 %collective-permute-start.7 = (bf16[96,1792]{1,0:T(8,128)(2,1)S(1)}, bf16[96,1792]{1,0:T(8,128)(2,1)S(1)}, u32[]{:S(2)}, u32[]{:S(2)}) collective-permute-start(bf16[96,1792]{1,0:T(8,128)(2,1)S(1)} %add_convert_fusion.13), channel_id=1, source_target_pairs={{0,2},{2,4},{4,6},{6,7},{7,5},{5,3},{3,1},{1,0},{8,10},{10,12},{12... | collective-permute-start | bytes 1032200 | tf_op jit(solution)/shard_map/ppermute | solution.py:97
  107.9 90.3 %collective-permute-start.15 = (bf16[896,1280]{1,0:T(8,128)(2,1)}, bf16[896,1280]{1,0:T(8,128)(2,1)S(1)}, u32[]{:S(2)}, u32[]{:S(2)}) collective-permute-start(bf16[896,1280]{1,0:T(8,128)(2,1)} %param.22), channel_id=1, source_target_pairs={{0,16},{8,24},{16,0},{24,8},{1,17},{9,25},{17,1},{25,9},{2,18},{10... | collective-permute-start | bytes 6881288 | tf_op jit(solution)/shard_map/ppermute | solution.py:45
  109.4 99.1 %collective-permute-start.16 = (bf16[896,1280]{1,0:T(8,128)(2,1)}, bf16[896,1280]{1,0:T(8,128)(2,1)S(1)}, u32[]{:S(2)}, u32[]{:S(2)}) collective-permute-start(bf16[896,1280]{1,0:T(8,128)(2,1)} %param.23), channel_id=1, source_target_pairs={{0,16},{8,24},{16,0},{24,8},{1,17},{9,25},{17,1},{25,9},{2,18},{10... | collective-permute-start | bytes 6881288 | tf_op jit(solution)/shard_map/ppermute | solution.py:45
  115.7 8.8 %collective-permute-start.24 = (bf16[96,1792]{1,0:T(8,128)(2,1)S(1)}, bf16[96,1792]{1,0:T(8,128)(2,1)S(1)}, u32[]{:S(2)}, u32[]{:S(2)}) collective-permute-start(bf16[96,1792]{1,0:T(8,128)(2,1)S(1)} %constant_dynamic-slice_fusion.2), channel_id=1, source_target_pairs={{0,1},{2,0},{4,2},{6,4},{7,6},{5,7},{3,5},{1,3},{8,9},{10,8},{12,1... | collective-permute-start | bytes 1032200 | tf_op jit(solution)/shard_map/ppermute | solution.py:97
  124.5 7.9 %collective-permute-start.8 = (bf16[96,1792]{1,0:T(8,128)(2,1)S(1)}, bf16[96,1792]{1,0:T(8,128)(2,1)S(1)}, u32[]{:S(2)}, u32[]{:S(2)}) collective-permute-start(bf16[96,1792]{1,0:T(8,128)(2,1)S(1)} %add_convert_fusion.12), channel_id=1, source_target_pairs={{0,2},{2,4},{4,6},{6,7},{7,5},{5,3},{3,1},{1,0},{8,10},{10,12},{12... | collective-permute-start | bytes 1032200 | tf_op jit(solution)/shard_map/ppermute | solution.py:97
  132.4 7.2 %collective-permute-start.25 = (bf16[96,1792]{1,0:T(8,128)(2,1)S(1)}, bf16[96,1792]{1,0:T(8,128)(2,1)S(1)}, u32[]{:S(2)}, u32[]{:S(2)}) collective-permute-start(bf16[96,1792]{1,0:T(8,128)(2,1)S(1)} %add_convert_fusion.6), channel_id=1, source_target_pairs={{0,1},{2,0},{4,2},{6,4},{7,6},{5,7},{3,5},{1,3},{8,9},{10,8},{12,1... | collective-permute-start | bytes 1032200 | tf_op jit(solution)/shard_map/ppermute | solution.py:97
  139.7 7.2 %collective-permute-start.9 = (bf16[96,1792]{1,0:T(8,128)(2,1)S(1)}, bf16[96,1792]{1,0:T(8,128)(2,1)S(1)}, u32[]{:S(2)}, u32[]{:S(2)}) collective-permute-start(bf16[96,1792]{1,0:T(8,128)(2,1)S(1)} %add_convert_fusion.11), channel_id=1, source_target_pairs={{0,2},{2,4},{4,6},{6,7},{7,5},{5,3},{3,1},{1,0},{8,10},{10,12},{12... | collective-permute-start | bytes 1032200 | tf_op jit(solution)/shard_map/ppermute | solution.py:97
  146.9 7.2 %collective-permute-start.26 = (bf16[96,1792]{1,0:T(8,128)(2,1)S(1)}, bf16[96,1792]{1,0:T(8,128)(2,1)S(1)}, u32[]{:S(2)}, u32[]{:S(2)}) collective-permute-start(bf16[96,1792]{1,0:T(8,128)(2,1)S(1)} %add_convert_fusion.5), channel_id=1, source_target_pairs={{0,1},{2,0},{4,2},{6,4},{7,6},{5,7},{3,5},{1,3},{8,9},{10,8},{12,1... | collective-permute-start | bytes 1032200 | tf_op jit(solution)/shard_map/ppermute | solution.py:97
  154.2 7.2 %collective-permute-start.10 = (bf16[96,1792]{1,0:T(8,128)(2,1)S(1)}, bf16[96,1792]{1,0:T(8,128)(2,1)S(1)}, u32[]{:S(2)}, u32[]{:S(2)}) collective-permute-start(bf16[96,1792]{1,0:T(8,128)(2,1)S(1)} %add_convert_fusion.10), channel_id=1, source_target_pairs={{0,2},{2,4},{4,6},{6,7},{7,5},{5,3},{3,1},{1,0},{8,10},{10,12},{12... | collective-permute-start | bytes 1032200 | tf_op jit(solution)/shard_map/ppermute | solution.py:97
  161.4 7.2 %collective-permute-start.27 = (bf16[96,1792]{1,0:T(8,128)(2,1)S(1)}, bf16[96,1792]{1,0:T(8,128)(2,1)S(1)}, u32[]{:S(2)}, u32[]{:S(2)}) collective-permute-start(bf16[96,1792]{1,0:T(8,128)(2,1)S(1)} %add_convert_fusion.4), channel_id=1, source_target_pairs={{0,1},{2,0},{4,2},{6,4},{7,6},{5,7},{3,5},{1,3},{8,9},{10,8},{12,1... | collective-permute-start | bytes 1032200 | tf_op jit(solution)/shard_map/ppermute | solution.py:97
  168.7 7.3 %collective-permute-start.11 = (bf16[96,1792]{1,0:T(8,128)(2,1)S(1)}, bf16[96,1792]{1,0:T(8,128)(2,1)S(1)}, u32[]{:S(2)}, u32[]{:S(2)}) collective-permute-start(bf16[96,1792]{1,0:T(8,128)(2,1)S(1)} %add_convert_fusion.9), channel_id=1, source_target_pairs={{0,2},{2,4},{4,6},{6,7},{7,5},{5,3},{3,1},{1,0},{8,10},{10,12},{12... | collective-permute-start | bytes 1032200 | tf_op jit(solution)/shard_map/ppermute | solution.py:97
  175.9 7.2 %collective-permute-start.28 = (bf16[96,1792]{1,0:T(8,128)(2,1)S(1)}, bf16[96,1792]{1,0:T(8,128)(2,1)S(1)}, u32[]{:S(2)}, u32[]{:S(2)}) collective-permute-start(bf16[96,1792]{1,0:T(8,128)(2,1)S(1)} %add_convert_fusion.3), channel_id=1, source_target_pairs={{0,1},{2,0},{4,2},{6,4},{7,6},{5,7},{3,5},{1,3},{8,9},{10,8},{12,1... | collective-permute-start | bytes 1032200 | tf_op jit(solution)/shard_map/ppermute | solution.py:97
  177.7 20.6 %copy-start.13 = (bf16[896,1280]{1,0:T(8,128)(2,1)S(1)}, bf16[896,1280]{1,0:T(8,128)(2,1)}, u32[]{:S(2)}) copy-start(bf16[896,1280]{1,0:T(8,128)(2,1)} %param.22) | copy-start | bytes 6881284
  183.2 10.5 %collective-permute-start.12 = (bf16[96,1792]{1,0:T(8,128)(2,1)S(1)}, bf16[96,1792]{1,0:T(8,128)(2,1)S(1)}, u32[]{:S(2)}, u32[]{:S(2)}) collective-permute-start(bf16[96,1792]{1,0:T(8,128)(2,1)S(1)} %add_convert_fusion.8), channel_id=1, source_target_pairs={{0,2},{2,4},{4,6},{6,7},{7,5},{5,3},{3,1},{1,0},{8,10},{10,12},{12... | collective-permute-start | bytes 1032200 | tf_op jit(solution)/shard_map/ppermute | solution.py:97
  193.7 19.0 %collective-permute-start.29 = (bf16[96,1792]{1,0:T(8,128)(2,1)S(1)}, bf16[96,1792]{1,0:T(8,128)(2,1)S(1)}, u32[]{:S(2)}, u32[]{:S(2)}) collective-permute-start(bf16[96,1792]{1,0:T(8,128)(2,1)S(1)} %add_convert_fusion.2), channel_id=1, source_target_pairs={{0,1},{2,0},{4,2},{6,4},{7,6},{5,7},{3,5},{1,3},{8,9},{10,8},{12,1... | collective-permute-start | bytes 1032200 | tf_op jit(solution)/shard_map/ppermute | solution.py:97
  198.2 7.3 %collective-permute-start.13 = (bf16[96,1792]{1,0:T(8,128)(2,1)S(1)}, bf16[96,1792]{1,0:T(8,128)(2,1)S(1)}, u32[]{:S(2)}, u32[]{:S(2)}) collective-permute-start(bf16[96,1792]{1,0:T(8,128)(2,1)S(1)} %get-tuple-element.32), channel_id=1, source_target_pairs={{0,2},{2,4},{4,6},{6,7},{7,5},{5,3},{3,1},{1,0},{8,10},{10,12},{12... | collective-permute-start | bytes 1032200 | tf_op jit(solution)/shard_map/ppermute | solution.py:103
  198.3 10.1 %copy-start.14 = (bf16[896,1280]{1,0:T(8,128)(2,1)S(1)}, bf16[896,1280]{1,0:T(8,128)(2,1)}, u32[]{:S(2)}) copy-start(bf16[896,1280]{1,0:T(8,128)(2,1)} %param.23) | copy-start | bytes 6881284
  205.4 7.2 %collective-permute-start.14 = (bf16[96,1792]{1,0:T(8,128)(2,1)S(1)}, bf16[96,1792]{1,0:T(8,128)(2,1)S(1)}, u32[]{:S(2)}, u32[]{:S(2)}) collective-permute-start(bf16[96,1792]{1,0:T(8,128)(2,1)S(1)} %collective-permute-done.13), channel_id=1, source_target_pairs={{0,2},{2,4},{4,6},{6,7},{7,5},{5,3},{3,1},{1,0},{8,10},{10,12},{12... | collective-permute-start | bytes 1032200 | tf_op jit(solution)/shard_map/ppermute | solution.py:103
  212.7 77.9 %collective-permute-start.23 = (bf16[2,896,1280]{2,1,0:T(8,128)(2,1)}, bf16[2,896,1280]{2,1,0:T(8,128)(2,1)}, u32[]{:S(2)}, u32[]{:S(2)}) collective-permute-start(bf16[2,896,1280]{2,1,0:T(8,128)(2,1)} %pad_maximum_fusion.4), channel_id=1, source_target_pairs={{0,8},{8,0},{16,24},{24,16},{1,9},{9,1},{17,25},{25,17},{2,10},{10... | collective-permute-start | bytes 13762568 | tf_op jit(solution)/shard_map/ppermute | solution.py:51
  212.8 10.6 %collective-permute-start.30 = (bf16[96,1792]{1,0:T(8,128)(2,1)S(1)}, bf16[96,1792]{1,0:T(8,128)(2,1)}, u32[]{:S(2)}, u32[]{:S(2)}) collective-permute-start(bf16[96,1792]{1,0:T(8,128)(2,1)S(1)} %add_convert_fusion.1), channel_id=1, source_target_pairs={{0,1},{2,0},{4,2},{6,4},{7,6},{5,7},{3,5},{1,3},{8,9},{10,8},{12,1... | collective-permute-start | bytes 1032200 | tf_op jit(solution)/shard_map/ppermute | solution.py:97
  216.1 12.6 %collective-permute-start.1 = (s32[2,16]{1,0:T(2,128)S(1)}, s32[2,16]{1,0:T(2,128)S(1)}, u32[]{:S(2)}, u32[]{:S(2)}) collective-permute-start(s32[2,16]{1,0:T(2,128)S(1)} %get-tuple-element.75), channel_id=1, source_target_pairs={{0,8},{8,0},{16,24},{24,16},{1,9},{9,1},{17,25},{25,17},{2,10},{10... | collective-permute-start | bytes 392 | tf_op jit(solution)/shard_map/ppermute | solution.py:51
  216.3 126.9 %collective-permute-start.49 = (s32[2,16]{1,0:T(2,128)S(1)}, s32[2,16]{1,0:T(2,128)S(1)}, u32[]{:S(2)}, u32[]{:S(2)}) collective-permute-start(s32[2,16]{1,0:T(2,128)S(1)} %get-tuple-element.76), channel_id=1, source_target_pairs={{0,8},{8,0},{16,24},{24,16},{1,9},{9,1},{17,25},{25,17},{2,10},{10... | collective-permute-start | bytes 392 | tf_op jit(solution)/shard_map/ppermute | solution.py:51
  216.6 79.1 %collective-permute-start.22 = (bf16[2,896,1280]{2,1,0:T(8,128)(2,1)}, bf16[2,896,1280]{2,1,0:T(8,128)(2,1)}, u32[]{:S(2)}, u32[]{:S(2)}) collective-permute-start(bf16[2,896,1280]{2,1,0:T(8,128)(2,1)} %pad_maximum_fusion.3), channel_id=1, source_target_pairs={{0,8},{8,0},{16,24},{24,16},{1,9},{9,1},{17,25},{25,17},{2,10},{10... | collective-permute-start | bytes 13762568 | tf_op jit(solution)/shard_map/ppermute | solution.py:51
  227.2 9.9 %collective-permute-start.31 = (bf16[96,1792]{1,0:T(8,128)(2,1)}, bf16[96,1792]{1,0:T(8,128)(2,1)S(1)}, u32[]{:S(2)}, u32[]{:S(2)}) collective-permute-start(bf16[96,1792]{1,0:T(8,128)(2,1)} %get-tuple-element.34), channel_id=1, source_target_pairs={{0,1},{2,0},{4,2},{6,4},{7,6},{5,7},{3,5},{1,3},{8,9},{10,8},{12,1... | collective-permute-start | bytes 1032200 | tf_op jit(solution)/shard_map/ppermute | solution.py:103
  237.1 8.8 %collective-permute-start.32 = (bf16[96,1792]{1,0:T(8,128)(2,1)S(1)}, bf16[96,1792]{1,0:T(8,128)(2,1)S(1)}, u32[]{:S(2)}, u32[]{:S(2)}) collective-permute-start(bf16[96,1792]{1,0:T(8,128)(2,1)S(1)} %collective-permute-done.31), channel_id=1, source_target_pairs={{0,1},{2,0},{4,2},{6,4},{7,6},{5,7},{3,5},{1,3},{8,9},{10,8},{12,1... | collective-permute-start | bytes 1032200 | tf_op jit(solution)/shard_map/ppermute | solution.py:103
  240.2 8.8 %collective-permute-start.17 = (bf16[96,1792]{1,0:T(8,128)(2,1)S(1)}, bf16[96,1792]{1,0:T(8,128)(2,1)S(1)}, u32[]{:S(2)}, u32[]{:S(2)}) collective-permute-start(bf16[96,1792]{1,0:T(8,128)(2,1)S(1)} %collective-permute-done.14), channel_id=1, source_target_pairs={{0,2},{2,4},{4,6},{6,7},{7,5},{5,3},{3,1},{1,0},{8,10},{10,12},{12... | collective-permute-start | bytes 1032200 | tf_op jit(solution)/shard_map/ppermute | solution.py:103
  245.9 8.2 %collective-permute-start.33 = (bf16[96,1792]{1,0:T(8,128)(2,1)S(1)}, bf16[96,1792]{1,0:T(8,128)(2,1)S(1)}, u32[]{:S(2)}, u32[]{:S(2)}) collective-permute-start(bf16[96,1792]{1,0:T(8,128)(2,1)S(1)} %collective-permute-done.32), channel_id=1, source_target_pairs={{0,1},{2,0},{4,2},{6,4},{7,6},{5,7},{3,5},{1,3},{8,9},{10,8},{12,1... | collective-permute-start | bytes 1032200 | tf_op jit(solution)/shard_map/ppermute | solution.py:103
  248.9 8.2 %collective-permute-start.18 = (bf16[96,1792]{1,0:T(8,128)(2,1)S(1)}, bf16[96,1792]{1,0:T(8,128)(2,1)S(1)}, u32[]{:S(2)}, u32[]{:S(2)}) collective-permute-start(bf16[96,1792]{1,0:T(8,128)(2,1)S(1)} %collective-permute-done.17), channel_id=1, source_target_pairs={{0,2},{2,4},{4,6},{6,7},{7,5},{5,3},{3,1},{1,0},{8,10},{10,12},{12... | collective-permute-start | bytes 1032200 | tf_op jit(solution)/shard_map/ppermute | solution.py:103
  254.1 8.7 %collective-permute-start.34 = (bf16[96,1792]{1,0:T(8,128)(2,1)S(1)}, bf16[96,1792]{1,0:T(8,128)(2,1)S(1)}, u32[]{:S(2)}, u32[]{:S(2)}) collective-permute-start(bf16[96,1792]{1,0:T(8,128)(2,1)S(1)} %collective-permute-done.33), channel_id=1, source_target_pairs={{0,1},{2,0},{4,2},{6,4},{7,6},{5,7},{3,5},{1,3},{8,9},{10,8},{12,1... | collective-permute-start | bytes 1032200 | tf_op jit(solution)/shard_map/ppermute | solution.py:103
  257.2 8.7 %collective-permute-start.19 = (bf16[96,1792]{1,0:T(8,128)(2,1)S(1)}, bf16[96,1792]{1,0:T(8,128)(2,1)S(1)}, u32[]{:S(2)}, u32[]{:S(2)}) collective-permute-start(bf16[96,1792]{1,0:T(8,128)(2,1)S(1)} %collective-permute-done.18), channel_id=1, source_target_pairs={{0,2},{2,4},{4,6},{6,7},{7,5},{5,3},{3,1},{1,0},{8,10},{10,12},{12... | collective-permute-start | bytes 1032200 | tf_op jit(solution)/shard_map/ppermute | solution.py:103
  262.8 9.5 %collective-permute-start.35 = (bf16[96,1792]{1,0:T(8,128)(2,1)S(1)}, bf16[96,1792]{1,0:T(8,128)(2,1)S(1)}, u32[]{:S(2)}, u32[]{:S(2)}) collective-permute-start(bf16[96,1792]{1,0:T(8,128)(2,1)S(1)} %collective-permute-done.34), channel_id=1, source_target_pairs={{0,1},{2,0},{4,2},{6,4},{7,6},{5,7},{3,5},{1,3},{8,9},{10,8},{12,1... | collective-permute-start | bytes 1032200 | tf_op jit(solution)/shard_map/ppermute | solution.py:103
  265.9 9.5 %collective-permute-start.20 = (bf16[96,1792]{1,0:T(8,128)(2,1)S(1)}, bf16[96,1792]{1,0:T(8,128)(2,1)S(1)}, u32[]{:S(2)}, u32[]{:S(2)}) collective-permute-start(bf16[96,1792]{1,0:T(8,128)(2,1)S(1)} %collective-permute-done.19), channel_id=1, source_target_pairs={{0,2},{2,4},{4,6},{6,7},{7,5},{5,3},{3,1},{1,0},{8,10},{10,12},{12... | collective-permute-start | bytes 1032200 | tf_op jit(solution)/shard_map/ppermute | solution.py:103
  272.2 10.4 %collective-permute-start.36 = (bf16[96,1792]{1,0:T(8,128)(2,1)S(1)}, bf16[96,1792]{1,0:T(8,128)(2,1)S(1)}, u32[]{:S(2)}, u32[]{:S(2)}) collective-permute-start(bf16[96,1792]{1,0:T(8,128)(2,1)S(1)} %collective-permute-done.35), channel_id=1, source_target_pairs={{0,1},{2,0},{4,2},{6,4},{7,6},{5,7},{3,5},{1,3},{8,9},{10,8},{12,1... | collective-permute-start | bytes 1032200 | tf_op jit(solution)/shard_map/ppermute | solution.py:103
  275.4 28.5 %collective-permute-start.21 = (bf16[96,1792]{1,0:T(8,128)(2,1)S(1)}, bf16[96,1792]{1,0:T(8,128)(2,1)S(1)}, u32[]{:S(2)}, u32[]{:S(2)}) collective-permute-start(bf16[96,1792]{1,0:T(8,128)(2,1)S(1)} %collective-permute-done.20), channel_id=1, source_target_pairs={{0,2},{2,4},{4,6},{6,7},{7,5},{5,3},{3,1},{1,0},{8,10},{10,12},{12... | collective-permute-start | bytes 1032200 | tf_op jit(solution)/shard_map/ppermute | solution.py:103
  282.6 7.2 %collective-permute-start.37 = (bf16[96,1792]{1,0:T(8,128)(2,1)S(1)}, bf16[96,1792]{1,0:T(8,128)(2,1)S(1)}, u32[]{:S(2)}, u32[]{:S(2)}) collective-permute-start(bf16[96,1792]{1,0:T(8,128)(2,1)S(1)} %collective-permute-done.36), channel_id=1, source_target_pairs={{0,1},{2,0},{4,2},{6,4},{7,6},{5,7},{3,5},{1,3},{8,9},{10,8},{12,1... | collective-permute-start | bytes 1032200 | tf_op jit(solution)/shard_map/ppermute | solution.py:103
  295.6 9.1 %copy-start.3 = (bf16[768,896]{1,0:T(8,128)(2,1)S(1)}, bf16[768,896]{1,0:T(8,128)(2,1)}, u32[]{:S(2)}) copy-start(bf16[768,896]{1,0:T(8,128)(2,1)} %copy-done.2) | copy-start | bytes 4128772
  295.6 9.1 %copy-start.5 = (bf16[768,896]{1,0:T(8,128)(2,1)S(1)}, bf16[768,896]{1,0:T(8,128)(2,1)}, u32[]{:S(2)}) copy-start(bf16[768,896]{1,0:T(8,128)(2,1)} %copy-done.4) | copy-start | bytes 4128772
  295.6 9.1 %copy-start.7 = (bf16[768,896]{1,0:T(8,128)(2,1)S(1)}, bf16[768,896]{1,0:T(8,128)(2,1)}, u32[]{:S(2)}) copy-start(bf16[768,896]{1,0:T(8,128)(2,1)} %copy-done.6) | copy-start | bytes 4128772
  338.6 4.4 %collective-permute-start.38 = (f32[16,1280]{1,0:T(8,128)S(1)}, f32[16,1280]{1,0:T(8,128)S(1)}, u32[]{:S(2)}, u32[]{:S(2)}) collective-permute-start(f32[16,1280]{1,0:T(8,128)S(1)} %fusion.9), channel_id=1, source_target_pairs={{0,16},{8,24},{16,0},{24,8},{1,17},{9,25},{17,1},{25,9},{2,18},{10... | collective-permute-start | bytes 245768 | tf_op jit(solution)/shard_map/ppermute | solution.py:45
  343.1 3.2 collective-permute-start.39
  348.9 14.9 %collective-permute-start.40 = (f32[16,448]{1,0:T(8,128)S(1)}, f32[16,448]{1,0:T(8,128)S(1)}, u32[]{:S(2)}, u32[]{:S(2)}) collective-permute-start(f32[16,448]{1,0:T(8,128)S(1)} %get-tuple-element.52), channel_id=1, source_target_pairs={{0,0},{1,1},{2,8},{3,9},{4,16},{5,17},{6,24},{7,25},{8,2},{9,3},{1... | collective-permute-start | bytes 86024 | tf_op jit(solution)/shard_map/ppermute | solution.py:253
  349.6 15.9 %collective-permute-start.41 = (f32[16,448]{1,0:T(8,128)S(1)}, f32[16,448]{1,0:T(8,128)S(1)}, u32[]{:S(2)}, u32[]{:S(2)}) collective-permute-start(f32[16,448]{1,0:T(8,128)S(1)} %get-tuple-element.45), channel_id=1, source_target_pairs={{0,25},{1,0},{2,1},{3,8},{4,9},{5,16},{6,17},{7,24},{8,27},{9,2},{... | collective-permute-start | bytes 86024 | tf_op jit(solution)/shard_map/ppermute | solution.py:253
  355.3 10.5 %collective-permute-start.42 = (f32[16,448]{1,0:T(8,128)S(1)}, f32[16,448]{1,0:T(8,128)S(1)}, u32[]{:S(2)}, u32[]{:S(2)}) collective-permute-start(f32[16,448]{1,0:T(8,128)S(1)} %get-tuple-element.51), channel_id=1, source_target_pairs={{0,24},{1,25},{2,0},{3,1},{4,8},{5,9},{6,16},{7,17},{8,26},{9,27},... | collective-permute-start | bytes 86024 | tf_op jit(solution)/shard_map/ppermute | solution.py:253
  356.1 11.8 %all-to-all-start.1 = ((f32[4,4,448]{2,1,0:T(4,128)}), f32[4,4,448]{2,1,0:T(4,128)S(1)}, u32[]{:S(2)}, u32[]{:S(2)}) async-start(f32[4,4,448]{2,1,0:T(4,128)} %fusion.51), calls=%async_computation.1 | async-start | bytes 65536 | tf_op jit(solution)/shard_map/all_to_all | solution.py:257
  360.3 7.7 %collective-permute-start.43 = (f32[16,448]{1,0:T(8,128)S(1)}, f32[16,448]{1,0:T(8,128)S(1)}, u32[]{:S(2)}, u32[]{:S(2)}) collective-permute-start(f32[16,448]{1,0:T(8,128)S(1)} %get-tuple-element.50), channel_id=1, source_target_pairs={{0,17},{1,24},{2,25},{3,0},{4,1},{5,8},{6,9},{7,16},{8,19},{9,26},... | collective-permute-start | bytes 86024 | tf_op jit(solution)/shard_map/ppermute | solution.py:253
  363.9 4.9 %collective-permute-start.44 = (f32[16,448]{1,0:T(8,128)S(1)}, f32[16,448]{1,0:T(8,128)S(1)}, u32[]{:S(2)}, u32[]{:S(2)}) collective-permute-start(f32[16,448]{1,0:T(8,128)S(1)} %get-tuple-element.49), channel_id=1, source_target_pairs={{0,16},{1,17},{2,24},{3,25},{4,0},{5,1},{6,8},{7,9},{8,18},{9,19},... | collective-permute-start | bytes 86024 | tf_op jit(solution)/shard_map/ppermute | solution.py:253
  363.9 5.7 %collective-permute-start.45 = (f32[16,448]{1,0:T(8,128)S(1)}, f32[16,448]{1,0:T(8,128)S(1)}, u32[]{:S(2)}, u32[]{:S(2)}) collective-permute-start(f32[16,448]{1,0:T(8,128)S(1)} %get-tuple-element.48), channel_id=1, source_target_pairs={{0,9},{1,16},{2,17},{3,24},{4,25},{5,0},{6,1},{7,8},{8,11},{9,18},... | collective-permute-start | bytes 86024 | tf_op jit(solution)/shard_map/ppermute | solution.py:253
  365.5 6.2 %collective-permute-start.46 = (f32[16,448]{1,0:T(8,128)S(1)}, f32[16,448]{1,0:T(8,128)S(1)}, u32[]{:S(2)}, u32[]{:S(2)}) collective-permute-start(f32[16,448]{1,0:T(8,128)S(1)} %get-tuple-element.47), channel_id=1, source_target_pairs={{0,8},{1,9},{2,16},{3,17},{4,24},{5,25},{6,0},{7,1},{8,10},{9,11},... | collective-permute-start | bytes 86024 | tf_op jit(solution)/shard_map/ppermute | solution.py:253
  365.9 7.0 %collective-permute-start.47 = (f32[16,448]{1,0:T(8,128)S(1)}, f32[16,448]{1,0:T(8,128)S(1)}, u32[]{:S(2)}, u32[]{:S(2)}) collective-permute-start(f32[16,448]{1,0:T(8,128)S(1)} %get-tuple-element.46), channel_id=1, source_target_pairs={{0,1},{1,8},{2,9},{3,16},{4,17},{5,24},{6,25},{7,0},{8,3},{9,10},{... | collective-permute-start | bytes 86024 | tf_op jit(solution)/shard_map/ppermute | solution.py:253
  (13 other events, 60.9 us)

commit v8 on v5

--- a/solution.py
+++ b/solution.py
@@ -34,6 +34,25 @@
     return lax.dot_general(
         left, right, (((1,), (1,)), ((), ())), preferred_element_type=jnp.float32
     )
+
+
+def gather_grp_halves(piece, chips):
+    held = [piece]
+    moving = piece
+    if chips > 1:
+        ring = [(2 * i + c, 2 * ((i + 1) % chips) + c) for i in range(chips) for c in range(2)]
+        for _ in range(chips - 1):
+            moving = lax.ppermute(moving, "grp", ring)
+            held.append(moving)
+    mine = jnp.stack(held)
+    other = lax.ppermute(mine, "grp", [(g, g ^ 1) for g in range(2 * chips)])
+    return mine.reshape(-1, piece.shape[1]), other.reshape(-1, piece.shape[1])
+
+
+def halves_dot(x, halves):
+    cut = halves[0].shape[0]
+    first = jnp.dot(x[:, :cut], halves[0], preferred_element_type=jnp.float32)
+    return first + jnp.dot(x[:, cut:], halves[1], preferred_element_type=jnp.float32)
 
 
 def gather_grp(piece, chips):
@@ -136,8 +155,8 @@
     o_after, qkv_full = lax.optimization_barrier((o_weight, qkv_full))
     o_full = gather_grp(o_after, chips).reshape(width, -1)
     gate_after, up_after, o_full = lax.optimization_barrier((gate_weight, up_weight, o_full))
-    gate_full = gather_grp(gate_after, chips).reshape(width, -1)
-    up_full = gather_grp(up_after, chips).reshape(width, -1)
+    gate_halves = gather_grp_halves(gate_after, chips)
+    up_halves = gather_grp_halves(up_after, chips)
 
     hidden_perm = take_blocks(hidden_in, order, d_grp, 1)
     attn_gain_perm = take_blocks(attn_gain, order, d_grp, 0)
@@ -184,8 +203,8 @@
     attn_total = ring_psum(attn_term, "tp", tp_size).astype(jnp.float32)
     residual = hidden_perm.astype(jnp.float32) + attn_total
     norm_mid = rms_scale(residual, ffn_gain_perm)
-    gate_pre = jnp.dot(norm_mid, gate_full, preferred_element_type=jnp.float32)
-    up_pre = jnp.dot(norm_mid, up_full, preferred_element_type=jnp.float32)
+    gate_pre = halves_dot(norm_mid, gate_halves)
+    up_pre = halves_dot(norm_mid, up_halves)
     hidden_ffn = (jax.nn.silu(gate_pre) * up_pre).astype(jnp.bfloat16)
 
     block_index = lax.broadcasted_iota(jnp.int32, (blocks, block_rows), 0)

time: 328 us -> 333 us (1.015)
  matrix products: 45.1 us -> 54.5 us
  waiting for transfers between devices: 131 us -> 123 us
  other arithmetic: 51 us -> 46.2 us
  starting transfers between devices: 61.6 us -> 66 us
    ppermute x7 -> x5, waiting for transfers between devices: 43.9 us -> 2.94 us  [gather_grp(): moving = lax.ppermute(moving, 'grp', ring)]
    ppermute x0 -> x4, waiting for transfers between devices: none -> 36.1 us  [the longest x2 36.1 us: gather_grp_halves(): moving = lax.ppermute(moving, 'grp', ring)]
    concatenate x6 -> x4, other arithmetic: 18 us -> 3.04 us  [gather_grp(): return jnp.concatenate([mine, other], 0)]
    dot_general x1 -> x3, matrix products: 11.9 us -> 25.9 us  [the longest x2 15.9 us: halves_dot(): jnp.dot(x[:, cut:], halves[1], preferred_element_type=jnp.float32)]
    convert_element_type x0 -> x1, other arithmetic: none -> 5.87 us  [rms_scale(): return (rows * factor * gain[None, :]).astype(jnp.bfloat16)]
    another operation x7 -> x5, other arithmetic: 9.92 us -> 4.66 us  [gather_grp(): mine = jnp.stack(held)]
    another operation x0 -> x2, other arithmetic: none -> 4.95 us  [gather_grp_halves(): mine = jnp.stack(held)]
    dot_general x1, matrix products: 15.6 us -> 10.9 us  [on_device(): jnp.dot(selector.astype(jnp.bfloat16), hidden_ffn, preferred_element_type...]
  transfers between devices with their start and end apart: 52 -> 52, of which waited for: 25 -> 22; matrix products, arithmetic and copies ran while one was open for 33% -> 35% of each run, Pallas kernels for 0% -> 0%
where the time goes in v8:
time: 333 us; the launch traced here: 329 us
  waiting for transfers between devices  123 us (37%)
  starting transfers between devices  66 us (20%)
  matrix products  54.5 us (16%)
  other arithmetic  46.2 us (14%)
  local copies, waits for them, and re-layouts  23.9 us (7%)
  between operations  15.3 us (5%)
    ppermute x14, waiting for transfers between devices, ring_psum(): moving = lax.ppermute(moving, axis, pairs)  41.9 us
    ppermute x14, waiting for transfers between devices, ring_psum(): got = lax.ppermute(acc, axis, pairs)  39.5 us
    ppermute x2, waiting for transfers between devices, gather_grp_halves(): moving = lax.ppermute(moving, 'grp', ring)  36.1 us
    dot_general x2, matrix products, halves_dot(): jnp.dot(x[:, cut:], halves[1], preferred_element_type=jnp.float32)  15.9 us
    ppermute x14, starting transfers between devices, ring_psum(): got = lax.ppermute(acc, axis, pairs)  15.4 us
    ppermute x14, starting transfers between devices, ring_psum(): moving = lax.ppermute(moving, axis, pairs)  14.6 us
    ppermute x8, starting transfers between devices, on_device(): totals = totals + lax.ppermute(piece, ('grp', 'tp'), pairs)  14.6 us
    dot_general x1, matrix products, on_device(): jnp.dot(selector.astype(jnp.bfloat16), hidden_ffn, preferred_element_type...  10.9 us
  transfers between devices with their start and end apart: 52, of which 22 were waited for; matrix products, arithmetic and copies ran while one was open for 35% of the time, Pallas kernels for 0%

profile of v8, /device:TPU:0, one launch (start us, length us, event | category | flops | bytes accessed | tf_op | source)
XLA Modules:
  0.0 328.5 jit_solution(14558569920051549980)
XLA Ops:
  2.3 2.0 pad_maximum_fusion.7
  4.3 2.9 collective-permute-start.2
  8.6 2.0 collective-permute-start.48
  32.2 3.1 constant_dynamic-slice_fusion.7
  35.3 1.4 fusion.1
  38.2 4.4 %fusion.21 = bf16[768,384]{0,1:T(8,128)(2,1)S(1)} fusion(bf16[3584,384]{1,0:T(8,128)(2,1)S(1)} %bitcast.149, f32[3584]{0:T(1024)S(1)} %pad_maximum_fusion.10, f32[768]{0:T(1024)S(1)} %add_rsqrt_fusion.1, bf16[768,896]{1,0:T(8,128)(2,1)S(1)} %get-tuple-element.27, bf16[768,896]{1,0:T(8,128)(2,1)S(1)} %get-tuple-element.28, ...), kind=kOutput, calls=%fused_computation.34 | convolution fusion | flops 2144501760 | bytes 8864768 | tf_op jit(solution)/shard_map/dot_general | solution.py:166
  48.8 5.8 %all-to-all-start = ((bf16[8,768,32]{1,2,0:T(8,128)(2,1)}), bf16[8,768,32]{1,2,0:T(8,128)(2,1)S(1)}, u32[]{:S(2)}, u32[]{:S(2)}) async-start(bf16[8,768,32]{1,2,0:T(8,128)(2,1)} %fusion.50), calls=%async_computation | async-start | bytes 786432 | tf_op jit(solution)/shard_map/all_to_all | solution.py:181
  65.1 1.3 fusion.47
  66.5 1.4 reduce_window_sum.22
  68.7 2.0 pad_maximum_fusion.6
  71.1 4.1 %fusion.80 = (f32[2,2,384]{2,1,0:T(2,128)}, f32[2,2,384,384]{2,3,1,0:T(8,128)}) fusion(pred[2,384,384]{1,2,0:T(8,128)(4,1)} %broadcast_compare_fusion, bf16[2,384,2,128]{1,0,3,2:T(2,128)(2,1)} %reshape.146, bf16[2,384,128,1]{1,0,2,3:T(2,128)(2,1)S(1)} %bitcast.180), kind=kOutput, calls=%fused_computation.172 | convolution fusion | flops 153354624 | bytes 3250176 | tf_op jit(solution)/shard_map/sub | solution.py:29
  75.1 2.0 fusion.24
  77.6 1.5 pad_maximum_fusion.4
  79.1 1.6 convolution_convert_fusion
  80.8 1.9 fusion.72
  82.7 1.6 copy-done.10
  84.3 2.1 collective-permute-start.20
  87.9 1.5 collective-permute-start.36
  90.0 4.9 %collective-permute-done.20 = bf16[96,1792]{1,0:T(8,128)(2,1)S(1)} collective-permute-done((bf16[96,1792]{1,0:T(8,128)(2,1)S(1)}, bf16[96,1792]{1,0:T(8,128)(2,1)S(1)}, u32[]{:S(2)}, u32[]{:S(2)}) %collective-permute-start.20) | collective-permute-done | bytes 344096 | tf_op jit(solution)/shard_map/ppermute | solution.py:109
  96.0 1.8 collective-permute-start.21
  99.6 6.2 %collective-permute-done.21 = bf16[96,1792]{1,0:T(8,128)(2,1)S(1)} collective-permute-done((bf16[96,1792]{1,0:T(8,128)(2,1)S(1)}, bf16[96,1792]{1,0:T(8,128)(2,1)S(1)}, u32[]{:S(2)}, u32[]{:S(2)}) %collective-permute-start.21) | collective-permute-done | bytes 344096 | tf_op jit(solution)/shard_map/ppermute | solution.py:109
  106.9 1.5 collective-permute-start.22
  109.2 6.7 %collective-permute-done.22 = bf16[96,1792]{1,0:T(8,128)(2,1)S(1)} collective-permute-done((bf16[96,1792]{1,0:T(8,128)(2,1)S(1)}, bf16[96,1792]{1,0:T(8,128)(2,1)S(1)}, u32[]{:S(2)}, u32[]{:S(2)}) %collective-permute-start.22) | collective-permute-done | bytes 344096 | tf_op jit(solution)/shard_map/ppermute | solution.py:109
  116.9 1.3 collective-permute-start.23
  119.3 5.9 %collective-permute-done.23 = bf16[96,1792]{1,0:T(8,128)(2,1)S(1)} collective-permute-done((bf16[96,1792]{1,0:T(8,128)(2,1)S(1)}, bf16[96,1792]{1,0:T(8,128)(2,1)S(1)}, u32[]{:S(2)}, u32[]{:S(2)}) %collective-permute-start.23) | collective-permute-done | bytes 344096 | tf_op jit(solution)/shard_map/ppermute | solution.py:109
  127.6 5.9 %collective-permute-done.24 = bf16[96,1792]{1,0:T(8,128)(2,1)S(1)} collective-permute-done((bf16[96,1792]{1,0:T(8,128)(2,1)S(1)}, bf16[96,1792]{1,0:T(8,128)(2,1)S(1)}, u32[]{:S(2)}, u32[]{:S(2)}) %collective-permute-start.24) | collective-permute-done | bytes 344096 | tf_op jit(solution)/shard_map/ppermute | solution.py:109
  133.6 1.5 collective-permute-start.25
  136.1 6.5 %collective-permute-done.25 = bf16[96,1792]{1,0:T(8,128)(2,1)S(1)} collective-permute-done((bf16[96,1792]{1,0:T(8,128)(2,1)S(1)}, bf16[96,1792]{1,0:T(8,128)(2,1)S(1)}, u32[]{:S(2)}, u32[]{:S(2)}) %collective-permute-start.25) | collective-permute-done | bytes 344096 | tf_op jit(solution)/shard_map/ppermute | solution.py:109
  142.6 1.8 collective-permute-start.26
  145.4 2.5 pad_maximum_fusion.2
  147.9 2.0 collective-permute-done.26
  150.2 1.8 collective-permute-start.27
  153.0 36.1 %collective-permute-done.34 = bf16[896,1280]{1,0:T(8,128)(2,1)S(1)} collective-permute-done((bf16[896,1280]{1,0:T(8,128)(2,1)}, bf16[896,1280]{1,0:T(8,128)(2,1)S(1)}, u32[]{:S(2)}, u32[]{:S(2)}) %collective-permute-start.34) | collective-permute-done | bytes 2293792 | tf_op jit(solution)/shard_map/ppermute | solution.py:45
  189.1 2.5 pad_maximum_fusion.1
  191.6 1.7 collective-permute-start.28
  193.7 8.3 %collective-permute-done.28 = bf16[96,1792]{1,0:T(8,128)(2,1)S(1)} collective-permute-done((bf16[96,1792]{1,0:T(8,128)(2,1)S(1)}, bf16[96,1792]{1,0:T(8,128)(2,1)S(1)}, u32[]{:S(2)}, u32[]{:S(2)}) %collective-permute-start.28) | collective-permute-done | bytes 344096 | tf_op jit(solution)/shard_map/ppermute | solution.py:115
  202.0 1.7 collective-permute-start.29
  204.2 7.5 %collective-permute-done.29 = bf16[96,1792]{1,0:T(8,128)(2,1)S(1)} collective-permute-done((bf16[96,1792]{1,0:T(8,128)(2,1)S(1)}, bf16[96,1792]{1,0:T(8,128)(2,1)S(1)}, u32[]{:S(2)}, u32[]{:S(2)}) %collective-permute-start.29) | collective-permute-done | bytes 344096 | tf_op jit(solution)/shard_map/ppermute | solution.py:115
  211.7 1.7 collective-permute-start.30
  213.9 6.6 %collective-permute-done.30 = bf16[96,1792]{1,0:T(8,128)(2,1)S(1)} collective-permute-done((bf16[96,1792]{1,0:T(8,128)(2,1)S(1)}, bf16[96,1792]{1,0:T(8,128)(2,1)S(1)}, u32[]{:S(2)}, u32[]{:S(2)}) %collective-permute-start.30) | collective-permute-done | bytes 344096 | tf_op jit(solution)/shard_map/ppermute | solution.py:115
  220.5 1.7 collective-permute-start.31
  222.7 6.1 %collective-permute-done.31 = bf16[96,1792]{1,0:T(8,128)(2,1)S(1)} collective-permute-done((bf16[96,1792]{1,0:T(8,128)(2,1)S(1)}, bf16[96,1792]{1,0:T(8,128)(2,1)S(1)}, u32[]{:S(2)}, u32[]{:S(2)}) %collective-permute-start.31) | collective-permute-done | bytes 344096 | tf_op jit(solution)/shard_map/ppermute | solution.py:115
  228.8 1.7 collective-permute-start.32
  230.9 6.5 %collective-permute-done.32 = bf16[96,1792]{1,0:T(8,128)(2,1)S(1)} collective-permute-done((bf16[96,1792]{1,0:T(8,128)(2,1)S(1)}, bf16[96,1792]{1,0:T(8,128)(2,1)S(1)}, u32[]{:S(2)}, u32[]{:S(2)}) %collective-permute-start.32) | collective-permute-done | bytes 344096 | tf_op jit(solution)/shard_map/ppermute | solution.py:115
  237.4 1.7 collective-permute-start.33
  239.7 5.0 %collective-permute-done.33 = bf16[96,1792]{1,0:T(8,128)(2,1)S(1)} collective-permute-done((bf16[96,1792]{1,0:T(8,128)(2,1)S(1)}, bf16[96,1792]{1,0:T(8,128)(2,1)S(1)}, u32[]{:S(2)}, u32[]{:S(2)}) %collective-permute-start.33) | collective-permute-done | bytes 344096 | tf_op jit(solution)/shard_map/ppermute | solution.py:115
  244.7 1.7 collective-permute-done.19
  246.5 5.8 %multiply_reduce_fusion = (f32[768]{0:T(1024)S(1)}, f32[768,3584]{1,0:T(8,128)}) fusion(bf16[768,1792]{1,0:T(8,128)(2,1)S(1)} %constant_dynamic-update-slice_fusion, bf16[768,1792]{1,0:T(8,128)(2,1)S(1)} %constant_dynamic-update-slice_fusion.8, bf16[768,896]{1,0:T(8,128)(2,1)S(1)} %copy-done.6, bf16[768,896]{1,0:T(8,128)(2,1)S(1)} %copy-done.8, ...), kind=kLoop, calls=%fused_computation.8 | loop fusion | flops 41286912 | bytes 22023168 | tf_op jit(solution)/shard_map/reduce_sum | solution.py:17
  252.3 5.9 %multiply_convert_fusion = bf16[768,3584]{1,0:T(8,128)(2,1)S(1)} fusion(f32[768,3584]{1,0:T(8,128)} %get-tuple-element.18, f32[3584]{0:T(1024)S(1)} %pad_maximum_fusion.11, f32[768]{0:T(1024)S(1)} %add_rsqrt_fusion), kind=kLoop, calls=%fused_computation.7 | loop fusion | flops 8257536 | bytes 16532480 | tf_op jit(solution)/shard_map/convert_element_type | solution.py:18
  258.2 9.9 %fusion.13 = f32[768,1280]{1,0:T(8,128)} fusion(bf16[1792,1280]{1,0:T(8,128)(2,1)} %bitcast.34, bf16[768,3584]{1,0:T(8,128)(2,1)S(1)} %multiply_convert_fusion), kind=kOutput, calls=%fused_computation.23 | convolution fusion | flops 3523215360 | bytes 11272192 | tf_op jit(solution)/shard_map/dot_general | solution.py:54
  268.1 7.9 %fusion.8 = f32[768,1280]{1,0:T(8,128)} fusion(bf16[1792,1280]{1,0:T(8,128)(2,1)} %bitcast.39, bf16[768,3584]{1,0:T(8,128)(2,1)S(1)} %multiply_convert_fusion), kind=kOutput, calls=%fused_computation.18 | convolution fusion | flops 3523215360 | bytes 11272192 | tf_op jit(solution)/shard_map/dot_general | solution.py:55
  276.0 8.0 %fusion.10 = f32[768,1280]{1,0:T(8,128)} fusion(bf16[1792,1280]{1,0:T(8,128)(2,1)} %bitcast.35, bf16[768,3584]{1,0:T(8,128)(2,1)S(1)} %multiply_convert_fusion), kind=kOutput, calls=%fused_computation.20 | convolution fusion | flops 3523215360 | bytes 11272192 | tf_op jit(solution)/shard_map/dot_general | solution.py:55
  284.1 10.9 %fusion.19 = f32[16,1280]{1,0:T(8,128)S(1)} fusion(f32[768,1280]{1,0:T(8,128)} %fusion.8, f32[768,1280]{1,0:T(8,128)} %fusion.13, f32[768,1280]{1,0:T(8,128)} %fusion.10, bf16[1792,1280]{1,0:T(8,128)(2,1)} %bitcast.38, bf16[768,3584]{1,0:T(8,128)(2,1)} %copy-done.12, s32[768]{0:T(1024)S(1)} %copy-done.19), kind=kOutput, calls=%fused_computation.32 | convolution fusion | flops 3562573824 | bytes 19221504 | tf_op jit(solution)/shard_map/dot_general | solution.py:214
  294.9 1.5 collective-permute-start.38
  296.4 2.9 collective-permute-done.38
  300.3 2.3 fusion.28
  302.7 2.1 convolution_bitcast_fusion
  305.2 1.5 collective-permute-start.47
  308.9 5.6 %all-to-all-start.1 = ((f32[4,4,448]{2,1,0:T(4,128)}), f32[4,4,448]{2,1,0:T(4,128)S(1)}, u32[]{:S(2)}, u32[]{:S(2)}) async-start(f32[4,4,448]{2,1,0:T(4,128)} %fusion.60), calls=%async_computation.1 | async-start | bytes 65536 | tf_op jit(solution)/shard_map/all_to_all | solution.py:257
  314.5 2.0 collective-permute-start.44
  316.5 2.5 collective-permute-start.43
  319.0 1.3 collective-permute-start.42
  321.0 5.2 %collective-permute-start.41 = (f32[16,448]{1,0:T(8,128)S(1)}, f32[16,448]{1,0:T(8,128)S(1)}, u32[]{:S(2)}, u32[]{:S(2)}) collective-permute-start(f32[16,448]{1,0:T(8,128)S(1)} %get-tuple-element.33), channel_id=1, source_target_pairs={{0,25},{1,0},{2,1},{3,8},{4,9},{5,16},{6,17},{7,24},{8,27},{9,2},{... | collective-permute-start | bytes 86024 | tf_op jit(solution)/shard_map/ppermute | solution.py:253
  326.4 1.4 collective-permute-done.41
  (223 shorter events, 53.0 us)
Async XLA Ops:
  0.0 302.7 %copy-start = (bf16[896,1280]{1,0:T(8,128)(2,1)S(1)}, bf16[896,1280]{1,0:T(8,128)(2,1)}, u32[]{:S(2)}) copy-start(bf16[896,1280]{1,0:T(8,128)(2,1)} %param.24) | copy-start | bytes 6881284
  0.0 29.2 %copy-start.26 = (s32[2,8]{1,0:T(2,128)S(1)}, s32[2,8]{1,0:T(2,128)}, u32[]{:S(2)}) copy-start(s32[2,8]{1,0:T(2,128)} %param.14) | copy-start | bytes 196
  0.0 29.9 %copy-start.20 = (f32[3584]{0:T(1024)S(1)}, f32[3584]{0:T(1024)}, u32[]{:S(2)}) copy-start(f32[3584]{0:T(1024)} %param.16) | copy-start | bytes 43012
  0.0 30.0 %copy-start.21 = (f32[3584]{0:T(1024)S(1)}, f32[3584]{0:T(1024)}, u32[]{:S(2)}) copy-start(f32[3584]{0:T(1024)} %param.21) | copy-start | bytes 43012
  4.3 27.6 %collective-permute-start.2 = (bf16[896,384]{1,0:T(8,128)(2,1)}, bf16[896,384]{1,0:T(8,128)(2,1)S(1)}, u32[]{:S(2)}, u32[]{:S(2)}) collective-permute-start(bf16[896,384]{1,0:T(8,128)(2,1)} %pad_maximum_fusion.7), channel_id=1, source_target_pairs={{0,16},{8,24},{16,0},{24,8},{1,17},{9,25},{17,1},{25,9},{2,18},{10... | collective-permute-start | bytes 2064392 | tf_op jit(solution)/shard_map/ppermute | solution.py:64
  7.3 53.0 %collective-permute-start = (s32[16]{0:T(128)}, s32[16]{0:T(128)}, u32[]{:S(2)}, u32[]{:S(2)}) collective-permute-start(s32[16]{0:T(128)} %bitcast.183), channel_id=1, source_target_pairs={{0,16},{8,24},{16,0},{24,8},{1,17},{9,25},{17,1},{25,9},{2,18},{10... | collective-permute-start | bytes 200 | tf_op jit(solution)/shard_map/ppermute | solution.py:64
  8.6 51.7 %collective-permute-start.48 = (s32[16]{0:T(128)}, s32[16]{0:T(128)}, u32[]{:S(2)}, u32[]{:S(2)}) collective-permute-start(s32[16]{0:T(128)} %reshape.155), channel_id=1, source_target_pairs={{0,16},{8,24},{16,0},{24,8},{1,17},{9,25},{17,1},{25,9},{2,18},{10... | collective-permute-start | bytes 200 | tf_op jit(solution)/shard_map/ppermute | solution.py:64
  32.1 5.7 %collective-permute-start.3 = (bf16[2,896,384]{2,1,0:T(8,128)(2,1)S(1)}, bf16[2,896,384]{2,1,0:T(8,128)(2,1)S(1)}, u32[]{:S(2)}, u32[]{:S(2)}) collective-permute-start(bf16[2,896,384]{2,1,0:T(8,128)(2,1)S(1)} %pad_maximum_fusion.5), channel_id=1, source_target_pairs={{0,8},{8,0},{16,24},{24,16},{1,9},{9,1},{17,25},{25,17},{2,10},{10... | collective-permute-start | bytes 4128776 | tf_op jit(solution)/shard_map/ppermute | solution.py:67
  43.4 24.5 %slice-start = ((bf16[768,384]{0,1:T(8,128)(2,1)}), bf16[768,256]{0,1:T(8,128)(2,1)S(1)}, s32[]{:S(2)}) async-start(bf16[768,384]{0,1:T(8,128)(2,1)} %copy-done.16), calls=%async_computation.2 | async-start | bytes 786432 | tf_op jit(solution)/shard_map/slice | solution.py:167
  48.8 22.1 %all-to-all-start = ((bf16[8,768,32]{1,2,0:T(8,128)(2,1)}), bf16[8,768,32]{1,2,0:T(8,128)(2,1)S(1)}, u32[]{:S(2)}, u32[]{:S(2)}) async-start(bf16[8,768,32]{1,2,0:T(8,128)(2,1)} %fusion.50), calls=%async_computation | async-start | bytes 786432 | tf_op jit(solution)/shard_map/all_to_all | solution.py:181
  55.9 12.8 %collective-permute-start.4 = (bf16[896,256]{1,0:T(8,128)(2,1)S(1)}, bf16[896,256]{1,0:T(8,128)(2,1)}, u32[]{:S(2)}, u32[]{:S(2)}) collective-permute-start(bf16[896,256]{1,0:T(8,128)(2,1)S(1)} %copy-done.15), channel_id=1, source_target_pairs={{0,16},{8,24},{16,0},{24,8},{1,17},{9,25},{17,1},{25,9},{2,18},{10... | collective-permute-start | bytes 1376264 | tf_op jit(solution)/shard_map/ppermute | solution.py:64
  61.6 1.1 collective-permute-start.1
  61.6 237.9 %collective-permute-start.49 = (s32[2,16]{1,0:T(2,128)}, s32[2,16]{1,0:T(2,128)}, u32[]{:S(2)}, u32[]{:S(2)}) collective-permute-start(s32[2,16]{1,0:T(2,128)} %get-tuple-element.64), channel_id=1, source_target_pairs={{0,8},{8,0},{16,24},{24,16},{1,9},{9,1},{17,25},{25,17},{2,10},{10... | collective-permute-start | bytes 392 | tf_op jit(solution)/shard_map/ppermute | solution.py:67
  70.7 6.9 %collective-permute-start.5 = (bf16[2,896,256]{2,1,0:T(8,128)(2,1)}, bf16[2,896,256]{2,1,0:T(8,128)(2,1)}, u32[]{:S(2)}, u32[]{:S(2)}) collective-permute-start(bf16[2,896,256]{2,1,0:T(8,128)(2,1)} %pad_maximum_fusion.6), channel_id=1, source_target_pairs={{0,8},{8,0},{16,24},{24,16},{1,9},{9,1},{17,25},{25,17},{2,10},{10... | collective-permute-start | bytes 2752520 | tf_op jit(solution)/shard_map/ppermute | solution.py:67
  84.3 10.6 %collective-permute-start.20 = (bf16[96,1792]{1,0:T(8,128)(2,1)S(1)}, bf16[96,1792]{1,0:T(8,128)(2,1)S(1)}, u32[]{:S(2)}, u32[]{:S(2)}) collective-permute-start(bf16[96,1792]{1,0:T(8,128)(2,1)S(1)} %constant_dynamic-slice_fusion.2), channel_id=1, source_target_pairs={{0,1},{2,0},{4,2},{6,4},{7,6},{5,7},{3,5},{1,3},{8,9},{10,8},{12,1... | collective-permute-start | bytes 1032200 | tf_op jit(solution)/shard_map/ppermute | solution.py:109
  86.6 21.7 %copy-start.9 = (bf16[768,1792]{1,0:T(8,128)(2,1)S(1)}, bf16[768,1792]{1,0:T(8,128)(2,1)}, u32[]{:S(2)}) copy-start(bf16[768,1792]{1,0:T(8,128)(2,1)} %get-tuple-element.23) | copy-start | bytes 8257540
  87.8 10.1 %collective-permute-start.6 = (bf16[96,1792]{1,0:T(8,128)(2,1)S(1)}, bf16[96,1792]{1,0:T(8,128)(2,1)S(1)}, u32[]{:S(2)}, u32[]{:S(2)}) collective-permute-start(bf16[96,1792]{1,0:T(8,128)(2,1)S(1)} %constant_dynamic-slice_fusion.3), channel_id=1, source_target_pairs={{0,2},{2,4},{4,6},{6,7},{7,5},{5,3},{3,1},{1,0},{8,10},{10,12},{12... | collective-permute-start | bytes 1032200 | tf_op jit(solution)/shard_map/ppermute | solution.py:109
  87.9 57.5 %collective-permute-start.36 = (bf16[896,1280]{1,0:T(8,128)(2,1)}, bf16[896,1280]{1,0:T(8,128)(2,1)S(1)}, u32[]{:S(2)}, u32[]{:S(2)}) collective-permute-start(bf16[896,1280]{1,0:T(8,128)(2,1)} %param.23), channel_id=1, source_target_pairs={{0,16},{8,24},{16,0},{24,8},{1,17},{9,25},{17,1},{25,9},{2,18},{10... | collective-permute-start | bytes 6881288 | tf_op jit(solution)/shard_map/ppermute | solution.py:45
  89.4 99.7 %collective-permute-start.34 = (bf16[896,1280]{1,0:T(8,128)(2,1)}, bf16[896,1280]{1,0:T(8,128)(2,1)S(1)}, u32[]{:S(2)}, u32[]{:S(2)}) collective-permute-start(bf16[896,1280]{1,0:T(8,128)(2,1)} %param.22), channel_id=1, source_target_pairs={{0,16},{8,24},{16,0},{24,8},{1,17},{9,25},{17,1},{25,9},{2,18},{10... | collective-permute-start | bytes 6881288 | tf_op jit(solution)/shard_map/ppermute | solution.py:45
  95.9 29.3 %copy-start.11 = (bf16[768,1792]{1,0:T(8,128)(2,1)S(1)}, bf16[768,1792]{1,0:T(8,128)(2,1)}, u32[]{:S(2)}) copy-start(bf16[768,1792]{1,0:T(8,128)(2,1)} %copy-done.10) | copy-start | bytes 8257540
  96.0 9.9 %collective-permute-start.21 = (bf16[96,1792]{1,0:T(8,128)(2,1)S(1)}, bf16[96,1792]{1,0:T(8,128)(2,1)S(1)}, u32[]{:S(2)}, u32[]{:S(2)}) collective-permute-start(bf16[96,1792]{1,0:T(8,128)(2,1)S(1)} %add_convert_fusion.6), channel_id=1, source_target_pairs={{0,1},{2,0},{4,2},{6,4},{7,6},{5,7},{3,5},{1,3},{8,9},{10,8},{12,1... | collective-permute-start | bytes 1032200 | tf_op jit(solution)/shard_map/ppermute | solution.py:109
  98.9 9.4 %collective-permute-start.7 = (bf16[96,1792]{1,0:T(8,128)(2,1)S(1)}, bf16[96,1792]{1,0:T(8,128)(2,1)S(1)}, u32[]{:S(2)}, u32[]{:S(2)}) collective-permute-start(bf16[96,1792]{1,0:T(8,128)(2,1)S(1)} %add_convert_fusion.13), channel_id=1, source_target_pairs={{0,2},{2,4},{4,6},{6,7},{7,5},{5,3},{3,1},{1,0},{8,10},{10,12},{12... | collective-permute-start | bytes 1032200 | tf_op jit(solution)/shard_map/ppermute | solution.py:109
  106.9 9.0 %collective-permute-start.22 = (bf16[96,1792]{1,0:T(8,128)(2,1)S(1)}, bf16[96,1792]{1,0:T(8,128)(2,1)S(1)}, u32[]{:S(2)}, u32[]{:S(2)}) collective-permute-start(bf16[96,1792]{1,0:T(8,128)(2,1)S(1)} %add_convert_fusion.5), channel_id=1, source_target_pairs={{0,1},{2,0},{4,2},{6,4},{7,6},{5,7},{3,5},{1,3},{8,9},{10,8},{12,1... | collective-permute-start | bytes 1032200 | tf_op jit(solution)/shard_map/ppermute | solution.py:109
  108.4 9.8 %collective-permute-start.8 = (bf16[96,1792]{1,0:T(8,128)(2,1)S(1)}, bf16[96,1792]{1,0:T(8,128)(2,1)S(1)}, u32[]{:S(2)}, u32[]{:S(2)}) collective-permute-start(bf16[96,1792]{1,0:T(8,128)(2,1)S(1)} %add_convert_fusion.12), channel_id=1, source_target_pairs={{0,2},{2,4},{4,6},{6,7},{7,5},{5,3},{3,1},{1,0},{8,10},{10,12},{12... | collective-permute-start | bytes 1032200 | tf_op jit(solution)/shard_map/ppermute | solution.py:109
  116.9 8.3 %collective-permute-start.23 = (bf16[96,1792]{1,0:T(8,128)(2,1)S(1)}, bf16[96,1792]{1,0:T(8,128)(2,1)S(1)}, u32[]{:S(2)}, u32[]{:S(2)}) collective-permute-start(bf16[96,1792]{1,0:T(8,128)(2,1)S(1)} %add_convert_fusion.4), channel_id=1, source_target_pairs={{0,1},{2,0},{4,2},{6,4},{7,6},{5,7},{3,5},{1,3},{8,9},{10,8},{12,1... | collective-permute-start | bytes 1032200 | tf_op jit(solution)/shard_map/ppermute | solution.py:109
  118.3 8.1 %collective-permute-start.9 = (bf16[96,1792]{1,0:T(8,128)(2,1)S(1)}, bf16[96,1792]{1,0:T(8,128)(2,1)S(1)}, u32[]{:S(2)}, u32[]{:S(2)}) collective-permute-start(bf16[96,1792]{1,0:T(8,128)(2,1)S(1)} %add_convert_fusion.11), channel_id=1, source_target_pairs={{0,2},{2,4},{4,6},{6,7},{7,5},{5,3},{3,1},{1,0},{8,10},{10,12},{12... | collective-permute-start | bytes 1032200 | tf_op jit(solution)/shard_map/ppermute | solution.py:109
  125.3 8.2 %collective-permute-start.24 = (bf16[96,1792]{1,0:T(8,128)(2,1)S(1)}, bf16[96,1792]{1,0:T(8,128)(2,1)S(1)}, u32[]{:S(2)}, u32[]{:S(2)}) collective-permute-start(bf16[96,1792]{1,0:T(8,128)(2,1)S(1)} %add_convert_fusion.3), channel_id=1, source_target_pairs={{0,1},{2,0},{4,2},{6,4},{7,6},{5,7},{3,5},{1,3},{8,9},{10,8},{12,1... | collective-permute-start | bytes 1032200 | tf_op jit(solution)/shard_map/ppermute | solution.py:109
  126.5 8.8 %collective-permute-start.10 = (bf16[96,1792]{1,0:T(8,128)(2,1)S(1)}, bf16[96,1792]{1,0:T(8,128)(2,1)S(1)}, u32[]{:S(2)}, u32[]{:S(2)}) collective-permute-start(bf16[96,1792]{1,0:T(8,128)(2,1)S(1)} %add_convert_fusion.10), channel_id=1, source_target_pairs={{0,2},{2,4},{4,6},{6,7},{7,5},{5,3},{3,1},{1,0},{8,10},{10,12},{12... | collective-permute-start | bytes 1032200 | tf_op jit(solution)/shard_map/ppermute | solution.py:109
  133.6 9.0 %collective-permute-start.25 = (bf16[96,1792]{1,0:T(8,128)(2,1)S(1)}, bf16[96,1792]{1,0:T(8,128)(2,1)S(1)}, u32[]{:S(2)}, u32[]{:S(2)}) collective-permute-start(bf16[96,1792]{1,0:T(8,128)(2,1)S(1)} %add_convert_fusion.2), channel_id=1, source_target_pairs={{0,1},{2,0},{4,2},{6,4},{7,6},{5,7},{3,5},{1,3},{8,9},{10,8},{12,1... | collective-permute-start | bytes 1032200 | tf_op jit(solution)/shard_map/ppermute | solution.py:109
  135.4 9.6 %collective-permute-start.11 = (bf16[96,1792]{1,0:T(8,128)(2,1)S(1)}, bf16[96,1792]{1,0:T(8,128)(2,1)S(1)}, u32[]{:S(2)}, u32[]{:S(2)}) collective-permute-start(bf16[96,1792]{1,0:T(8,128)(2,1)S(1)} %add_convert_fusion.9), channel_id=1, source_target_pairs={{0,2},{2,4},{4,6},{6,7},{7,5},{5,3},{3,1},{1,0},{8,10},{10,12},{12... | collective-permute-start | bytes 1032200 | tf_op jit(solution)/shard_map/ppermute | solution.py:109
  142.6 7.3 %collective-permute-start.26 = (bf16[96,1792]{1,0:T(8,128)(2,1)S(1)}, bf16[96,1792]{1,0:T(8,128)(2,1)S(1)}, u32[]{:S(2)}, u32[]{:S(2)}) collective-permute-start(bf16[96,1792]{1,0:T(8,128)(2,1)S(1)} %add_convert_fusion.1), channel_id=1, source_target_pairs={{0,1},{2,0},{4,2},{6,4},{7,6},{5,7},{3,5},{1,3},{8,9},{10,8},{12,1... | collective-permute-start | bytes 1032200 | tf_op jit(solution)/shard_map/ppermute | solution.py:109
  145.2 7.3 %collective-permute-start.12 = (bf16[96,1792]{1,0:T(8,128)(2,1)S(1)}, bf16[96,1792]{1,0:T(8,128)(2,1)S(1)}, u32[]{:S(2)}, u32[]{:S(2)}) collective-permute-start(bf16[96,1792]{1,0:T(8,128)(2,1)S(1)} %add_convert_fusion.8), channel_id=1, source_target_pairs={{0,2},{2,4},{4,6},{6,7},{7,5},{5,3},{3,1},{1,0},{8,10},{10,12},{12... | collective-permute-start | bytes 1032200 | tf_op jit(solution)/shard_map/ppermute | solution.py:109
  147.9 120.2 %collective-permute-start.37 = (bf16[2,896,1280]{2,1,0:T(8,128)(2,1)}, bf16[2,896,1280]{2,1,0:T(8,128)(2,1)}, u32[]{:S(2)}, u32[]{:S(2)}) collective-permute-start(bf16[2,896,1280]{2,1,0:T(8,128)(2,1)} %pad_maximum_fusion.2), channel_id=1, source_target_pairs={{0,8},{8,0},{16,24},{24,16},{1,9},{9,1},{17,25},{25,17},{2,10},{10... | collective-permute-start | bytes 13762568 | tf_op jit(solution)/shard_map/ppermute | solution.py:48
  150.1 39.0 %copy-start.14 = (bf16[896,1280]{1,0:T(8,128)(2,1)S(1)}, bf16[896,1280]{1,0:T(8,128)(2,1)}, u32[]{:S(2)}) copy-start(bf16[896,1280]{1,0:T(8,128)(2,1)} %param.22) | copy-start | bytes 6881284
  150.2 41.3 %collective-permute-start.27 = (bf16[96,1792]{1,0:T(8,128)(2,1)S(1)}, bf16[96,1792]{1,0:T(8,128)(2,1)S(1)}, u32[]{:S(2)}, u32[]{:S(2)}) collective-permute-start(bf16[96,1792]{1,0:T(8,128)(2,1)S(1)} %get-tuple-element.22), channel_id=1, source_target_pairs={{0,1},{2,0},{4,2},{6,4},{7,6},{5,7},{3,5},{1,3},{8,9},{10,8},{12,1... | collective-permute-start | bytes 1032200 | tf_op jit(solution)/shard_map/ppermute | solution.py:115
  152.7 40.5 %collective-permute-start.13 = (bf16[96,1792]{1,0:T(8,128)(2,1)S(1)}, bf16[96,1792]{1,0:T(8,128)(2,1)S(1)}, u32[]{:S(2)}, u32[]{:S(2)}) collective-permute-start(bf16[96,1792]{1,0:T(8,128)(2,1)S(1)} %get-tuple-element.20), channel_id=1, source_target_pairs={{0,2},{2,4},{4,6},{6,7},{7,5},{5,3},{3,1},{1,0},{8,10},{10,12},{12... | collective-permute-start | bytes 1032200 | tf_op jit(solution)/shard_map/ppermute | solution.py:115
  191.6 84.4 %collective-permute-start.35 = (bf16[2,896,1280]{2,1,0:T(8,128)(2,1)}, bf16[2,896,1280]{2,1,0:T(8,128)(2,1)}, u32[]{:S(2)}, u32[]{:S(2)}) collective-permute-start(bf16[2,896,1280]{2,1,0:T(8,128)(2,1)} %pad_maximum_fusion.1), channel_id=1, source_target_pairs={{0,8},{8,0},{16,24},{24,16},{1,9},{9,1},{17,25},{25,17},{2,10},{10... | collective-permute-start | bytes 13762568 | tf_op jit(solution)/shard_map/ppermute | solution.py:48
  191.6 10.5 %collective-permute-start.28 = (bf16[96,1792]{1,0:T(8,128)(2,1)S(1)}, bf16[96,1792]{1,0:T(8,128)(2,1)S(1)}, u32[]{:S(2)}, u32[]{:S(2)}) collective-permute-start(bf16[96,1792]{1,0:T(8,128)(2,1)S(1)} %collective-permute-done.27), channel_id=1, source_target_pairs={{0,1},{2,0},{4,2},{6,4},{7,6},{5,7},{3,5},{1,3},{8,9},{10,8},{12,1... | collective-permute-start | bytes 1032200 | tf_op jit(solution)/shard_map/ppermute | solution.py:115
  193.3 10.5 %collective-permute-start.14 = (bf16[96,1792]{1,0:T(8,128)(2,1)S(1)}, bf16[96,1792]{1,0:T(8,128)(2,1)S(1)}, u32[]{:S(2)}, u32[]{:S(2)}) collective-permute-start(bf16[96,1792]{1,0:T(8,128)(2,1)S(1)} %collective-permute-done.13), channel_id=1, source_target_pairs={{0,2},{2,4},{4,6},{6,7},{7,5},{5,3},{3,1},{1,0},{8,10},{10,12},{12... | collective-permute-start | bytes 1032200 | tf_op jit(solution)/shard_map/ppermute | solution.py:115
  202.0 9.7 %collective-permute-start.29 = (bf16[96,1792]{1,0:T(8,128)(2,1)S(1)}, bf16[96,1792]{1,0:T(8,128)(2,1)S(1)}, u32[]{:S(2)}, u32[]{:S(2)}) collective-permute-start(bf16[96,1792]{1,0:T(8,128)(2,1)S(1)} %collective-permute-done.28), channel_id=1, source_target_pairs={{0,1},{2,0},{4,2},{6,4},{7,6},{5,7},{3,5},{1,3},{8,9},{10,8},{12,1... | collective-permute-start | bytes 1032200 | tf_op jit(solution)/shard_map/ppermute | solution.py:115
  203.7 9.7 %collective-permute-start.15 = (bf16[96,1792]{1,0:T(8,128)(2,1)S(1)}, bf16[96,1792]{1,0:T(8,128)(2,1)S(1)}, u32[]{:S(2)}, u32[]{:S(2)}) collective-permute-start(bf16[96,1792]{1,0:T(8,128)(2,1)S(1)} %collective-permute-done.14), channel_id=1, source_target_pairs={{0,2},{2,4},{4,6},{6,7},{7,5},{5,3},{3,1},{1,0},{8,10},{10,12},{12... | collective-permute-start | bytes 1032200 | tf_op jit(solution)/shard_map/ppermute | solution.py:115
  211.7 8.8 %collective-permute-start.30 = (bf16[96,1792]{1,0:T(8,128)(2,1)S(1)}, bf16[96,1792]{1,0:T(8,128)(2,1)S(1)}, u32[]{:S(2)}, u32[]{:S(2)}) collective-permute-start(bf16[96,1792]{1,0:T(8,128)(2,1)S(1)} %collective-permute-done.29), channel_id=1, source_target_pairs={{0,1},{2,0},{4,2},{6,4},{7,6},{5,7},{3,5},{1,3},{8,9},{10,8},{12,1... | collective-permute-start | bytes 1032200 | tf_op jit(solution)/shard_map/ppermute | solution.py:115
  213.4 8.8 %collective-permute-start.16 = (bf16[96,1792]{1,0:T(8,128)(2,1)S(1)}, bf16[96,1792]{1,0:T(8,128)(2,1)S(1)}, u32[]{:S(2)}, u32[]{:S(2)}) collective-permute-start(bf16[96,1792]{1,0:T(8,128)(2,1)S(1)} %collective-permute-done.15), channel_id=1, source_target_pairs={{0,2},{2,4},{4,6},{6,7},{7,5},{5,3},{3,1},{1,0},{8,10},{10,12},{12... | collective-permute-start | bytes 1032200 | tf_op jit(solution)/shard_map/ppermute | solution.py:115
  213.9 32.6 %copy-start.2 = (bf16[768,896]{1,0:T(8,128)(2,1)S(1)}, bf16[768,896]{1,0:T(8,128)(2,1)}, u32[]{:S(2)}) copy-start(bf16[768,896]{1,0:T(8,128)(2,1)} %copy-done.1) | copy-start | bytes 4128772
  213.9 32.6 %copy-start.4 = (bf16[768,896]{1,0:T(8,128)(2,1)S(1)}, bf16[768,896]{1,0:T(8,128)(2,1)}, u32[]{:S(2)}) copy-start(bf16[768,896]{1,0:T(8,128)(2,1)} %copy-done.3) | copy-start | bytes 4128772
  213.9 32.6 %copy-start.6 = (bf16[768,896]{1,0:T(8,128)(2,1)S(1)}, bf16[768,896]{1,0:T(8,128)(2,1)}, u32[]{:S(2)}) copy-start(bf16[768,896]{1,0:T(8,128)(2,1)} %copy-done.5) | copy-start | bytes 4128772
  213.9 32.6 %copy-start.8 = (bf16[768,896]{1,0:T(8,128)(2,1)S(1)}, bf16[768,896]{1,0:T(8,128)(2,1)}, u32[]{:S(2)}) copy-start(bf16[768,896]{1,0:T(8,128)(2,1)} %copy-done.7) | copy-start | bytes 4128772
  220.5 8.2 %collective-permute-start.31 = (bf16[96,1792]{1,0:T(8,128)(2,1)S(1)}, bf16[96,1792]{1,0:T(8,128)(2,1)S(1)}, u32[]{:S(2)}, u32[]{:S(2)}) collective-permute-start(bf16[96,1792]{1,0:T(8,128)(2,1)S(1)} %collective-permute-done.30), channel_id=1, source_target_pairs={{0,1},{2,0},{4,2},{6,4},{7,6},{5,7},{3,5},{1,3},{8,9},{10,8},{12,1... | collective-permute-start | bytes 1032200 | tf_op jit(solution)/shard_map/ppermute | solution.py:115
  222.2 8.2 %collective-permute-start.17 = (bf16[96,1792]{1,0:T(8,128)(2,1)S(1)}, bf16[96,1792]{1,0:T(8,128)(2,1)S(1)}, u32[]{:S(2)}, u32[]{:S(2)}) collective-permute-start(bf16[96,1792]{1,0:T(8,128)(2,1)S(1)} %collective-permute-done.16), channel_id=1, source_target_pairs={{0,2},{2,4},{4,6},{6,7},{7,5},{5,3},{3,1},{1,0},{8,10},{10,12},{12... | collective-permute-start | bytes 1032200 | tf_op jit(solution)/shard_map/ppermute | solution.py:115
  228.8 8.7 %collective-permute-start.32 = (bf16[96,1792]{1,0:T(8,128)(2,1)S(1)}, bf16[96,1792]{1,0:T(8,128)(2,1)S(1)}, u32[]{:S(2)}, u32[]{:S(2)}) collective-permute-start(bf16[96,1792]{1,0:T(8,128)(2,1)S(1)} %collective-permute-done.31), channel_id=1, source_target_pairs={{0,1},{2,0},{4,2},{6,4},{7,6},{5,7},{3,5},{1,3},{8,9},{10,8},{12,1... | collective-permute-start | bytes 1032200 | tf_op jit(solution)/shard_map/ppermute | solution.py:115
  230.5 8.7 %collective-permute-start.18 = (bf16[96,1792]{1,0:T(8,128)(2,1)S(1)}, bf16[96,1792]{1,0:T(8,128)(2,1)S(1)}, u32[]{:S(2)}, u32[]{:S(2)}) collective-permute-start(bf16[96,1792]{1,0:T(8,128)(2,1)S(1)} %collective-permute-done.17), channel_id=1, source_target_pairs={{0,2},{2,4},{4,6},{6,7},{7,5},{5,3},{3,1},{1,0},{8,10},{10,12},{12... | collective-permute-start | bytes 1032200 | tf_op jit(solution)/shard_map/ppermute | solution.py:115
  237.4 7.2 %collective-permute-start.33 = (bf16[96,1792]{1,0:T(8,128)(2,1)S(1)}, bf16[96,1792]{1,0:T(8,128)(2,1)S(1)}, u32[]{:S(2)}, u32[]{:S(2)}) collective-permute-start(bf16[96,1792]{1,0:T(8,128)(2,1)S(1)} %collective-permute-done.32), channel_id=1, source_target_pairs={{0,1},{2,0},{4,2},{6,4},{7,6},{5,7},{3,5},{1,3},{8,9},{10,8},{12,1... | collective-permute-start | bytes 1032200 | tf_op jit(solution)/shard_map/ppermute | solution.py:115
  239.2 7.3 %collective-permute-start.19 = (bf16[96,1792]{1,0:T(8,128)(2,1)S(1)}, bf16[96,1792]{1,0:T(8,128)(2,1)S(1)}, u32[]{:S(2)}, u32[]{:S(2)}) collective-permute-start(bf16[96,1792]{1,0:T(8,128)(2,1)S(1)} %collective-permute-done.18), channel_id=1, source_target_pairs={{0,2},{2,4},{4,6},{6,7},{7,5},{5,3},{3,1},{1,0},{8,10},{10,12},{12... | collective-permute-start | bytes 1032200 | tf_op jit(solution)/shard_map/ppermute | solution.py:115
  294.9 4.4 %collective-permute-start.38 = (f32[16,1280]{1,0:T(8,128)S(1)}, f32[16,1280]{1,0:T(8,128)S(1)}, u32[]{:S(2)}, u32[]{:S(2)}) collective-permute-start(f32[16,1280]{1,0:T(8,128)S(1)} %fusion.19), channel_id=1, source_target_pairs={{0,16},{8,24},{16,0},{24,8},{1,17},{9,25},{17,1},{25,9},{2,18},{10... | collective-permute-start | bytes 245768 | tf_op jit(solution)/shard_map/ppermute | solution.py:64
  299.4 3.2 collective-permute-start.39
  305.2 13.7 %collective-permute-start.47 = (f32[16,448]{1,0:T(8,128)S(1)}, f32[16,448]{1,0:T(8,128)S(1)}, u32[]{:S(2)}, u32[]{:S(2)}) collective-permute-start(f32[16,448]{1,0:T(8,128)S(1)} %get-tuple-element.34), channel_id=1, source_target_pairs={{0,1},{1,8},{2,9},{3,16},{4,17},{5,24},{6,25},{7,0},{8,3},{9,10},{... | collective-permute-start | bytes 86024 | tf_op jit(solution)/shard_map/ppermute | solution.py:253
  306.8 13.5 %collective-permute-start.46 = (f32[16,448]{1,0:T(8,128)S(1)}, f32[16,448]{1,0:T(8,128)S(1)}, u32[]{:S(2)}, u32[]{:S(2)}) collective-permute-start(f32[16,448]{1,0:T(8,128)S(1)} %get-tuple-element.35), channel_id=1, source_target_pairs={{0,8},{1,9},{2,16},{3,17},{4,24},{5,25},{6,0},{7,1},{8,10},{9,11},... | collective-permute-start | bytes 86024 | tf_op jit(solution)/shard_map/ppermute | solution.py:253
  307.8 13.2 %collective-permute-start.45 = (f32[16,448]{1,0:T(8,128)S(1)}, f32[16,448]{1,0:T(8,128)S(1)}, u32[]{:S(2)}, u32[]{:S(2)}) collective-permute-start(f32[16,448]{1,0:T(8,128)S(1)} %get-tuple-element.36), channel_id=1, source_target_pairs={{0,9},{1,16},{2,17},{3,24},{4,25},{5,0},{6,1},{7,8},{8,11},{9,18},... | collective-permute-start | bytes 86024 | tf_op jit(solution)/shard_map/ppermute | solution.py:253
  308.9 17.5 %all-to-all-start.1 = ((f32[4,4,448]{2,1,0:T(4,128)}), f32[4,4,448]{2,1,0:T(4,128)S(1)}, u32[]{:S(2)}, u32[]{:S(2)}) async-start(f32[4,4,448]{2,1,0:T(4,128)} %fusion.60), calls=%async_computation.1 | async-start | bytes 65536 | tf_op jit(solution)/shard_map/all_to_all | solution.py:257
  314.5 11.9 %collective-permute-start.44 = (f32[16,448]{1,0:T(8,128)S(1)}, f32[16,448]{1,0:T(8,128)S(1)}, u32[]{:S(2)}, u32[]{:S(2)}) collective-permute-start(f32[16,448]{1,0:T(8,128)S(1)} %get-tuple-element.37), channel_id=1, source_target_pairs={{0,16},{1,17},{2,24},{3,25},{4,0},{5,1},{6,8},{7,9},{8,18},{9,19},... | collective-permute-start | bytes 86024 | tf_op jit(solution)/shard_map/ppermute | solution.py:253
  316.5 9.9 %collective-permute-start.43 = (f32[16,448]{1,0:T(8,128)S(1)}, f32[16,448]{1,0:T(8,128)S(1)}, u32[]{:S(2)}, u32[]{:S(2)}) collective-permute-start(f32[16,448]{1,0:T(8,128)S(1)} %get-tuple-element.38), channel_id=1, source_target_pairs={{0,17},{1,24},{2,25},{3,0},{4,1},{5,8},{6,9},{7,16},{8,19},{9,26},... | collective-permute-start | bytes 86024 | tf_op jit(solution)/shard_map/ppermute | solution.py:253
  319.0 7.4 %collective-permute-start.42 = (f32[16,448]{1,0:T(8,128)S(1)}, f32[16,448]{1,0:T(8,128)S(1)}, u32[]{:S(2)}, u32[]{:S(2)}) collective-permute-start(f32[16,448]{1,0:T(8,128)S(1)} %get-tuple-element.39), channel_id=1, source_target_pairs={{0,24},{1,25},{2,0},{3,1},{4,8},{5,9},{6,16},{7,17},{8,26},{9,27},... | collective-permute-start | bytes 86024 | tf_op jit(solution)/shard_map/ppermute | solution.py:253
  320.3 6.1 %collective-permute-start.40 = (f32[16,448]{1,0:T(8,128)S(1)}, f32[16,448]{1,0:T(8,128)S(1)}, u32[]{:S(2)}, u32[]{:S(2)}) collective-permute-start(f32[16,448]{1,0:T(8,128)S(1)} %get-tuple-element.40), channel_id=1, source_target_pairs={{0,0},{1,1},{2,8},{3,9},{4,16},{5,17},{6,24},{7,25},{8,2},{9,3},{1... | collective-permute-start | bytes 86024 | tf_op jit(solution)/shard_map/ppermute | solution.py:253
  321.0 6.8 %collective-permute-start.41 = (f32[16,448]{1,0:T(8,128)S(1)}, f32[16,448]{1,0:T(8,128)S(1)}, u32[]{:S(2)}, u32[]{:S(2)}) collective-permute-start(f32[16,448]{1,0:T(8,128)S(1)} %get-tuple-element.33), channel_id=1, source_target_pairs={{0,25},{1,0},{2,1},{3,8},{4,9},{5,16},{6,17},{7,24},{8,27},{9,2},{... | collective-permute-start | bytes 86024 | tf_op jit(solution)/shard_map/ppermute | solution.py:253
  (17 other events, 150.1 us)

commit v9 on v5

--- a/solution.py
+++ b/solution.py
@@ -131,25 +131,10 @@
     order = source_order(chips)
 
     q_cols, k_cols = q_weight.shape[1], k_weight.shape[1]
-    qkv_full = gather_grp(jnp.concatenate([q_weight, k_weight, v_weight], 1), chips)
-    qkv_full = qkv_full.reshape(width, -1)
-    o_after, qkv_full = lax.optimization_barrier((o_weight, qkv_full))
-    o_full = gather_grp(o_after, chips).reshape(width, -1)
-    gate_after, up_after, o_full = lax.optimization_barrier((gate_weight, up_weight, o_full))
-    gate_full = gather_grp(gate_after, chips).reshape(width, -1)
-    up_full = gather_grp(up_after, chips).reshape(width, -1)
-
-    hidden_perm = take_blocks(hidden_in, order, d_grp, 1)
-    attn_gain_perm = take_blocks(attn_gain, order, d_grp, 0)
-    ffn_gain_perm = take_blocks(ffn_gain, order, d_grp, 0)
-
-    norm_in = rms_scale(hidden_perm, attn_gain_perm)
-    qkv = jnp.dot(norm_in, qkv_full, preferred_element_type=jnp.float32).astype(jnp.bfloat16)
-    queries = qkv[:, :q_cols]
     per_dev = k_cols // KVH
     group_heads = HEADS // KVH
-    key_split = qkv[:, q_cols : q_cols + k_cols].reshape(row_count, per_dev, KVH)
-    value_split = qkv[:, q_cols + k_cols :].reshape(row_count, per_dev, KVH)
+    key_split = k_weight.reshape(d_grp, per_dev, KVH)
+    value_split = v_weight.reshape(d_grp, per_dev, KVH)
     outgoing_kv = jnp.stack(
         [
             jnp.concatenate(
@@ -160,8 +145,25 @@
         ]
     )
     kv_in = lax.all_to_all(outgoing_kv, "tp", 0, 0, tiled=True)
-    key_head = kv_in[:, :, :per_dev].transpose(1, 0, 2).reshape(row_count, tp_size * per_dev)
-    value_head = kv_in[:, :, per_dev:].transpose(1, 0, 2).reshape(row_count, tp_size * per_dev)
+    key_cols = kv_in[:, :, :per_dev].transpose(1, 0, 2).reshape(d_grp, tp_size * per_dev)
+    value_cols = kv_in[:, :, per_dev:].transpose(1, 0, 2).reshape(d_grp, tp_size * per_dev)
+    q_full = gather_grp(q_weight, chips).reshape(width, -1)
+    kv_full = gather_grp(jnp.concatenate([key_cols, value_cols], 1), chips).reshape(width, -1)
+    o_after, q_full, kv_full = lax.optimization_barrier((o_weight, q_full, kv_full))
+    o_full = gather_grp(o_after, chips).reshape(width, -1)
+    gate_after, up_after, o_full = lax.optimization_barrier((gate_weight, up_weight, o_full))
+    gate_full = gather_grp(gate_after, chips).reshape(width, -1)
+    up_full = gather_grp(up_after, chips).reshape(width, -1)
+
+    hidden_perm = take_blocks(hidden_in, order, d_grp, 1)
+    attn_gain_perm = take_blocks(attn_gain, order, d_grp, 0)
+    ffn_gain_perm = take_blocks(ffn_gain, order, d_grp, 0)
+
+    norm_in = rms_scale(hidden_perm, attn_gain_perm)
+    queries = jnp.dot(norm_in, q_full, preferred_element_type=jnp.float32).astype(jnp.bfloat16)
+    kv_rows = jnp.dot(norm_in, kv_full, preferred_element_type=jnp.float32).astype(jnp.bfloat16)
+    key_head = kv_rows[:, : tp_size * per_dev]
+    value_head = kv_rows[:, tp_size * per_dev :]
 
     segs = segment_ids(lengths, block_rows)
     same = segs[:, :, None] == segs[:, None, :]

time: 328 us -> 350 us (1.067)
  local copies, waits for them, and re-layouts: 21.1 us -> 27.3 us
  waiting for transfers between devices: 131 us -> 135 us
  starting transfers between devices: 61.6 us -> 65.6 us
    ppermute x7 -> x8, waiting for transfers between devices: 43.9 us -> 51.9 us  [gather_grp(): moving = lax.ppermute(moving, 'grp', ring)]
    reshape x2 -> x4, local copies, waits for them, and re-layouts: 0.06 us -> 4.46 us  [the longest x1 1.77 us: on_device(): kv_in[:, :, per_dev:].transpose(1, 0, 2).reshape(d_grp, tp_size * per_dev)]
    ppermute x8, waiting for transfers between devices: 5.49 us -> 1.42 us  [on_device(): totals = totals + lax.ppermute(piece, ('grp', 'tp'), pairs)]
    concatenate x6 -> x7, other arithmetic: 18 us -> 20.4 us  [gather_grp(): return jnp.concatenate([mine, other], 0)]
    another operation x7 -> x8, other arithmetic: 9.92 us -> 11.8 us  [gather_grp(): mine = jnp.stack(held)]
    ppermute x7 -> x8, starting transfers between devices: 8.07 us -> 8.98 us  [gather_grp(): moving = lax.ppermute(moving, 'grp', ring)]
  transfers between devices with their start and end apart: 52 -> 54, of which waited for: 25 -> 25; matrix products, arithmetic and copies ran while one was open for 33% -> 35% of each run, Pallas kernels for 0% -> 0%
where the time goes in v9:
time: 350 us; the launch traced here: 347 us
  waiting for transfers between devices  135 us (39%)
  starting transfers between devices  65.6 us (19%)
  other arithmetic  54.4 us (16%)
  matrix products  48.5 us (14%)
  local copies, waits for them, and re-layouts  27.3 us (8%)
  between operations  15.5 us (4%)
    ppermute x8, waiting for transfers between devices, gather_grp(): moving = lax.ppermute(moving, 'grp', ring)  51.9 us
    ppermute x14, waiting for transfers between devices, ring_psum(): moving = lax.ppermute(moving, axis, pairs)  41.9 us
    ppermute x14, waiting for transfers between devices, ring_psum(): got = lax.ppermute(acc, axis, pairs)  39.3 us
    concatenate x7, other arithmetic, gather_grp(): return jnp.concatenate([mine, other], 0)  20.4 us
    ppermute x8, starting transfers between devices, on_device(): totals = totals + lax.ppermute(piece, ('grp', 'tp'), pairs)  15.5 us
    ppermute x14, starting transfers between devices, ring_psum(): got = lax.ppermute(acc, axis, pairs)  15.4 us
    ppermute x14, starting transfers between devices, ring_psum(): moving = lax.ppermute(moving, axis, pairs)  14.6 us
    dot_general x1, matrix products, on_device(): jnp.dot(selector.astype(jnp.bfloat16), hidden_ffn, preferred_element_type...  14.5 us
  transfers between devices with their start and end apart: 54, of which 25 were waited for; matrix products, arithmetic and copies ran while one was open for 35% of the time, Pallas kernels for 0%

profile of v9, /device:TPU:0, one launch (start us, length us, event | category | flops | bytes accessed | tf_op | source)
XLA Modules:
  0.0 346.5 jit_solution(8393574379484283035)
XLA Ops:
  0.0 3.0 collective-permute-start.2
  10.3 5.8 %all-to-all-start = ((bf16[8,896,32]{1,2,0:T(8,128)(2,1)}), bf16[8,896,32]{1,2,0:T(8,128)(2,1)S(1)}, u32[]{:S(2)}, u32[]{:S(2)}) async-start(bf16[8,896,32]{1,2,0:T(8,128)(2,1)} %fusion.34), calls=%async_computation | async-start | bytes 917504 | tf_op jit(solution)/shard_map/all_to_all | solution.py:147
  38.1 3.1 constant_dynamic-slice_fusion.7
  45.6 1.8 copy.85
  50.6 2.0 pad_maximum_fusion.8
  52.6 7.9 %collective-permute-done.4 = bf16[896,256]{1,0:T(8,128)(2,1)S(1)} collective-permute-done((bf16[896,256]{1,0:T(8,128)(2,1)S(1)}, bf16[896,256]{1,0:T(8,128)(2,1)S(1)}, u32[]{:S(2)}, u32[]{:S(2)}) %collective-permute-start.4) | collective-permute-done | bytes 458784 | tf_op jit(solution)/shard_map/ppermute | solution.py:45
  68.1 1.6 pad_maximum_fusion.5
  69.8 1.5 pad_maximum_fusion.6
  72.0 3.3 fusion.12
  75.3 3.3 fusion.15
  78.5 1.8 reshape.160
  80.4 3.7 %collective-permute-done.6 = bf16[896,256]{1,0:T(8,128)(2,1)S(1)} collective-permute-done((bf16[896,256]{1,0:T(8,128)(2,1)S(1)}, bf16[896,256]{1,0:T(8,128)(2,1)S(1)}, u32[]{:S(2)}, u32[]{:S(2)}) %collective-permute-start.6) | collective-permute-done | bytes 458784 | tf_op jit(solution)/shard_map/ppermute | solution.py:45
  85.2 1.8 fusion.65
  87.0 4.0 %fusion.72 = (f32[2,2,384]{2,1,0:T(2,128)}, f32[2,2,384,384]{2,3,1,0:T(8,128)}) fusion(pred[2,384,384]{1,2,0:T(8,128)(4,1)S(1)} %broadcast_compare_fusion, bf16[2,384,128,1]{2,1,3,0:T(8,128)(2,1)} %bitcast.176, bf16[2,384,2,128]{3,2,1,0:T(2,128)(2,1)} %reshape.160), kind=kOutput, calls=%fused_computation.168 | convolution fusion | flops 153354624 | bytes 3250176 | tf_op jit(solution)/shard_map/sub | solution.py:29
  91.0 2.8 fusion.18
  95.2 1.5 pad_maximum_fusion.7
  96.6 1.6 convolution_convert_fusion
  98.3 1.9 fusion.63
  100.2 1.6 copy-done.16
  101.7 1.7 collective-permute-start.22
  105.9 1.5 collective-permute-start.36
  107.4 4.9 %collective-permute-done.22 = bf16[96,1792]{1,0:T(8,128)(2,1)S(1)} collective-permute-done((bf16[96,1792]{1,0:T(8,128)(2,1)S(1)}, bf16[96,1792]{1,0:T(8,128)(2,1)S(1)}, u32[]{:S(2)}, u32[]{:S(2)}) %collective-permute-start.22) | collective-permute-done | bytes 344096 | tf_op jit(solution)/shard_map/ppermute | solution.py:90
  113.3 1.7 collective-permute-start.23
  116.9 6.2 %collective-permute-done.23 = bf16[96,1792]{1,0:T(8,128)(2,1)S(1)} collective-permute-done((bf16[96,1792]{1,0:T(8,128)(2,1)S(1)}, bf16[96,1792]{1,0:T(8,128)(2,1)S(1)}, u32[]{:S(2)}, u32[]{:S(2)}) %collective-permute-start.23) | collective-permute-done | bytes 344096 | tf_op jit(solution)/shard_map/ppermute | solution.py:90
  124.2 1.7 collective-permute-start.24
  126.4 6.6 %collective-permute-done.24 = bf16[96,1792]{1,0:T(8,128)(2,1)S(1)} collective-permute-done((bf16[96,1792]{1,0:T(8,128)(2,1)S(1)}, bf16[96,1792]{1,0:T(8,128)(2,1)S(1)}, u32[]{:S(2)}, u32[]{:S(2)}) %collective-permute-start.24) | collective-permute-done | bytes 344096 | tf_op jit(solution)/shard_map/ppermute | solution.py:90
  134.1 1.7 collective-permute-start.25
  136.5 5.7 %collective-permute-done.25 = bf16[96,1792]{1,0:T(8,128)(2,1)S(1)} collective-permute-done((bf16[96,1792]{1,0:T(8,128)(2,1)S(1)}, bf16[96,1792]{1,0:T(8,128)(2,1)S(1)}, u32[]{:S(2)}, u32[]{:S(2)}) %collective-permute-start.25) | collective-permute-done | bytes 344096 | tf_op jit(solution)/shard_map/ppermute | solution.py:90
  142.3 1.7 collective-permute-start.26
  144.6 6.0 %collective-permute-done.26 = bf16[96,1792]{1,0:T(8,128)(2,1)S(1)} collective-permute-done((bf16[96,1792]{1,0:T(8,128)(2,1)S(1)}, bf16[96,1792]{1,0:T(8,128)(2,1)S(1)}, u32[]{:S(2)}, u32[]{:S(2)}) %collective-permute-start.26) | collective-permute-done | bytes 344096 | tf_op jit(solution)/shard_map/ppermute | solution.py:90
  150.7 1.7 collective-permute-start.27
  153.2 6.6 %collective-permute-done.27 = bf16[96,1792]{1,0:T(8,128)(2,1)S(1)} collective-permute-done((bf16[96,1792]{1,0:T(8,128)(2,1)S(1)}, bf16[96,1792]{1,0:T(8,128)(2,1)S(1)}, u32[]{:S(2)}, u32[]{:S(2)}) %collective-permute-start.27) | collective-permute-done | bytes 344096 | tf_op jit(solution)/shard_map/ppermute | solution.py:90
  159.9 1.7 collective-permute-start.28
  162.5 2.5 pad_maximum_fusion.4
  164.9 2.2 collective-permute-done.28
  167.5 1.7 collective-permute-start.29
  170.1 36.4 %collective-permute-done.36 = bf16[896,1280]{1,0:T(8,128)(2,1)S(1)} collective-permute-done((bf16[896,1280]{1,0:T(8,128)(2,1)}, bf16[896,1280]{1,0:T(8,128)(2,1)S(1)}, u32[]{:S(2)}, u32[]{:S(2)}) %collective-permute-start.36) | collective-permute-done | bytes 2293792 | tf_op jit(solution)/shard_map/ppermute | solution.py:45
  206.4 2.9 pad_maximum_fusion.3
  209.3 1.7 collective-permute-start.30
  211.5 8.3 %collective-permute-done.30 = bf16[96,1792]{1,0:T(8,128)(2,1)S(1)} collective-permute-done((bf16[96,1792]{1,0:T(8,128)(2,1)S(1)}, bf16[96,1792]{1,0:T(8,128)(2,1)S(1)}, u32[]{:S(2)}, u32[]{:S(2)}) %collective-permute-start.30) | collective-permute-done | bytes 344096 | tf_op jit(solution)/shard_map/ppermute | solution.py:96
  219.8 1.7 collective-permute-start.31
  222.0 7.5 %collective-permute-done.31 = bf16[96,1792]{1,0:T(8,128)(2,1)S(1)} collective-permute-done((bf16[96,1792]{1,0:T(8,128)(2,1)S(1)}, bf16[96,1792]{1,0:T(8,128)(2,1)S(1)}, u32[]{:S(2)}, u32[]{:S(2)}) %collective-permute-start.31) | collective-permute-done | bytes 344096 | tf_op jit(solution)/shard_map/ppermute | solution.py:96
  229.5 1.7 collective-permute-start.32
  231.7 6.6 %collective-permute-done.32 = bf16[96,1792]{1,0:T(8,128)(2,1)S(1)} collective-permute-done((bf16[96,1792]{1,0:T(8,128)(2,1)S(1)}, bf16[96,1792]{1,0:T(8,128)(2,1)S(1)}, u32[]{:S(2)}, u32[]{:S(2)}) %collective-permute-start.32) | collective-permute-done | bytes 344096 | tf_op jit(solution)/shard_map/ppermute | solution.py:96
  238.3 1.7 collective-permute-start.33
  240.4 6.1 %collective-permute-done.33 = bf16[96,1792]{1,0:T(8,128)(2,1)S(1)} collective-permute-done((bf16[96,1792]{1,0:T(8,128)(2,1)S(1)}, bf16[96,1792]{1,0:T(8,128)(2,1)S(1)}, u32[]{:S(2)}, u32[]{:S(2)}) %collective-permute-start.33) | collective-permute-done | bytes 344096 | tf_op jit(solution)/shard_map/ppermute | solution.py:96
  246.5 1.7 collective-permute-start.34
  248.7 6.5 %collective-permute-done.34 = bf16[96,1792]{1,0:T(8,128)(2,1)S(1)} collective-permute-done((bf16[96,1792]{1,0:T(8,128)(2,1)S(1)}, bf16[96,1792]{1,0:T(8,128)(2,1)S(1)}, u32[]{:S(2)}, u32[]{:S(2)}) %collective-permute-start.34) | collective-permute-done | bytes 344096 | tf_op jit(solution)/shard_map/ppermute | solution.py:96
  255.2 1.7 collective-permute-start.35
  257.4 5.0 %collective-permute-done.35 = bf16[96,1792]{1,0:T(8,128)(2,1)S(1)} collective-permute-done((bf16[96,1792]{1,0:T(8,128)(2,1)S(1)}, bf16[96,1792]{1,0:T(8,128)(2,1)S(1)}, u32[]{:S(2)}, u32[]{:S(2)}) %collective-permute-start.35) | collective-permute-done | bytes 344096 | tf_op jit(solution)/shard_map/ppermute | solution.py:96
  262.5 1.7 collective-permute-done.21
  264.3 5.7 %multiply_reduce_fusion = (f32[768]{0:T(1024)S(1)}, f32[768,3584]{1,0:T(8,128)}) fusion(bf16[768,1792]{1,0:T(8,128)(2,1)S(1)} %constant_dynamic-update-slice_fusion, bf16[768,1792]{1,0:T(8,128)(2,1)S(1)} %constant_dynamic-update-slice_fusion.8, bf16[768,896]{1,0:T(8,128)(2,1)S(1)} %copy-done.9, bf16[768,896]{1,0:T(8,128)(2,1)S(1)} %copy-done.12, ...), kind=kLoop, calls=%fused_computation.8 | loop fusion | flops 41286912 | bytes 22023168 | tf_op jit(solution)/shard_map/reduce_sum | solution.py:17
  270.0 7.0 %pad_maximum_fusion.1 = bf16[4,896,1280]{2,1,0:T(8,128)(2,1)} fusion(bf16[2,896,1280]{2,1,0:T(8,128)(2,1)} %collective-permute-done.39, bf16[1,896,1280]{2,1,0:T(8,128)(2,1)S(1)} %bitcast.153, bf16[1,896,1280]{2,1,0:T(8,128)(2,1)S(1)} %bitcast.147), kind=kLoop, calls=%fused_computation.10 | loop fusion | flops 9175040 | bytes 18350080 | tf_op jit(solution)/shard_map/concatenate | solution.py:49
  277.0 13.4 %fusion.61 = f32[768,1280]{1,0:T(8,128)} fusion(bf16[3584,1280]{1,0:T(8,128)(2,1)} %bitcast.155, f32[3584]{0:T(1024)S(1)} %copy-done.28, f32[768]{0:T(1024)S(1)} %add_rsqrt_fusion, bf16[768,1792]{1,0:T(8,128)(2,1)S(1)} %constant_dynamic-update-slice_fusion, bf16[768,1792]{1,0:T(8,128)(2,1)S(1)} %constant_dynamic-update-slice_fusion.8, ...), kind=kOutput, calls=%fused_computation.157 | convolution fusion | flops 7090470912 | bytes 24134656 | tf_op jit(solution)/shard_map/dot_general | solution.py:190
  290.3 8.1 %pad_maximum_fusion = bf16[4,896,1280]{2,1,0:T(8,128)(2,1)} fusion(bf16[2,896,1280]{2,1,0:T(8,128)(2,1)} %collective-permute-done.37, bf16[1,896,1280]{2,1,0:T(8,128)(2,1)} %bitcast.151, bf16[1,896,1280]{2,1,0:T(8,128)(2,1)S(1)} %bitcast.149), kind=kLoop, calls=%fused_computation.9 | loop fusion | flops 9175040 | bytes 18350080 | tf_op jit(solution)/shard_map/concatenate | solution.py:49
  298.4 14.5 %fusion.5 = f32[16,1280]{1,0:T(8,128)S(1)} fusion(f32[768,1280]{1,0:T(8,128)} %fusion.61, s32[768]{0:T(1024)S(1)} %add.528, bf16[3584,1280]{1,0:T(8,128)(2,1)} %bitcast.154, f32[3584]{0:T(1024)S(1)} %copy-done.28, f32[768]{0:T(1024)S(1)} %add_rsqrt_fusion, bf16[768,1792]{1,0:T(8,128)(2,1)} %copy-done.14, bf16[768,1792]{1,0:T(8,128)(2,1)} %copy-done.13, ...), kind=kOutput, calls=%fused_computation.20 | convolution fusion | flops 7127863296 | bytes 24219648 | tf_op jit(solution)/shard_map/dot_general | solution.py:197
  313.6 3.9 %collective-permute-done.40 = f32[16,1280]{1,0:T(8,128)S(1)} collective-permute-done((f32[16,1280]{1,0:T(8,128)S(1)}, f32[16,1280]{1,0:T(8,128)S(1)}, u32[]{:S(2)}, u32[]{:S(2)}) %collective-permute-start.40) | collective-permute-done | bytes 81952 | tf_op jit(solution)/shard_map/ppermute | solution.py:45
  318.3 2.3 fusion.22
  320.7 2.1 convolution_bitcast_fusion
  323.3 1.5 collective-permute-start.49
  326.9 4.7 %all-to-all-start.1 = ((f32[4,4,448]{2,1,0:T(4,128)}), f32[4,4,448]{2,1,0:T(4,128)S(1)}, u32[]{:S(2)}, u32[]{:S(2)}) async-start(f32[4,4,448]{2,1,0:T(4,128)} %fusion.46), calls=%async_computation.1 | async-start | bytes 65536 | tf_op jit(solution)/shard_map/all_to_all | solution.py:240
  331.6 2.0 collective-permute-start.46
  333.6 3.4 collective-permute-start.45
  339.0 5.2 %collective-permute-start.43 = (f32[16,448]{1,0:T(8,128)S(1)}, f32[16,448]{1,0:T(8,128)S(1)}, u32[]{:S(2)}, u32[]{:S(2)}) collective-permute-start(f32[16,448]{1,0:T(8,128)S(1)} %get-tuple-element.37), channel_id=1, source_target_pairs={{0,25},{1,0},{2,1},{3,8},{4,9},{5,16},{6,17},{7,24},{8,27},{9,2},{... | collective-permute-start | bytes 86024 | tf_op jit(solution)/shard_map/ppermute | solution.py:236
  (236 shorter events, 56.2 us)
Async XLA Ops:
  0.0 320.7 %copy-start = (bf16[896,1280]{1,0:T(8,128)(2,1)S(1)}, bf16[896,1280]{1,0:T(8,128)(2,1)}, u32[]{:S(2)}) copy-start(bf16[896,1280]{1,0:T(8,128)(2,1)} %param.24) | copy-start | bytes 6881284
  0.0 37.7 %copy-start.26 = (f32[3584]{0:T(1024)S(1)}, f32[3584]{0:T(1024)}, u32[]{:S(2)}) copy-start(f32[3584]{0:T(1024)} %param.16) | copy-start | bytes 43012
  0.0 37.8 %copy-start.27 = (f32[3584]{0:T(1024)S(1)}, f32[3584]{0:T(1024)}, u32[]{:S(2)}) copy-start(f32[3584]{0:T(1024)} %param.21) | copy-start | bytes 43012
  0.0 50.5 %collective-permute-start.2 = (bf16[896,256]{1,0:T(8,128)(2,1)}, bf16[896,256]{1,0:T(8,128)(2,1)}, u32[]{:S(2)}, u32[]{:S(2)}) collective-permute-start(bf16[896,256]{1,0:T(8,128)(2,1)} %param.17), channel_id=1, source_target_pairs={{0,16},{8,24},{16,0},{24,8},{1,17},{9,25},{17,1},{25,9},{2,18},{10... | collective-permute-start | bytes 1376264 | tf_op jit(solution)/shard_map/ppermute | solution.py:45
  10.3 34.6 %all-to-all-start = ((bf16[8,896,32]{1,2,0:T(8,128)(2,1)}), bf16[8,896,32]{1,2,0:T(8,128)(2,1)S(1)}, u32[]{:S(2)}, u32[]{:S(2)}) async-start(bf16[8,896,32]{1,2,0:T(8,128)(2,1)} %fusion.34), calls=%async_computation | async-start | bytes 917504 | tf_op jit(solution)/shard_map/all_to_all | solution.py:147
  16.1 47.0 %collective-permute-start = (s32[16]{0:T(128)S(1)}, s32[16]{0:T(128)}, u32[]{:S(2)}, u32[]{:S(2)}) collective-permute-start(s32[16]{0:T(128)S(1)} %bitcast.178), channel_id=1, source_target_pairs={{0,16},{8,24},{16,0},{24,8},{1,17},{9,25},{17,1},{25,9},{2,18},{10... | collective-permute-start | bytes 200 | tf_op jit(solution)/shard_map/ppermute | solution.py:45
  17.4 45.7 %collective-permute-start.50 = (s32[16]{0:T(128)}, s32[16]{0:T(128)}, u32[]{:S(2)}, u32[]{:S(2)}) collective-permute-start(s32[16]{0:T(128)} %reshape.167), channel_id=1, source_target_pairs={{0,16},{8,24},{16,0},{24,8},{1,17},{9,25},{17,1},{25,9},{2,18},{10... | collective-permute-start | bytes 200 | tf_op jit(solution)/shard_map/ppermute | solution.py:45
  49.3 11.2 %collective-permute-start.4 = (bf16[896,256]{1,0:T(8,128)(2,1)S(1)}, bf16[896,256]{1,0:T(8,128)(2,1)S(1)}, u32[]{:S(2)}, u32[]{:S(2)}) collective-permute-start(bf16[896,256]{1,0:T(8,128)(2,1)S(1)} %get-tuple-element.32), channel_id=1, source_target_pairs={{0,16},{8,24},{16,0},{24,8},{1,17},{9,25},{17,1},{25,9},{2,18},{10... | collective-permute-start | bytes 1376264 | tf_op jit(solution)/shard_map/ppermute | solution.py:45
  52.6 15.4 %collective-permute-start.3 = (bf16[2,896,256]{2,1,0:T(8,128)(2,1)}, bf16[2,896,256]{2,1,0:T(8,128)(2,1)}, u32[]{:S(2)}, u32[]{:S(2)}) collective-permute-start(bf16[2,896,256]{2,1,0:T(8,128)(2,1)} %pad_maximum_fusion.8), channel_id=1, source_target_pairs={{0,8},{8,0},{16,24},{24,16},{1,9},{9,1},{17,25},{25,17},{2,10},{10... | collective-permute-start | bytes 2752520 | tf_op jit(solution)/shard_map/ppermute | solution.py:48
  62.3 7.4 %collective-permute-start.5 = (bf16[2,896,256]{2,1,0:T(8,128)(2,1)}, bf16[2,896,256]{2,1,0:T(8,128)(2,1)}, u32[]{:S(2)}, u32[]{:S(2)}) collective-permute-start(bf16[2,896,256]{2,1,0:T(8,128)(2,1)} %pad_maximum_fusion.9), channel_id=1, source_target_pairs={{0,8},{8,0},{16,24},{24,16},{1,9},{9,1},{17,25},{25,17},{2,10},{10... | collective-permute-start | bytes 2752520 | tf_op jit(solution)/shard_map/ppermute | solution.py:48
  64.5 1.3 collective-permute-start.1
  65.0 252.6 %collective-permute-start.51 = (s32[2,16]{1,0:T(2,128)}, s32[2,16]{1,0:T(2,128)}, u32[]{:S(2)}, u32[]{:S(2)}) collective-permute-start(s32[2,16]{1,0:T(2,128)} %get-tuple-element.68), channel_id=1, source_target_pairs={{0,8},{8,0},{16,24},{24,16},{1,9},{9,1},{17,25},{25,17},{2,10},{10... | collective-permute-start | bytes 392 | tf_op jit(solution)/shard_map/ppermute | solution.py:48
  71.3 12.8 %collective-permute-start.6 = (bf16[896,256]{1,0:T(8,128)(2,1)S(1)}, bf16[896,256]{1,0:T(8,128)(2,1)S(1)}, u32[]{:S(2)}, u32[]{:S(2)}) collective-permute-start(bf16[896,256]{1,0:T(8,128)(2,1)S(1)} %copy-done.22), channel_id=1, source_target_pairs={{0,16},{8,24},{16,0},{24,8},{1,17},{9,25},{17,1},{25,9},{2,18},{10... | collective-permute-start | bytes 1376264 | tf_op jit(solution)/shard_map/ppermute | solution.py:45
  85.2 10.0 %collective-permute-start.7 = (bf16[2,896,256]{2,1,0:T(8,128)(2,1)}, bf16[2,896,256]{2,1,0:T(8,128)(2,1)}, u32[]{:S(2)}, u32[]{:S(2)}) collective-permute-start(bf16[2,896,256]{2,1,0:T(8,128)(2,1)} %pad_maximum_fusion.10), channel_id=1, source_target_pairs={{0,8},{8,0},{16,24},{24,16},{1,9},{9,1},{17,25},{25,17},{2,10},{10... | collective-permute-start | bytes 2752520 | tf_op jit(solution)/shard_map/ppermute | solution.py:48
  101.7 10.5 %collective-permute-start.22 = (bf16[96,1792]{1,0:T(8,128)(2,1)S(1)}, bf16[96,1792]{1,0:T(8,128)(2,1)S(1)}, u32[]{:S(2)}, u32[]{:S(2)}) collective-permute-start(bf16[96,1792]{1,0:T(8,128)(2,1)S(1)} %constant_dynamic-slice_fusion.2), channel_id=1, source_target_pairs={{0,1},{2,0},{4,2},{6,4},{7,6},{5,7},{3,5},{1,3},{8,9},{10,8},{12,1... | collective-permute-start | bytes 1032200 | tf_op jit(solution)/shard_map/ppermute | solution.py:90
  103.8 22.1 %copy-start.15 = (bf16[768,1792]{1,0:T(8,128)(2,1)S(1)}, bf16[768,1792]{1,0:T(8,128)(2,1)}, u32[]{:S(2)}) copy-start(bf16[768,1792]{1,0:T(8,128)(2,1)} %get-tuple-element.25) | copy-start | bytes 8257540
  105.0 10.2 %collective-permute-start.8 = (bf16[96,1792]{1,0:T(8,128)(2,1)S(1)}, bf16[96,1792]{1,0:T(8,128)(2,1)S(1)}, u32[]{:S(2)}, u32[]{:S(2)}) collective-permute-start(bf16[96,1792]{1,0:T(8,128)(2,1)S(1)} %constant_dynamic-slice_fusion.3), channel_id=1, source_target_pairs={{0,2},{2,4},{4,6},{6,7},{7,5},{5,3},{3,1},{1,0},{8,10},{10,12},{12... | collective-permute-start | bytes 1032200 | tf_op jit(solution)/shard_map/ppermute | solution.py:90
  105.4 57.1 %collective-permute-start.38 = (bf16[896,1280]{1,0:T(8,128)(2,1)}, bf16[896,1280]{1,0:T(8,128)(2,1)S(1)}, u32[]{:S(2)}, u32[]{:S(2)}) collective-permute-start(bf16[896,1280]{1,0:T(8,128)(2,1)} %param.23), channel_id=1, source_target_pairs={{0,16},{8,24},{16,0},{24,8},{1,17},{9,25},{17,1},{25,9},{2,18},{10... | collective-permute-start | bytes 6881288 | tf_op jit(solution)/shard_map/ppermute | solution.py:45
  105.9 100.5 %collective-permute-start.36 = (bf16[896,1280]{1,0:T(8,128)(2,1)}, bf16[896,1280]{1,0:T(8,128)(2,1)S(1)}, u32[]{:S(2)}, u32[]{:S(2)}) collective-permute-start(bf16[896,1280]{1,0:T(8,128)(2,1)} %param.22), channel_id=1, source_target_pairs={{0,16},{8,24},{16,0},{24,8},{1,17},{9,25},{17,1},{25,9},{2,18},{10... | collective-permute-start | bytes 6881288 | tf_op jit(solution)/shard_map/ppermute | solution.py:45
  113.3 28.9 %copy-start.17 = (bf16[768,1792]{1,0:T(8,128)(2,1)S(1)}, bf16[768,1792]{1,0:T(8,128)(2,1)}, u32[]{:S(2)}) copy-start(bf16[768,1792]{1,0:T(8,128)(2,1)} %copy-done.16) | copy-start | bytes 8257540
  113.3 9.8 %collective-permute-start.23 = (bf16[96,1792]{1,0:T(8,128)(2,1)S(1)}, bf16[96,1792]{1,0:T(8,128)(2,1)S(1)}, u32[]{:S(2)}, u32[]{:S(2)}) collective-permute-start(bf16[96,1792]{1,0:T(8,128)(2,1)S(1)} %add_convert_fusion.6), channel_id=1, source_target_pairs={{0,1},{2,0},{4,2},{6,4},{7,6},{5,7},{3,5},{1,3},{8,9},{10,8},{12,1... | collective-permute-start | bytes 1032200 | tf_op jit(solution)/shard_map/ppermute | solution.py:90
  116.3 9.6 %collective-permute-start.9 = (bf16[96,1792]{1,0:T(8,128)(2,1)S(1)}, bf16[96,1792]{1,0:T(8,128)(2,1)S(1)}, u32[]{:S(2)}, u32[]{:S(2)}) collective-permute-start(bf16[96,1792]{1,0:T(8,128)(2,1)S(1)} %add_convert_fusion.13), channel_id=1, source_target_pairs={{0,2},{2,4},{4,6},{6,7},{7,5},{5,3},{3,1},{1,0},{8,10},{10,12},{12... | collective-permute-start | bytes 1032200 | tf_op jit(solution)/shard_map/ppermute | solution.py:90
  124.2 8.9 %collective-permute-start.24 = (bf16[96,1792]{1,0:T(8,128)(2,1)S(1)}, bf16[96,1792]{1,0:T(8,128)(2,1)S(1)}, u32[]{:S(2)}, u32[]{:S(2)}) collective-permute-start(bf16[96,1792]{1,0:T(8,128)(2,1)S(1)} %add_convert_fusion.5), channel_id=1, source_target_pairs={{0,1},{2,0},{4,2},{6,4},{7,6},{5,7},{3,5},{1,3},{8,9},{10,8},{12,1... | collective-permute-start | bytes 1032200 | tf_op jit(solution)/shard_map/ppermute | solution.py:90
  126.0 9.8 %collective-permute-start.10 = (bf16[96,1792]{1,0:T(8,128)(2,1)S(1)}, bf16[96,1792]{1,0:T(8,128)(2,1)S(1)}, u32[]{:S(2)}, u32[]{:S(2)}) collective-permute-start(bf16[96,1792]{1,0:T(8,128)(2,1)S(1)} %add_convert_fusion.12), channel_id=1, source_target_pairs={{0,2},{2,4},{4,6},{6,7},{7,5},{5,3},{3,1},{1,0},{8,10},{10,12},{12... | collective-permute-start | bytes 1032200 | tf_op jit(solution)/shard_map/ppermute | solution.py:90
  134.1 8.1 %collective-permute-start.25 = (bf16[96,1792]{1,0:T(8,128)(2,1)S(1)}, bf16[96,1792]{1,0:T(8,128)(2,1)S(1)}, u32[]{:S(2)}, u32[]{:S(2)}) collective-permute-start(bf16[96,1792]{1,0:T(8,128)(2,1)S(1)} %add_convert_fusion.4), channel_id=1, source_target_pairs={{0,1},{2,0},{4,2},{6,4},{7,6},{5,7},{3,5},{1,3},{8,9},{10,8},{12,1... | collective-permute-start | bytes 1032200 | tf_op jit(solution)/shard_map/ppermute | solution.py:90
  135.9 8.2 %collective-permute-start.11 = (bf16[96,1792]{1,0:T(8,128)(2,1)S(1)}, bf16[96,1792]{1,0:T(8,128)(2,1)S(1)}, u32[]{:S(2)}, u32[]{:S(2)}) collective-permute-start(bf16[96,1792]{1,0:T(8,128)(2,1)S(1)} %add_convert_fusion.11), channel_id=1, source_target_pairs={{0,2},{2,4},{4,6},{6,7},{7,5},{5,3},{3,1},{1,0},{8,10},{10,12},{12... | collective-permute-start | bytes 1032200 | tf_op jit(solution)/shard_map/ppermute | solution.py:90
  142.3 8.3 %collective-permute-start.26 = (bf16[96,1792]{1,0:T(8,128)(2,1)S(1)}, bf16[96,1792]{1,0:T(8,128)(2,1)S(1)}, u32[]{:S(2)}, u32[]{:S(2)}) collective-permute-start(bf16[96,1792]{1,0:T(8,128)(2,1)S(1)} %add_convert_fusion.3), channel_id=1, source_target_pairs={{0,1},{2,0},{4,2},{6,4},{7,6},{5,7},{3,5},{1,3},{8,9},{10,8},{12,1... | collective-permute-start | bytes 1032200 | tf_op jit(solution)/shard_map/ppermute | solution.py:90
  144.2 8.5 %collective-permute-start.12 = (bf16[96,1792]{1,0:T(8,128)(2,1)S(1)}, bf16[96,1792]{1,0:T(8,128)(2,1)S(1)}, u32[]{:S(2)}, u32[]{:S(2)}) collective-permute-start(bf16[96,1792]{1,0:T(8,128)(2,1)S(1)} %add_convert_fusion.10), channel_id=1, source_target_pairs={{0,2},{2,4},{4,6},{6,7},{7,5},{5,3},{3,1},{1,0},{8,10},{10,12},{12... | collective-permute-start | bytes 1032200 | tf_op jit(solution)/shard_map/ppermute | solution.py:90
  150.7 9.1 %collective-permute-start.27 = (bf16[96,1792]{1,0:T(8,128)(2,1)S(1)}, bf16[96,1792]{1,0:T(8,128)(2,1)S(1)}, u32[]{:S(2)}, u32[]{:S(2)}) collective-permute-start(bf16[96,1792]{1,0:T(8,128)(2,1)S(1)} %add_convert_fusion.2), channel_id=1, source_target_pairs={{0,1},{2,0},{4,2},{6,4},{7,6},{5,7},{3,5},{1,3},{8,9},{10,8},{12,1... | collective-permute-start | bytes 1032200 | tf_op jit(solution)/shard_map/ppermute | solution.py:90
  152.7 9.2 %collective-permute-start.13 = (bf16[96,1792]{1,0:T(8,128)(2,1)S(1)}, bf16[96,1792]{1,0:T(8,128)(2,1)S(1)}, u32[]{:S(2)}, u32[]{:S(2)}) collective-permute-start(bf16[96,1792]{1,0:T(8,128)(2,1)S(1)} %add_convert_fusion.9), channel_id=1, source_target_pairs={{0,2},{2,4},{4,6},{6,7},{7,5},{5,3},{3,1},{1,0},{8,10},{10,12},{12... | collective-permute-start | bytes 1032200 | tf_op jit(solution)/shard_map/ppermute | solution.py:90
  159.9 7.3 %collective-permute-start.28 = (bf16[96,1792]{1,0:T(8,128)(2,1)S(1)}, bf16[96,1792]{1,0:T(8,128)(2,1)S(1)}, u32[]{:S(2)}, u32[]{:S(2)}) collective-permute-start(bf16[96,1792]{1,0:T(8,128)(2,1)S(1)} %add_convert_fusion.1), channel_id=1, source_target_pairs={{0,1},{2,0},{4,2},{6,4},{7,6},{5,7},{3,5},{1,3},{8,9},{10,8},{12,1... | collective-permute-start | bytes 1032200 | tf_op jit(solution)/shard_map/ppermute | solution.py:90
  162.1 7.3 %collective-permute-start.14 = (bf16[96,1792]{1,0:T(8,128)(2,1)S(1)}, bf16[96,1792]{1,0:T(8,128)(2,1)S(1)}, u32[]{:S(2)}, u32[]{:S(2)}) collective-permute-start(bf16[96,1792]{1,0:T(8,128)(2,1)S(1)} %add_convert_fusion.8), channel_id=1, source_target_pairs={{0,2},{2,4},{4,6},{6,7},{7,5},{5,3},{3,1},{1,0},{8,10},{10,12},{12... | collective-permute-start | bytes 1032200 | tf_op jit(solution)/shard_map/ppermute | solution.py:90
  164.9 105.1 %collective-permute-start.39 = (bf16[2,896,1280]{2,1,0:T(8,128)(2,1)}, bf16[2,896,1280]{2,1,0:T(8,128)(2,1)}, u32[]{:S(2)}, u32[]{:S(2)}) collective-permute-start(bf16[2,896,1280]{2,1,0:T(8,128)(2,1)} %pad_maximum_fusion.4), channel_id=1, source_target_pairs={{0,8},{8,0},{16,24},{24,16},{1,9},{9,1},{17,25},{25,17},{2,10},{10... | collective-permute-start | bytes 13762568 | tf_op jit(solution)/shard_map/ppermute | solution.py:48
  167.4 39.1 %copy-start.19 = (bf16[896,1280]{1,0:T(8,128)(2,1)S(1)}, bf16[896,1280]{1,0:T(8,128)(2,1)}, u32[]{:S(2)}) copy-start(bf16[896,1280]{1,0:T(8,128)(2,1)} %param.22) | copy-start | bytes 6881284
  167.5 41.9 %collective-permute-start.29 = (bf16[96,1792]{1,0:T(8,128)(2,1)S(1)}, bf16[96,1792]{1,0:T(8,128)(2,1)S(1)}, u32[]{:S(2)}, u32[]{:S(2)}) collective-permute-start(bf16[96,1792]{1,0:T(8,128)(2,1)S(1)} %get-tuple-element.22), channel_id=1, source_target_pairs={{0,1},{2,0},{4,2},{6,4},{7,6},{5,7},{3,5},{1,3},{8,9},{10,8},{12,1... | collective-permute-start | bytes 1032200 | tf_op jit(solution)/shard_map/ppermute | solution.py:96
  169.6 41.4 %collective-permute-start.15 = (bf16[96,1792]{1,0:T(8,128)(2,1)S(1)}, bf16[96,1792]{1,0:T(8,128)(2,1)S(1)}, u32[]{:S(2)}, u32[]{:S(2)}) collective-permute-start(bf16[96,1792]{1,0:T(8,128)(2,1)S(1)} %get-tuple-element.20), channel_id=1, source_target_pairs={{0,2},{2,4},{4,6},{6,7},{7,5},{5,3},{3,1},{1,0},{8,10},{10,12},{12... | collective-permute-start | bytes 1032200 | tf_op jit(solution)/shard_map/ppermute | solution.py:96
  209.3 81.0 %collective-permute-start.37 = (bf16[2,896,1280]{2,1,0:T(8,128)(2,1)}, bf16[2,896,1280]{2,1,0:T(8,128)(2,1)}, u32[]{:S(2)}, u32[]{:S(2)}) collective-permute-start(bf16[2,896,1280]{2,1,0:T(8,128)(2,1)} %pad_maximum_fusion.3), channel_id=1, source_target_pairs={{0,8},{8,0},{16,24},{24,16},{1,9},{9,1},{17,25},{25,17},{2,10},{10... | collective-permute-start | bytes 13762568 | tf_op jit(solution)/shard_map/ppermute | solution.py:48
  209.3 10.5 %collective-permute-start.30 = (bf16[96,1792]{1,0:T(8,128)(2,1)S(1)}, bf16[96,1792]{1,0:T(8,128)(2,1)S(1)}, u32[]{:S(2)}, u32[]{:S(2)}) collective-permute-start(bf16[96,1792]{1,0:T(8,128)(2,1)S(1)} %collective-permute-done.29), channel_id=1, source_target_pairs={{0,1},{2,0},{4,2},{6,4},{7,6},{5,7},{3,5},{1,3},{8,9},{10,8},{12,1... | collective-permute-start | bytes 1032200 | tf_op jit(solution)/shard_map/ppermute | solution.py:96
  211.1 10.5 %collective-permute-start.16 = (bf16[96,1792]{1,0:T(8,128)(2,1)S(1)}, bf16[96,1792]{1,0:T(8,128)(2,1)S(1)}, u32[]{:S(2)}, u32[]{:S(2)}) collective-permute-start(bf16[96,1792]{1,0:T(8,128)(2,1)S(1)} %collective-permute-done.15), channel_id=1, source_target_pairs={{0,2},{2,4},{4,6},{6,7},{7,5},{5,3},{3,1},{1,0},{8,10},{10,12},{12... | collective-permute-start | bytes 1032200 | tf_op jit(solution)/shard_map/ppermute | solution.py:96
  219.8 9.7 %collective-permute-start.31 = (bf16[96,1792]{1,0:T(8,128)(2,1)S(1)}, bf16[96,1792]{1,0:T(8,128)(2,1)S(1)}, u32[]{:S(2)}, u32[]{:S(2)}) collective-permute-start(bf16[96,1792]{1,0:T(8,128)(2,1)S(1)} %collective-permute-done.30), channel_id=1, source_target_pairs={{0,1},{2,0},{4,2},{6,4},{7,6},{5,7},{3,5},{1,3},{8,9},{10,8},{12,1... | collective-permute-start | bytes 1032200 | tf_op jit(solution)/shard_map/ppermute | solution.py:96
  221.5 9.7 %collective-permute-start.17 = (bf16[96,1792]{1,0:T(8,128)(2,1)S(1)}, bf16[96,1792]{1,0:T(8,128)(2,1)S(1)}, u32[]{:S(2)}, u32[]{:S(2)}) collective-permute-start(bf16[96,1792]{1,0:T(8,128)(2,1)S(1)} %collective-permute-done.16), channel_id=1, source_target_pairs={{0,2},{2,4},{4,6},{6,7},{7,5},{5,3},{3,1},{1,0},{8,10},{10,12},{12... | collective-permute-start | bytes 1032200 | tf_op jit(solution)/shard_map/ppermute | solution.py:96
  229.5 8.8 %collective-permute-start.32 = (bf16[96,1792]{1,0:T(8,128)(2,1)S(1)}, bf16[96,1792]{1,0:T(8,128)(2,1)S(1)}, u32[]{:S(2)}, u32[]{:S(2)}) collective-permute-start(bf16[96,1792]{1,0:T(8,128)(2,1)S(1)} %collective-permute-done.31), channel_id=1, source_target_pairs={{0,1},{2,0},{4,2},{6,4},{7,6},{5,7},{3,5},{1,3},{8,9},{10,8},{12,1... | collective-permute-start | bytes 1032200 | tf_op jit(solution)/shard_map/ppermute | solution.py:96
  231.2 8.8 %collective-permute-start.18 = (bf16[96,1792]{1,0:T(8,128)(2,1)S(1)}, bf16[96,1792]{1,0:T(8,128)(2,1)S(1)}, u32[]{:S(2)}, u32[]{:S(2)}) collective-permute-start(bf16[96,1792]{1,0:T(8,128)(2,1)S(1)} %collective-permute-done.17), channel_id=1, source_target_pairs={{0,2},{2,4},{4,6},{6,7},{7,5},{5,3},{3,1},{1,0},{8,10},{10,12},{12... | collective-permute-start | bytes 1032200 | tf_op jit(solution)/shard_map/ppermute | solution.py:96
  231.6 32.6 %copy-start.3 = (bf16[768,896]{1,0:T(8,128)(2,1)S(1)}, bf16[768,896]{1,0:T(8,128)(2,1)}, u32[]{:S(2)}) copy-start(bf16[768,896]{1,0:T(8,128)(2,1)} %copy-done.1) | copy-start | bytes 4128772
  231.7 32.6 %copy-start.6 = (bf16[768,896]{1,0:T(8,128)(2,1)S(1)}, bf16[768,896]{1,0:T(8,128)(2,1)}, u32[]{:S(2)}) copy-start(bf16[768,896]{1,0:T(8,128)(2,1)} %copy-done.4) | copy-start | bytes 4128772
  231.7 32.6 %copy-start.9 = (bf16[768,896]{1,0:T(8,128)(2,1)S(1)}, bf16[768,896]{1,0:T(8,128)(2,1)}, u32[]{:S(2)}) copy-start(bf16[768,896]{1,0:T(8,128)(2,1)} %copy-done.7) | copy-start | bytes 4128772
  231.7 32.6 %copy-start.12 = (bf16[768,896]{1,0:T(8,128)(2,1)S(1)}, bf16[768,896]{1,0:T(8,128)(2,1)}, u32[]{:S(2)}) copy-start(bf16[768,896]{1,0:T(8,128)(2,1)} %copy-done.10) | copy-start | bytes 4128772
  238.3 8.2 %collective-permute-start.33 = (bf16[96,1792]{1,0:T(8,128)(2,1)S(1)}, bf16[96,1792]{1,0:T(8,128)(2,1)S(1)}, u32[]{:S(2)}, u32[]{:S(2)}) collective-permute-start(bf16[96,1792]{1,0:T(8,128)(2,1)S(1)} %collective-permute-done.32), channel_id=1, source_target_pairs={{0,1},{2,0},{4,2},{6,4},{7,6},{5,7},{3,5},{1,3},{8,9},{10,8},{12,1... | collective-permute-start | bytes 1032200 | tf_op jit(solution)/shard_map/ppermute | solution.py:96
  240.0 8.2 %collective-permute-start.19 = (bf16[96,1792]{1,0:T(8,128)(2,1)S(1)}, bf16[96,1792]{1,0:T(8,128)(2,1)S(1)}, u32[]{:S(2)}, u32[]{:S(2)}) collective-permute-start(bf16[96,1792]{1,0:T(8,128)(2,1)S(1)} %collective-permute-done.18), channel_id=1, source_target_pairs={{0,2},{2,4},{4,6},{6,7},{7,5},{5,3},{3,1},{1,0},{8,10},{10,12},{12... | collective-permute-start | bytes 1032200 | tf_op jit(solution)/shard_map/ppermute | solution.py:96
  246.5 8.7 %collective-permute-start.34 = (bf16[96,1792]{1,0:T(8,128)(2,1)S(1)}, bf16[96,1792]{1,0:T(8,128)(2,1)S(1)}, u32[]{:S(2)}, u32[]{:S(2)}) collective-permute-start(bf16[96,1792]{1,0:T(8,128)(2,1)S(1)} %collective-permute-done.33), channel_id=1, source_target_pairs={{0,1},{2,0},{4,2},{6,4},{7,6},{5,7},{3,5},{1,3},{8,9},{10,8},{12,1... | collective-permute-start | bytes 1032200 | tf_op jit(solution)/shard_map/ppermute | solution.py:96
  248.2 8.7 %collective-permute-start.20 = (bf16[96,1792]{1,0:T(8,128)(2,1)S(1)}, bf16[96,1792]{1,0:T(8,128)(2,1)S(1)}, u32[]{:S(2)}, u32[]{:S(2)}) collective-permute-start(bf16[96,1792]{1,0:T(8,128)(2,1)S(1)} %collective-permute-done.19), channel_id=1, source_target_pairs={{0,2},{2,4},{4,6},{6,7},{7,5},{5,3},{3,1},{1,0},{8,10},{10,12},{12... | collective-permute-start | bytes 1032200 | tf_op jit(solution)/shard_map/ppermute | solution.py:96
  255.2 7.2 %collective-permute-start.35 = (bf16[96,1792]{1,0:T(8,128)(2,1)S(1)}, bf16[96,1792]{1,0:T(8,128)(2,1)S(1)}, u32[]{:S(2)}, u32[]{:S(2)}) collective-permute-start(bf16[96,1792]{1,0:T(8,128)(2,1)S(1)} %collective-permute-done.34), channel_id=1, source_target_pairs={{0,1},{2,0},{4,2},{6,4},{7,6},{5,7},{3,5},{1,3},{8,9},{10,8},{12,1... | collective-permute-start | bytes 1032200 | tf_op jit(solution)/shard_map/ppermute | solution.py:96
  256.9 7.3 %collective-permute-start.21 = (bf16[96,1792]{1,0:T(8,128)(2,1)S(1)}, bf16[96,1792]{1,0:T(8,128)(2,1)S(1)}, u32[]{:S(2)}, u32[]{:S(2)}) collective-permute-start(bf16[96,1792]{1,0:T(8,128)(2,1)S(1)} %collective-permute-done.20), channel_id=1, source_target_pairs={{0,2},{2,4},{4,6},{6,7},{7,5},{5,3},{3,1},{1,0},{8,10},{10,12},{12... | collective-permute-start | bytes 1032200 | tf_op jit(solution)/shard_map/ppermute | solution.py:96
  312.9 4.5 %collective-permute-start.40 = (f32[16,1280]{1,0:T(8,128)S(1)}, f32[16,1280]{1,0:T(8,128)S(1)}, u32[]{:S(2)}, u32[]{:S(2)}) collective-permute-start(f32[16,1280]{1,0:T(8,128)S(1)} %fusion.5), channel_id=1, source_target_pairs={{0,16},{8,24},{16,0},{24,8},{1,17},{9,25},{17,1},{25,9},{2,18},{10... | collective-permute-start | bytes 245768 | tf_op jit(solution)/shard_map/ppermute | solution.py:45
  317.5 3.2 collective-permute-start.41
  323.3 13.7 %collective-permute-start.49 = (f32[16,448]{1,0:T(8,128)S(1)}, f32[16,448]{1,0:T(8,128)S(1)}, u32[]{:S(2)}, u32[]{:S(2)}) collective-permute-start(f32[16,448]{1,0:T(8,128)S(1)} %get-tuple-element.38), channel_id=1, source_target_pairs={{0,1},{1,8},{2,9},{3,16},{4,17},{5,24},{6,25},{7,0},{8,3},{9,10},{... | collective-permute-start | bytes 86024 | tf_op jit(solution)/shard_map/ppermute | solution.py:236
  324.8 13.5 %collective-permute-start.48 = (f32[16,448]{1,0:T(8,128)S(1)}, f32[16,448]{1,0:T(8,128)S(1)}, u32[]{:S(2)}, u32[]{:S(2)}) collective-permute-start(f32[16,448]{1,0:T(8,128)S(1)} %get-tuple-element.39), channel_id=1, source_target_pairs={{0,8},{1,9},{2,16},{3,17},{4,24},{5,25},{6,0},{7,1},{8,10},{9,11},... | collective-permute-start | bytes 86024 | tf_op jit(solution)/shard_map/ppermute | solution.py:236
  325.8 13.2 %collective-permute-start.47 = (f32[16,448]{1,0:T(8,128)S(1)}, f32[16,448]{1,0:T(8,128)S(1)}, u32[]{:S(2)}, u32[]{:S(2)}) collective-permute-start(f32[16,448]{1,0:T(8,128)S(1)} %get-tuple-element.40), channel_id=1, source_target_pairs={{0,9},{1,16},{2,17},{3,24},{4,25},{5,0},{6,1},{7,8},{8,11},{9,18},... | collective-permute-start | bytes 86024 | tf_op jit(solution)/shard_map/ppermute | solution.py:236
  326.9 17.5 %all-to-all-start.1 = ((f32[4,4,448]{2,1,0:T(4,128)}), f32[4,4,448]{2,1,0:T(4,128)S(1)}, u32[]{:S(2)}, u32[]{:S(2)}) async-start(f32[4,4,448]{2,1,0:T(4,128)} %fusion.46), calls=%async_computation.1 | async-start | bytes 65536 | tf_op jit(solution)/shard_map/all_to_all | solution.py:240
  331.6 12.8 %collective-permute-start.46 = (f32[16,448]{1,0:T(8,128)S(1)}, f32[16,448]{1,0:T(8,128)S(1)}, u32[]{:S(2)}, u32[]{:S(2)}) collective-permute-start(f32[16,448]{1,0:T(8,128)S(1)} %get-tuple-element.41), channel_id=1, source_target_pairs={{0,16},{1,17},{2,24},{3,25},{4,0},{5,1},{6,8},{7,9},{8,18},{9,19},... | collective-permute-start | bytes 86024 | tf_op jit(solution)/shard_map/ppermute | solution.py:236
  333.6 10.8 %collective-permute-start.45 = (f32[16,448]{1,0:T(8,128)S(1)}, f32[16,448]{1,0:T(8,128)S(1)}, u32[]{:S(2)}, u32[]{:S(2)}) collective-permute-start(f32[16,448]{1,0:T(8,128)S(1)} %get-tuple-element.42), channel_id=1, source_target_pairs={{0,17},{1,24},{2,25},{3,0},{4,1},{5,8},{6,9},{7,16},{8,19},{9,26},... | collective-permute-start | bytes 86024 | tf_op jit(solution)/shard_map/ppermute | solution.py:236
  337.0 7.4 %collective-permute-start.44 = (f32[16,448]{1,0:T(8,128)S(1)}, f32[16,448]{1,0:T(8,128)S(1)}, u32[]{:S(2)}, u32[]{:S(2)}) collective-permute-start(f32[16,448]{1,0:T(8,128)S(1)} %get-tuple-element.43), channel_id=1, source_target_pairs={{0,24},{1,25},{2,0},{3,1},{4,8},{5,9},{6,16},{7,17},{8,26},{9,27},... | collective-permute-start | bytes 86024 | tf_op jit(solution)/shard_map/ppermute | solution.py:236
  338.3 6.1 %collective-permute-start.42 = (f32[16,448]{1,0:T(8,128)S(1)}, f32[16,448]{1,0:T(8,128)S(1)}, u32[]{:S(2)}, u32[]{:S(2)}) collective-permute-start(f32[16,448]{1,0:T(8,128)S(1)} %get-tuple-element.44), channel_id=1, source_target_pairs={{0,0},{1,1},{2,8},{3,9},{4,16},{5,17},{6,24},{7,25},{8,2},{9,3},{1... | collective-permute-start | bytes 86024 | tf_op jit(solution)/shard_map/ppermute | solution.py:236
  339.0 6.8 %collective-permute-start.43 = (f32[16,448]{1,0:T(8,128)S(1)}, f32[16,448]{1,0:T(8,128)S(1)}, u32[]{:S(2)}, u32[]{:S(2)}) collective-permute-start(f32[16,448]{1,0:T(8,128)S(1)} %get-tuple-element.37), channel_id=1, source_target_pairs={{0,25},{1,0},{2,1},{3,8},{4,9},{5,16},{6,17},{7,24},{8,27},{9,2},{... | collective-permute-start | bytes 86024 | tf_op jit(solution)/shard_map/ppermute | solution.py:236
  (26 other events, 188.3 us)

commit v10 on v5

--- a/solution.py
+++ b/solution.py
@@ -144,12 +144,11 @@
     ffn_gain_perm = take_blocks(ffn_gain, order, d_grp, 0)
 
     norm_in = rms_scale(hidden_perm, attn_gain_perm)
-    qkv = jnp.dot(norm_in, qkv_full, preferred_element_type=jnp.float32).astype(jnp.bfloat16)
-    queries = qkv[:, :q_cols]
+    kv = jnp.dot(norm_in, qkv_full[:, q_cols:], preferred_element_type=jnp.float32).astype(jnp.bfloat16)
     per_dev = k_cols // KVH
     group_heads = HEADS // KVH
-    key_split = qkv[:, q_cols : q_cols + k_cols].reshape(row_count, per_dev, KVH)
-    value_split = qkv[:, q_cols + k_cols :].reshape(row_count, per_dev, KVH)
+    key_split = kv[:, :k_cols].reshape(row_count, per_dev, KVH)
+    value_split = kv[:, k_cols:].reshape(row_count, per_dev, KVH)
     outgoing_kv = jnp.stack(
         [
             jnp.concatenate(
@@ -160,6 +159,7 @@
         ]
     )
     kv_in = lax.all_to_all(outgoing_kv, "tp", 0, 0, tiled=True)
+    queries = jnp.dot(norm_in, qkv_full[:, :q_cols], preferred_element_type=jnp.float32).astype(jnp.bfloat16)
     key_head = kv_in[:, :, :per_dev].transpose(1, 0, 2).reshape(row_count, tp_size * per_dev)
     value_head = kv_in[:, :, per_dev:].transpose(1, 0, 2).reshape(row_count, tp_size * per_dev)
 

time: 328 us -> 339 us (1.034)
  waiting for transfers between devices: 131 us -> 125 us
  local copies, waits for them, and re-layouts: 21.1 us -> 26.8 us
  matrix products: 45.1 us -> 48.6 us
  starting transfers between devices: 61.6 us -> 65.1 us
    all_to_all x1, waiting for transfers between devices: 0.01 us -> 4.25 us  [on_device(): kv_in = lax.all_to_all(outgoing_kv, 'tp', 0, 0, tiled=True)]
    ppermute x8, waiting for transfers between devices: 5.49 us -> 1.42 us  [on_device(): totals = totals + lax.ppermute(piece, ('grp', 'tp'), pairs)]
    ppermute x7, waiting for transfers between devices: 43.9 us -> 40.1 us  [gather_grp(): moving = lax.ppermute(moving, 'grp', ring)]
    dot_general x1 -> x2, matrix products: 4.33 us -> 7.03 us  [the longest x1 5.05 us: on_device(): jnp.dot(norm_in, qkv_full[:, :q_cols], preferred_element_type=jnp.float32)]
  transfers between devices with their start and end apart: 52 -> 52, of which waited for: 25 -> 20; matrix products, arithmetic and copies ran while one was open for 33% -> 35% of each run, Pallas kernels for 0% -> 0%
where the time goes in v10:
time: 339 us; the launch traced here: 335 us
  waiting for transfers between devices  125 us (37%)
  starting transfers between devices  65.1 us (19%)
  other arithmetic  54.1 us (16%)
  matrix products  48.6 us (14%)
  local copies, waits for them, and re-layouts  26.8 us (8%)
  between operations  15.5 us (5%)
    ppermute x14, waiting for transfers between devices, ring_psum(): moving = lax.ppermute(moving, axis, pairs)  41.8 us
    ppermute x7, waiting for transfers between devices, gather_grp(): moving = lax.ppermute(moving, 'grp', ring)  40.1 us
    ppermute x14, waiting for transfers between devices, ring_psum(): got = lax.ppermute(acc, axis, pairs)  36.9 us
    concatenate x6, other arithmetic, gather_grp(): return jnp.concatenate([mine, other], 0)  18.8 us
    ppermute x14, starting transfers between devices, ring_psum(): got = lax.ppermute(acc, axis, pairs)  16.3 us
    ppermute x14, starting transfers between devices, ring_psum(): moving = lax.ppermute(moving, axis, pairs)  15 us
    dot_general x1, matrix products, on_device(): jnp.dot(selector.astype(jnp.bfloat16), hidden_ffn, preferred_element_type...  14.5 us
    ppermute x8, starting transfers between devices, on_device(): totals = totals + lax.ppermute(piece, ('grp', 'tp'), pairs)  14.3 us
  transfers between devices with their start and end apart: 52, of which 20 were waited for; matrix products, arithmetic and copies ran while one was open for 35% of the time, Pallas kernels for 0%

profile of v10, /device:TPU:0, one launch (start us, length us, event | category | flops | bytes accessed | tf_op | source)
XLA Modules:
  0.0 335.4 jit_solution(6995580451842638322)
XLA Ops:
  2.3 2.0 pad_maximum_fusion.9
  4.3 2.9 collective-permute-start.2
  8.1 2.0 collective-permute-start.48
  31.9 3.1 constant_dynamic-slice_fusion.7
  35.0 2.9 pad_maximum_fusion.7
  43.0 2.0 pad_maximum_fusion.5
  46.7 2.0 fusion.22
  55.6 5.8 %all-to-all-start = ((bf16[8,768,32]{1,2,0:T(8,128)(2,1)}), bf16[8,768,32]{1,2,0:T(8,128)(2,1)}, u32[]{:S(2)}, u32[]{:S(2)}) async-start(bf16[8,768,32]{1,2,0:T(8,128)(2,1)} %fusion.48), calls=%async_computation | async-start | bytes 786432 | tf_op jit(solution)/shard_map/all_to_all | solution.py:161
  61.4 5.0 %fusion.13 = bf16[768,256]{1,0:T(8,128)(2,1)} fusion(bf16[3584,384]{1,0:T(8,128)(2,1)} %bitcast.153, f32[3584]{0:T(1024)} %copy-done.29, f32[768]{0:T(1024)S(1)} %add_rsqrt_fusion.1, bf16[768,896]{1,0:T(8,128)(2,1)} %copy-done.7, bf16[768,896]{1,0:T(8,128)(2,1)} %copy-done.10, bf16[768,896]{1,0:T(8,128)(2,1)} %copy-done.4, bf16[768,896]{1,0:T(8,128)(2,1)} %copy-done.1), kind=kOutput, calls=%fused_computation.29 | convolution fusion | flops 1439760384 | bytes 7752704 | tf_op jit(solution)/shard_map/dot_general | solution.py:162
  66.4 1.8 reshape.140
  69.4 4.3 %all-to-all-done = bf16[8,768,32]{1,2,0:T(8,128)(2,1)} async-done(((bf16[8,768,32]{1,2,0:T(8,128)(2,1)}), bf16[8,768,32]{1,2,0:T(8,128)(2,1)}, u32[]{:S(2)}, u32[]{:S(2)}) %all-to-all-start) | async-done | bytes 393248 | tf_op jit(solution)/shard_map/all_to_all | solution.py:161
  73.7 1.7 slice_bitcast_fusion.1
  75.4 1.7 reshape_reshape.7
  77.7 3.6 %fusion.80 = (f32[2,2,384]{2,1,0:T(2,128)S(1)}, f32[2,2,384,384]{2,3,1,0:T(8,128)}) fusion(pred[2,384,384]{1,2,0:T(8,128)(4,1)} %broadcast_compare_fusion, bf16[2,384,2,128]{3,2,1,0:T(2,128)(2,1)} %reshape.140, bf16[2,384,128,1]{1,0,2,3:T(2,128)(2,1)} %bitcast.180), kind=kOutput, calls=%fused_computation.171 | convolution fusion | flops 153354624 | bytes 3250176 | tf_op jit(solution)/shard_map/sub | solution.py:29
  81.4 2.8 fusion.18
  85.5 1.5 pad_maximum_fusion.6
  87.0 1.6 convolution_convert_fusion
  88.6 1.9 fusion.72
  90.5 1.5 copy-done.16
  92.1 1.7 collective-permute-start.20
  96.4 1.5 collective-permute-start.34
  97.9 3.6 %collective-permute-done.20 = bf16[96,1792]{1,0:T(8,128)(2,1)S(1)} collective-permute-done((bf16[96,1792]{1,0:T(8,128)(2,1)S(1)}, bf16[96,1792]{1,0:T(8,128)(2,1)S(1)}, u32[]{:S(2)}, u32[]{:S(2)}) %collective-permute-start.20) | collective-permute-done | bytes 344096 | tf_op jit(solution)/shard_map/ppermute | solution.py:90
  102.5 1.5 collective-permute-start.21
  105.9 5.0 %collective-permute-done.21 = bf16[96,1792]{1,0:T(8,128)(2,1)S(1)} collective-permute-done((bf16[96,1792]{1,0:T(8,128)(2,1)S(1)}, bf16[96,1792]{1,0:T(8,128)(2,1)S(1)}, u32[]{:S(2)}, u32[]{:S(2)}) %collective-permute-start.21) | collective-permute-done | bytes 344096 | tf_op jit(solution)/shard_map/ppermute | solution.py:90
  111.9 1.5 collective-permute-start.22
  114.1 5.1 %collective-permute-done.22 = bf16[96,1792]{1,0:T(8,128)(2,1)S(1)} collective-permute-done((bf16[96,1792]{1,0:T(8,128)(2,1)S(1)}, bf16[96,1792]{1,0:T(8,128)(2,1)S(1)}, u32[]{:S(2)}, u32[]{:S(2)}) %collective-permute-start.22) | collective-permute-done | bytes 344096 | tf_op jit(solution)/shard_map/ppermute | solution.py:90
  120.3 1.6 collective-permute-start.23
  122.6 5.9 %collective-permute-done.23 = bf16[96,1792]{1,0:T(8,128)(2,1)S(1)} collective-permute-done((bf16[96,1792]{1,0:T(8,128)(2,1)S(1)}, bf16[96,1792]{1,0:T(8,128)(2,1)S(1)}, u32[]{:S(2)}, u32[]{:S(2)}) %collective-permute-start.23) | collective-permute-done | bytes 344096 | tf_op jit(solution)/shard_map/ppermute | solution.py:90
  128.6 2.3 collective-permute-start.24
  131.1 7.0 %collective-permute-done.24 = bf16[96,1792]{1,0:T(8,128)(2,1)S(1)} collective-permute-done((bf16[96,1792]{1,0:T(8,128)(2,1)S(1)}, bf16[96,1792]{1,0:T(8,128)(2,1)S(1)}, u32[]{:S(2)}, u32[]{:S(2)}) %collective-permute-start.24) | collective-permute-done | bytes 344096 | tf_op jit(solution)/shard_map/ppermute | solution.py:90
  138.2 2.5 collective-permute-start.25
  140.9 8.0 %collective-permute-done.25 = bf16[96,1792]{1,0:T(8,128)(2,1)S(1)} collective-permute-done((bf16[96,1792]{1,0:T(8,128)(2,1)S(1)}, bf16[96,1792]{1,0:T(8,128)(2,1)S(1)}, u32[]{:S(2)}, u32[]{:S(2)}) %collective-permute-start.25) | collective-permute-done | bytes 344096 | tf_op jit(solution)/shard_map/ppermute | solution.py:90
  148.9 2.5 collective-permute-start.26
  151.7 2.5 pad_maximum_fusion.4
  154.1 2.1 collective-permute-done.26
  156.5 2.5 collective-permute-start.27
  159.4 36.2 %collective-permute-done.34 = bf16[896,1280]{1,0:T(8,128)(2,1)S(1)} collective-permute-done((bf16[896,1280]{1,0:T(8,128)(2,1)}, bf16[896,1280]{1,0:T(8,128)(2,1)S(1)}, u32[]{:S(2)}, u32[]{:S(2)}) %collective-permute-start.34) | collective-permute-done | bytes 2293792 | tf_op jit(solution)/shard_map/ppermute | solution.py:45
  195.6 2.8 pad_maximum_fusion.3
  198.5 1.5 collective-permute-start.28
  200.7 8.3 %collective-permute-done.28 = bf16[96,1792]{1,0:T(8,128)(2,1)S(1)} collective-permute-done((bf16[96,1792]{1,0:T(8,128)(2,1)S(1)}, bf16[96,1792]{1,0:T(8,128)(2,1)S(1)}, u32[]{:S(2)}, u32[]{:S(2)}) %collective-permute-start.28) | collective-permute-done | bytes 344096 | tf_op jit(solution)/shard_map/ppermute | solution.py:96
  209.0 1.5 collective-permute-start.29
  211.2 7.5 %collective-permute-done.29 = bf16[96,1792]{1,0:T(8,128)(2,1)S(1)} collective-permute-done((bf16[96,1792]{1,0:T(8,128)(2,1)S(1)}, bf16[96,1792]{1,0:T(8,128)(2,1)S(1)}, u32[]{:S(2)}, u32[]{:S(2)}) %collective-permute-start.29) | collective-permute-done | bytes 344096 | tf_op jit(solution)/shard_map/ppermute | solution.py:96
  218.7 1.5 collective-permute-start.30
  220.9 6.6 %collective-permute-done.30 = bf16[96,1792]{1,0:T(8,128)(2,1)S(1)} collective-permute-done((bf16[96,1792]{1,0:T(8,128)(2,1)S(1)}, bf16[96,1792]{1,0:T(8,128)(2,1)S(1)}, u32[]{:S(2)}, u32[]{:S(2)}) %collective-permute-start.30) | collective-permute-done | bytes 344096 | tf_op jit(solution)/shard_map/ppermute | solution.py:96
  227.5 1.5 collective-permute-start.31
  229.7 6.1 %collective-permute-done.31 = bf16[96,1792]{1,0:T(8,128)(2,1)S(1)} collective-permute-done((bf16[96,1792]{1,0:T(8,128)(2,1)S(1)}, bf16[96,1792]{1,0:T(8,128)(2,1)S(1)}, u32[]{:S(2)}, u32[]{:S(2)}) %collective-permute-start.31) | collective-permute-done | bytes 344096 | tf_op jit(solution)/shard_map/ppermute | solution.py:96
  235.7 1.5 collective-permute-start.32
  237.9 6.5 %collective-permute-done.32 = bf16[96,1792]{1,0:T(8,128)(2,1)S(1)} collective-permute-done((bf16[96,1792]{1,0:T(8,128)(2,1)S(1)}, bf16[96,1792]{1,0:T(8,128)(2,1)S(1)}, u32[]{:S(2)}, u32[]{:S(2)}) %collective-permute-start.32) | collective-permute-done | bytes 344096 | tf_op jit(solution)/shard_map/ppermute | solution.py:96
  244.4 1.5 collective-permute-start.33
  246.6 5.1 %collective-permute-done.33 = bf16[96,1792]{1,0:T(8,128)(2,1)S(1)} collective-permute-done((bf16[96,1792]{1,0:T(8,128)(2,1)S(1)}, bf16[96,1792]{1,0:T(8,128)(2,1)S(1)}, u32[]{:S(2)}, u32[]{:S(2)}) %collective-permute-start.33) | collective-permute-done | bytes 344096 | tf_op jit(solution)/shard_map/ppermute | solution.py:96
  251.7 1.5 collective-permute-done.19
  253.3 5.7 %multiply_reduce_fusion = (f32[768]{0:T(1024)S(1)}, f32[768,3584]{1,0:T(8,128)}) fusion(bf16[768,1792]{1,0:T(8,128)(2,1)S(1)} %constant_dynamic-update-slice_fusion, bf16[768,1792]{1,0:T(8,128)(2,1)S(1)} %constant_dynamic-update-slice_fusion.8, bf16[768,896]{1,0:T(8,128)(2,1)S(1)} %copy-done.9, bf16[768,896]{1,0:T(8,128)(2,1)S(1)} %copy-done.12, ...), kind=kLoop, calls=%fused_computation.8 | loop fusion | flops 41286912 | bytes 22023168 | tf_op jit(solution)/shard_map/reduce_sum | solution.py:17
  259.0 7.1 %pad_maximum_fusion.1 = bf16[4,896,1280]{2,1,0:T(8,128)(2,1)} fusion(bf16[2,896,1280]{2,1,0:T(8,128)(2,1)} %collective-permute-done.37, bf16[1,896,1280]{2,1,0:T(8,128)(2,1)S(1)} %bitcast.148, bf16[1,896,1280]{2,1,0:T(8,128)(2,1)S(1)} %bitcast.142), kind=kLoop, calls=%fused_computation.10 | loop fusion | flops 9175040 | bytes 18350080 | tf_op jit(solution)/shard_map/concatenate | solution.py:49
  266.1 13.4 %fusion.70 = f32[768,1280]{1,0:T(8,128)} fusion(bf16[3584,1280]{1,0:T(8,128)(2,1)} %bitcast.150, f32[3584]{0:T(1024)S(1)} %copy-done.28, f32[768]{0:T(1024)S(1)} %add_rsqrt_fusion, bf16[768,1792]{1,0:T(8,128)(2,1)S(1)} %constant_dynamic-update-slice_fusion, bf16[768,1792]{1,0:T(8,128)(2,1)S(1)} %constant_dynamic-update-slice_fusion.8, ...), kind=kOutput, calls=%fused_computation.161 | convolution fusion | flops 7090470912 | bytes 24134656 | tf_op jit(solution)/shard_map/dot_general | solution.py:188
  279.5 8.2 %pad_maximum_fusion = bf16[4,896,1280]{2,1,0:T(8,128)(2,1)} fusion(bf16[2,896,1280]{2,1,0:T(8,128)(2,1)} %collective-permute-done.35, bf16[1,896,1280]{2,1,0:T(8,128)(2,1)} %bitcast.146, bf16[1,896,1280]{2,1,0:T(8,128)(2,1)S(1)} %bitcast.144), kind=kLoop, calls=%fused_computation.9 | loop fusion | flops 9175040 | bytes 18350080 | tf_op jit(solution)/shard_map/concatenate | solution.py:49
  287.7 14.5 %fusion.5 = f32[16,1280]{1,0:T(8,128)S(1)} fusion(f32[768,1280]{1,0:T(8,128)} %fusion.70, s32[768]{0:T(1024)S(1)} %add.528, bf16[3584,1280]{1,0:T(8,128)(2,1)} %bitcast.149, f32[3584]{0:T(1024)S(1)} %copy-done.28, f32[768]{0:T(1024)S(1)} %add_rsqrt_fusion, bf16[768,1792]{1,0:T(8,128)(2,1)} %copy-done.14, bf16[768,1792]{1,0:T(8,128)(2,1)} %copy-done.13, ...), kind=kOutput, calls=%fused_computation.21 | convolution fusion | flops 7127863296 | bytes 24219648 | tf_op jit(solution)/shard_map/dot_general | solution.py:195
  302.8 3.9 %collective-permute-done.38 = f32[16,1280]{1,0:T(8,128)S(1)} collective-permute-done((f32[16,1280]{1,0:T(8,128)S(1)}, f32[16,1280]{1,0:T(8,128)S(1)}, u32[]{:S(2)}, u32[]{:S(2)}) %collective-permute-start.38) | collective-permute-done | bytes 81952 | tf_op jit(solution)/shard_map/ppermute | solution.py:45
  307.6 2.3 fusion.25
  310.0 2.1 convolution_bitcast_fusion
  315.4 5.4 %all-to-all-start.1 = ((f32[4,4,448]{2,1,0:T(4,128)}), f32[4,4,448]{2,1,0:T(4,128)S(1)}, u32[]{:S(2)}, u32[]{:S(2)}) async-start(f32[4,4,448]{2,1,0:T(4,128)} %fusion.58), calls=%async_computation.1 | async-start | bytes 65536 | tf_op jit(solution)/shard_map/all_to_all | solution.py:238
  320.8 2.0 collective-permute-start.44
  322.8 2.5 collective-permute-start.43
  327.3 5.7 %collective-permute-start.41 = (f32[16,448]{1,0:T(8,128)S(1)}, f32[16,448]{1,0:T(8,128)S(1)}, u32[]{:S(2)}, u32[]{:S(2)}) collective-permute-start(f32[16,448]{1,0:T(8,128)S(1)} %get-tuple-element.31), channel_id=1, source_target_pairs={{0,25},{1,0},{2,1},{3,8},{4,9},{5,16},{6,17},{7,24},{8,27},{9,2},{... | collective-permute-start | bytes 86024 | tf_op jit(solution)/shard_map/ppermute | solution.py:234
  333.3 1.4 collective-permute-done.41
  (239 shorter events, 48.8 us)
Async XLA Ops:
  0.0 310.0 %copy-start = (bf16[896,1280]{1,0:T(8,128)(2,1)S(1)}, bf16[896,1280]{1,0:T(8,128)(2,1)}, u32[]{:S(2)}) copy-start(bf16[896,1280]{1,0:T(8,128)(2,1)} %param.24) | copy-start | bytes 6881284
  0.0 28.7 %copy-start.35 = (s32[2,8]{1,0:T(2,128)S(1)}, s32[2,8]{1,0:T(2,128)}, u32[]{:S(2)}) copy-start(s32[2,8]{1,0:T(2,128)} %param.14) | copy-start | bytes 196
  0.0 29.9 %copy-start.26 = (f32[3584]{0:T(1024)S(1)}, f32[3584]{0:T(1024)}, u32[]{:S(2)}) copy-start(f32[3584]{0:T(1024)} %param.16) | copy-start | bytes 43012
  0.0 30.0 %copy-start.27 = (f32[3584]{0:T(1024)S(1)}, f32[3584]{0:T(1024)}, u32[]{:S(2)}) copy-start(f32[3584]{0:T(1024)} %param.21) | copy-start | bytes 43012
  4.3 30.7 %collective-permute-start.2 = (bf16[896,384]{1,0:T(8,128)(2,1)}, bf16[896,384]{1,0:T(8,128)(2,1)}, u32[]{:S(2)}, u32[]{:S(2)}) collective-permute-start(bf16[896,384]{1,0:T(8,128)(2,1)} %pad_maximum_fusion.9), channel_id=1, source_target_pairs={{0,16},{8,24},{16,0},{24,8},{1,17},{9,25},{17,1},{25,9},{2,18},{10... | collective-permute-start | bytes 2064392 | tf_op jit(solution)/shard_map/ppermute | solution.py:45
  7.3 33.0 %collective-permute-start = (s32[16]{0:T(128)}, s32[16]{0:T(128)S(1)}, u32[]{:S(2)}, u32[]{:S(2)}) collective-permute-start(s32[16]{0:T(128)} %bitcast.183), channel_id=1, source_target_pairs={{0,16},{8,24},{16,0},{24,8},{1,17},{9,25},{17,1},{25,9},{2,18},{10... | collective-permute-start | bytes 200 | tf_op jit(solution)/shard_map/ppermute | solution.py:45
  8.1 32.2 %collective-permute-start.48 = (s32[16]{0:T(128)S(1)}, s32[16]{0:T(128)S(1)}, u32[]{:S(2)}, u32[]{:S(2)}) collective-permute-start(s32[16]{0:T(128)S(1)} %reshape.147), channel_id=1, source_target_pairs={{0,16},{8,24},{16,0},{24,8},{1,17},{9,25},{17,1},{25,9},{2,18},{10... | collective-permute-start | bytes 200 | tf_op jit(solution)/shard_map/ppermute | solution.py:45
  37.9 5.1 %collective-permute-start.3 = (bf16[2,896,384]{2,1,0:T(8,128)(2,1)}, bf16[2,896,384]{2,1,0:T(8,128)(2,1)}, u32[]{:S(2)}, u32[]{:S(2)}) collective-permute-start(bf16[2,896,384]{2,1,0:T(8,128)(2,1)} %pad_maximum_fusion.7), channel_id=1, source_target_pairs={{0,8},{8,0},{16,24},{24,16},{1,9},{9,1},{17,25},{25,17},{2,10},{10... | collective-permute-start | bytes 4128776 | tf_op jit(solution)/shard_map/ppermute | solution.py:48
  40.9 1.3 collective-permute-start.1
  41.4 265.4 %collective-permute-start.49 = (s32[2,16]{1,0:T(2,128)}, s32[2,16]{1,0:T(2,128)}, u32[]{:S(2)}, u32[]{:S(2)}) collective-permute-start(s32[2,16]{1,0:T(2,128)} %get-tuple-element.64), channel_id=1, source_target_pairs={{0,8},{8,0},{16,24},{24,16},{1,9},{9,1},{17,25},{25,17},{2,10},{10... | collective-permute-start | bytes 392 | tf_op jit(solution)/shard_map/ppermute | solution.py:48
  45.0 23.2 %collective-permute-start.4 = (bf16[896,256]{1,0:T(8,128)(2,1)S(1)}, bf16[896,256]{1,0:T(8,128)(2,1)S(1)}, u32[]{:S(2)}, u32[]{:S(2)}) collective-permute-start(bf16[896,256]{1,0:T(8,128)(2,1)S(1)} %copy-done.22), channel_id=1, source_target_pairs={{0,16},{8,24},{16,0},{24,8},{1,17},{9,25},{17,1},{25,9},{2,18},{10... | collective-permute-start | bytes 1376264 | tf_op jit(solution)/shard_map/ppermute | solution.py:45
  55.6 18.1 %all-to-all-start = ((bf16[8,768,32]{1,2,0:T(8,128)(2,1)}), bf16[8,768,32]{1,2,0:T(8,128)(2,1)}, u32[]{:S(2)}, u32[]{:S(2)}) async-start(bf16[8,768,32]{1,2,0:T(8,128)(2,1)} %fusion.48), calls=%async_computation | async-start | bytes 786432 | tf_op jit(solution)/shard_map/all_to_all | solution.py:161
  69.4 16.1 %collective-permute-start.5 = (bf16[2,896,256]{2,1,0:T(8,128)(2,1)}, bf16[2,896,256]{2,1,0:T(8,128)(2,1)}, u32[]{:S(2)}, u32[]{:S(2)}) collective-permute-start(bf16[2,896,256]{2,1,0:T(8,128)(2,1)} %pad_maximum_fusion.8), channel_id=1, source_target_pairs={{0,8},{8,0},{16,24},{24,16},{1,9},{9,1},{17,25},{25,17},{2,10},{10... | collective-permute-start | bytes 2752520 | tf_op jit(solution)/shard_map/ppermute | solution.py:48
  92.1 9.4 %collective-permute-start.20 = (bf16[96,1792]{1,0:T(8,128)(2,1)S(1)}, bf16[96,1792]{1,0:T(8,128)(2,1)S(1)}, u32[]{:S(2)}, u32[]{:S(2)}) collective-permute-start(bf16[96,1792]{1,0:T(8,128)(2,1)S(1)} %constant_dynamic-slice_fusion.2), channel_id=1, source_target_pairs={{0,1},{2,0},{4,2},{6,4},{7,6},{5,7},{3,5},{1,3},{8,9},{10,8},{12,1... | collective-permute-start | bytes 1032200 | tf_op jit(solution)/shard_map/ppermute | solution.py:90
  94.1 19.4 %copy-start.15 = (bf16[768,1792]{1,0:T(8,128)(2,1)S(1)}, bf16[768,1792]{1,0:T(8,128)(2,1)}, u32[]{:S(2)}) copy-start(bf16[768,1792]{1,0:T(8,128)(2,1)} %get-tuple-element.23) | copy-start | bytes 8257540
  95.2 8.9 %collective-permute-start.6 = (bf16[96,1792]{1,0:T(8,128)(2,1)S(1)}, bf16[96,1792]{1,0:T(8,128)(2,1)S(1)}, u32[]{:S(2)}, u32[]{:S(2)}) collective-permute-start(bf16[96,1792]{1,0:T(8,128)(2,1)S(1)} %constant_dynamic-slice_fusion.3), channel_id=1, source_target_pairs={{0,2},{2,4},{4,6},{6,7},{7,5},{5,3},{3,1},{1,0},{8,10},{10,12},{12... | collective-permute-start | bytes 1032200 | tf_op jit(solution)/shard_map/ppermute | solution.py:90
  95.9 55.8 %collective-permute-start.36 = (bf16[896,1280]{1,0:T(8,128)(2,1)}, bf16[896,1280]{1,0:T(8,128)(2,1)S(1)}, u32[]{:S(2)}, u32[]{:S(2)}) collective-permute-start(bf16[896,1280]{1,0:T(8,128)(2,1)} %param.23), channel_id=1, source_target_pairs={{0,16},{8,24},{16,0},{24,8},{1,17},{9,25},{17,1},{25,9},{2,18},{10... | collective-permute-start | bytes 6881288 | tf_op jit(solution)/shard_map/ppermute | solution.py:45
  96.4 99.2 %collective-permute-start.34 = (bf16[896,1280]{1,0:T(8,128)(2,1)}, bf16[896,1280]{1,0:T(8,128)(2,1)S(1)}, u32[]{:S(2)}, u32[]{:S(2)}) collective-permute-start(bf16[896,1280]{1,0:T(8,128)(2,1)} %param.22), channel_id=1, source_target_pairs={{0,16},{8,24},{16,0},{24,8},{1,17},{9,25},{17,1},{25,9},{2,18},{10... | collective-permute-start | bytes 6881288 | tf_op jit(solution)/shard_map/ppermute | solution.py:45
  102.5 26.0 %copy-start.17 = (bf16[768,1792]{1,0:T(8,128)(2,1)S(1)}, bf16[768,1792]{1,0:T(8,128)(2,1)}, u32[]{:S(2)}) copy-start(bf16[768,1792]{1,0:T(8,128)(2,1)} %copy-done.16) | copy-start | bytes 8257540
  102.5 8.3 %collective-permute-start.21 = (bf16[96,1792]{1,0:T(8,128)(2,1)S(1)}, bf16[96,1792]{1,0:T(8,128)(2,1)S(1)}, u32[]{:S(2)}, u32[]{:S(2)}) collective-permute-start(bf16[96,1792]{1,0:T(8,128)(2,1)S(1)} %add_convert_fusion.6), channel_id=1, source_target_pairs={{0,1},{2,0},{4,2},{6,4},{7,6},{5,7},{3,5},{1,3},{8,9},{10,8},{12,1... | collective-permute-start | bytes 1032200 | tf_op jit(solution)/shard_map/ppermute | solution.py:90
  105.3 8.2 %collective-permute-start.7 = (bf16[96,1792]{1,0:T(8,128)(2,1)S(1)}, bf16[96,1792]{1,0:T(8,128)(2,1)S(1)}, u32[]{:S(2)}, u32[]{:S(2)}) collective-permute-start(bf16[96,1792]{1,0:T(8,128)(2,1)S(1)} %add_convert_fusion.13), channel_id=1, source_target_pairs={{0,2},{2,4},{4,6},{6,7},{7,5},{5,3},{3,1},{1,0},{8,10},{10,12},{12... | collective-permute-start | bytes 1032200 | tf_op jit(solution)/shard_map/ppermute | solution.py:90
  111.9 7.4 %collective-permute-start.22 = (bf16[96,1792]{1,0:T(8,128)(2,1)S(1)}, bf16[96,1792]{1,0:T(8,128)(2,1)S(1)}, u32[]{:S(2)}, u32[]{:S(2)}) collective-permute-start(bf16[96,1792]{1,0:T(8,128)(2,1)S(1)} %add_convert_fusion.5), channel_id=1, source_target_pairs={{0,1},{2,0},{4,2},{6,4},{7,6},{5,7},{3,5},{1,3},{8,9},{10,8},{12,1... | collective-permute-start | bytes 1032200 | tf_op jit(solution)/shard_map/ppermute | solution.py:90
  113.5 8.4 %collective-permute-start.8 = (bf16[96,1792]{1,0:T(8,128)(2,1)S(1)}, bf16[96,1792]{1,0:T(8,128)(2,1)S(1)}, u32[]{:S(2)}, u32[]{:S(2)}) collective-permute-start(bf16[96,1792]{1,0:T(8,128)(2,1)S(1)} %add_convert_fusion.12), channel_id=1, source_target_pairs={{0,2},{2,4},{4,6},{6,7},{7,5},{5,3},{3,1},{1,0},{8,10},{10,12},{12... | collective-permute-start | bytes 1032200 | tf_op jit(solution)/shard_map/ppermute | solution.py:90
  120.3 8.2 %collective-permute-start.23 = (bf16[96,1792]{1,0:T(8,128)(2,1)S(1)}, bf16[96,1792]{1,0:T(8,128)(2,1)S(1)}, u32[]{:S(2)}, u32[]{:S(2)}) collective-permute-start(bf16[96,1792]{1,0:T(8,128)(2,1)S(1)} %add_convert_fusion.4), channel_id=1, source_target_pairs={{0,1},{2,0},{4,2},{6,4},{7,6},{5,7},{3,5},{1,3},{8,9},{10,8},{12,1... | collective-permute-start | bytes 1032200 | tf_op jit(solution)/shard_map/ppermute | solution.py:90
  122.0 8.9 %collective-permute-start.9 = (bf16[96,1792]{1,0:T(8,128)(2,1)S(1)}, bf16[96,1792]{1,0:T(8,128)(2,1)S(1)}, u32[]{:S(2)}, u32[]{:S(2)}) collective-permute-start(bf16[96,1792]{1,0:T(8,128)(2,1)S(1)} %add_convert_fusion.11), channel_id=1, source_target_pairs={{0,2},{2,4},{4,6},{6,7},{7,5},{5,3},{3,1},{1,0},{8,10},{10,12},{12... | collective-permute-start | bytes 1032200 | tf_op jit(solution)/shard_map/ppermute | solution.py:90
  128.6 23.1 %copy-start.18 = (bf16[896,1280]{1,0:T(8,128)(2,1)S(1)}, bf16[896,1280]{1,0:T(8,128)(2,1)}, u32[]{:S(2)}) copy-start(bf16[896,1280]{1,0:T(8,128)(2,1)} %param.23) | copy-start | bytes 6881284
  128.6 9.5 %collective-permute-start.24 = (bf16[96,1792]{1,0:T(8,128)(2,1)S(1)}, bf16[96,1792]{1,0:T(8,128)(2,1)S(1)}, u32[]{:S(2)}, u32[]{:S(2)}) collective-permute-start(bf16[96,1792]{1,0:T(8,128)(2,1)S(1)} %add_convert_fusion.3), channel_id=1, source_target_pairs={{0,1},{2,0},{4,2},{6,4},{7,6},{5,7},{3,5},{1,3},{8,9},{10,8},{12,1... | collective-permute-start | bytes 1032200 | tf_op jit(solution)/shard_map/ppermute | solution.py:90
  131.0 9.7 %collective-permute-start.10 = (bf16[96,1792]{1,0:T(8,128)(2,1)S(1)}, bf16[96,1792]{1,0:T(8,128)(2,1)S(1)}, u32[]{:S(2)}, u32[]{:S(2)}) collective-permute-start(bf16[96,1792]{1,0:T(8,128)(2,1)S(1)} %add_convert_fusion.10), channel_id=1, source_target_pairs={{0,2},{2,4},{4,6},{6,7},{7,5},{5,3},{3,1},{1,0},{8,10},{10,12},{12... | collective-permute-start | bytes 1032200 | tf_op jit(solution)/shard_map/ppermute | solution.py:90
  138.2 10.7 %collective-permute-start.25 = (bf16[96,1792]{1,0:T(8,128)(2,1)S(1)}, bf16[96,1792]{1,0:T(8,128)(2,1)S(1)}, u32[]{:S(2)}, u32[]{:S(2)}) collective-permute-start(bf16[96,1792]{1,0:T(8,128)(2,1)S(1)} %add_convert_fusion.2), channel_id=1, source_target_pairs={{0,1},{2,0},{4,2},{6,4},{7,6},{5,7},{3,5},{1,3},{8,9},{10,8},{12,1... | collective-permute-start | bytes 1032200 | tf_op jit(solution)/shard_map/ppermute | solution.py:90
  140.8 10.7 %collective-permute-start.11 = (bf16[96,1792]{1,0:T(8,128)(2,1)S(1)}, bf16[96,1792]{1,0:T(8,128)(2,1)S(1)}, u32[]{:S(2)}, u32[]{:S(2)}) collective-permute-start(bf16[96,1792]{1,0:T(8,128)(2,1)S(1)} %add_convert_fusion.9), channel_id=1, source_target_pairs={{0,2},{2,4},{4,6},{6,7},{7,5},{5,3},{3,1},{1,0},{8,10},{10,12},{12... | collective-permute-start | bytes 1032200 | tf_op jit(solution)/shard_map/ppermute | solution.py:90
  148.9 7.3 %collective-permute-start.26 = (bf16[96,1792]{1,0:T(8,128)(2,1)S(1)}, bf16[96,1792]{1,0:T(8,128)(2,1)S(1)}, u32[]{:S(2)}, u32[]{:S(2)}) collective-permute-start(bf16[96,1792]{1,0:T(8,128)(2,1)S(1)} %add_convert_fusion.1), channel_id=1, source_target_pairs={{0,1},{2,0},{4,2},{6,4},{7,6},{5,7},{3,5},{1,3},{8,9},{10,8},{12,1... | collective-permute-start | bytes 1032200 | tf_op jit(solution)/shard_map/ppermute | solution.py:90
  151.6 7.5 %collective-permute-start.12 = (bf16[96,1792]{1,0:T(8,128)(2,1)S(1)}, bf16[96,1792]{1,0:T(8,128)(2,1)S(1)}, u32[]{:S(2)}, u32[]{:S(2)}) collective-permute-start(bf16[96,1792]{1,0:T(8,128)(2,1)S(1)} %add_convert_fusion.8), channel_id=1, source_target_pairs={{0,2},{2,4},{4,6},{6,7},{7,5},{5,3},{3,1},{1,0},{8,10},{10,12},{12... | collective-permute-start | bytes 1032200 | tf_op jit(solution)/shard_map/ppermute | solution.py:90
  154.1 104.9 %collective-permute-start.37 = (bf16[2,896,1280]{2,1,0:T(8,128)(2,1)}, bf16[2,896,1280]{2,1,0:T(8,128)(2,1)}, u32[]{:S(2)}, u32[]{:S(2)}) collective-permute-start(bf16[2,896,1280]{2,1,0:T(8,128)(2,1)} %pad_maximum_fusion.4), channel_id=1, source_target_pairs={{0,8},{8,0},{16,24},{24,16},{1,9},{9,1},{17,25},{25,17},{2,10},{10... | collective-permute-start | bytes 13762568 | tf_op jit(solution)/shard_map/ppermute | solution.py:48
  156.4 39.2 %copy-start.19 = (bf16[896,1280]{1,0:T(8,128)(2,1)S(1)}, bf16[896,1280]{1,0:T(8,128)(2,1)}, u32[]{:S(2)}) copy-start(bf16[896,1280]{1,0:T(8,128)(2,1)} %param.22) | copy-start | bytes 6881284
  156.5 42.0 %collective-permute-start.27 = (bf16[96,1792]{1,0:T(8,128)(2,1)S(1)}, bf16[96,1792]{1,0:T(8,128)(2,1)S(1)}, u32[]{:S(2)}, u32[]{:S(2)}) collective-permute-start(bf16[96,1792]{1,0:T(8,128)(2,1)S(1)} %get-tuple-element.20), channel_id=1, source_target_pairs={{0,1},{2,0},{4,2},{6,4},{7,6},{5,7},{3,5},{1,3},{8,9},{10,8},{12,1... | collective-permute-start | bytes 1032200 | tf_op jit(solution)/shard_map/ppermute | solution.py:96
  159.4 40.7 %collective-permute-start.13 = (bf16[96,1792]{1,0:T(8,128)(2,1)S(1)}, bf16[96,1792]{1,0:T(8,128)(2,1)S(1)}, u32[]{:S(2)}, u32[]{:S(2)}) collective-permute-start(bf16[96,1792]{1,0:T(8,128)(2,1)S(1)} %get-tuple-element.18), channel_id=1, source_target_pairs={{0,2},{2,4},{4,6},{6,7},{7,5},{5,3},{3,1},{1,0},{8,10},{10,12},{12... | collective-permute-start | bytes 1032200 | tf_op jit(solution)/shard_map/ppermute | solution.py:96
  198.5 81.0 %collective-permute-start.35 = (bf16[2,896,1280]{2,1,0:T(8,128)(2,1)}, bf16[2,896,1280]{2,1,0:T(8,128)(2,1)}, u32[]{:S(2)}, u32[]{:S(2)}) collective-permute-start(bf16[2,896,1280]{2,1,0:T(8,128)(2,1)} %pad_maximum_fusion.3), channel_id=1, source_target_pairs={{0,8},{8,0},{16,24},{24,16},{1,9},{9,1},{17,25},{25,17},{2,10},{10... | collective-permute-start | bytes 13762568 | tf_op jit(solution)/shard_map/ppermute | solution.py:48
  198.5 10.5 %collective-permute-start.28 = (bf16[96,1792]{1,0:T(8,128)(2,1)S(1)}, bf16[96,1792]{1,0:T(8,128)(2,1)S(1)}, u32[]{:S(2)}, u32[]{:S(2)}) collective-permute-start(bf16[96,1792]{1,0:T(8,128)(2,1)S(1)} %collective-permute-done.27), channel_id=1, source_target_pairs={{0,1},{2,0},{4,2},{6,4},{7,6},{5,7},{3,5},{1,3},{8,9},{10,8},{12,1... | collective-permute-start | bytes 1032200 | tf_op jit(solution)/shard_map/ppermute | solution.py:96
  200.0 10.5 %collective-permute-start.14 = (bf16[96,1792]{1,0:T(8,128)(2,1)S(1)}, bf16[96,1792]{1,0:T(8,128)(2,1)S(1)}, u32[]{:S(2)}, u32[]{:S(2)}) collective-permute-start(bf16[96,1792]{1,0:T(8,128)(2,1)S(1)} %collective-permute-done.13), channel_id=1, source_target_pairs={{0,2},{2,4},{4,6},{6,7},{7,5},{5,3},{3,1},{1,0},{8,10},{10,12},{12... | collective-permute-start | bytes 1032200 | tf_op jit(solution)/shard_map/ppermute | solution.py:96
  209.0 9.7 %collective-permute-start.29 = (bf16[96,1792]{1,0:T(8,128)(2,1)S(1)}, bf16[96,1792]{1,0:T(8,128)(2,1)S(1)}, u32[]{:S(2)}, u32[]{:S(2)}) collective-permute-start(bf16[96,1792]{1,0:T(8,128)(2,1)S(1)} %collective-permute-done.28), channel_id=1, source_target_pairs={{0,1},{2,0},{4,2},{6,4},{7,6},{5,7},{3,5},{1,3},{8,9},{10,8},{12,1... | collective-permute-start | bytes 1032200 | tf_op jit(solution)/shard_map/ppermute | solution.py:96
  210.5 9.7 %collective-permute-start.15 = (bf16[96,1792]{1,0:T(8,128)(2,1)S(1)}, bf16[96,1792]{1,0:T(8,128)(2,1)S(1)}, u32[]{:S(2)}, u32[]{:S(2)}) collective-permute-start(bf16[96,1792]{1,0:T(8,128)(2,1)S(1)} %collective-permute-done.14), channel_id=1, source_target_pairs={{0,2},{2,4},{4,6},{6,7},{7,5},{5,3},{3,1},{1,0},{8,10},{10,12},{12... | collective-permute-start | bytes 1032200 | tf_op jit(solution)/shard_map/ppermute | solution.py:96
  218.7 8.8 %collective-permute-start.30 = (bf16[96,1792]{1,0:T(8,128)(2,1)S(1)}, bf16[96,1792]{1,0:T(8,128)(2,1)S(1)}, u32[]{:S(2)}, u32[]{:S(2)}) collective-permute-start(bf16[96,1792]{1,0:T(8,128)(2,1)S(1)} %collective-permute-done.29), channel_id=1, source_target_pairs={{0,1},{2,0},{4,2},{6,4},{7,6},{5,7},{3,5},{1,3},{8,9},{10,8},{12,1... | collective-permute-start | bytes 1032200 | tf_op jit(solution)/shard_map/ppermute | solution.py:96
  220.2 8.8 %collective-permute-start.16 = (bf16[96,1792]{1,0:T(8,128)(2,1)S(1)}, bf16[96,1792]{1,0:T(8,128)(2,1)S(1)}, u32[]{:S(2)}, u32[]{:S(2)}) collective-permute-start(bf16[96,1792]{1,0:T(8,128)(2,1)S(1)} %collective-permute-done.15), channel_id=1, source_target_pairs={{0,2},{2,4},{4,6},{6,7},{7,5},{5,3},{3,1},{1,0},{8,10},{10,12},{12... | collective-permute-start | bytes 1032200 | tf_op jit(solution)/shard_map/ppermute | solution.py:96
  220.8 32.4 %copy-start.3 = (bf16[768,896]{1,0:T(8,128)(2,1)S(1)}, bf16[768,896]{1,0:T(8,128)(2,1)}, u32[]{:S(2)}) copy-start(bf16[768,896]{1,0:T(8,128)(2,1)} %copy-done.1) | copy-start | bytes 4128772
  220.9 32.4 %copy-start.6 = (bf16[768,896]{1,0:T(8,128)(2,1)S(1)}, bf16[768,896]{1,0:T(8,128)(2,1)}, u32[]{:S(2)}) copy-start(bf16[768,896]{1,0:T(8,128)(2,1)} %copy-done.4) | copy-start | bytes 4128772
  220.9 32.4 %copy-start.9 = (bf16[768,896]{1,0:T(8,128)(2,1)S(1)}, bf16[768,896]{1,0:T(8,128)(2,1)}, u32[]{:S(2)}) copy-start(bf16[768,896]{1,0:T(8,128)(2,1)} %copy-done.7) | copy-start | bytes 4128772
  220.9 32.4 %copy-start.12 = (bf16[768,896]{1,0:T(8,128)(2,1)S(1)}, bf16[768,896]{1,0:T(8,128)(2,1)}, u32[]{:S(2)}) copy-start(bf16[768,896]{1,0:T(8,128)(2,1)} %copy-done.10) | copy-start | bytes 4128772
  227.5 8.2 %collective-permute-start.31 = (bf16[96,1792]{1,0:T(8,128)(2,1)S(1)}, bf16[96,1792]{1,0:T(8,128)(2,1)S(1)}, u32[]{:S(2)}, u32[]{:S(2)}) collective-permute-start(bf16[96,1792]{1,0:T(8,128)(2,1)S(1)} %collective-permute-done.30), channel_id=1, source_target_pairs={{0,1},{2,0},{4,2},{6,4},{7,6},{5,7},{3,5},{1,3},{8,9},{10,8},{12,1... | collective-permute-start | bytes 1032200 | tf_op jit(solution)/shard_map/ppermute | solution.py:96
  229.0 8.2 %collective-permute-start.17 = (bf16[96,1792]{1,0:T(8,128)(2,1)S(1)}, bf16[96,1792]{1,0:T(8,128)(2,1)S(1)}, u32[]{:S(2)}, u32[]{:S(2)}) collective-permute-start(bf16[96,1792]{1,0:T(8,128)(2,1)S(1)} %collective-permute-done.16), channel_id=1, source_target_pairs={{0,2},{2,4},{4,6},{6,7},{7,5},{5,3},{3,1},{1,0},{8,10},{10,12},{12... | collective-permute-start | bytes 1032200 | tf_op jit(solution)/shard_map/ppermute | solution.py:96
  235.7 8.7 %collective-permute-start.32 = (bf16[96,1792]{1,0:T(8,128)(2,1)S(1)}, bf16[96,1792]{1,0:T(8,128)(2,1)S(1)}, u32[]{:S(2)}, u32[]{:S(2)}) collective-permute-start(bf16[96,1792]{1,0:T(8,128)(2,1)S(1)} %collective-permute-done.31), channel_id=1, source_target_pairs={{0,1},{2,0},{4,2},{6,4},{7,6},{5,7},{3,5},{1,3},{8,9},{10,8},{12,1... | collective-permute-start | bytes 1032200 | tf_op jit(solution)/shard_map/ppermute | solution.py:96
  237.2 8.7 %collective-permute-start.18 = (bf16[96,1792]{1,0:T(8,128)(2,1)S(1)}, bf16[96,1792]{1,0:T(8,128)(2,1)S(1)}, u32[]{:S(2)}, u32[]{:S(2)}) collective-permute-start(bf16[96,1792]{1,0:T(8,128)(2,1)S(1)} %collective-permute-done.17), channel_id=1, source_target_pairs={{0,2},{2,4},{4,6},{6,7},{7,5},{5,3},{3,1},{1,0},{8,10},{10,12},{12... | collective-permute-start | bytes 1032200 | tf_op jit(solution)/shard_map/ppermute | solution.py:96
  244.4 7.2 %collective-permute-start.33 = (bf16[96,1792]{1,0:T(8,128)(2,1)S(1)}, bf16[96,1792]{1,0:T(8,128)(2,1)S(1)}, u32[]{:S(2)}, u32[]{:S(2)}) collective-permute-start(bf16[96,1792]{1,0:T(8,128)(2,1)S(1)} %collective-permute-done.32), channel_id=1, source_target_pairs={{0,1},{2,0},{4,2},{6,4},{7,6},{5,7},{3,5},{1,3},{8,9},{10,8},{12,1... | collective-permute-start | bytes 1032200 | tf_op jit(solution)/shard_map/ppermute | solution.py:96
  246.0 7.3 %collective-permute-start.19 = (bf16[96,1792]{1,0:T(8,128)(2,1)S(1)}, bf16[96,1792]{1,0:T(8,128)(2,1)S(1)}, u32[]{:S(2)}, u32[]{:S(2)}) collective-permute-start(bf16[96,1792]{1,0:T(8,128)(2,1)S(1)} %collective-permute-done.18), channel_id=1, source_target_pairs={{0,2},{2,4},{4,6},{6,7},{7,5},{5,3},{3,1},{1,0},{8,10},{10,12},{12... | collective-permute-start | bytes 1032200 | tf_op jit(solution)/shard_map/ppermute | solution.py:96
  302.2 4.5 %collective-permute-start.38 = (f32[16,1280]{1,0:T(8,128)S(1)}, f32[16,1280]{1,0:T(8,128)S(1)}, u32[]{:S(2)}, u32[]{:S(2)}) collective-permute-start(f32[16,1280]{1,0:T(8,128)S(1)} %fusion.5), channel_id=1, source_target_pairs={{0,16},{8,24},{16,0},{24,8},{1,17},{9,25},{17,1},{25,9},{2,18},{10... | collective-permute-start | bytes 245768 | tf_op jit(solution)/shard_map/ppermute | solution.py:45
  306.7 3.2 collective-permute-start.39
  312.6 12.8 %collective-permute-start.47 = (f32[16,448]{1,0:T(8,128)S(1)}, f32[16,448]{1,0:T(8,128)S(1)}, u32[]{:S(2)}, u32[]{:S(2)}) collective-permute-start(f32[16,448]{1,0:T(8,128)S(1)} %get-tuple-element.32), channel_id=1, source_target_pairs={{0,1},{1,8},{2,9},{3,16},{4,17},{5,24},{6,25},{7,0},{8,3},{9,10},{... | collective-permute-start | bytes 86024 | tf_op jit(solution)/shard_map/ppermute | solution.py:234
  313.2 13.4 %collective-permute-start.46 = (f32[16,448]{1,0:T(8,128)S(1)}, f32[16,448]{1,0:T(8,128)S(1)}, u32[]{:S(2)}, u32[]{:S(2)}) collective-permute-start(f32[16,448]{1,0:T(8,128)S(1)} %get-tuple-element.33), channel_id=1, source_target_pairs={{0,8},{1,9},{2,16},{3,17},{4,24},{5,25},{6,0},{7,1},{8,10},{9,11},... | collective-permute-start | bytes 86024 | tf_op jit(solution)/shard_map/ppermute | solution.py:234
  313.9 13.4 %collective-permute-start.45 = (f32[16,448]{1,0:T(8,128)S(1)}, f32[16,448]{1,0:T(8,128)S(1)}, u32[]{:S(2)}, u32[]{:S(2)}) collective-permute-start(f32[16,448]{1,0:T(8,128)S(1)} %get-tuple-element.34), channel_id=1, source_target_pairs={{0,9},{1,16},{2,17},{3,24},{4,25},{5,0},{6,1},{7,8},{8,11},{9,18},... | collective-permute-start | bytes 86024 | tf_op jit(solution)/shard_map/ppermute | solution.py:234
  315.4 17.8 %all-to-all-start.1 = ((f32[4,4,448]{2,1,0:T(4,128)}), f32[4,4,448]{2,1,0:T(4,128)S(1)}, u32[]{:S(2)}, u32[]{:S(2)}) async-start(f32[4,4,448]{2,1,0:T(4,128)} %fusion.58), calls=%async_computation.1 | async-start | bytes 65536 | tf_op jit(solution)/shard_map/all_to_all | solution.py:238
  320.8 12.4 %collective-permute-start.44 = (f32[16,448]{1,0:T(8,128)S(1)}, f32[16,448]{1,0:T(8,128)S(1)}, u32[]{:S(2)}, u32[]{:S(2)}) collective-permute-start(f32[16,448]{1,0:T(8,128)S(1)} %get-tuple-element.35), channel_id=1, source_target_pairs={{0,16},{1,17},{2,24},{3,25},{4,0},{5,1},{6,8},{7,9},{8,18},{9,19},... | collective-permute-start | bytes 86024 | tf_op jit(solution)/shard_map/ppermute | solution.py:234
  322.8 10.4 %collective-permute-start.43 = (f32[16,448]{1,0:T(8,128)S(1)}, f32[16,448]{1,0:T(8,128)S(1)}, u32[]{:S(2)}, u32[]{:S(2)}) collective-permute-start(f32[16,448]{1,0:T(8,128)S(1)} %get-tuple-element.36), channel_id=1, source_target_pairs={{0,17},{1,24},{2,25},{3,0},{4,1},{5,8},{6,9},{7,16},{8,19},{9,26},... | collective-permute-start | bytes 86024 | tf_op jit(solution)/shard_map/ppermute | solution.py:234
  325.3 7.9 %collective-permute-start.42 = (f32[16,448]{1,0:T(8,128)S(1)}, f32[16,448]{1,0:T(8,128)S(1)}, u32[]{:S(2)}, u32[]{:S(2)}) collective-permute-start(f32[16,448]{1,0:T(8,128)S(1)} %get-tuple-element.37), channel_id=1, source_target_pairs={{0,24},{1,25},{2,0},{3,1},{4,8},{5,9},{6,16},{7,17},{8,26},{9,27},... | collective-permute-start | bytes 86024 | tf_op jit(solution)/shard_map/ppermute | solution.py:234
  326.7 6.6 %collective-permute-start.40 = (f32[16,448]{1,0:T(8,128)S(1)}, f32[16,448]{1,0:T(8,128)S(1)}, u32[]{:S(2)}, u32[]{:S(2)}) collective-permute-start(f32[16,448]{1,0:T(8,128)S(1)} %get-tuple-element.38), channel_id=1, source_target_pairs={{0,0},{1,1},{2,8},{3,9},{4,16},{5,17},{6,24},{7,25},{8,2},{9,3},{1... | collective-permute-start | bytes 86024 | tf_op jit(solution)/shard_map/ppermute | solution.py:234
  327.3 7.3 %collective-permute-start.41 = (f32[16,448]{1,0:T(8,128)S(1)}, f32[16,448]{1,0:T(8,128)S(1)}, u32[]{:S(2)}, u32[]{:S(2)}) collective-permute-start(f32[16,448]{1,0:T(8,128)S(1)} %get-tuple-element.31), channel_id=1, source_target_pairs={{0,25},{1,0},{2,1},{3,8},{4,9},{5,16},{6,17},{7,24},{8,27},{9,2},{... | collective-permute-start | bytes 86024 | tf_op jit(solution)/shard_map/ppermute | solution.py:234
  (25 other events, 177.1 us)

commit v11 on v5

--- a/solution.py
+++ b/solution.py
@@ -70,7 +70,7 @@
     return list(range(0, n, 2)) + list(range(n - 1, 0, -2))
 
 
-def ring_psum(x, axis, n):
+def ring_psum(x, axis, n, ride):
     walk = ring_walk(n)
     place = [0] * n
     for p, t in enumerate(walk):
@@ -94,10 +94,12 @@
         for step in range(n):
             if step:
                 moving = lax.ppermute(moving, axis, pairs)
+            if step == n - 1 and sign == 1:
+                moving, ride = lax.optimization_barrier((moving, ride))
             where = ((pos + sign - sign * step) % n) * size
             out = lax.dynamic_update_slice_in_dim(out, moving, where, 0)
         parts.append(out)
-    return jnp.concatenate(parts, 1)
+    return jnp.concatenate(parts, 1), ride
 
 
 def on_device(
@@ -181,7 +183,8 @@
     )
     attended_rows = attended_rows.astype(jnp.bfloat16).reshape(row_count, local_heads * HEAD_SIZE)
     attn_term = transposed_dot(attended_rows, o_full).astype(jnp.bfloat16)
-    attn_total = ring_psum(attn_term, "tp", tp_size).astype(jnp.float32)
+    attn_total, (gate_full, up_full) = ring_psum(attn_term, "tp", tp_size, (gate_full, up_full))
+    attn_total = attn_total.astype(jnp.float32)
     residual = hidden_perm.astype(jnp.float32) + attn_total
     norm_mid = rms_scale(residual, ffn_gain_perm)
     gate_pre = jnp.dot(norm_mid, gate_full, preferred_element_type=jnp.float32)

time: 328 us -> 331 us (level)
  local copies, waits for them, and re-layouts: 21.1 us -> 38.2 us
  waiting for transfers between devices: 131 us -> 121 us
    dynamic_update_slice x14, local copies, waits for them, and re-layouts: 0.38 us -> 10.6 us  [ring_psum(): out = lax.dynamic_update_slice_in_dim(out, moving, where, 0)]
    ppermute x14, waiting for transfers between devices: 41.9 us -> 33.3 us  [ring_psum(): moving = lax.ppermute(moving, axis, pairs)]
    ppermute x7, waiting for transfers between devices: 43.9 us -> 38.7 us  [gather_grp(): moving = lax.ppermute(moving, 'grp', ring)]
    unnamed x64 -> x68, local copies, waits for them, and re-layouts: 4.84 us -> 9.55 us
    ppermute x14, waiting for transfers between devices: 39.5 us -> 43 us  [ring_psum(): got = lax.ppermute(acc, axis, pairs)]
  transfers between devices with their start and end apart: 52 -> 52, of which waited for: 25 -> 23; matrix products, arithmetic and copies ran while one was open for 33% -> 35% of each run, Pallas kernels for 0% -> 0%
where the time goes in v11:
time: 331 us; the launch traced here: 328 us
  waiting for transfers between devices  121 us (37%)
  starting transfers between devices  61.2 us (18%)
  other arithmetic  50.5 us (15%)
  matrix products  42.4 us (13%)
  local copies, waits for them, and re-layouts  38.2 us (12%)
  between operations  15.2 us (5%)
    ppermute x14, waiting for transfers between devices, ring_psum(): got = lax.ppermute(acc, axis, pairs)  43 us
    ppermute x7, waiting for transfers between devices, gather_grp(): moving = lax.ppermute(moving, 'grp', ring)  38.7 us
    ppermute x14, waiting for transfers between devices, ring_psum(): moving = lax.ppermute(moving, axis, pairs)  33.3 us
    dot_general x1, matrix products, on_device(): jnp.dot(selector.astype(jnp.bfloat16), hidden_ffn, preferred_element_type...  15.5 us
    concatenate x6, other arithmetic, gather_grp(): return jnp.concatenate([mine, other], 0)  15.5 us
    ppermute x14, starting transfers between devices, ring_psum(): got = lax.ppermute(acc, axis, pairs)  15.1 us
    ppermute x14, starting transfers between devices, ring_psum(): moving = lax.ppermute(moving, axis, pairs)  14.2 us
    ppermute x8, starting transfers between devices, on_device(): totals = totals + lax.ppermute(piece, ('grp', 'tp'), pairs)  13.9 us
  transfers between devices with their start and end apart: 52, of which 23 were waited for; matrix products, arithmetic and copies ran while one was open for 35% of the time, Pallas kernels for 0%

profile of v11, /device:TPU:0, one launch (start us, length us, event | category | flops | bytes accessed | tf_op | source)
XLA Modules:
  0.0 328.2 jit_solution(13326752378896634655)
XLA Ops:
  2.3 2.0 pad_maximum_fusion.9
  4.4 2.9 collective-permute-start.2
  8.6 2.0 collective-permute-start
  33.1 3.1 constant_dynamic-slice_fusion.7
  36.2 1.4 fusion.1
  38.5 4.3 %fusion.12 = bf16[768,384]{0,1:T(8,128)(2,1)S(1)} fusion(bf16[3584,384]{1,0:T(8,128)(2,1)S(1)} %bitcast.155, f32[3584]{0:T(1024)S(1)} %pad_maximum_fusion.12, f32[768]{0:T(1024)S(1)} %add_rsqrt_fusion.1, bf16[768,896]{1,0:T(8,128)(2,1)S(1)} %get-tuple-element.33, bf16[768,896]{1,0:T(8,128)(2,1)S(1)} %get-tuple-element.34, ...), kind=kOutput, calls=%fused_computation.29 | convolution fusion | flops 2144501760 | bytes 8864768 | tf_op jit(solution)/shard_map/dot_general | solution.py:149
  49.1 5.8 %all-to-all-start = ((bf16[8,768,32]{1,2,0:T(8,128)(2,1)}), bf16[8,768,32]{1,2,0:T(8,128)(2,1)S(1)}, u32[]{:S(2)}, u32[]{:S(2)}) async-start(bf16[8,768,32]{1,2,0:T(8,128)(2,1)} %fusion.41), calls=%async_computation | async-start | bytes 786432 | tf_op jit(solution)/shard_map/all_to_all | solution.py:164
  61.1 7.9 %collective-permute-done.4 = bf16[896,256]{1,0:T(8,128)(2,1)} collective-permute-done((bf16[896,256]{1,0:T(8,128)(2,1)S(1)}, bf16[896,256]{1,0:T(8,128)(2,1)}, u32[]{:S(2)}, u32[]{:S(2)}) %collective-permute-start.4) | collective-permute-done | bytes 458784 | tf_op jit(solution)/shard_map/ppermute | solution.py:45
  69.0 2.0 pad_maximum_fusion.8
  71.2 4.1 %fusion.73 = (f32[2,2,384]{2,1,0:T(2,128)}, f32[2,2,384,384]{2,3,1,0:T(8,128)}) fusion(pred[2,384,384]{1,2,0:T(8,128)(4,1)} %broadcast_compare_fusion, bf16[2,384,2,128]{1,0,3,2:T(2,128)(2,1)} %reshape.140, bf16[2,384,128,1]{1,0,2,3:T(2,128)(2,1)S(1)} %bitcast.182), kind=kOutput, calls=%fused_computation.169 | convolution fusion | flops 153354624 | bytes 3250176 | tf_op jit(solution)/shard_map/sub | solution.py:29
  75.3 2.0 fusion.15
  77.8 1.5 pad_maximum_fusion.6
  79.2 1.6 convolution_convert_fusion
  80.9 1.9 fusion.65
  82.8 1.6 copy-done.11
  84.3 1.8 collective-permute-start.6
  86.9 1.5 collective-permute-start.22
  89.8 5.1 %collective-permute-done.6 = bf16[96,1792]{1,0:T(8,128)(2,1)S(1)} collective-permute-done((bf16[96,1792]{1,0:T(8,128)(2,1)S(1)}, bf16[96,1792]{1,0:T(8,128)(2,1)S(1)}, u32[]{:S(2)}, u32[]{:S(2)}) %collective-permute-start.6) | collective-permute-done | bytes 344096 | tf_op jit(solution)/shard_map/ppermute | solution.py:90
  95.9 1.8 collective-permute-start.7
  97.7 1.4 collective-permute-done.24
  100.5 5.1 %collective-permute-done.7 = bf16[96,1792]{1,0:T(8,128)(2,1)S(1)} collective-permute-done((bf16[96,1792]{1,0:T(8,128)(2,1)S(1)}, bf16[96,1792]{1,0:T(8,128)(2,1)S(1)}, u32[]{:S(2)}, u32[]{:S(2)}) %collective-permute-start.7) | collective-permute-done | bytes 344096 | tf_op jit(solution)/shard_map/ppermute | solution.py:90
  106.8 1.8 collective-permute-start.8
  109.5 6.2 %collective-permute-done.8 = bf16[96,1792]{1,0:T(8,128)(2,1)S(1)} collective-permute-done((bf16[96,1792]{1,0:T(8,128)(2,1)S(1)}, bf16[96,1792]{1,0:T(8,128)(2,1)S(1)}, u32[]{:S(2)}, u32[]{:S(2)}) %collective-permute-start.8) | collective-permute-done | bytes 344096 | tf_op jit(solution)/shard_map/ppermute | solution.py:90
  116.7 2.0 collective-permute-start.9
  119.1 5.9 %collective-permute-done.9 = bf16[96,1792]{1,0:T(8,128)(2,1)S(1)} collective-permute-done((bf16[96,1792]{1,0:T(8,128)(2,1)S(1)}, bf16[96,1792]{1,0:T(8,128)(2,1)S(1)}, u32[]{:S(2)}, u32[]{:S(2)}) %collective-permute-start.9) | collective-permute-done | bytes 344096 | tf_op jit(solution)/shard_map/ppermute | solution.py:90
  125.1 1.8 collective-permute-start.10
  127.3 6.1 %collective-permute-done.10 = bf16[96,1792]{1,0:T(8,128)(2,1)S(1)} collective-permute-done((bf16[96,1792]{1,0:T(8,128)(2,1)S(1)}, bf16[96,1792]{1,0:T(8,128)(2,1)S(1)}, u32[]{:S(2)}, u32[]{:S(2)}) %collective-permute-start.10) | collective-permute-done | bytes 344096 | tf_op jit(solution)/shard_map/ppermute | solution.py:90
  133.5 1.8 collective-permute-start.11
  136.0 6.6 %collective-permute-done.11 = bf16[96,1792]{1,0:T(8,128)(2,1)S(1)} collective-permute-done((bf16[96,1792]{1,0:T(8,128)(2,1)S(1)}, bf16[96,1792]{1,0:T(8,128)(2,1)S(1)}, u32[]{:S(2)}, u32[]{:S(2)}) %collective-permute-start.11) | collective-permute-done | bytes 344096 | tf_op jit(solution)/shard_map/ppermute | solution.py:90
  142.6 1.8 collective-permute-start.12
  144.4 2.8 pad_maximum_fusion.3
  147.7 2.2 collective-permute-done.12
  149.9 1.7 broadcast.177.clone.1
  152.4 1.8 collective-permute-start.13
  154.2 3.7 %collective-permute-done.30 = bf16[96,1792]{1,0:T(8,128)(2,1)S(1)} collective-permute-done((bf16[96,1792]{1,0:T(8,128)(2,1)S(1)}, bf16[96,1792]{1,0:T(8,128)(2,1)S(1)}, u32[]{:S(2)}, u32[]{:S(2)}) %collective-permute-start.30) | collective-permute-done | bytes 344096 | tf_op jit(solution)/shard_map/ppermute | solution.py:90
  157.9 1.7 broadcast.177.clone
  160.8 26.9 %collective-permute-done.22 = bf16[896,1280]{1,0:T(8,128)(2,1)S(1)} collective-permute-done((bf16[896,1280]{1,0:T(8,128)(2,1)}, bf16[896,1280]{1,0:T(8,128)(2,1)S(1)}, u32[]{:S(2)}, u32[]{:S(2)}) %collective-permute-start.22) | collective-permute-done | bytes 2293792 | tf_op jit(solution)/shard_map/ppermute | solution.py:45
  187.8 2.8 pad_maximum_fusion.4
  190.9 1.5 collective-permute-start.14
  194.5 6.9 %collective-permute-done.14 = bf16[96,1792]{1,0:T(8,128)(2,1)S(1)} collective-permute-done((bf16[96,1792]{1,0:T(8,128)(2,1)S(1)}, bf16[96,1792]{1,0:T(8,128)(2,1)S(1)}, u32[]{:S(2)}, u32[]{:S(2)}) %collective-permute-start.14) | collective-permute-done | bytes 344096 | tf_op jit(solution)/shard_map/ppermute | solution.py:96
  201.5 1.5 collective-permute-start.15
  205.0 6.1 %collective-permute-done.15 = bf16[96,1792]{1,0:T(8,128)(2,1)S(1)} collective-permute-done((bf16[96,1792]{1,0:T(8,128)(2,1)S(1)}, bf16[96,1792]{1,0:T(8,128)(2,1)S(1)}, u32[]{:S(2)}, u32[]{:S(2)}) %collective-permute-start.15) | collective-permute-done | bytes 344096 | tf_op jit(solution)/shard_map/ppermute | solution.py:96
  211.2 1.5 collective-permute-start.16
  214.7 5.3 %collective-permute-done.16 = bf16[96,1792]{1,0:T(8,128)(2,1)S(1)} collective-permute-done((bf16[96,1792]{1,0:T(8,128)(2,1)S(1)}, bf16[96,1792]{1,0:T(8,128)(2,1)S(1)}, u32[]{:S(2)}, u32[]{:S(2)}) %collective-permute-start.16) | collective-permute-done | bytes 344096 | tf_op jit(solution)/shard_map/ppermute | solution.py:96
  220.0 1.5 collective-permute-start.17
  223.5 4.6 %collective-permute-done.17 = bf16[96,1792]{1,0:T(8,128)(2,1)S(1)} collective-permute-done((bf16[96,1792]{1,0:T(8,128)(2,1)S(1)}, bf16[96,1792]{1,0:T(8,128)(2,1)S(1)}, u32[]{:S(2)}, u32[]{:S(2)}) %collective-permute-start.17) | collective-permute-done | bytes 344096 | tf_op jit(solution)/shard_map/ppermute | solution.py:96
  228.2 1.5 collective-permute-start.18
  231.7 5.1 %collective-permute-done.18 = bf16[96,1792]{1,0:T(8,128)(2,1)S(1)} collective-permute-done((bf16[96,1792]{1,0:T(8,128)(2,1)S(1)}, bf16[96,1792]{1,0:T(8,128)(2,1)S(1)}, u32[]{:S(2)}, u32[]{:S(2)}) %collective-permute-start.18) | collective-permute-done | bytes 344096 | tf_op jit(solution)/shard_map/ppermute | solution.py:96
  236.9 1.5 collective-permute-start.19
  240.4 5.2 %collective-permute-done.37 = bf16[96,1792]{1,0:T(8,128)(2,1)S(1)} collective-permute-done((bf16[96,1792]{1,0:T(8,128)(2,1)S(1)}, bf16[96,1792]{1,0:T(8,128)(2,1)S(1)}, u32[]{:S(2)}, u32[]{:S(2)}) %collective-permute-start.37) | collective-permute-done | bytes 344096 | tf_op jit(solution)/shard_map/ppermute | solution.py:96
  246.4 8.0 %pad_maximum_fusion = bf16[4,896,1280]{2,1,0:T(8,128)(2,1)} fusion(bf16[2,896,1280]{2,1,0:T(8,128)(2,1)} %collective-permute-done.21, bf16[1,896,1280]{2,1,0:T(8,128)(2,1)S(1)} %bitcast.151, bf16[1,896,1280]{2,1,0:T(8,128)(2,1)S(1)} %bitcast.145), kind=kLoop, calls=%fused_computation.9 | loop fusion | flops 9175040 | bytes 18350080 | tf_op jit(solution)/shard_map/concatenate | solution.py:49
  254.4 5.0 %pad_maximum_fusion.1 = bf16[4,896,1280]{2,1,0:T(8,128)(2,1)S(1)} fusion(bf16[2,896,1280]{2,1,0:T(8,128)(2,1)} %collective-permute-done.23, bf16[1,896,1280]{2,1,0:T(8,128)(2,1)S(1)} %bitcast.149, bf16[1,896,1280]{2,1,0:T(8,128)(2,1)S(1)} %bitcast.147), kind=kLoop, calls=%fused_computation.10 | loop fusion | flops 9175040 | bytes 18350080 | tf_op jit(solution)/shard_map/concatenate | solution.py:49
  260.2 5.1 %multiply_reduce_fusion = (f32[768]{0:T(1024)S(1)}, f32[768,3584]{1,0:T(8,128)S(1)}) fusion(bf16[768,1792]{1,0:T(8,128)(2,1)} %constant_dynamic-update-slice_fusion, bf16[768,1792]{1,0:T(8,128)(2,1)} %constant_dynamic-update-slice_fusion.8, bf16[768,896]{1,0:T(8,128)(2,1)S(1)} %copy-done.7, bf16[768,896]{1,0:T(8,128)(2,1)S(1)} %copy-done.9, ...), kind=kLoop, calls=%fused_computation.8 | loop fusion | flops 41286912 | bytes 22023168 | tf_op jit(solution)/shard_map/reduce_sum | solution.py:17
  265.3 4.1 %copy-done.1 = f32[768,3584]{1,0:T(8,128)} copy-done((f32[768,3584]{1,0:T(8,128)}, f32[768,3584]{1,0:T(8,128)S(1)}, u32[]{:S(2)}) %copy-start.1) | copy-done | bytes 11010072
  269.4 9.2 %fusion.63 = f32[768,1280]{1,0:T(8,128)} fusion(bf16[3584,1280]{1,0:T(8,128)(2,1)S(1)} %bitcast.153, f32[768,3584]{1,0:T(8,128)S(1)} %get-tuple-element.24, f32[3584]{0:T(1024)S(1)} %copy-done.25, f32[768]{0:T(1024)S(1)} %add_rsqrt_fusion), kind=kOutput, calls=%fused_computation.159 | convolution fusion | flops 7054688256 | bytes 24134656 | tf_op jit(solution)/shard_map/dot_general | solution.py:191
  278.6 15.5 %fusion.9 = f32[16,1280]{1,0:T(8,128)S(1)} fusion(f32[768,1280]{1,0:T(8,128)} %fusion.63, s32[768]{0:T(1024)S(1)} %add.528, bf16[3584,1280]{1,0:T(8,128)(2,1)} %bitcast.152, f32[768,3584]{1,0:T(8,128)} %copy-done.1, f32[3584]{0:T(1024)S(1)} %copy-done.25, f32[768]{0:T(1024)S(1)} %add_rsqrt_fusion), kind=kOutput, calls=%fused_computation.24 | convolution fusion | flops 7092080640 | bytes 24219648 | tf_op jit(solution)/shard_map/dot_general | solution.py:198
  294.7 3.9 %collective-permute-done.38 = f32[16,1280]{1,0:T(8,128)S(1)} collective-permute-done((f32[16,1280]{1,0:T(8,128)S(1)}, f32[16,1280]{1,0:T(8,128)S(1)}, u32[]{:S(2)}, u32[]{:S(2)}) %collective-permute-start.38) | collective-permute-done | bytes 81952 | tf_op jit(solution)/shard_map/ppermute | solution.py:45
  299.4 2.3 fusion.19
  301.8 2.1 convolution_bitcast_fusion
  305.1 4.7 %collective-permute-start.41 = (f32[16,448]{1,0:T(8,128)S(1)}, f32[16,448]{1,0:T(8,128)S(1)}, u32[]{:S(2)}, u32[]{:S(2)}) collective-permute-start(f32[16,448]{1,0:T(8,128)S(1)} %get-tuple-element.39), channel_id=1, source_target_pairs={{0,25},{1,0},{2,1},{3,8},{4,9},{5,16},{6,17},{7,24},{8,27},{9,2},{... | collective-permute-start | bytes 86024 | tf_op jit(solution)/shard_map/ppermute | solution.py:237
  310.8 3.3 all-to-all-start.1
  314.1 4.3 %collective-permute-start.43 = (f32[16,448]{1,0:T(8,128)S(1)}, f32[16,448]{1,0:T(8,128)S(1)}, u32[]{:S(2)}, u32[]{:S(2)}) collective-permute-start(f32[16,448]{1,0:T(8,128)S(1)} %get-tuple-element.44), channel_id=1, source_target_pairs={{0,17},{1,24},{2,25},{3,0},{4,1},{5,8},{6,9},{7,16},{8,19},{9,26},... | collective-permute-start | bytes 86024 | tf_op jit(solution)/shard_map/ppermute | solution.py:237
  320.1 2.2 collective-permute-start.47
  323.8 3.7 %collective-permute-done.45 = f32[16,448]{1,0:T(8,128)S(1)} collective-permute-done((f32[16,448]{1,0:T(8,128)S(1)}, f32[16,448]{1,0:T(8,128)S(1)}, u32[]{:S(2)}, u32[]{:S(2)}) %collective-permute-start.45) | collective-permute-done | bytes 28704 | tf_op jit(solution)/shard_map/ppermute | solution.py:237
  (224 shorter events, 59.2 us)
Async XLA Ops:
  0.0 301.8 %copy-start = (bf16[896,1280]{1,0:T(8,128)(2,1)S(1)}, bf16[896,1280]{1,0:T(8,128)(2,1)}, u32[]{:S(2)}) copy-start(bf16[896,1280]{1,0:T(8,128)(2,1)} %param.24) | copy-start | bytes 6881284
  0.0 27.9 %copy-start.27 = (s32[2,8]{1,0:T(2,128)S(1)}, s32[2,8]{1,0:T(2,128)}, u32[]{:S(2)}) copy-start(s32[2,8]{1,0:T(2,128)} %param.14) | copy-start | bytes 196
  4.4 27.7 %collective-permute-start.2 = (bf16[896,384]{1,0:T(8,128)(2,1)}, bf16[896,384]{1,0:T(8,128)(2,1)S(1)}, u32[]{:S(2)}, u32[]{:S(2)}) collective-permute-start(bf16[896,384]{1,0:T(8,128)(2,1)} %pad_maximum_fusion.9), channel_id=1, source_target_pairs={{0,16},{8,24},{16,0},{24,8},{1,17},{9,25},{17,1},{25,9},{2,18},{10... | collective-permute-start | bytes 2064392 | tf_op jit(solution)/shard_map/ppermute | solution.py:45
  8.6 49.1 %collective-permute-start.48 = (s32[16]{0:T(128)}, s32[16]{0:T(128)}, u32[]{:S(2)}, u32[]{:S(2)}) collective-permute-start(s32[16]{0:T(128)} %reshape.147), channel_id=1, source_target_pairs={{0,16},{8,24},{16,0},{24,8},{1,17},{9,25},{17,1},{25,9},{2,18},{10... | collective-permute-start | bytes 200 | tf_op jit(solution)/shard_map/ppermute | solution.py:45
  8.6 49.1 %collective-permute-start = (s32[16]{0:T(128)}, s32[16]{0:T(128)}, u32[]{:S(2)}, u32[]{:S(2)}) collective-permute-start(s32[16]{0:T(128)} %bitcast.185), channel_id=1, source_target_pairs={{0,16},{8,24},{16,0},{24,8},{1,17},{9,25},{17,1},{25,9},{2,18},{10... | collective-permute-start | bytes 200 | tf_op jit(solution)/shard_map/ppermute | solution.py:45
  12.5 19.8 %copy-start.23 = (f32[3584]{0:T(1024)S(1)}, f32[3584]{0:T(1024)}, u32[]{:S(2)}) copy-start(f32[3584]{0:T(1024)} %param.16) | copy-start | bytes 43012
  15.4 17.1 %copy-start.24 = (f32[3584]{0:T(1024)S(1)}, f32[3584]{0:T(1024)}, u32[]{:S(2)}) copy-start(f32[3584]{0:T(1024)} %param.21) | copy-start | bytes 43012
  32.3 5.4 %collective-permute-start.3 = (bf16[2,896,384]{2,1,0:T(8,128)(2,1)S(1)}, bf16[2,896,384]{2,1,0:T(8,128)(2,1)S(1)}, u32[]{:S(2)}, u32[]{:S(2)}) collective-permute-start(bf16[2,896,384]{2,1,0:T(8,128)(2,1)S(1)} %pad_maximum_fusion.7), channel_id=1, source_target_pairs={{0,8},{8,0},{16,24},{24,16},{1,9},{9,1},{17,25},{25,17},{2,10},{10... | collective-permute-start | bytes 4128776 | tf_op jit(solution)/shard_map/ppermute | solution.py:48
  43.7 16.6 %slice-start = ((bf16[768,384]{0,1:T(8,128)(2,1)}), bf16[768,256]{0,1:T(8,128)(2,1)S(1)}, s32[]{:S(2)}) async-start(bf16[768,384]{0,1:T(8,128)(2,1)} %copy-done.22), calls=%async_computation.2 | async-start | bytes 786432 | tf_op jit(solution)/shard_map/slice | solution.py:150
  49.1 21.9 %all-to-all-start = ((bf16[8,768,32]{1,2,0:T(8,128)(2,1)}), bf16[8,768,32]{1,2,0:T(8,128)(2,1)S(1)}, u32[]{:S(2)}, u32[]{:S(2)}) async-start(bf16[8,768,32]{1,2,0:T(8,128)(2,1)} %fusion.41), calls=%async_computation | async-start | bytes 786432 | tf_op jit(solution)/shard_map/all_to_all | solution.py:164
  56.3 12.7 %collective-permute-start.4 = (bf16[896,256]{1,0:T(8,128)(2,1)S(1)}, bf16[896,256]{1,0:T(8,128)(2,1)}, u32[]{:S(2)}, u32[]{:S(2)}) collective-permute-start(bf16[896,256]{1,0:T(8,128)(2,1)S(1)} %copy-done.21), channel_id=1, source_target_pairs={{0,16},{8,24},{16,0},{24,8},{1,17},{9,25},{17,1},{25,9},{2,18},{10... | collective-permute-start | bytes 1376264 | tf_op jit(solution)/shard_map/ppermute | solution.py:45
  58.4 1.2 collective-permute-start.1
  58.5 240.2 %collective-permute-start.49 = (s32[2,16]{1,0:T(2,128)S(1)}, s32[2,16]{1,0:T(2,128)S(1)}, u32[]{:S(2)}, u32[]{:S(2)}) collective-permute-start(s32[2,16]{1,0:T(2,128)S(1)} %get-tuple-element.70), channel_id=1, source_target_pairs={{0,8},{8,0},{16,24},{24,16},{1,9},{9,1},{17,25},{25,17},{2,10},{10... | collective-permute-start | bytes 392 | tf_op jit(solution)/shard_map/ppermute | solution.py:48
  71.0 6.7 %collective-permute-start.5 = (bf16[2,896,256]{2,1,0:T(8,128)(2,1)}, bf16[2,896,256]{2,1,0:T(8,128)(2,1)}, u32[]{:S(2)}, u32[]{:S(2)}) collective-permute-start(bf16[2,896,256]{2,1,0:T(8,128)(2,1)} %pad_maximum_fusion.8), channel_id=1, source_target_pairs={{0,8},{8,0},{16,24},{24,16},{1,9},{9,1},{17,25},{25,17},{2,10},{10... | collective-permute-start | bytes 2752520 | tf_op jit(solution)/shard_map/ppermute | solution.py:48
  84.3 10.5 %collective-permute-start.6 = (bf16[96,1792]{1,0:T(8,128)(2,1)S(1)}, bf16[96,1792]{1,0:T(8,128)(2,1)S(1)}, u32[]{:S(2)}, u32[]{:S(2)}) collective-permute-start(bf16[96,1792]{1,0:T(8,128)(2,1)S(1)} %constant_dynamic-slice_fusion.3), channel_id=1, source_target_pairs={{0,2},{2,4},{4,6},{6,7},{7,5},{5,3},{3,1},{1,0},{8,10},{10,12},{12... | collective-permute-start | bytes 1032200 | tf_op jit(solution)/shard_map/ppermute | solution.py:90
  86.3 22.7 %copy-start.10 = (bf16[768,1792]{1,0:T(8,128)(2,1)S(1)}, bf16[768,1792]{1,0:T(8,128)(2,1)}, u32[]{:S(2)}) copy-start(bf16[768,1792]{1,0:T(8,128)(2,1)} %get-tuple-element.30) | copy-start | bytes 8257540
  86.3 58.1 %collective-permute-start.20 = (bf16[896,1280]{1,0:T(8,128)(2,1)}, bf16[896,1280]{1,0:T(8,128)(2,1)S(1)}, u32[]{:S(2)}, u32[]{:S(2)}) collective-permute-start(bf16[896,1280]{1,0:T(8,128)(2,1)} %param.22), channel_id=1, source_target_pairs={{0,16},{8,24},{16,0},{24,8},{1,17},{9,25},{17,1},{25,9},{2,18},{10... | collective-permute-start | bytes 6881288 | tf_op jit(solution)/shard_map/ppermute | solution.py:45
  86.9 100.8 %collective-permute-start.22 = (bf16[896,1280]{1,0:T(8,128)(2,1)}, bf16[896,1280]{1,0:T(8,128)(2,1)S(1)}, u32[]{:S(2)}, u32[]{:S(2)}) collective-permute-start(bf16[896,1280]{1,0:T(8,128)(2,1)} %param.23), channel_id=1, source_target_pairs={{0,16},{8,24},{16,0},{24,8},{1,17},{9,25},{17,1},{25,9},{2,18},{10... | collective-permute-start | bytes 6881288 | tf_op jit(solution)/shard_map/ppermute | solution.py:45
  89.4 9.7 %collective-permute-start.24 = (bf16[96,1792]{1,0:T(8,128)(2,1)S(1)}, bf16[96,1792]{1,0:T(8,128)(2,1)S(1)}, u32[]{:S(2)}, u32[]{:S(2)}) collective-permute-start(bf16[96,1792]{1,0:T(8,128)(2,1)S(1)} %constant_dynamic-slice_fusion.2), channel_id=1, source_target_pairs={{0,1},{2,0},{4,2},{6,4},{7,6},{5,7},{3,5},{1,3},{8,9},{10,8},{12,1... | collective-permute-start | bytes 1032200 | tf_op jit(solution)/shard_map/ppermute | solution.py:90
  95.9 29.1 %copy-start.12 = (bf16[768,1792]{1,0:T(8,128)(2,1)S(1)}, bf16[768,1792]{1,0:T(8,128)(2,1)}, u32[]{:S(2)}) copy-start(bf16[768,1792]{1,0:T(8,128)(2,1)} %copy-done.11) | copy-start | bytes 8257540
  95.9 9.8 %collective-permute-start.7 = (bf16[96,1792]{1,0:T(8,128)(2,1)S(1)}, bf16[96,1792]{1,0:T(8,128)(2,1)S(1)}, u32[]{:S(2)}, u32[]{:S(2)}) collective-permute-start(bf16[96,1792]{1,0:T(8,128)(2,1)S(1)} %add_convert_fusion.13), channel_id=1, source_target_pairs={{0,2},{2,4},{4,6},{6,7},{7,5},{5,3},{3,1},{1,0},{8,10},{10,12},{12... | collective-permute-start | bytes 1032200 | tf_op jit(solution)/shard_map/ppermute | solution.py:90
  100.2 8.8 %collective-permute-start.25 = (bf16[96,1792]{1,0:T(8,128)(2,1)S(1)}, bf16[96,1792]{1,0:T(8,128)(2,1)S(1)}, u32[]{:S(2)}, u32[]{:S(2)}) collective-permute-start(bf16[96,1792]{1,0:T(8,128)(2,1)S(1)} %add_convert_fusion.6), channel_id=1, source_target_pairs={{0,1},{2,0},{4,2},{6,4},{7,6},{5,7},{3,5},{1,3},{8,9},{10,8},{12,1... | collective-permute-start | bytes 1032200 | tf_op jit(solution)/shard_map/ppermute | solution.py:90
  106.8 8.9 %collective-permute-start.8 = (bf16[96,1792]{1,0:T(8,128)(2,1)S(1)}, bf16[96,1792]{1,0:T(8,128)(2,1)S(1)}, u32[]{:S(2)}, u32[]{:S(2)}) collective-permute-start(bf16[96,1792]{1,0:T(8,128)(2,1)S(1)} %add_convert_fusion.12), channel_id=1, source_target_pairs={{0,2},{2,4},{4,6},{6,7},{7,5},{5,3},{3,1},{1,0},{8,10},{10,12},{12... | collective-permute-start | bytes 1032200 | tf_op jit(solution)/shard_map/ppermute | solution.py:90
  109.1 9.6 %collective-permute-start.26 = (bf16[96,1792]{1,0:T(8,128)(2,1)S(1)}, bf16[96,1792]{1,0:T(8,128)(2,1)S(1)}, u32[]{:S(2)}, u32[]{:S(2)}) collective-permute-start(bf16[96,1792]{1,0:T(8,128)(2,1)S(1)} %add_convert_fusion.5), channel_id=1, source_target_pairs={{0,1},{2,0},{4,2},{6,4},{7,6},{5,7},{3,5},{1,3},{8,9},{10,8},{12,1... | collective-permute-start | bytes 1032200 | tf_op jit(solution)/shard_map/ppermute | solution.py:90
  116.7 8.3 %collective-permute-start.9 = (bf16[96,1792]{1,0:T(8,128)(2,1)S(1)}, bf16[96,1792]{1,0:T(8,128)(2,1)S(1)}, u32[]{:S(2)}, u32[]{:S(2)}) collective-permute-start(bf16[96,1792]{1,0:T(8,128)(2,1)S(1)} %add_convert_fusion.11), channel_id=1, source_target_pairs={{0,2},{2,4},{4,6},{6,7},{7,5},{5,3},{3,1},{1,0},{8,10},{10,12},{12... | collective-permute-start | bytes 1032200 | tf_op jit(solution)/shard_map/ppermute | solution.py:90
  118.7 25.7 %copy-start.13 = (bf16[896,1280]{1,0:T(8,128)(2,1)S(1)}, bf16[896,1280]{1,0:T(8,128)(2,1)}, u32[]{:S(2)}) copy-start(bf16[896,1280]{1,0:T(8,128)(2,1)} %param.22) | copy-start | bytes 6881284
  118.8 8.1 %collective-permute-start.27 = (bf16[96,1792]{1,0:T(8,128)(2,1)S(1)}, bf16[96,1792]{1,0:T(8,128)(2,1)S(1)}, u32[]{:S(2)}, u32[]{:S(2)}) collective-permute-start(bf16[96,1792]{1,0:T(8,128)(2,1)S(1)} %add_convert_fusion.4), channel_id=1, source_target_pairs={{0,1},{2,0},{4,2},{6,4},{7,6},{5,7},{3,5},{1,3},{8,9},{10,8},{12,1... | collective-permute-start | bytes 1032200 | tf_op jit(solution)/shard_map/ppermute | solution.py:90
  125.1 8.3 %collective-permute-start.10 = (bf16[96,1792]{1,0:T(8,128)(2,1)S(1)}, bf16[96,1792]{1,0:T(8,128)(2,1)S(1)}, u32[]{:S(2)}, u32[]{:S(2)}) collective-permute-start(bf16[96,1792]{1,0:T(8,128)(2,1)S(1)} %add_convert_fusion.10), channel_id=1, source_target_pairs={{0,2},{2,4},{4,6},{6,7},{7,5},{5,3},{3,1},{1,0},{8,10},{10,12},{12... | collective-permute-start | bytes 1032200 | tf_op jit(solution)/shard_map/ppermute | solution.py:90
  127.0 8.6 %collective-permute-start.28 = (bf16[96,1792]{1,0:T(8,128)(2,1)S(1)}, bf16[96,1792]{1,0:T(8,128)(2,1)S(1)}, u32[]{:S(2)}, u32[]{:S(2)}) collective-permute-start(bf16[96,1792]{1,0:T(8,128)(2,1)S(1)} %add_convert_fusion.3), channel_id=1, source_target_pairs={{0,1},{2,0},{4,2},{6,4},{7,6},{5,7},{3,5},{1,3},{8,9},{10,8},{12,1... | collective-permute-start | bytes 1032200 | tf_op jit(solution)/shard_map/ppermute | solution.py:90
  133.5 9.1 %collective-permute-start.11 = (bf16[96,1792]{1,0:T(8,128)(2,1)S(1)}, bf16[96,1792]{1,0:T(8,128)(2,1)S(1)}, u32[]{:S(2)}, u32[]{:S(2)}) collective-permute-start(bf16[96,1792]{1,0:T(8,128)(2,1)S(1)} %add_convert_fusion.9), channel_id=1, source_target_pairs={{0,2},{2,4},{4,6},{6,7},{7,5},{5,3},{3,1},{1,0},{8,10},{10,12},{12... | collective-permute-start | bytes 1032200 | tf_op jit(solution)/shard_map/ppermute | solution.py:90
  135.6 11.7 %collective-permute-start.29 = (bf16[96,1792]{1,0:T(8,128)(2,1)S(1)}, bf16[96,1792]{1,0:T(8,128)(2,1)S(1)}, u32[]{:S(2)}, u32[]{:S(2)}) collective-permute-start(bf16[96,1792]{1,0:T(8,128)(2,1)S(1)} %add_convert_fusion.2), channel_id=1, source_target_pairs={{0,1},{2,0},{4,2},{6,4},{7,6},{5,7},{3,5},{1,3},{8,9},{10,8},{12,1... | collective-permute-start | bytes 1032200 | tf_op jit(solution)/shard_map/ppermute | solution.py:90
  142.6 7.3 %collective-permute-start.12 = (bf16[96,1792]{1,0:T(8,128)(2,1)S(1)}, bf16[96,1792]{1,0:T(8,128)(2,1)S(1)}, u32[]{:S(2)}, u32[]{:S(2)}) collective-permute-start(bf16[96,1792]{1,0:T(8,128)(2,1)S(1)} %add_convert_fusion.8), channel_id=1, source_target_pairs={{0,2},{2,4},{4,6},{6,7},{7,5},{5,3},{3,1},{1,0},{8,10},{10,12},{12... | collective-permute-start | bytes 1032200 | tf_op jit(solution)/shard_map/ppermute | solution.py:90
  147.3 99.1 %collective-permute-start.21 = (bf16[2,896,1280]{2,1,0:T(8,128)(2,1)}, bf16[2,896,1280]{2,1,0:T(8,128)(2,1)}, u32[]{:S(2)}, u32[]{:S(2)}) collective-permute-start(bf16[2,896,1280]{2,1,0:T(8,128)(2,1)} %pad_maximum_fusion.3), channel_id=1, source_target_pairs={{0,8},{8,0},{16,24},{24,16},{1,9},{9,1},{17,25},{25,17},{2,10},{10... | collective-permute-start | bytes 13762568 | tf_op jit(solution)/shard_map/ppermute | solution.py:48
  147.4 10.5 %collective-permute-start.30 = (bf16[96,1792]{1,0:T(8,128)(2,1)S(1)}, bf16[96,1792]{1,0:T(8,128)(2,1)S(1)}, u32[]{:S(2)}, u32[]{:S(2)}) collective-permute-start(bf16[96,1792]{1,0:T(8,128)(2,1)S(1)} %add_convert_fusion.1), channel_id=1, source_target_pairs={{0,1},{2,0},{4,2},{6,4},{7,6},{5,7},{3,5},{1,3},{8,9},{10,8},{12,1... | collective-permute-start | bytes 1032200 | tf_op jit(solution)/shard_map/ppermute | solution.py:90
  151.6 36.1 %copy-start.15 = (bf16[896,1280]{1,0:T(8,128)(2,1)S(1)}, bf16[896,1280]{1,0:T(8,128)(2,1)}, u32[]{:S(2)}) copy-start(bf16[896,1280]{1,0:T(8,128)(2,1)} %param.23) | copy-start | bytes 6881284
  152.4 38.5 %collective-permute-start.13 = (bf16[96,1792]{1,0:T(8,128)(2,1)S(1)}, bf16[96,1792]{1,0:T(8,128)(2,1)S(1)}, u32[]{:S(2)}, u32[]{:S(2)}) collective-permute-start(bf16[96,1792]{1,0:T(8,128)(2,1)S(1)} %get-tuple-element.26), channel_id=1, source_target_pairs={{0,2},{2,4},{4,6},{6,7},{7,5},{5,3},{3,1},{1,0},{8,10},{10,12},{12... | collective-permute-start | bytes 1032200 | tf_op jit(solution)/shard_map/ppermute | solution.py:96
  160.6 31.9 %collective-permute-start.31 = (bf16[96,1792]{1,0:T(8,128)(2,1)}, bf16[96,1792]{1,0:T(8,128)(2,1)S(1)}, u32[]{:S(2)}, u32[]{:S(2)}) collective-permute-start(bf16[96,1792]{1,0:T(8,128)(2,1)} %get-tuple-element.28), channel_id=1, source_target_pairs={{0,1},{2,0},{4,2},{6,4},{7,6},{5,7},{3,5},{1,3},{8,9},{10,8},{12,1... | collective-permute-start | bytes 1032200 | tf_op jit(solution)/shard_map/ppermute | solution.py:96
  190.6 63.8 %collective-permute-start.23 = (bf16[2,896,1280]{2,1,0:T(8,128)(2,1)}, bf16[2,896,1280]{2,1,0:T(8,128)(2,1)}, u32[]{:S(2)}, u32[]{:S(2)}) collective-permute-start(bf16[2,896,1280]{2,1,0:T(8,128)(2,1)} %pad_maximum_fusion.4), channel_id=1, source_target_pairs={{0,8},{8,0},{16,24},{24,16},{1,9},{9,1},{17,25},{25,17},{2,10},{10... | collective-permute-start | bytes 13762568 | tf_op jit(solution)/shard_map/ppermute | solution.py:48
  190.9 10.5 %collective-permute-start.14 = (bf16[96,1792]{1,0:T(8,128)(2,1)S(1)}, bf16[96,1792]{1,0:T(8,128)(2,1)S(1)}, u32[]{:S(2)}, u32[]{:S(2)}) collective-permute-start(bf16[96,1792]{1,0:T(8,128)(2,1)S(1)} %collective-permute-done.13), channel_id=1, source_target_pairs={{0,2},{2,4},{4,6},{6,7},{7,5},{5,3},{3,1},{1,0},{8,10},{10,12},{12... | collective-permute-start | bytes 1032200 | tf_op jit(solution)/shard_map/ppermute | solution.py:96
  192.5 10.5 %collective-permute-start.32 = (bf16[96,1792]{1,0:T(8,128)(2,1)S(1)}, bf16[96,1792]{1,0:T(8,128)(2,1)S(1)}, u32[]{:S(2)}, u32[]{:S(2)}) collective-permute-start(bf16[96,1792]{1,0:T(8,128)(2,1)S(1)} %collective-permute-done.31), channel_id=1, source_target_pairs={{0,1},{2,0},{4,2},{6,4},{7,6},{5,7},{3,5},{1,3},{8,9},{10,8},{12,1... | collective-permute-start | bytes 1032200 | tf_op jit(solution)/shard_map/ppermute | solution.py:96
  201.5 9.7 %collective-permute-start.15 = (bf16[96,1792]{1,0:T(8,128)(2,1)S(1)}, bf16[96,1792]{1,0:T(8,128)(2,1)S(1)}, u32[]{:S(2)}, u32[]{:S(2)}) collective-permute-start(bf16[96,1792]{1,0:T(8,128)(2,1)S(1)} %collective-permute-done.14), channel_id=1, source_target_pairs={{0,2},{2,4},{4,6},{6,7},{7,5},{5,3},{3,1},{1,0},{8,10},{10,12},{12... | collective-permute-start | bytes 1032200 | tf_op jit(solution)/shard_map/ppermute | solution.py:96
  202.9 9.7 %collective-permute-start.33 = (bf16[96,1792]{1,0:T(8,128)(2,1)S(1)}, bf16[96,1792]{1,0:T(8,128)(2,1)S(1)}, u32[]{:S(2)}, u32[]{:S(2)}) collective-permute-start(bf16[96,1792]{1,0:T(8,128)(2,1)S(1)} %collective-permute-done.32), channel_id=1, source_target_pairs={{0,1},{2,0},{4,2},{6,4},{7,6},{5,7},{3,5},{1,3},{8,9},{10,8},{12,1... | collective-permute-start | bytes 1032200 | tf_op jit(solution)/shard_map/ppermute | solution.py:96
  211.2 8.8 %collective-permute-start.16 = (bf16[96,1792]{1,0:T(8,128)(2,1)S(1)}, bf16[96,1792]{1,0:T(8,128)(2,1)S(1)}, u32[]{:S(2)}, u32[]{:S(2)}) collective-permute-start(bf16[96,1792]{1,0:T(8,128)(2,1)S(1)} %collective-permute-done.15), channel_id=1, source_target_pairs={{0,2},{2,4},{4,6},{6,7},{7,5},{5,3},{3,1},{1,0},{8,10},{10,12},{12... | collective-permute-start | bytes 1032200 | tf_op jit(solution)/shard_map/ppermute | solution.py:96
  212.6 8.8 %collective-permute-start.34 = (bf16[96,1792]{1,0:T(8,128)(2,1)S(1)}, bf16[96,1792]{1,0:T(8,128)(2,1)S(1)}, u32[]{:S(2)}, u32[]{:S(2)}) collective-permute-start(bf16[96,1792]{1,0:T(8,128)(2,1)S(1)} %collective-permute-done.33), channel_id=1, source_target_pairs={{0,1},{2,0},{4,2},{6,4},{7,6},{5,7},{3,5},{1,3},{8,9},{10,8},{12,1... | collective-permute-start | bytes 1032200 | tf_op jit(solution)/shard_map/ppermute | solution.py:96
  213.9 32.4 %copy-start.14 = (bf16[896,1280]{1,0:T(8,128)(2,1)S(1)}, bf16[896,1280]{1,0:T(8,128)(2,1)}, u32[]{:S(2)}) copy-start(bf16[896,1280]{1,0:T(8,128)(2,1)} %param.22) | copy-start | bytes 6881284
  213.9 32.4 %copy-start.20 = (bf16[896,1280]{1,0:T(8,128)(2,1)S(1)}, bf16[896,1280]{1,0:T(8,128)(2,1)}, u32[]{:S(2)}) copy-start(bf16[896,1280]{1,0:T(8,128)(2,1)} %copy-done.19) | copy-start | bytes 6881284
  220.0 8.2 %collective-permute-start.17 = (bf16[96,1792]{1,0:T(8,128)(2,1)S(1)}, bf16[96,1792]{1,0:T(8,128)(2,1)S(1)}, u32[]{:S(2)}, u32[]{:S(2)}) collective-permute-start(bf16[96,1792]{1,0:T(8,128)(2,1)S(1)} %collective-permute-done.16), channel_id=1, source_target_pairs={{0,2},{2,4},{4,6},{6,7},{7,5},{5,3},{3,1},{1,0},{8,10},{10,12},{12... | collective-permute-start | bytes 1032200 | tf_op jit(solution)/shard_map/ppermute | solution.py:96
  221.4 8.2 %collective-permute-start.35 = (bf16[96,1792]{1,0:T(8,128)(2,1)S(1)}, bf16[96,1792]{1,0:T(8,128)(2,1)S(1)}, u32[]{:S(2)}, u32[]{:S(2)}) collective-permute-start(bf16[96,1792]{1,0:T(8,128)(2,1)S(1)} %collective-permute-done.34), channel_id=1, source_target_pairs={{0,1},{2,0},{4,2},{6,4},{7,6},{5,7},{3,5},{1,3},{8,9},{10,8},{12,1... | collective-permute-start | bytes 1032200 | tf_op jit(solution)/shard_map/ppermute | solution.py:96
  228.2 8.7 %collective-permute-start.18 = (bf16[96,1792]{1,0:T(8,128)(2,1)S(1)}, bf16[96,1792]{1,0:T(8,128)(2,1)S(1)}, u32[]{:S(2)}, u32[]{:S(2)}) collective-permute-start(bf16[96,1792]{1,0:T(8,128)(2,1)S(1)} %collective-permute-done.17), channel_id=1, source_target_pairs={{0,2},{2,4},{4,6},{6,7},{7,5},{5,3},{3,1},{1,0},{8,10},{10,12},{12... | collective-permute-start | bytes 1032200 | tf_op jit(solution)/shard_map/ppermute | solution.py:96
  229.7 8.7 %collective-permute-start.36 = (bf16[96,1792]{1,0:T(8,128)(2,1)S(1)}, bf16[96,1792]{1,0:T(8,128)(2,1)S(1)}, u32[]{:S(2)}, u32[]{:S(2)}) collective-permute-start(bf16[96,1792]{1,0:T(8,128)(2,1)S(1)} %collective-permute-done.35), channel_id=1, source_target_pairs={{0,1},{2,0},{4,2},{6,4},{7,6},{5,7},{3,5},{1,3},{8,9},{10,8},{12,1... | collective-permute-start | bytes 1032200 | tf_op jit(solution)/shard_map/ppermute | solution.py:96
  236.9 22.6 %collective-permute-start.19 = (bf16[96,1792]{1,0:T(8,128)(2,1)S(1)}, bf16[96,1792]{1,0:T(8,128)(2,1)S(1)}, u32[]{:S(2)}, u32[]{:S(2)}) collective-permute-start(bf16[96,1792]{1,0:T(8,128)(2,1)S(1)} %collective-permute-done.18), channel_id=1, source_target_pairs={{0,2},{2,4},{4,6},{6,7},{7,5},{5,3},{3,1},{1,0},{8,10},{10,12},{12... | collective-permute-start | bytes 1032200 | tf_op jit(solution)/shard_map/ppermute | solution.py:96
  238.3 7.3 %collective-permute-start.37 = (bf16[96,1792]{1,0:T(8,128)(2,1)S(1)}, bf16[96,1792]{1,0:T(8,128)(2,1)S(1)}, u32[]{:S(2)}, u32[]{:S(2)}) collective-permute-start(bf16[96,1792]{1,0:T(8,128)(2,1)S(1)} %collective-permute-done.36), channel_id=1, source_target_pairs={{0,1},{2,0},{4,2},{6,4},{7,6},{5,7},{3,5},{1,3},{8,9},{10,8},{12,1... | collective-permute-start | bytes 1032200 | tf_op jit(solution)/shard_map/ppermute | solution.py:96
  278.6 20.1 %copy-start.26 = (s32[1,16]{1,0:T(1,128)S(1)}, s32[1,16]{1,0:T(1,128)}, u32[]{:S(2)}) copy-start(s32[1,16]{1,0:T(1,128)} %stack_reshape.3) | copy-start | bytes 196
  294.2 4.4 %collective-permute-start.38 = (f32[16,1280]{1,0:T(8,128)S(1)}, f32[16,1280]{1,0:T(8,128)S(1)}, u32[]{:S(2)}, u32[]{:S(2)}) collective-permute-start(f32[16,1280]{1,0:T(8,128)S(1)} %fusion.9), channel_id=1, source_target_pairs={{0,16},{8,24},{16,0},{24,8},{1,17},{9,25},{17,1},{25,9},{2,18},{10... | collective-permute-start | bytes 245768 | tf_op jit(solution)/shard_map/ppermute | solution.py:45
  298.6 3.2 collective-permute-start.39
  304.4 15.1 %collective-permute-start.40 = (f32[16,448]{1,0:T(8,128)S(1)}, f32[16,448]{1,0:T(8,128)S(1)}, u32[]{:S(2)}, u32[]{:S(2)}) collective-permute-start(f32[16,448]{1,0:T(8,128)S(1)} %get-tuple-element.46), channel_id=1, source_target_pairs={{0,0},{1,1},{2,8},{3,9},{4,16},{5,17},{6,24},{7,25},{8,2},{9,3},{1... | collective-permute-start | bytes 86024 | tf_op jit(solution)/shard_map/ppermute | solution.py:237
  305.1 14.6 %collective-permute-start.41 = (f32[16,448]{1,0:T(8,128)S(1)}, f32[16,448]{1,0:T(8,128)S(1)}, u32[]{:S(2)}, u32[]{:S(2)}) collective-permute-start(f32[16,448]{1,0:T(8,128)S(1)} %get-tuple-element.39), channel_id=1, source_target_pairs={{0,25},{1,0},{2,1},{3,8},{4,9},{5,16},{6,17},{7,24},{8,27},{9,2},{... | collective-permute-start | bytes 86024 | tf_op jit(solution)/shard_map/ppermute | solution.py:237
  309.8 10.4 %collective-permute-start.42 = (f32[16,448]{1,0:T(8,128)S(1)}, f32[16,448]{1,0:T(8,128)S(1)}, u32[]{:S(2)}, u32[]{:S(2)}) collective-permute-start(f32[16,448]{1,0:T(8,128)S(1)} %get-tuple-element.45), channel_id=1, source_target_pairs={{0,24},{1,25},{2,0},{3,1},{4,8},{5,9},{6,16},{7,17},{8,26},{9,27},... | collective-permute-start | bytes 86024 | tf_op jit(solution)/shard_map/ppermute | solution.py:237
  310.8 11.7 %all-to-all-start.1 = ((f32[4,4,448]{2,1,0:T(4,128)}), f32[4,4,448]{2,1,0:T(4,128)S(1)}, u32[]{:S(2)}, u32[]{:S(2)}) async-start(f32[4,4,448]{2,1,0:T(4,128)} %fusion.51), calls=%async_computation.1 | async-start | bytes 65536 | tf_op jit(solution)/shard_map/all_to_all | solution.py:241
  314.1 8.4 %collective-permute-start.43 = (f32[16,448]{1,0:T(8,128)S(1)}, f32[16,448]{1,0:T(8,128)S(1)}, u32[]{:S(2)}, u32[]{:S(2)}) collective-permute-start(f32[16,448]{1,0:T(8,128)S(1)} %get-tuple-element.44), channel_id=1, source_target_pairs={{0,17},{1,24},{2,25},{3,0},{4,1},{5,8},{6,9},{7,16},{8,19},{9,26},... | collective-permute-start | bytes 86024 | tf_op jit(solution)/shard_map/ppermute | solution.py:237
  318.4 5.5 %collective-permute-start.44 = (f32[16,448]{1,0:T(8,128)S(1)}, f32[16,448]{1,0:T(8,128)S(1)}, u32[]{:S(2)}, u32[]{:S(2)}) collective-permute-start(f32[16,448]{1,0:T(8,128)S(1)} %get-tuple-element.43), channel_id=1, source_target_pairs={{0,16},{1,17},{2,24},{3,25},{4,0},{5,1},{6,8},{7,9},{8,18},{9,19},... | collective-permute-start | bytes 86024 | tf_op jit(solution)/shard_map/ppermute | solution.py:237
  319.5 8.0 %collective-permute-start.45 = (f32[16,448]{1,0:T(8,128)S(1)}, f32[16,448]{1,0:T(8,128)S(1)}, u32[]{:S(2)}, u32[]{:S(2)}) collective-permute-start(f32[16,448]{1,0:T(8,128)S(1)} %get-tuple-element.42), channel_id=1, source_target_pairs={{0,9},{1,16},{2,17},{3,24},{4,25},{5,0},{6,1},{7,8},{8,11},{9,18},... | collective-permute-start | bytes 86024 | tf_op jit(solution)/shard_map/ppermute | solution.py:237
  319.7 7.9 %collective-permute-start.46 = (f32[16,448]{1,0:T(8,128)S(1)}, f32[16,448]{1,0:T(8,128)S(1)}, u32[]{:S(2)}, u32[]{:S(2)}) collective-permute-start(f32[16,448]{1,0:T(8,128)S(1)} %get-tuple-element.41), channel_id=1, source_target_pairs={{0,8},{1,9},{2,16},{3,17},{4,24},{5,25},{6,0},{7,1},{8,10},{9,11},... | collective-permute-start | bytes 86024 | tf_op jit(solution)/shard_map/ppermute | solution.py:237
  320.1 7.4 %collective-permute-start.47 = (f32[16,448]{1,0:T(8,128)S(1)}, f32[16,448]{1,0:T(8,128)S(1)}, u32[]{:S(2)}, u32[]{:S(2)}) collective-permute-start(f32[16,448]{1,0:T(8,128)S(1)} %get-tuple-element.40), channel_id=1, source_target_pairs={{0,1},{1,8},{2,9},{3,16},{4,17},{5,24},{6,25},{7,0},{8,3},{9,10},{... | collective-permute-start | bytes 86024 | tf_op jit(solution)/shard_map/ppermute | solution.py:237
  (18 other events, 84.4 us)
